TPU v7x, 32 devices: a whole 2x2x4 slice. The times are simulated.
32 devices in a mesh: slab: 8 (over z, y), chan: 4 (over x, core).
Axes of the slice: x: 2, y: 2, z: 4, core: 2. Of those that a mesh axis runs over, the one named last changes fastest.
Arguments:
- image: bfloat16 [32, 256, 1024], P('slab', None, 'chan'), may hold values from -6 to 6
- weight: bfloat16 [3, 3, 1024, 1024], P(None, None, None, 'chan'), may hold values from -0.0625 to 0.0625
- grad_out: bfloat16 [32, 256, 1024], P('slab', 'chan'), may hold values from -6 to 6
Outputs:
- normed: bfloat16 [32, 256, 1024], P('slab', 'chan')
- grad_input: bfloat16 [32, 256, 1024], P('slab', None, 'chan')
- grad_weight: float32 [3, 3, 1024, 1024], P(None, None, 'slab', 'chan')
All inputs are finite; a program needn't handle non-finite values.
Results may differ from a plain program's by a relative error of at most 0.012.
Values may be sent and summed in bfloat16 or wider, within the bound.
No kernel may reach another device: no remote copies, remote signals or barrier semaphores. Data moves between devices by JAX's collectives and lax.ppermute only.
A program may use at most 128 MiB of HBM per device.

v0:
```python
import jax
import jax.numpy as jnp
from jax import lax
from jax.sharding import PartitionSpec as P


def with_halo(cells, sides, width):
    for axis, dim in sides:
        count = lax.axis_size(axis)
        ends = count - 1
        head = lax.slice_in_dim(cells, 0, width, axis=dim)
        tail = lax.slice_in_dim(cells, cells.shape[dim] - width, cells.shape[dim], axis=dim)
        cells = jnp.concatenate(
            [
                lax.ppermute(tail, axis, [(i, (i + 1) % count) for i in range(ends)]),
                cells,
                lax.ppermute(head, axis, [((i + 1) % count, i) for i in range(ends)]),
            ],
            axis=dim,
        )
    return cells


def on_device(image, weight, grad_out):
    height = image.shape[0]
    breadth = image.shape[1]
    all_chans = weight.shape[2]
    local_filters = weight.shape[3]
    rimmed = with_halo(image, (("slab", 0),), 1)
    padded = jnp.pad(rimmed, ((0, 0), (1, 1), (0, 0)))
    conv_zero = jnp.zeros((height * breadth, local_filters), jnp.float32)
    running = conv_zero
    shard_piece = lax.all_gather(padded, "chan", axis=2, tiled=True)
    width_in = shard_piece.shape[2]
    for forward_tap_row in range(3):
        for forward_tap_col in range(3):
            forward_window = shard_piece[
                forward_tap_row : forward_tap_row + height,
                forward_tap_col : forward_tap_col + breadth,
            ].reshape(height * breadth, width_in)
            taps = weight[forward_tap_row, forward_tap_col]
            running = running + jnp.dot(forward_window, taps, preferred_element_type=jnp.float32)
    conv_out = running.astype(jnp.bfloat16).reshape(height, breadth, local_filters)
    spread = lax.all_to_all(conv_out, "chan", split_axis=1, concat_axis=2, tiled=True)
    spread_wide = spread.astype(jnp.float32)
    inverse_rms = lax.rsqrt(jnp.mean(spread_wide * spread_wide, axis=-1, keepdims=True) + 1e-06)
    unit = spread_wide * inverse_rms
    normed = unit.astype(jnp.bfloat16)
    upstream = grad_out.astype(jnp.float32)
    grad_columns = (
        inverse_rms * (upstream - unit * jnp.mean(upstream * unit, axis=-1, keepdims=True))
    ).astype(jnp.bfloat16)
    grad_conv = lax.all_to_all(grad_columns, "chan", split_axis=2, concat_axis=1, tiled=True)
    grad_flat = grad_conv.reshape(height * breadth, local_filters)
    shard_piece = lax.all_gather(padded, "chan", axis=2, tiled=True)
    width_in = shard_piece.shape[2]
    blocks = []
    for weight_tap_row in range(3):
        for weight_tap_col in range(3):
            weight_window = shard_piece[
                weight_tap_row : weight_tap_row + height, weight_tap_col : weight_tap_col + breadth
            ].reshape(height * breadth, width_in)
            blocks.append(
                lax.dot_general(
                    weight_window,
                    grad_flat,
                    (((0,), (0,)), ((), ())),
                    preferred_element_type=jnp.float32,
                )
            )
    stacked = jnp.stack(blocks).reshape(3, 3, width_in, local_filters)
    grad_weight = lax.psum_scatter(
        stacked.astype(jnp.bfloat16), "slab", scatter_dimension=2, tiled=True
    ).astype(jnp.float32)
    grad_rimmed = with_halo(grad_conv, (("slab", 0),), 1)
    grad_padded = jnp.pad(grad_rimmed, ((0, 0), (1, 1), (0, 0)))
    input_term = jnp.zeros((height * breadth, all_chans), jnp.float32)
    for tap_row in range(3):
        for tap_col in range(3):
            window = grad_padded[
                2 - tap_row : 2 - tap_row + height, 2 - tap_col : 2 - tap_col + breadth
            ].reshape(height * breadth, local_filters)
            input_term = input_term + lax.dot_general(
                window,
                weight[tap_row, tap_col],
                (((1,), (1,)), ((), ())),
                preferred_element_type=jnp.float32,
            )
    input_sum = lax.psum_scatter(
        input_term.reshape(height, breadth, all_chans), "chan", scatter_dimension=2, tiled=True
    )
    grad_input = input_sum.astype(jnp.bfloat16)
    return (normed, grad_input, grad_weight)


def solution(mesh):
    return jax.shard_map(
        on_device,
        mesh=mesh,
        in_specs=(P("slab", None, "chan"), P(None, None, None, "chan"), P("slab", "chan", None)),
        out_specs=(P("slab", "chan", None), P("slab", None, "chan"), P(None, None, "slab", "chan")),
        check_vma=False,
    )
```

profile of v0, /device:TPU:4, one launch (start us, length us, event | category | flops | bytes accessed | tf_op | source)
XLA Modules:
  0.0 306.8 jit_solution(14523792158794297086)
XLA Ops:
  8.2 3.4 %collective-permute-start = (bf16[1,256,256]{2,1,0:T(8,128)(2,1)S(1)}, bf16[1,256,256]{2,1,0:T(8,128)(2,1)S(1)}, u32[]{:S(2)}, u32[]{:S(2)}) collective-permute-start(bf16[1,256,256]{2,1,0:T(8,128)(2,1)S(1)} %get-tuple-element.39), channel_id=1, source_target_pairs={{0,4},{4,8},{8,12},{12,16},{16,20},{20,24},{24,28},{1,5},{5,9},{9,... | collective-permute-start | bytes 393224 | tf_op jit(solution)/shard_map/ppermute | solution.py:15
  11.6 2.4 collective-permute-start.1
  15.3 4.1 %collective-permute-done.1 = bf16[1,256,256]{2,1,0:T(8,128)(2,1)S(1)} collective-permute-done((bf16[1,256,256]{2,1,0:T(8,128)(2,1)S(1)}, bf16[1,256,256]{2,1,0:T(8,128)(2,1)S(1)}, u32[]{:S(2)}, u32[]{:S(2)}) %collective-permute-start.1) | collective-permute-done | bytes 131104 | tf_op jit(solution)/shard_map/ppermute | solution.py:17
  21.5 29.8 %all-gather.2.cloned.1.call-done = bf16[6,258,1024]{2,1,0:T(8,128)(2,1)} async-done(((bf16[6,258,256]{2,1,0:T(8,128)(2,1)}), bf16[6,258,1024]{2,1,0:T(8,128)(2,1)}) %all-gather.2.cloned.1.call-update) | async-done | bytes 3170320 | tf_op jit(solution)/shard_map/all_gather | solution.py:33
  51.4 13.1 %fusion.70 = (bf16[4,256,1024]{2,1,0:T(8,128)(2,1)}, bf16[4,256,1024]{2,1,0:T(8,128)(2,1)S(1)}, bf16[4,256,1024]{2,1,0:T(8,128)(2,1)S(1)}, bf16[4,256,1024]{2,1,...) fusion(bf16[6,258,1024]{2,1,0:T(8,128)(2,1)} %all-gather.2.clon, ...), kind=kLoop, calls=%fused_computation.102 | loop fusion | bytes 37748736 | tf_op jit(solution)/shard_map/slice | solution.py:37
  64.6 4.5 %fusion.50 = f32[1024,256]{1,0:T(8,128)S(1)} fusion(bf16[1024,1024]{1,0:T(8,128)(2,1)} %bitcast.200, bf16[3,3,1024,256]{3,2,1,0:T(8,128)(2,1)} %param.4), kind=kOutput, calls=%fused_computation.80 | convolution fusion | flops 536870912 | bytes 3670016 | tf_op jit(solution)/shard_map/dot_general | solution.py:42
  69.1 4.3 %convolution_add_fusion.7 = f32[1024,256]{1,0:T(8,128)S(1)} fusion(f32[1024,256]{1,0:T(8,128)S(1)} %fusion.50, bf16[1024,1024]{1,0:T(8,128)(2,1)S(1)} %bitcast.174, bf16[3,3,1024,256]{3,2,1,0:T(8,128)(2,1)} %param.4), kind=kOutput, calls=%fused_computation.18 | convolution fusion | flops 537133056 | bytes 4718592 | tf_op jit(solution)/shard_map/dot_general | solution.py:42
  80.7 3.5 %all-to-all-start = ((bf16[4,256,256]{2,0,1:T(4,128)(2,1)}), bf16[4,256,256]{2,0,1:T(4,128)(2,1)S(1)}, u32[]{:S(2)}, u32[]{:S(2)}) async-start(bf16[4,256,256]{2,0,1:T(4,128)(2,1)} %copy.53), calls=%async_computation | async-start | bytes 1048576 | tf_op jit(solution)/shard_map/all_to_all | solution.py:44
  85.1 7.9 %all-to-all-done = bf16[4,256,256]{2,0,1:T(4,128)(2,1)S(1)} async-done(((bf16[4,256,256]{2,0,1:T(4,128)(2,1)}), bf16[4,256,256]{2,0,1:T(4,128)(2,1)S(1)}, u32[]{:S(2)}, u32[]{:S(2)}) %all-to-all-start) | async-done | bytes 524320 | tf_op jit(solution)/shard_map/all_to_all | solution.py:44
  97.6 2.4 fusion.2
  101.9 11.2 %all_to_all.27 = bf16[4,2,32768]{2,1,0:T(2,128)(2,1)S(1)} all-to-all(bf16[4,2,32768]{2,1,0:T(2,128)(2,1)S(1)} %reshape.123), channel_id=1, replica_groups=mesh['slab'=8,'chan'=4] {'chan'}, dimensions={0} | all-to-all | bytes 1048576 | tf_op jit(solution)/shard_map/all_to_all | solution.py:53
  115.5 2.5 collective-permute-start.3
  117.9 4.5 %collective-permute-start.2 = (bf16[1,256,256]{2,1,0:T(8,128)(2,1)S(1)}, bf16[1,256,256]{2,1,0:T(8,128)(2,1)S(1)}, u32[]{:S(2)}, u32[]{:S(2)}) collective-permute-start(bf16[1,256,256]{2,1,0:T(8,128)(2,1)S(1)} %bitcast.212), channel_id=1, source_target_pairs={{0,4},{4,8},{8,12},{12,16},{16,20},{20,24},{24,28},{1,5},{5,9},{9,... | collective-permute-start | bytes 393224 | tf_op jit(solution)/shard_map/ppermute | solution.py:15
  128.6 2.7 fusion.45
  131.3 2.7 fusion.33
  134.0 2.8 fusion.39
  136.7 2.7 fusion.42
  139.5 2.7 fusion.25
  142.2 11.7 %add_add_fusion = f32[1024,1024]{1,0:T(8,128)} fusion(f32[1024,1024]{1,0:T(8,128)} %fusion.25, f32[1024,1024]{1,0:T(8,128)S(1)} %fusion.30, f32[1024,1024]{1,0:T(8,128)} %fusion.33, f32[1024,1024]{1,0:T(8,128)S(1)} %fusion.36, f32[1024,1024]{1,0:T(8,128)} %fusion.39, f32[1024,1024]{1,0:T(8,128)} %fusion.42, f32[1024,1024]{1,0:T(8,128)S(1)} %fusion.48, ...), kind=kOutput, calls=%fused_computation | convolution fusion | flops 545259520 | bytes 38797312 | tf_op jit(solution)/shard_map/dot_general | solution.py:83
  154.2 2.5 fusion.7
  169.8 2.1 copy-done.14
  174.8 23.5 %reduce-scatter.3.cloned.1.call-done = f32[4,256,256]{2,1,0:T(8,128)} async-done(((f32[4,256,1024]{2,1,0:T(8,128)}), f32[4,256,256]{2,1,0:T(8,128)}) %reduce-scatter.3.cloned.1.call-update) | async-done | bytes 1048592 | tf_op jit(solution)/shard_map/reduce_scatter | solution.py:89
  200.4 97.7 %reduce-scatter.5.cloned.1.call-done = bf16[3,3,128,256]{3,2,1,0:T(8,128)(2,1)} async-done(((bf16[3,3,1024,256]{3,2,1,0:T(8,128)(2,1)}), bf16[3,3,128,256]{3,2,1,0:T(8,128)(2,1)}) %reduce-scatter.5.cloned.1.call-update) | async-done | bytes 589840 | tf_op jit(solution)/shard_map/reduce_scatter | solution.py:72
  298.1 2.2 convert_element_type.53
  (98 shorter events, 45.6 us)
Async XLA Ops:
  7.2 44.2 %all-gather.2.cloned.1.call-start = ((), (), s32[]{:S(2)}) async-start(), calls=%async_computation.4 | async-start | bytes 4055040 | tf_op jit(solution)/shard_map/all_gather | solution.py:33
  8.2 7.1 %collective-permute-start = (bf16[1,256,256]{2,1,0:T(8,128)(2,1)S(1)}, bf16[1,256,256]{2,1,0:T(8,128)(2,1)S(1)}, u32[]{:S(2)}, u32[]{:S(2)}) collective-permute-start(bf16[1,256,256]{2,1,0:T(8,128)(2,1)S(1)} %get-tuple-element.39), channel_id=1, source_target_pairs={{0,4},{4,8},{8,12},{12,16},{16,20},{20,24},{24,28},{1,5},{5,9},{9,... | collective-permute-start | bytes 393224 | tf_op jit(solution)/shard_map/ppermute | solution.py:15
  11.6 7.8 %collective-permute-start.1 = (bf16[1,256,256]{2,1,0:T(8,128)(2,1)S(1)}, bf16[1,256,256]{2,1,0:T(8,128)(2,1)S(1)}, u32[]{:S(2)}, u32[]{:S(2)}) collective-permute-start(bf16[1,256,256]{2,1,0:T(8,128)(2,1)S(1)} %get-tuple-element.40), channel_id=1, source_target_pairs={{4,0},{8,4},{12,8},{16,12},{20,16},{24,20},{28,24},{5,1},{9,5},{13... | collective-permute-start | bytes 393224 | tf_op jit(solution)/shard_map/ppermute | solution.py:17
  64.5 8.9 %copy-start.12 = (bf16[4,256,1024]{2,1,0:T(8,128)(2,1)}, bf16[4,256,1024]{2,1,0:T(8,128)(2,1)S(1)}, u32[]{:S(2)}) copy-start(bf16[4,256,1024]{2,1,0:T(8,128)(2,1)S(1)} %get-tuple-element.25) | copy-start | bytes 6291460
  64.5 8.9 %copy-start.10 = (bf16[4,256,1024]{2,1,0:T(8,128)(2,1)}, bf16[4,256,1024]{2,1,0:T(8,128)(2,1)S(1)}, u32[]{:S(2)}) copy-start(bf16[4,256,1024]{2,1,0:T(8,128)(2,1)S(1)} %get-tuple-element.24) | copy-start | bytes 6291460
  64.5 9.6 %copy-start.8 = (bf16[4,256,1024]{2,1,0:T(8,128)(2,1)}, bf16[4,256,1024]{2,1,0:T(8,128)(2,1)S(1)}, u32[]{:S(2)}) copy-start(bf16[4,256,1024]{2,1,0:T(8,128)(2,1)S(1)} %get-tuple-element.23) | copy-start | bytes 6291460
  64.5 10.4 %copy-start.6 = (bf16[4,256,1024]{2,1,0:T(8,128)(2,1)}, bf16[4,256,1024]{2,1,0:T(8,128)(2,1)S(1)}, u32[]{:S(2)}) copy-start(bf16[4,256,1024]{2,1,0:T(8,128)(2,1)S(1)} %get-tuple-element.22) | copy-start | bytes 6291460
  64.5 11.1 %copy-start.4 = (bf16[4,256,1024]{2,1,0:T(8,128)(2,1)}, bf16[4,256,1024]{2,1,0:T(8,128)(2,1)S(1)}, u32[]{:S(2)}) copy-start(bf16[4,256,1024]{2,1,0:T(8,128)(2,1)S(1)} %get-tuple-element.21) | copy-start | bytes 6291460
  64.5 11.8 %copy-start.2 = (bf16[4,256,1024]{2,1,0:T(8,128)(2,1)}, bf16[4,256,1024]{2,1,0:T(8,128)(2,1)S(1)}, u32[]{:S(2)}) copy-start(bf16[4,256,1024]{2,1,0:T(8,128)(2,1)S(1)} %get-tuple-element.20) | copy-start | bytes 6291460
  64.6 12.6 %copy-start = (bf16[4,256,1024]{2,1,0:T(8,128)(2,1)}, bf16[4,256,1024]{2,1,0:T(8,128)(2,1)S(1)}, u32[]{:S(2)}) copy-start(bf16[4,256,1024]{2,1,0:T(8,128)(2,1)S(1)} %get-tuple-element.19) | copy-start | bytes 6291460
  64.6 8.8 %slice-start = ((s8[4718592]{0:T(1024)(128)(4,1)}), s8[4194304]{0:T(1024)(128)(4,1)S(1)}, s32[]{:S(2)}) async-start(s8[4718592]{0:T(1024)(128)(4,1)} %bitcast.176), calls=%async_computation.7 | async-start | bytes 8388608
  69.1 4.3 %slice-start.1 = ((s8[4718592]{0:T(1024)(128)(4,1)}), s8[524288]{0:T(1024)(128)(4,1)S(1)}, s32[]{:S(2)}) async-start(s8[4718592]{0:T(1024)(128)(4,1)} %bitcast.176), calls=%async_computation.8 | async-start | bytes 1048576
  79.5 4.9 %copy-start.18 = (bf16[4,64,1024]{2,1,0:T(8,128)(2,1)S(1)}, bf16[4,64,1024]{2,1,0:T(8,128)(2,1)}, u32[]{:S(2)}) copy-start(bf16[4,64,1024]{2,1,0:T(8,128)(2,1)} %param.5) | copy-start | bytes 1572868
  80.7 12.3 %all-to-all-start = ((bf16[4,256,256]{2,0,1:T(4,128)(2,1)}), bf16[4,256,256]{2,0,1:T(4,128)(2,1)S(1)}, u32[]{:S(2)}, u32[]{:S(2)}) async-start(bf16[4,256,256]{2,0,1:T(4,128)(2,1)} %copy.53), calls=%async_computation | async-start | bytes 1048576 | tf_op jit(solution)/shard_map/all_to_all | solution.py:44
  84.2 114.1 %reduce-scatter.3.cloned.1.call-start = ((), (), s32[]{:S(2)}) async-start(), calls=%async_computation.5 | async-start | bytes 5242880 | tf_op jit(solution)/shard_map/reduce_scatter | solution.py:89
  115.5 8.9 %collective-permute-start.3 = (bf16[1,256,256]{2,1,0:T(8,128)(2,1)S(1)}, bf16[1,256,256]{2,1,0:T(8,128)(2,1)S(1)}, u32[]{:S(2)}, u32[]{:S(2)}) collective-permute-start(bf16[1,256,256]{2,1,0:T(8,128)(2,1)S(1)} %bitcast.213), channel_id=1, source_target_pairs={{4,0},{8,4},{12,8},{16,12},{20,16},{24,20},{28,24},{5,1},{9,5},{13... | collective-permute-start | bytes 393224 | tf_op jit(solution)/shard_map/ppermute | solution.py:17
  117.9 8.0 %collective-permute-start.2 = (bf16[1,256,256]{2,1,0:T(8,128)(2,1)S(1)}, bf16[1,256,256]{2,1,0:T(8,128)(2,1)S(1)}, u32[]{:S(2)}, u32[]{:S(2)}) collective-permute-start(bf16[1,256,256]{2,1,0:T(8,128)(2,1)S(1)} %bitcast.212), channel_id=1, source_target_pairs={{0,4},{4,8},{8,12},{12,16},{16,20},{20,24},{24,28},{1,5},{5,9},{9,... | collective-permute-start | bytes 393224 | tf_op jit(solution)/shard_map/ppermute | solution.py:15
  122.4 4.1 %slice-start.2 = ((s8[4718592]{0:T(1024)(128)(4,1)}), s8[4194304]{0:T(1024)(128)(4,1)S(1)}, s32[]{:S(2)}) async-start(s8[4718592]{0:T(1024)(128)(4,1)} %bitcast.178), calls=%async_computation.9 | async-start | bytes 8388608
  153.9 2.8 copy-start.13
  153.9 144.2 %reduce-scatter.5.cloned.1.call-start = ((), (), s32[]{:S(2)}) async-start(), calls=%async_computation.6 | async-start | bytes 5308416 | tf_op jit(solution)/shard_map/reduce_scatter | solution.py:72
  158.3 2.0 copy-start.9
  162.0 2.1 copy-start.5
  164.1 1.7 copy-start.3
  169.8 2.1 copy-start.14
  (7 other events, 10.6 us)
Sparse Core Ops, SparseCore 0:
  21.7 29.6 all-gather.1
  154.0 44.2 reduce-scatter.2
  202.4 95.6 reduce-scatter.4
where the time goes:
time: 309 us; the launch traced here: 307 us
  waiting for transfers between devices  166 us (54%)
  matrix products  51.1 us (17%)
  local copies, waits for them, and re-layouts  35.7 us (12%)
  starting transfers between devices  16.8 us (5%)
  between operations  14.3 us (5%)
  other arithmetic  11.8 us (4%)
  blocking collectives  11.2 us (4%)
    reduce_scatter x1, waiting for transfers between devices, on_device(): lax.psum_scatter(stacked.astype(jnp.bfloat16), 'slab', scatter_dimension=...  97.7 us
    all_gather x1, waiting for transfers between devices, on_device(): shard_piece = lax.all_gather(padded, 'chan', axis=2, tiled=True)  29.8 us
    dot_general x9, matrix products, on_device(): lax.dot_general(window, weight[tap_row, tap_col], (((1,), (1,)), ((), ())...  28.7 us
    reduce_scatter x1, waiting for transfers between devices, on_device(): lax.psum_scatter(input_term.reshape(height, breadth, all_chans), 'chan',...  23.5 us
    unnamed x50, local copies, waits for them, and re-layouts  16.5 us
    dot_general x9, matrix products, on_device(): jnp.dot(forward_window, taps, preferred_element_type=jnp.float32)  13.8 us
    slice x1, local copies, waits for them, and re-layouts, on_device(): shard_piece[forward_tap_row:forward_tap_row + height, forward_tap_col:for...  13.1 us
    all_to_all x1, blocking collectives, on_device(): lax.all_to_all(grad_columns, 'chan', split_axis=2, concat_axis=1, tiled=T...  11.2 us
  transfers between devices with their start and end apart: 8, of which 7 were waited for; matrix products, arithmetic and copies ran while one was open for 5% of the time, Pallas kernels for 0%

commit v1 on v0

v1 whole, which is shorter than its diff:
```python
import jax
import jax.numpy as jnp
from jax import lax
from jax.sharding import PartitionSpec as P


def with_halo(cells, sides, width):
    for axis, dim in sides:
        count = lax.axis_size(axis)
        ends = count - 1
        head = lax.slice_in_dim(cells, 0, width, axis=dim)
        tail = lax.slice_in_dim(cells, cells.shape[dim] - width, cells.shape[dim], axis=dim)
        cells = jnp.concatenate(
            [
                lax.ppermute(tail, axis, [(i, (i + 1) % count) for i in range(ends)]),
                cells,
                lax.ppermute(head, axis, [((i + 1) % count, i) for i in range(ends)]),
            ],
            axis=dim,
        )
    return cells


def on_device(image, weight, grad_out):
    height = image.shape[0]
    breadth = image.shape[1]
    all_chans = weight.shape[2]
    local_filters = weight.shape[3]
    all_filters = local_filters * lax.axis_size("chan")
    slabs = lax.axis_size("slab")

    grad_filters = lax.all_to_all(grad_out, "chan", split_axis=2, concat_axis=1, tiled=True)

    rimmed = with_halo(image, (("slab", 0),), 1)
    padded = jnp.pad(rimmed, ((0, 0), (1, 1), (0, 0)))
    shard_piece = lax.all_gather(padded, "chan", axis=2, tiled=True)
    width_in = shard_piece.shape[2]

    core_rows = shard_piece[1 : 1 + height]
    column_image = lax.all_to_all(core_rows, "slab", split_axis=2, concat_axis=0, tiled=True)
    column_image = jnp.pad(column_image, ((1, 1), (0, 0), (0, 0)))

    running = jnp.zeros((height * breadth, local_filters), jnp.float32)
    for forward_tap_row in range(3):
        for forward_tap_col in range(3):
            forward_window = shard_piece[
                forward_tap_row : forward_tap_row + height,
                forward_tap_col : forward_tap_col + breadth,
            ].reshape(height * breadth, width_in)
            taps = weight[forward_tap_row, forward_tap_col]
            running = running + jnp.dot(forward_window, taps, preferred_element_type=jnp.float32)
    conv_out = running.astype(jnp.bfloat16).reshape(height, breadth, local_filters)

    conv_wide = conv_out.astype(jnp.float32)
    upstream = grad_filters.astype(jnp.float32)
    partial = jnp.stack(
        [jnp.sum(conv_wide * conv_wide, axis=-1), jnp.sum(upstream * conv_wide, axis=-1)], axis=-1
    )
    totals = lax.psum(partial, "chan")
    inverse_rms = lax.rsqrt(totals[..., 0:1] / all_filters + 1e-06)
    mean_gu = inverse_rms * (totals[..., 1:2] / all_filters)
    unit = conv_wide * inverse_rms
    normed_filters = unit.astype(jnp.bfloat16)
    grad_conv = (inverse_rms * (upstream - unit * mean_gu)).astype(jnp.bfloat16)
    normed = lax.all_to_all(normed_filters, "chan", split_axis=1, concat_axis=2, tiled=True)

    grad_rows = lax.all_gather(grad_conv, "slab", axis=0, tiled=True)
    total_rows = grad_rows.shape[0]
    grad_rows_flat = grad_rows.reshape(total_rows * breadth, local_filters)
    width_w = column_image.shape[2]
    blocks = []
    for weight_tap_row in range(3):
        for weight_tap_col in range(3):
            weight_window = column_image[
                weight_tap_row : weight_tap_row + total_rows,
                weight_tap_col : weight_tap_col + breadth,
            ].reshape(total_rows * breadth, width_w)
            blocks.append(
                lax.dot_general(
                    weight_window,
                    grad_rows_flat,
                    (((0,), (0,)), ((), ())),
                    preferred_element_type=jnp.float32,
                )
            )
    grad_weight = jnp.stack(blocks).reshape(3, 3, width_w, local_filters)

    grad_rimmed = with_halo(grad_conv, (("slab", 0),), 1)
    grad_padded = jnp.pad(grad_rimmed, ((0, 0), (1, 1), (0, 0)))
    input_term = jnp.zeros((height * breadth, all_chans), jnp.float32)
    for tap_row in range(3):
        for tap_col in range(3):
            window = grad_padded[
                2 - tap_row : 2 - tap_row + height, 2 - tap_col : 2 - tap_col + breadth
            ].reshape(height * breadth, local_filters)
            input_term = input_term + lax.dot_general(
                window,
                weight[tap_row, tap_col],
                (((1,), (1,)), ((), ())),
                preferred_element_type=jnp.float32,
            )
    grad_input = lax.psum_scatter(
        input_term.reshape(height, breadth, all_chans).astype(jnp.bfloat16),
        "chan",
        scatter_dimension=2,
        tiled=True,
    )
    return (normed, grad_input, grad_weight)


def solution(mesh):
    return jax.shard_map(
        on_device,
        mesh=mesh,
        in_specs=(P("slab", None, "chan"), P(None, None, None, "chan"), P("slab", "chan", None)),
        out_specs=(P("slab", "chan", None), P("slab", None, "chan"), P(None, None, "slab", "chan")),
        check_vma=False,
    )
```

time: 309 us -> 252 us (0.82)
  waiting for transfers between devices: 166 us -> 90.2 us
  matrix products: 51.1 us -> 67 us
  blocking collectives: 11.2 us -> 20.3 us
  other arithmetic: 11.8 us -> 4.13 us
  starting transfers between devices: 16.8 us -> 22 us
  local copies, waits for them, and re-layouts: 35.7 us -> 31.9 us
    reduce_scatter x2 -> x1, waiting for transfers between devices: 121 us -> 0.01 us  [on_device(): lax.psum_scatter(input_term.reshape(height, breadth, all_chans).astype(jn...]
    all_to_all x1 -> x2, waiting for transfers between devices: 7.85 us -> 69.7 us  [the longest x1 69.7 us: on_device(): lax.all_to_all(core_rows, 'slab', split_axis=2, concat_axis=0, tiled=True)]
    all_gather x1, waiting for transfers between devices: 29.8 us -> 15.1 us  [on_device(): shard_piece = lax.all_gather(padded, 'chan', axis=2, tiled=True)]
    unnamed x50 -> x29, local copies, waits for them, and re-layouts: 16.5 us -> 2.59 us
    dot_general x9, matrix products: 28.7 us -> 40.1 us  [on_device(): lax.dot_general(window, weight[tap_row, tap_col], (((1,), (1,)), ((), ())...]
    dot_general x9, matrix products: 8.56 us -> 17.3 us  [on_device(): lax.dot_general(weight_window, grad_rows_flat, (((0,), (0,)), ((), ())),...]
    all_to_all x1 -> x2, starting transfers between devices: 3.47 us -> 10 us  [the longest x1 5.87 us: on_device(): lax.all_to_all(core_rows, 'slab', split_axis=2, concat_axis=0, tiled=True)]
    convert_element_type x4 -> x2, other arithmetic: 7.77 us -> 1.48 us  [on_device(): grad_conv = (inverse_rms * (upstream - unit * mean_gu)).astype(jnp.bfloat16)]
  transfers between devices with their start and end apart: 8 -> 9, of which waited for: 7 -> 4; matrix products, arithmetic and copies ran while one was open for 5% -> 29% of each run, Pallas kernels for 0% -> 0%
where the time goes in v1:
time: 252 us; the launch traced here: 250 us
  waiting for transfers between devices  90.2 us (36%)
  matrix products  67 us (27%)
  local copies, waits for them, and re-layouts  31.9 us (13%)
  starting transfers between devices  22 us (9%)
  blocking collectives  20.3 us (8%)
  between operations  14.1 us (6%)
  other arithmetic  4.13 us (2%)
    all_to_all x1, waiting for transfers between devices, on_device(): lax.all_to_all(core_rows, 'slab', split_axis=2, concat_axis=0, tiled=True)  69.7 us
    dot_general x9, matrix products, on_device(): lax.dot_general(window, weight[tap_row, tap_col], (((1,), (1,)), ((), ())...  40.1 us
    dot_general x9, matrix products, on_device(): lax.dot_general(weight_window, grad_rows_flat, (((0,), (0,)), ((), ())),...  17.3 us
    all_gather x1, waiting for transfers between devices, on_device(): shard_piece = lax.all_gather(padded, 'chan', axis=2, tiled=True)  15.1 us
    all_to_all x1, blocking collectives, on_device(): lax.all_to_all(grad_out, 'chan', split_axis=2, concat_axis=1, tiled=True)  14.3 us
    slice x1, local copies, waits for them, and re-layouts, on_device(): shard_piece[forward_tap_row:forward_tap_row + height, forward_tap_col:for...  12.8 us
    dot_general x9, matrix products, on_device(): jnp.dot(forward_window, taps, preferred_element_type=jnp.float32)  9.54 us
    ppermute x2, starting transfers between devices, with_halo(): lax.ppermute(tail, axis, [(i, (i + 1) % count) for i in range(ends)])  6.48 us
  transfers between devices with their start and end apart: 9, of which 4 were waited for; matrix products, arithmetic and copies ran while one was open for 29% of the time, Pallas kernels for 0%

profile of v1, /device:TPU:4, one launch (start us, length us, event | category | flops | bytes accessed | tf_op | source)
XLA Modules:
  0.0 249.6 jit_solution(305388931405245149)
XLA Ops:
  8.3 3.4 %collective-permute-start = (bf16[1,256,256]{2,1,0:T(8,128)(2,1)S(1)}, bf16[1,256,256]{2,1,0:T(8,128)(2,1)S(1)}, u32[]{:S(2)}, u32[]{:S(2)}) collective-permute-start(bf16[1,256,256]{2,1,0:T(8,128)(2,1)S(1)} %get-tuple-element.24), channel_id=1, source_target_pairs={{0,4},{4,8},{8,12},{12,16},{16,20},{20,24},{24,28},{1,5},{5,9},{9,... | collective-permute-start | bytes 393224 | tf_op jit(solution)/shard_map/ppermute | solution.py:15
  15.4 4.1 %collective-permute-done.1 = bf16[1,256,256]{2,1,0:T(8,128)(2,1)S(1)} collective-permute-done((bf16[1,256,256]{2,1,0:T(8,128)(2,1)S(1)}, bf16[1,256,256]{2,1,0:T(8,128)(2,1)S(1)}, u32[]{:S(2)}, u32[]{:S(2)}) %collective-permute-start.1) | collective-permute-done | bytes 131104 | tf_op jit(solution)/shard_map/ppermute | solution.py:17
  23.2 14.3 %all_to_all.45 = bf16[4,2,32768]{2,1,0:T(2,128)(2,1)S(1)} all-to-all(bf16[4,2,32768]{2,1,0:T(2,128)(2,1)S(1)} %reshape.134), channel_id=1, replica_groups=mesh['slab'=8,'chan'=4] {'chan'}, dimensions={0} | all-to-all | bytes 1048576 | tf_op jit(solution)/shard_map/all_to_all | solution.py:32
  38.9 15.1 %all-gather.3.cloned.1.call-done = bf16[6,258,1024]{2,1,0:T(8,128)(2,1)} async-done(((bf16[6,258,256]{2,1,0:T(8,128)(2,1)}), bf16[6,258,1024]{2,1,0:T(8,128)(2,1)}) %all-gather.3.cloned.1.call-update) | async-done | bytes 3170320 | tf_op jit(solution)/shard_map/all_gather | solution.py:36
  54.0 12.8 %fusion.145 = (bf16[4,256,1024]{2,1,0:T(8,128)(2,1)S(1)}, bf16[4,256,1024]{2,1,0:T(8,128)(2,1)S(1)}, bf16[4,256,1024]{2,1,0:T(8,128)(2,1)S(1)}, bf16[4,256,1024]...) fusion(bf16[6,258,1024]{2,1,0:T(8,128)(2,1)} %all-gather.3.clon, ...), kind=kLoop, calls=%fused_computation.134 | loop fusion | bytes 37748736 | tf_op jit(solution)/shard_map/slice | solution.py:46
  66.8 2.5 %fusion.112 = f32[1024,256]{1,0:T(8,128)S(1)} fusion(bf16[1024,1024]{1,0:T(8,128)(2,1)} %bitcast.206, bf16[3,3,1024,256]{3,2,1,0:T(8,128)(2,1)} %param.4), kind=kOutput, calls=%fused_computation.98 | convolution fusion | flops 536870912 | bytes 3670016 | tf_op jit(solution)/shard_map/dot_general | solution.py:51
  77.1 6.0 %psum.7 = f32[4,256,2]{1,0,2:T(4,128)S(1)} all-reduce(f32[4,256,2]{1,0,2:T(4,128)S(1)} %pad_maximum_fusion.2), channel_id=1, replica_groups=mesh['slab'=8,'chan'=4] {'chan'}, use_global_device_ids=true, to_apply=%region_2.3 | all-reduce | flops 2048 | bytes 16384 | tf_op jit(solution)/shard_map/psum | solution.py:59
  85.9 3.1 %collective-permute-start.2 = (bf16[1,256,256]{2,1,0:T(8,128)(2,1)}, bf16[1,256,256]{2,1,0:T(8,128)(2,1)S(1)}, u32[]{:S(2)}, u32[]{:S(2)}) collective-permute-start(bf16[1,256,256]{2,1,0:T(8,128)(2,1)} %get-tuple-element.22), channel_id=1, source_target_pairs={{0,4},{4,8},{8,12},{12,16},{16,20},{20,24},{24,28},{1,5},{5,9},{9,... | collective-permute-start | bytes 393224 | tf_op jit(solution)/shard_map/ppermute | solution.py:15
  89.0 3.0 %collective-permute-start.3 = (bf16[1,256,256]{2,1,0:T(8,128)(2,1)}, bf16[1,256,256]{2,1,0:T(8,128)(2,1)S(1)}, u32[]{:S(2)}, u32[]{:S(2)}) collective-permute-start(bf16[1,256,256]{2,1,0:T(8,128)(2,1)} %get-tuple-element.23), channel_id=1, source_target_pairs={{4,0},{8,4},{12,8},{16,12},{20,16},{24,20},{28,24},{5,1},{9,5},{13... | collective-permute-start | bytes 393224 | tf_op jit(solution)/shard_map/ppermute | solution.py:17
  92.3 3.9 %fusion.98 = f32[1024,1024]{1,0:T(8,128)} fusion(bf16[1024,256]{1,0:T(8,128)(2,1)S(1)} %fusion.82, bf16[3,3,1024,256]{3,2,1,0:T(8,128)(2,1)} %param.4), kind=kOutput, calls=%fused_computation.84 | convolution fusion | flops 536870912 | bytes 5242880 | tf_op jit(solution)/shard_map/dot_general | solution.py:96
  97.8 3.8 %copy.23 = bf16[4,258,1024]{1,0,2:T(4,128)(2,1)} copy(bf16[4,258,1024]{2,1,0:T(8,128)(2,1)S(1)} %slice-done) | data formatting | bytes 4227072 | tf_op jit(solution)/shard_map/slice | solution.py:39
  102.8 4.1 %all-to-all-start.1 = ((bf16[4,256,256]{2,0,1:T(4,128)(2,1)}), bf16[4,256,256]{2,0,1:T(4,128)(2,1)}, u32[]{:S(2)}, u32[]{:S(2)}) async-start(bf16[4,256,256]{2,0,1:T(4,128)(2,1)} %copy.21), calls=%async_computation.1 | async-start | bytes 1048576 | tf_op jit(solution)/shard_map/all_to_all | solution.py:65
  108.5 3.8 %fusion.92 = f32[1024,1024]{1,0:T(8,128)} fusion(bf16[1024,256]{1,0:T(8,128)(2,1)S(1)} %bitcast.213, bf16[3,3,1024,256]{3,2,1,0:T(8,128)(2,1)} %param.4), kind=kOutput, calls=%fused_computation.78 | convolution fusion | flops 536870912 | bytes 5242880 | tf_op jit(solution)/shard_map/dot_general | solution.py:96
  112.4 3.8 %fusion.110 = f32[1024,1024]{1,0:T(8,128)} fusion(bf16[1024,256]{1,0:T(8,128)(2,1)S(1)} %bitcast.212, bf16[3,3,1024,256]{3,2,1,0:T(8,128)(2,1)} %param.4), kind=kOutput, calls=%fused_computation.96 | convolution fusion | flops 536870912 | bytes 5242880 | tf_op jit(solution)/shard_map/dot_general | solution.py:96
  116.2 5.9 %all-to-all-start.2 = ((bf16[4,258,1024]{1,0,2:T(4,128)(2,1)}), bf16[4,258,1024]{1,0,2:T(4,128)(2,1)}, u32[]{:S(2)}, u32[]{:S(2)}) async-start(bf16[4,258,1024]{1,0,2:T(4,128)(2,1)} %copy.23), calls=%async_computation.3 | async-start | bytes 6291456 | tf_op jit(solution)/shard_map/all_to_all | solution.py:40
  122.1 3.8 %fusion.107 = f32[1024,1024]{1,0:T(8,128)} fusion(bf16[1024,256]{1,0:T(8,128)(2,1)S(1)} %bitcast.211, bf16[3,3,1024,256]{3,2,1,0:T(8,128)(2,1)} %param.4), kind=kOutput, calls=%fused_computation.93 | convolution fusion | flops 536870912 | bytes 5242880 | tf_op jit(solution)/shard_map/dot_general | solution.py:96
  125.9 3.8 %fusion.95 = f32[1024,1024]{1,0:T(8,128)} fusion(bf16[1024,256]{1,0:T(8,128)(2,1)S(1)} %bitcast.210, bf16[3,3,1024,256]{3,2,1,0:T(8,128)(2,1)} %param.4), kind=kOutput, calls=%fused_computation.81 | convolution fusion | flops 536870912 | bytes 5242880 | tf_op jit(solution)/shard_map/dot_general | solution.py:96
  129.7 3.9 %fusion.101 = f32[1024,1024]{1,0:T(8,128)} fusion(bf16[1024,256]{1,0:T(8,128)(2,1)S(1)} %bitcast.209, bf16[3,3,1024,256]{3,2,1,0:T(8,128)(2,1)} %param.4), kind=kOutput, calls=%fused_computation.87 | convolution fusion | flops 536870912 | bytes 5242880 | tf_op jit(solution)/shard_map/dot_general | solution.py:96
  133.6 3.9 %fusion.104 = f32[1024,1024]{1,0:T(8,128)} fusion(bf16[1024,256]{1,0:T(8,128)(2,1)S(1)} %bitcast.208, bf16[3,3,1024,256]{3,2,1,0:T(8,128)(2,1)} %param.4), kind=kOutput, calls=%fused_computation.90 | convolution fusion | flops 536870912 | bytes 5242880 | tf_op jit(solution)/shard_map/dot_general | solution.py:96
  137.5 3.9 %fusion.87 = f32[1024,1024]{1,0:T(8,128)} fusion(bf16[1024,256]{1,0:T(8,128)(2,1)S(1)} %bitcast.207, bf16[3,3,1024,256]{3,2,1,0:T(8,128)(2,1)} %param.4), kind=kOutput, calls=%fused_computation.73 | convolution fusion | flops 536870912 | bytes 5242880 | tf_op jit(solution)/shard_map/dot_general | solution.py:96
  141.5 9.3 %add_convert_fusion = bf16[1024,1024]{1,0:T(8,128)(2,1)} fusion(f32[1024,1024]{1,0:T(8,128)} %fusion.87, f32[1024,1024]{1,0:T(8,128)S(1)} %copy-done.2, f32[1024,1024]{1,0:T(8,128)} %fusion.95, f32[1024,1024]{1,0:T(8,128)S(1)} %copy-done.1, f32[1024,1024]{1,0:T(8,128)} %fusion.101, f32[1024,1024]{1,0:T(8,128)} %fusion.104, f32[1024,1024]{1,0:T(8,128)S(1)} %copy-done.3, ...), kind=kOutput, calls=%fused_computation | convolution fusion | flops 546308096 | bytes 36700160 | tf_op jit(solution)/shard_map/dot_general | solution.py:96
  153.4 69.7 %all-to-all-done.2 = bf16[4,258,1024]{1,0,2:T(4,128)(2,1)} async-done(((bf16[4,258,1024]{1,0,2:T(4,128)(2,1)}), bf16[4,258,1024]{1,0,2:T(4,128)(2,1)}, u32[]{:S(2)}, u32[]{:S(2)}) %all-to-all-start.2) | async-done | bytes 2113568 | tf_op jit(solution)/shard_map/all_to_all | solution.py:40
  223.1 2.6 %copy.24 = bf16[4,258,8,128]{1,3,0,2:T(8,128)(2,1)S(1)} copy(bf16[4,258,8,128]{1,0,3,2:T(4,128)(2,1)} %bitcast.37) | data formatting | bytes 4227072 | tf_op jit(solution)/shard_map/all_to_all | solution.py:40
  225.7 3.9 %fusion.48 = f32[9,128,256]{2,1,0:T(8,128)} fusion(bf16[32,256,256]{2,1,0:T(8,128)(2,1)} %all-gather.5.cloned.1.call-done, bf16[32,258,128]{1,2,0:T(8,128)(2,1)S(1)} %bitcast.181), kind=kOutput, calls=%fused_computation.45 | convolution fusion | flops 536870912 | bytes 6438912 | tf_op jit(solution)/shard_map/dot_general | solution.py:79
  (78 shorter events, 41.2 us)
Async XLA Ops:
  7.2 14.5 %copy-start.9 = (bf16[4,64,1024]{2,1,0:T(8,128)(2,1)S(1)}, bf16[4,64,1024]{2,1,0:T(8,128)(2,1)}, u32[]{:S(2)}) copy-start(bf16[4,64,1024]{2,1,0:T(8,128)(2,1)} %param.5) | copy-start | bytes 1572868
  7.2 46.9 %all-gather.3.cloned.1.call-start = ((), (), s32[]{:S(2)}) async-start(), calls=%async_computation.4 | async-start | bytes 4055040 | tf_op jit(solution)/shard_map/all_gather | solution.py:36
  8.3 7.1 %collective-permute-start = (bf16[1,256,256]{2,1,0:T(8,128)(2,1)S(1)}, bf16[1,256,256]{2,1,0:T(8,128)(2,1)S(1)}, u32[]{:S(2)}, u32[]{:S(2)}) collective-permute-start(bf16[1,256,256]{2,1,0:T(8,128)(2,1)S(1)} %get-tuple-element.24), channel_id=1, source_target_pairs={{0,4},{4,8},{8,12},{12,16},{16,20},{20,24},{24,28},{1,5},{5,9},{9,... | collective-permute-start | bytes 393224 | tf_op jit(solution)/shard_map/ppermute | solution.py:15
  11.7 7.8 %collective-permute-start.1 = (bf16[1,256,256]{2,1,0:T(8,128)(2,1)S(1)}, bf16[1,256,256]{2,1,0:T(8,128)(2,1)S(1)}, u32[]{:S(2)}, u32[]{:S(2)}) collective-permute-start(bf16[1,256,256]{2,1,0:T(8,128)(2,1)S(1)} %get-tuple-element.25), channel_id=1, source_target_pairs={{4,0},{8,4},{12,8},{16,12},{20,16},{24,20},{28,24},{5,1},{9,5},{13... | collective-permute-start | bytes 393224 | tf_op jit(solution)/shard_map/ppermute | solution.py:17
  21.6 204.1 %all-gather.5.cloned.1.call-start = ((), (), s32[]{:S(2)}) async-start(), calls=%async_computation.6 | async-start | bytes 4718592 | tf_op jit(solution)/shard_map/all_gather | solution.py:67
  66.8 2.6 %copy-start.5 = (bf16[4,256,1024]{2,1,0:T(8,128)(2,1)S(1)}, bf16[4,256,1024]{2,1,0:T(8,128)(2,1)}, u32[]{:S(2)}) copy-start(bf16[4,256,1024]{2,1,0:T(8,128)(2,1)} %get-tuple-element.10) | copy-start | bytes 6291460
  66.8 4.5 %slice-start.1 = ((s8[4718592]{0:T(1024)(128)(4,1)}), s8[4194304]{0:T(1024)(128)(4,1)S(1)}, s32[]{:S(2)}) async-start(s8[4718592]{0:T(1024)(128)(4,1)} %bitcast.192), calls=%async_computation.8 | async-start | bytes 8388608
  69.4 1.9 slice-start.2
  69.4 2.2 copy-start.4
  85.9 21.0 %collective-permute-start.2 = (bf16[1,256,256]{2,1,0:T(8,128)(2,1)}, bf16[1,256,256]{2,1,0:T(8,128)(2,1)S(1)}, u32[]{:S(2)}, u32[]{:S(2)}) collective-permute-start(bf16[1,256,256]{2,1,0:T(8,128)(2,1)} %get-tuple-element.22), channel_id=1, source_target_pairs={{0,4},{4,8},{8,12},{12,16},{16,20},{20,24},{24,28},{1,5},{5,9},{9,... | collective-permute-start | bytes 393224 | tf_op jit(solution)/shard_map/ppermute | solution.py:15
  89.0 17.9 %collective-permute-start.3 = (bf16[1,256,256]{2,1,0:T(8,128)(2,1)}, bf16[1,256,256]{2,1,0:T(8,128)(2,1)S(1)}, u32[]{:S(2)}, u32[]{:S(2)}) collective-permute-start(bf16[1,256,256]{2,1,0:T(8,128)(2,1)} %get-tuple-element.23), channel_id=1, source_target_pairs={{4,0},{8,4},{12,8},{16,12},{20,16},{24,20},{28,24},{5,1},{9,5},{13... | collective-permute-start | bytes 393224 | tf_op jit(solution)/shard_map/ppermute | solution.py:17
  96.2 1.6 slice-start
  97.8 9.2 %copy-start.6 = (bf16[4,256,256]{2,1,0:T(8,128)(2,1)S(1)}, bf16[4,256,256]{2,1,0:T(8,128)(2,1)}, u32[]{:S(2)}) copy-start(bf16[4,256,256]{2,1,0:T(8,128)(2,1)} %get-tuple-element.12) | copy-start | bytes 1572868
  102.8 13.4 %all-to-all-start.1 = ((bf16[4,256,256]{2,0,1:T(4,128)(2,1)}), bf16[4,256,256]{2,0,1:T(4,128)(2,1)}, u32[]{:S(2)}, u32[]{:S(2)}) async-start(bf16[4,256,256]{2,0,1:T(4,128)(2,1)} %copy.21), calls=%async_computation.1 | async-start | bytes 1048576 | tf_op jit(solution)/shard_map/all_to_all | solution.py:65
  116.2 106.9 %all-to-all-start.2 = ((bf16[4,258,1024]{1,0,2:T(4,128)(2,1)}), bf16[4,258,1024]{1,0,2:T(4,128)(2,1)}, u32[]{:S(2)}, u32[]{:S(2)}) async-start(bf16[4,258,1024]{1,0,2:T(4,128)(2,1)} %copy.23), calls=%async_computation.3 | async-start | bytes 6291456 | tf_op jit(solution)/shard_map/all_to_all | solution.py:40
  122.1 120.9 %reduce-scatter.2.cloned.1.call-start = ((), (), s32[]{:S(2)}) async-start(), calls=%async_computation.5 | async-start | bytes 2621440 | tf_op jit(solution)/shard_map/reduce_scatter | solution.py:102
  125.9 3.8 %copy-start.8 = (bf16[4,256,256]{2,1,0:T(8,128)(2,1)S(1)}, bf16[4,256,256]{2,1,0:T(8,128)(2,1)}, u32[]{:S(2)}) copy-start(bf16[4,256,256]{2,1,0:T(8,128)(2,1)} %get-tuple-element.17) | copy-start | bytes 1572868
  129.7 3.9 %copy-start.7 = (bf16[4,256,256]{2,1,0:T(8,128)(2,1)S(1)}, bf16[4,256,256]{2,1,0:T(8,128)(2,1)}, u32[]{:S(2)}) copy-start(bf16[4,256,256]{2,1,0:T(8,128)(2,1)} %get-tuple-element.18) | copy-start | bytes 1572868
  129.7 11.7 %copy-start.3 = (f32[1024,1024]{1,0:T(8,128)S(1)}, f32[1024,1024]{1,0:T(8,128)}, u32[]{:S(2)}) copy-start(f32[1024,1024]{1,0:T(8,128)} %fusion.110) | copy-start | bytes 12582916
  133.6 7.8 %copy-start.2 = (f32[1024,1024]{1,0:T(8,128)S(1)}, f32[1024,1024]{1,0:T(8,128)}, u32[]{:S(2)}) copy-start(f32[1024,1024]{1,0:T(8,128)} %fusion.92) | copy-start | bytes 12582916
  137.5 3.9 %copy-start.1 = (f32[1024,1024]{1,0:T(8,128)S(1)}, f32[1024,1024]{1,0:T(8,128)}, u32[]{:S(2)}) copy-start(f32[1024,1024]{1,0:T(8,128)} %fusion.98) | copy-start | bytes 12582916
  225.7 4.0 %copy-start = (bf16[32,256,256]{2,1,0:T(8,128)(2,1)S(1)}, bf16[32,256,256]{2,1,0:T(8,128)(2,1)}, u32[]{:S(2)}) copy-start(bf16[32,256,256]{2,1,0:T(8,128)(2,1)} %all-gather.5.cloned.1.call-done) | copy-start | bytes 12582916
Sparse Core Ops, SparseCore 0:
  21.7 32.2 all-gather.2
  84.4 123.3 all-gather.4
  210.9 29.5 reduce-scatter.1

commit v2 on v1

v2 whole, which is shorter than its diff:
```python
import jax
import jax.numpy as jnp
from jax import lax
from jax.sharding import Mesh
from jax.sharding import PartitionSpec as P

SLAB = ("hi", "lo")


def shift_rows(rows, upward):
    count = lax.axis_size(SLAB)
    if upward:
        pairs = [((i + 1), i) for i in range(count - 1)]
    else:
        pairs = [(i, i + 1) for i in range(count - 1)]
    return lax.ppermute(rows, SLAB, pairs)


def with_halo(cells):
    top = shift_rows(cells[-1:], upward=False)
    bottom = shift_rows(cells[:1], upward=True)
    return jnp.concatenate([top, cells, bottom], axis=0)


def conv(lhs, rhs, rhs_spec):
    out = lax.conv_general_dilated(
        lhs[None],
        rhs,
        window_strides=(1, 1),
        padding=((0, 0), (1, 1)),
        dimension_numbers=("NHWC", rhs_spec, "NHWC"),
        preferred_element_type=jnp.float32,
    )
    return out[0]


def on_device(image, weight, grad_out):
    height = image.shape[0]
    breadth = image.shape[1]
    all_chans = weight.shape[2]
    local_filters = weight.shape[3]
    chans = lax.axis_size("chan")
    all_filters = local_filters * chans
    n_hi = lax.axis_size("hi")
    n_lo = lax.axis_size("lo")
    lo = lax.axis_index("lo")
    piece = all_chans // (n_hi * n_lo)

    grad_filters = lax.all_to_all(grad_out, "chan", split_axis=2, concat_axis=1, tiled=True)

    gathered = lax.all_gather(image, "chan", axis=2, tiled=True)
    edges = jnp.concatenate(
        [shift_rows(image[-1:], upward=False), shift_rows(image[:1], upward=True)], axis=0
    )
    edges = lax.all_gather(edges, "chan", axis=2, tiled=True)
    rows6 = jnp.concatenate([edges[0:1], gathered, edges[1:2]], axis=0)

    def subset(x, which):
        shaped = x.reshape(x.shape[0], x.shape[1], n_hi, n_lo, piece)
        taken = lax.dynamic_index_in_dim(shaped, which, axis=3, keepdims=False)
        return taken.reshape(x.shape[0], x.shape[1], n_hi * piece)

    send_rows = lax.dynamic_slice_in_dim(rows6, 2 * lo, height, axis=0)
    sent_img = lax.ppermute(subset(send_rows, 1 - lo), "lo", [(0, 1), (1, 0)])

    conv_out = conv(rows6, weight, "HWIO").astype(jnp.bfloat16)

    conv_wide = conv_out.astype(jnp.float32)
    upstream = grad_filters.astype(jnp.float32)
    partial = jnp.stack(
        [jnp.sum(conv_wide * conv_wide, axis=-1), jnp.sum(upstream * conv_wide, axis=-1)], axis=-1
    )
    totals = lax.psum(partial, "chan")
    inverse_rms = lax.rsqrt(totals[..., 0:1] / all_filters + 1e-06)
    mean_gu = inverse_rms * (totals[..., 1:2] / all_filters)
    unit = conv_wide * inverse_rms
    normed_filters = unit.astype(jnp.bfloat16)
    grad_conv = (inverse_rms * (upstream - unit * mean_gu)).astype(jnp.bfloat16)
    normed = lax.all_to_all(normed_filters, "chan", split_axis=1, concat_axis=2, tiled=True)

    sent_grad = lax.ppermute(grad_conv, "lo", [(0, 1), (1, 0)])
    own_img = subset(rows6, lo)
    img_block = lax.dynamic_slice_in_dim(
        jnp.concatenate([sent_img, own_img, sent_img], axis=0), height * (1 - lo), 2 * height + 2, axis=0
    )
    img_block = jnp.pad(img_block, ((0, 0), (1, 1), (0, 0)))
    grad_block = lax.dynamic_slice_in_dim(
        jnp.concatenate([sent_grad, grad_conv, sent_grad], axis=0), height * (1 - lo), 2 * height, axis=0
    )
    pair_rows = 2 * height
    grad_flat = grad_block.reshape(pair_rows * breadth, local_filters)
    width_w = img_block.shape[2]
    blocks = []
    for weight_tap_row in range(3):
        for weight_tap_col in range(3):
            weight_window = img_block[
                weight_tap_row : weight_tap_row + pair_rows,
                weight_tap_col : weight_tap_col + breadth,
            ].reshape(pair_rows * breadth, width_w)
            blocks.append(
                lax.dot_general(
                    weight_window,
                    grad_flat,
                    (((0,), (0,)), ((), ())),
                    preferred_element_type=jnp.float32,
                )
            )
    stacked = jnp.stack(blocks).reshape(3, 3, width_w, local_filters)
    grad_weight = lax.psum_scatter(
        stacked.astype(jnp.bfloat16), "hi", scatter_dimension=2, tiled=True
    ).astype(jnp.float32)

    grad_rimmed = with_halo(grad_conv)
    input_term = conv(grad_rimmed, weight[::-1, ::-1], "HWOI")
    split = input_term.astype(jnp.bfloat16).reshape(height, breadth, chans, all_chans // chans)
    received = lax.all_to_all(split, "chan", split_axis=2, concat_axis=2, tiled=True)
    grad_input = jnp.sum(received.astype(jnp.float32), axis=2).astype(jnp.bfloat16)
    return (normed, grad_input, grad_weight)


def solution(mesh):
    slabs = mesh.shape["slab"]
    chans = mesh.shape["chan"]
    split_mesh = Mesh(mesh.devices.reshape(slabs // 2, 2, chans), ("hi", "lo", "chan"))
    return jax.shard_map(
        on_device,
        mesh=split_mesh,
        in_specs=(P(SLAB, None, "chan"), P(None, None, None, "chan"), P(SLAB, "chan", None)),
        out_specs=(P(SLAB, "chan", None), P(SLAB, None, "chan"), P(None, None, SLAB, "chan")),
        check_vma=False,
    )
```

time: 252 us -> 232 us (0.921)
  matrix products: 67 us -> 22.5 us
  blocking collectives: 20.3 us -> 6.33 us
  waiting for transfers between devices: 90.2 us -> 104 us
  local copies, waits for them, and re-layouts: 31.9 us -> 44.7 us
  other arithmetic: 4.13 us -> 14.6 us
    dot_general x27 -> x9, matrix products: 67 us -> 7.78 us  [on_device(): lax.dot_general(weight_window, grad_flat, (((0,), (0,)), ((), ())), prefe...]
    ppermute x4 -> x6, waiting for transfers between devices: 5.34 us -> 44.3 us  [the longest x1 32.6 us: on_device(): sent_grad = lax.ppermute(grad_conv, 'lo', [(0, 1), (1, 0)])]
    all_to_all x1 -> x2, waiting for transfers between devices: 69.7 us -> 38.5 us  [the longest x1 24.1 us: on_device(): lax.all_to_all(split, 'chan', split_axis=2, concat_axis=2, tiled=True)]
    slice x7 -> x3, local copies, waits for them, and re-layouts: 22.2 us -> 3.24 us  [the longest x1 2.23 us: on_device(): rows6 = jnp.concatenate([edges[0:1], gathered, edges[1:2]], axis=0)]
    conv_general_dilated x0 -> x2, matrix products: none -> 14.7 us  [conv(): lax.conv_general_dilated(lhs[None], rhs, window_strides=(1, 1), padding=(...]
    all_to_all x1 -> x0, blocking collectives: 14.3 us -> none  [on_device(): lax.all_to_all(grad_out, 'chan', split_axis=2, concat_axis=1, tiled=True)]
    conv_general_dilated x0 -> x6, local copies, waits for them, and re-layouts: none -> 10.3 us  [conv(): lax.conv_general_dilated(lhs[None], rhs, window_strides=(1, 1), padding=(...]
    unnamed x29 -> x24, local copies, waits for them, and re-layouts: 2.59 us -> 12.1 us
  transfers between devices with their start and end apart: 9 -> 12, of which waited for: 4 -> 7; matrix products, arithmetic and copies ran while one was open for 29% -> 14% of each run, Pallas kernels for 0% -> 0%
where the time goes in v2:
time: 232 us; the launch traced here: 231 us
  waiting for transfers between devices  104 us (45%)
  local copies, waits for them, and re-layouts  44.7 us (19%)
  starting transfers between devices  24.5 us (11%)
  matrix products  22.5 us (10%)
  other arithmetic  14.6 us (6%)
  between operations  14.2 us (6%)
  blocking collectives  6.33 us (3%)
    ppermute x1, waiting for transfers between devices, on_device(): sent_grad = lax.ppermute(grad_conv, 'lo', [(0, 1), (1, 0)])  32.6 us
    all_to_all x1, waiting for transfers between devices, on_device(): lax.all_to_all(split, 'chan', split_axis=2, concat_axis=2, tiled=True)  24.1 us
    all_gather x1, waiting for transfers between devices, on_device(): gathered = lax.all_gather(image, 'chan', axis=2, tiled=True)  20.5 us
    conv_general_dilated x2, matrix products, conv(): lax.conv_general_dilated(lhs[None], rhs, window_strides=(1, 1), padding=(...  14.7 us
    all_to_all x1, waiting for transfers between devices, on_device(): lax.all_to_all(grad_out, 'chan', split_axis=2, concat_axis=1, tiled=True)  14.4 us
    unnamed x24, local copies, waits for them, and re-layouts  12.1 us
    ppermute x4, waiting for transfers between devices, shift_rows(): return lax.ppermute(rows, SLAB, pairs)  11.7 us
    ppermute x4, starting transfers between devices, shift_rows(): return lax.ppermute(rows, SLAB, pairs)  11.7 us
  transfers between devices with their start and end apart: 12, of which 7 were waited for; matrix products, arithmetic and copies ran while one was open for 14% of the time, Pallas kernels for 0%

profile of v2, /device:TPU:4, one launch (start us, length us, event | category | flops | bytes accessed | tf_op | source)
XLA Modules:
  0.0 230.8 jit_solution(17873537817195875277)
XLA Ops:
  8.6 3.4 %collective-permute-start = (bf16[1,256,256]{1,2,0:T(8,128)(2,1)S(1)}, bf16[1,256,256]{1,2,0:T(8,128)(2,1)S(1)}, u32[]{:S(2)}, u32[]{:S(2)}) collective-permute-start(bf16[1,256,256]{1,2,0:T(8,128)(2,1)S(1)} %get-tuple-element.14), channel_id=1, source_target_pairs={{0,4},{4,8},{8,12},{12,16},{16,20},{20,24},{24,28},{1,5},{5,9},{9,... | collective-permute-start | bytes 393224 | tf_op jit(solution)/shard_map/ppermute | solution.py:16
  12.0 2.4 %collective-permute-start.1 = (bf16[1,256,256]{1,2,0:T(8,128)(2,1)S(1)}, bf16[1,256,256]{1,2,0:T(8,128)(2,1)S(1)}, u32[]{:S(2)}, u32[]{:S(2)}) collective-permute-start(bf16[1,256,256]{1,2,0:T(8,128)(2,1)S(1)} %get-tuple-element.15), channel_id=1, source_target_pairs={{4,0},{8,4},{12,8},{16,12},{20,16},{24,20},{28,24},{5,1},{9,5},{13... | collective-permute-start | bytes 393224 | tf_op jit(solution)/shard_map/ppermute | solution.py:16
  15.7 4.1 %collective-permute-done.1 = bf16[1,256,256]{1,2,0:T(8,128)(2,1)S(1)} collective-permute-done((bf16[1,256,256]{1,2,0:T(8,128)(2,1)S(1)}, bf16[1,256,256]{1,2,0:T(8,128)(2,1)S(1)}, u32[]{:S(2)}, u32[]{:S(2)}) %collective-permute-start.1) | collective-permute-done | bytes 131104 | tf_op jit(solution)/shard_map/ppermute | solution.py:16
  23.5 3.5 %all-to-all-start = ((bf16[4,2,32768]{2,1,0:T(2,128)(2,1)}), bf16[4,2,32768]{2,1,0:T(2,128)(2,1)S(1)}, u32[]{:S(2)}, u32[]{:S(2)}) async-start(bf16[4,2,32768]{2,1,0:T(2,128)(2,1)} %reshape.99), calls=%async_computation | async-start | bytes 1048576 | tf_op jit(solution)/shard_map/all_to_all | solution.py:49
  27.1 14.4 %all-to-all-done = bf16[4,2,32768]{2,1,0:T(2,128)(2,1)S(1)} async-done(((bf16[4,2,32768]{2,1,0:T(2,128)(2,1)}), bf16[4,2,32768]{2,1,0:T(2,128)(2,1)S(1)}, u32[]{:S(2)}, u32[]{:S(2)}) %all-to-all-start) | async-done | bytes 524320 | tf_op jit(solution)/shard_map/all_to_all | solution.py:49
  43.6 2.2 fusion.89
  45.8 20.5 %all-gather.5.cloned.1.call-done = bf16[4,256,1024]{1,2,0:T(8,128)(2,1)} async-done(((bf16[4,256,256]{1,2,0:T(8,128)(2,1)}), bf16[4,256,1024]{1,2,0:T(8,128)(2,1)}) %all-gather.5.cloned.1.call-update) | async-done | bytes 2097168 | tf_op jit(solution)/shard_map/all_gather | solution.py:51
  66.4 3.3 %pad_maximum_fusion = (bf16[6,256,1024]{1,2,0:T(8,128)(2,1)S(1)}, bf16[6,1,256,1024]{2,3,0,1:T(8,128)(2,1)}) fusion(bf16[1,256,1024]{1,2,0:T(8,128)(2,1)} %get-tuple-element.9, bf16[4,256,1024]{1,2,0:T(8,128)(2,1)} %all-gather.5.cloned.1.call-done, bf16[1,256,1024]{1,2,0:T(8,128)(2,1)} %get-tuple-element.8), kind=kLoop, calls=%fused_computation.18 | loop fusion | flops 3145728 | bytes 9437184 | tf_op jit(solution)/shard_map/concatenate | solution.py:56
  69.6 4.7 %copy.45 = bf16[6,1,256,1024]{3,2,0,1:T(8,128)(2,1)} copy(bf16[6,1,256,1024]{2,3,0,1:T(8,128)(2,1)} %get-tuple-element.7) | data formatting | bytes 6291456
  74.3 4.5 %pad.5.clone = bf16[6,1,264,1024]{3,2,0,1:T(8,128)(2,1)} pad(bf16[6,1,256,1024]{3,2,0,1:T(8,128)(2,1)} %copy.45, bf16[]{:T(256)} %constant.17.clone.1), padding=0_0x0_0x1_7x0_0 | pad | bytes 6389762 | tf_op jit(solution)/shard_map/broadcast_in_dim | solution.py:27
  78.8 5.8 %reshape.56 = bf16[6,1,8,33,1024]{4,3,2,0,1:T(8,128)(2,1)} reshape(bf16[6,1,264,1024]{3,2,0,1:T(8,128)(2,1)} %pad.5.clone) | data formatting | bytes 6488064 | tf_op jit(solution)/shard_map/conv_general_dilated | solution.py:26
  84.6 4.0 %copy.28 = bf16[6,1,8,33,1024]{4,2,3,0,1:T(8,128)(2,1)S(1)} copy(bf16[6,1,8,33,1024]{4,3,2,0,1:T(8,128)(2,1)} %reshape.56) | data formatting | bytes 6488064 | tf_op jit(solution)/shard_map/conv_general_dilated | solution.py:26
  88.7 7.5 %fusion.21 = bf16[4,8,33,256]{3,1,2,0:T(8,128)(2,1)S(1)} fusion(bf16[3,3,1024,256]{3,2,1,0:T(8,128)(2,1)} %param.4, bf16[6,1,7,2,1024]{4,2,3,0,1:T(8,128)(2,1)S(1)} %slice.79, bf16[6,1,8,33,1024]{4,2,3,0,1:T(8,128)(2,1)S(1)} %copy.28, pred[8,33]{0,1:T(8,128)(4,1)S(1)} %copy-done.8), kind=kOutput, calls=%fused_computation.34 | convolution fusion | flops 4993695744 | bytes 8675592 | tf_op jit(solution)/shard_map/conv_general_dilated | solution.py:26
  98.0 6.3 %psum.7 = f32[4,256,2]{1,0,2:T(4,128)S(1)} all-reduce(f32[4,256,2]{1,0,2:T(4,128)S(1)} %pad_maximum_fusion.2), channel_id=1, replica_groups=mesh['hi'=4,'lo'=2,'chan'=4] {'chan'}, use_global_device_ids=true, to_apply=%region_2.3 | all-reduce | flops 2048 | bytes 16384 | tf_op jit(solution)/shard_map/psum | solution.py:73
  109.1 32.6 %collective-permute-done.5 = bf16[4,256,256]{2,1,0:T(8,128)(2,1)} collective-permute-done((bf16[4,256,256]{2,1,0:T(8,128)(2,1)}, bf16[4,256,256]{2,1,0:T(8,128)(2,1)}, u32[]{:S(2)}, u32[]{:S(2)}) %collective-permute-start.5) | collective-permute-done | bytes 524320 | tf_op jit(solution)/shard_map/ppermute | solution.py:81
  143.4 2.4 %fusion.9 = bf16[10,256,512]{1,2,0:T(8,128)(2,1)S(1)} fusion(s32[]{:T(128)S(6)} %select_n.20, bf16[4,256,512]{1,2,0:T(8,128)(2,1)} %collective-permute-done.4, bf16[6,256,512]{1,2,0:T(8,128)(2,1)S(1)} %bitcast.190), kind=kLoop, calls=%fused_computation.20 | loop fusion | flops 2621440 | bytes 5242884 | tf_op jit(solution)/shard_map/concatenate | solution.py:84
  156.0 3.4 %collective-permute-start.2 = (bf16[1,256,256]{2,1,0:T(8,128)(2,1)S(1)}, bf16[1,256,256]{2,1,0:T(8,128)(2,1)S(1)}, u32[]{:S(2)}, u32[]{:S(2)}) collective-permute-start(bf16[1,256,256]{2,1,0:T(8,128)(2,1)S(1)} %get-tuple-element.12), channel_id=1, source_target_pairs={{0,4},{4,8},{8,12},{12,16},{16,20},{20,24},{24,28},{1,5},{5,9},{9,... | collective-permute-start | bytes 393224 | tf_op jit(solution)/shard_map/ppermute | solution.py:16
  159.4 2.5 %collective-permute-start.3 = (bf16[1,256,256]{2,1,0:T(8,128)(2,1)S(1)}, bf16[1,256,256]{2,1,0:T(8,128)(2,1)S(1)}, u32[]{:S(2)}, u32[]{:S(2)}) collective-permute-start(bf16[1,256,256]{2,1,0:T(8,128)(2,1)S(1)} %get-tuple-element.13), channel_id=1, source_target_pairs={{4,0},{8,4},{12,8},{16,12},{20,16},{24,20},{28,24},{5,1},{9,5},{13... | collective-permute-start | bytes 393224 | tf_op jit(solution)/shard_map/ppermute | solution.py:16
  163.1 3.7 %all-to-all-start.1 = ((bf16[4,256,256]{2,0,1:T(4,128)(2,1)}), bf16[4,256,256]{2,0,1:T(4,128)(2,1)S(1)}, u32[]{:S(2)}, u32[]{:S(2)}) async-start(bf16[4,256,256]{2,0,1:T(4,128)(2,1)} %copy.33), calls=%async_computation.1 | async-start | bytes 1048576 | tf_op jit(solution)/shard_map/all_to_all | solution.py:79
  166.8 6.4 %collective-permute-done.3 = bf16[1,256,256]{2,1,0:T(8,128)(2,1)S(1)} collective-permute-done((bf16[1,256,256]{2,1,0:T(8,128)(2,1)S(1)}, bf16[1,256,256]{2,1,0:T(8,128)(2,1)S(1)}, u32[]{:S(2)}, u32[]{:S(2)}) %collective-permute-start.3) | collective-permute-done | bytes 131104 | tf_op jit(solution)/shard_map/ppermute | solution.py:16
  175.0 7.2 %select_convert_fusion = bf16[4,8,33,1024]{3,1,2,0:T(8,128)(2,1)S(1)} fusion(pred[8,33]{0,1:T(8,128)(4,1)S(1)} %copy-done.8, bf16[3,3,1024,256]{3,2,1,0:T(8,128)(2,1)} %param.4, bf16[6,1,7,2,256]{4,2,3,0,1:T(8,128)(2,1)S(1)} %slice.85, bf16[6,1,8,33,256]{4,2,3,0,1:T(8,128)(2,1)S(1)} %copy.36), kind=kOutput, calls=%fused_computation.8 | convolution fusion | flops 4987576320 | bytes 7735560 | tf_op jit(solution)/shard_map/conv_general_dilated | solution.py:26
  186.7 3.7 %copy.38 = bf16[4,256,4,256]{3,0,1,2:T(4,128)(2,1)} copy(bf16[4,256,4,256]{3,2,0,1:T(4,128)(2,1)} %convert_element_type.72) | data formatting | bytes 4194304 | tf_op jit(solution)/shard_map/convert_element_type | solution.py:115
  190.5 3.6 %all-to-all-start.2 = ((bf16[4,256,4,256]{3,0,1,2:T(4,128)(2,1)}), bf16[4,256,4,256]{3,0,1,2:T(4,128)(2,1)S(1)}, u32[]{:S(2)}, u32[]{:S(2)}) async-start(bf16[4,256,4,256]{3,0,1,2:T(4,128)(2,1)} %copy.38), calls=%async_computation.2 | async-start | bytes 4194304 | tf_op jit(solution)/shard_map/all_to_all | solution.py:116
  195.7 24.1 %all-to-all-done.2 = bf16[4,256,4,256]{3,0,1,2:T(4,128)(2,1)S(1)} async-done(((bf16[4,256,4,256]{3,0,1,2:T(4,128)(2,1)}), bf16[4,256,4,256]{3,0,1,2:T(4,128)(2,1)S(1)}, u32[]{:S(2)}, u32[]{:S(2)}) %all-to-all-start.2) | async-done | bytes 2097184 | tf_op jit(solution)/shard_map/all_to_all | solution.py:116
  (77 shorter events, 40.6 us)
Async XLA Ops:
  7.2 14.1 %copy-start.7 = (bf16[4,64,1024]{2,1,0:T(8,128)(2,1)S(1)}, bf16[4,64,1024]{2,1,0:T(8,128)(2,1)}, u32[]{:S(2)}) copy-start(bf16[4,64,1024]{2,1,0:T(8,128)(2,1)} %param.5) | copy-start | bytes 1572868
  7.2 36.4 %all-gather.3.cloned.1.call-start = ((), (), s32[]{:S(2)}) async-start(), calls=%async_computation.4 | async-start | bytes 1310720 | tf_op jit(solution)/shard_map/all_gather | solution.py:55
  8.5 12.0 %copy-start.4 = (bf16[4,256,256]{1,2,0:T(8,128)(2,1)}, bf16[4,256,256]{1,2,0:T(8,128)(2,1)S(1)}, u32[]{:S(2)}) copy-start(bf16[4,256,256]{1,2,0:T(8,128)(2,1)S(1)} %copy.23) | copy-start | bytes 1572868
  8.6 7.1 %collective-permute-start = (bf16[1,256,256]{1,2,0:T(8,128)(2,1)S(1)}, bf16[1,256,256]{1,2,0:T(8,128)(2,1)S(1)}, u32[]{:S(2)}, u32[]{:S(2)}) collective-permute-start(bf16[1,256,256]{1,2,0:T(8,128)(2,1)S(1)} %get-tuple-element.14), channel_id=1, source_target_pairs={{0,4},{4,8},{8,12},{12,16},{16,20},{20,24},{24,28},{1,5},{5,9},{9,... | collective-permute-start | bytes 393224 | tf_op jit(solution)/shard_map/ppermute | solution.py:16
  12.0 7.8 %collective-permute-start.1 = (bf16[1,256,256]{1,2,0:T(8,128)(2,1)S(1)}, bf16[1,256,256]{1,2,0:T(8,128)(2,1)S(1)}, u32[]{:S(2)}, u32[]{:S(2)}) collective-permute-start(bf16[1,256,256]{1,2,0:T(8,128)(2,1)S(1)} %get-tuple-element.15), channel_id=1, source_target_pairs={{4,0},{8,4},{12,8},{16,12},{20,16},{24,20},{28,24},{5,1},{9,5},{13... | collective-permute-start | bytes 393224 | tf_op jit(solution)/shard_map/ppermute | solution.py:16
  20.5 45.9 %all-gather.5.cloned.1.call-start = ((), (), s32[]{:S(2)}) async-start(), calls=%async_computation.5 | async-start | bytes 2621440 | tf_op jit(solution)/shard_map/all_gather | solution.py:51
  23.5 17.9 %all-to-all-start = ((bf16[4,2,32768]{2,1,0:T(2,128)(2,1)}), bf16[4,2,32768]{2,1,0:T(2,128)(2,1)S(1)}, u32[]{:S(2)}, u32[]{:S(2)}) async-start(bf16[4,2,32768]{2,1,0:T(2,128)(2,1)} %reshape.99), calls=%async_computation | async-start | bytes 1048576 | tf_op jit(solution)/shard_map/all_to_all | solution.py:49
  27.0 195.1 %reduce-scatter.2.cloned.1.call-start = ((), (), s32[]{:S(2)}) async-start(), calls=%async_computation.6 | async-start | bytes 2949120 | tf_op jit(solution)/shard_map/reduce_scatter | solution.py:109
  84.6 4.1 %copy-start.8 = (pred[8,33]{0,1:T(8,128)(4,1)S(1)}, pred[8,33]{0,1:T(8,128)(4,1)}, u32[]{:S(2)}) copy-start(pred[8,33]{0,1:T(8,128)(4,1)} %constant.53) | copy-start | bytes 796
  96.3 1.4 copy-start
  96.7 0.8 copy-start.2
  104.4 1.6 copy-start.1
  104.4 1.7 copy-start.3
  105.6 37.7 %collective-permute-start.4 = (bf16[4,256,512]{1,2,0:T(8,128)(2,1)}, bf16[4,256,512]{1,2,0:T(8,128)(2,1)}, u32[]{:S(2)}, u32[]{:S(2)}) collective-permute-start(bf16[4,256,512]{1,2,0:T(8,128)(2,1)} %bitcast.17), channel_id=1, source_target_pairs={{0,4},{4,0},{1,5},{5,1},{2,6},{6,2},{3,7},{7,3},{8,12},{12,8},{9,1... | collective-permute-start | bytes 3145736 | tf_op jit(solution)/shard_map/ppermute | solution.py:64
  107.4 34.3 %collective-permute-start.5 = (bf16[4,256,256]{2,1,0:T(8,128)(2,1)}, bf16[4,256,256]{2,1,0:T(8,128)(2,1)}, u32[]{:S(2)}, u32[]{:S(2)}) collective-permute-start(bf16[4,256,256]{2,1,0:T(8,128)(2,1)} %get-tuple-element.10), channel_id=1, source_target_pairs={{0,4},{4,0},{1,5},{5,1},{2,6},{6,2},{3,7},{7,3},{8,12},{12,8},{9,1... | collective-permute-start | bytes 1572872 | tf_op jit(solution)/shard_map/ppermute | solution.py:81
  153.5 1.4 copy-start.5
  153.6 8.3 %copy-start.6 = (bf16[4,256,256]{2,1,0:T(8,128)(2,1)S(1)}, bf16[4,256,256]{2,1,0:T(8,128)(2,1)}, u32[]{:S(2)}) copy-start(bf16[4,256,256]{2,1,0:T(8,128)(2,1)} %get-tuple-element.11) | copy-start | bytes 1572868
  156.0 10.8 %collective-permute-start.2 = (bf16[1,256,256]{2,1,0:T(8,128)(2,1)S(1)}, bf16[1,256,256]{2,1,0:T(8,128)(2,1)S(1)}, u32[]{:S(2)}, u32[]{:S(2)}) collective-permute-start(bf16[1,256,256]{2,1,0:T(8,128)(2,1)S(1)} %get-tuple-element.12), channel_id=1, source_target_pairs={{0,4},{4,8},{8,12},{12,16},{16,20},{20,24},{24,28},{1,5},{5,9},{9,... | collective-permute-start | bytes 393224 | tf_op jit(solution)/shard_map/ppermute | solution.py:16
  159.4 13.8 %collective-permute-start.3 = (bf16[1,256,256]{2,1,0:T(8,128)(2,1)S(1)}, bf16[1,256,256]{2,1,0:T(8,128)(2,1)S(1)}, u32[]{:S(2)}, u32[]{:S(2)}) collective-permute-start(bf16[1,256,256]{2,1,0:T(8,128)(2,1)S(1)} %get-tuple-element.13), channel_id=1, source_target_pairs={{4,0},{8,4},{12,8},{16,12},{20,16},{24,20},{28,24},{5,1},{9,5},{13... | collective-permute-start | bytes 393224 | tf_op jit(solution)/shard_map/ppermute | solution.py:16
  163.1 27.4 %all-to-all-start.1 = ((bf16[4,256,256]{2,0,1:T(4,128)(2,1)}), bf16[4,256,256]{2,0,1:T(4,128)(2,1)S(1)}, u32[]{:S(2)}, u32[]{:S(2)}) async-start(bf16[4,256,256]{2,0,1:T(4,128)(2,1)} %copy.33), calls=%async_computation.1 | async-start | bytes 1048576 | tf_op jit(solution)/shard_map/all_to_all | solution.py:79
  190.5 29.3 %all-to-all-start.2 = ((bf16[4,256,4,256]{3,0,1,2:T(4,128)(2,1)}), bf16[4,256,4,256]{3,0,1,2:T(4,128)(2,1)S(1)}, u32[]{:S(2)}, u32[]{:S(2)}) async-start(bf16[4,256,4,256]{3,0,1,2:T(4,128)(2,1)} %copy.38), calls=%async_computation.2 | async-start | bytes 4194304 | tf_op jit(solution)/shard_map/all_to_all | solution.py:116
Sparse Core Ops, SparseCore 0:
  20.6 22.2 all-gather.2
  44.5 21.8 all-gather.4
  155.1 48.0 reduce-scatter.1

commit v3 on v2

--- a/solution.py
+++ b/solution.py
@@ -16,27 +16,17 @@
     return lax.ppermute(rows, SLAB, pairs)
 
 
-def with_halo(cells):
-    top = shift_rows(cells[-1:], upward=False)
-    bottom = shift_rows(cells[:1], upward=True)
-    return jnp.concatenate([top, cells, bottom], axis=0)
-
-
-def conv(lhs, rhs, rhs_spec):
-    out = lax.conv_general_dilated(
-        lhs[None],
-        rhs,
-        window_strides=(1, 1),
-        padding=((0, 0), (1, 1)),
-        dimension_numbers=("NHWC", rhs_spec, "NHWC"),
-        preferred_element_type=jnp.float32,
-    )
-    return out[0]
+def shift_sum(z):
+    breadth = z.shape[-3]
+    widths = [(0, 0)] * (z.ndim - 3) + [(1, 1), (0, 0), (0, 0)]
+    zp = jnp.pad(z, widths)
+    return zp[..., 0:breadth, 0, :] + zp[..., 1 : breadth + 1, 1, :] + zp[..., 2 : breadth + 2, 2, :]
 
 
 def on_device(image, weight, grad_out):
     height = image.shape[0]
     breadth = image.shape[1]
+    local_chans = image.shape[2]
     all_chans = weight.shape[2]
     local_filters = weight.shape[3]
     chans = lax.axis_size("chan")
@@ -45,25 +35,46 @@
     n_lo = lax.axis_size("lo")
     lo = lax.axis_index("lo")
     piece = all_chans // (n_hi * n_lo)
+    per_chan = local_chans // (n_lo * piece)
 
     grad_filters = lax.all_to_all(grad_out, "chan", split_axis=2, concat_axis=1, tiled=True)
+    gathered = lax.all_gather(image, "chan", axis=2, tiled=True)
 
-    gathered = lax.all_gather(image, "chan", axis=2, tiled=True)
-    edges = jnp.concatenate(
-        [shift_rows(image[-1:], upward=False), shift_rows(image[:1], upward=True)], axis=0
+    by_row = jnp.transpose(weight, (0, 2, 1, 3)).reshape(3, all_chans, 3 * local_filters)
+
+    def taps(rows, a):
+        count = rows.shape[0]
+        flat = rows.reshape(count * breadth, all_chans)
+        out = jnp.dot(flat, by_row[a], preferred_element_type=jnp.float32)
+        return out.reshape(count, breadth, 3, local_filters)
+
+    to_next = lax.ppermute(shift_sum(taps(gathered[-1:], 0)), SLAB, [(i, i + 1) for i in range(lax.axis_size(SLAB) - 1)])
+    to_prev = lax.ppermute(shift_sum(taps(gathered[:1], 2)), SLAB, [(i + 1, i) for i in range(lax.axis_size(SLAB) - 1)])
+
+    def local_subset(x, which):
+        shaped = x.reshape(x.shape[0], x.shape[1], per_chan, n_lo, piece)
+        taken = lax.dynamic_index_in_dim(shaped, which, axis=3, keepdims=False)
+        return taken.reshape(x.shape[0], x.shape[1], per_chan * piece)
+
+    raw6 = jnp.concatenate(
+        [shift_rows(image[-1:], upward=False), image, shift_rows(image[:1], upward=True)], axis=0
     )
-    edges = lax.all_gather(edges, "chan", axis=2, tiled=True)
-    rows6 = jnp.concatenate([edges[0:1], gathered, edges[1:2]], axis=0)
+    send_rows = lax.dynamic_slice_in_dim(raw6, 2 * lo, height, axis=0)
+    sent_img = lax.ppermute(local_subset(send_rows, 1 - lo), "lo", [(0, 1), (1, 0)])
+    own_img = local_subset(raw6, lo)
+    block_piece = lax.dynamic_slice_in_dim(
+        jnp.concatenate([sent_img, own_img, sent_img], axis=0), height * (1 - lo), 2 * height + 2, axis=0
+    )
+    img_block = lax.all_gather(block_piece, "chan", axis=2, tiled=True)
 
-    def subset(x, which):
-        shaped = x.reshape(x.shape[0], x.shape[1], n_hi, n_lo, piece)
-        taken = lax.dynamic_index_in_dim(shaped, which, axis=3, keepdims=False)
-        return taken.reshape(x.shape[0], x.shape[1], n_hi * piece)
-
-    send_rows = lax.dynamic_slice_in_dim(rows6, 2 * lo, height, axis=0)
-    sent_img = lax.ppermute(subset(send_rows, 1 - lo), "lo", [(0, 1), (1, 0)])
-
-    conv_out = conv(rows6, weight, "HWIO").astype(jnp.bfloat16)
+    interior = taps(gathered, 1)
+    interior = interior + jnp.pad(taps(gathered[:-1], 0), ((1, 0), (0, 0), (0, 0), (0, 0)))
+    interior = interior + jnp.pad(taps(gathered[1:], 2), ((0, 1), (0, 0), (0, 0), (0, 0)))
+    conv_sum = shift_sum(interior)
+    conv_sum = conv_sum + jnp.concatenate(
+        [to_next, jnp.zeros((height - 2, breadth, local_filters), jnp.float32), to_prev], axis=0
+    )
+    conv_out = conv_sum.astype(jnp.bfloat16)
 
     conv_wide = conv_out.astype(jnp.float32)
     upstream = grad_filters.astype(jnp.float32)
@@ -79,10 +90,6 @@
     normed = lax.all_to_all(normed_filters, "chan", split_axis=1, concat_axis=2, tiled=True)
 
     sent_grad = lax.ppermute(grad_conv, "lo", [(0, 1), (1, 0)])
-    own_img = subset(rows6, lo)
-    img_block = lax.dynamic_slice_in_dim(
-        jnp.concatenate([sent_img, own_img, sent_img], axis=0), height * (1 - lo), 2 * height + 2, axis=0
-    )
     img_block = jnp.pad(img_block, ((0, 0), (1, 1), (0, 0)))
     grad_block = lax.dynamic_slice_in_dim(
         jnp.concatenate([sent_grad, grad_conv, sent_grad], axis=0), height * (1 - lo), 2 * height, axis=0
@@ -110,8 +117,20 @@
         stacked.astype(jnp.bfloat16), "hi", scatter_dimension=2, tiled=True
     ).astype(jnp.float32)
 
-    grad_rimmed = with_halo(grad_conv)
-    input_term = conv(grad_rimmed, weight[::-1, ::-1], "HWOI")
+    grad_rimmed = jnp.concatenate(
+        [shift_rows(grad_conv[-1:], upward=False), grad_conv, shift_rows(grad_conv[:1], upward=True)], axis=0
+    )
+    grad_padded = jnp.pad(grad_rimmed, ((0, 0), (1, 1), (0, 0)))
+    columns = jnp.concatenate(
+        [
+            grad_padded[a : a + height, b : b + breadth]
+            for a in range(3)
+            for b in range(3)
+        ],
+        axis=-1,
+    ).reshape(height * breadth, 9 * local_filters)
+    flipped = jnp.transpose(weight[::-1, ::-1], (0, 1, 3, 2)).reshape(9 * local_filters, all_chans)
+    input_term = jnp.dot(columns, flipped, preferred_element_type=jnp.float32)
     split = input_term.astype(jnp.bfloat16).reshape(height, breadth, chans, all_chans // chans)
     received = lax.all_to_all(split, "chan", split_axis=2, concat_axis=2, tiled=True)
     grad_input = jnp.sum(received.astype(jnp.float32), axis=2).astype(jnp.bfloat16)

time: 232 us -> 156 us (0.67)
  waiting for transfers between devices: 104 us -> 37.6 us
  local copies, waits for them, and re-layouts: 44.7 us -> 27.4 us
  starting transfers between devices: 24.5 us -> 31.4 us
  other arithmetic: 14.6 us -> 9.48 us
  matrix products: 22.5 us -> 27.5 us
    ppermute x1, waiting for transfers between devices: 32.6 us -> 0.01 us  [on_device(): sent_grad = lax.ppermute(grad_conv, 'lo', [(0, 1), (1, 0)])]
    all_gather x1, waiting for transfers between devices: 20.5 us -> 1.43 us  [on_device(): gathered = lax.all_gather(image, 'chan', axis=2, tiled=True)]
    dot_general x0 -> x5, matrix products: none -> 15.9 us  [the longest x1 8.7 us: on_device(): input_term = jnp.dot(columns, flipped, preferred_element_type=jnp.float32)]
    conv_general_dilated x2 -> x0, matrix products: 14.7 us -> none  [conv(): lax.conv_general_dilated(lhs[None], rhs, window_strides=(1, 1), padding=(...]
    ppermute x4, waiting for transfers between devices: 11.7 us -> 0.01 us  [shift_rows(): return lax.ppermute(rows, SLAB, pairs)]
    conv_general_dilated x6 -> x0, local copies, waits for them, and re-layouts: 10.3 us -> none  [conv(): lax.conv_general_dilated(lhs[None], rhs, window_strides=(1, 1), padding=(...]
    all_to_all x1, waiting for transfers between devices: 14.4 us -> 4.61 us  [on_device(): lax.all_to_all(grad_out, 'chan', split_axis=2, concat_axis=1, tiled=True)]
    convert_element_type x6 -> x0, local copies, waits for them, and re-layouts: 8.74 us -> none  [the longest x4 8.35 us: on_device(): input_term.astype(jnp.bfloat16)]
  transfers between devices with their start and end apart: 12 -> 14, of which waited for: 7 -> 6; matrix products, arithmetic and copies ran while one was open for 14% -> 39% of each run, Pallas kernels for 0% -> 0%
where the time goes in v3:
time: 156 us; the launch traced here: 154 us
  waiting for transfers between devices  37.6 us (24%)
  starting transfers between devices  31.4 us (20%)
  matrix products  27.5 us (18%)
  local copies, waits for them, and re-layouts  27.4 us (18%)
  between operations  14.2 us (9%)
  other arithmetic  9.48 us (6%)
  blocking collectives  6.58 us (4%)
    all_to_all x1, waiting for transfers between devices, on_device(): lax.all_to_all(split, 'chan', split_axis=2, concat_axis=2, tiled=True)  24.1 us
    ppermute x4, starting transfers between devices, shift_rows(): return lax.ppermute(rows, SLAB, pairs)  13.7 us
    unnamed x23, local copies, waits for them, and re-layouts  12.8 us
    dot_general x9, matrix products, on_device(): lax.dot_general(weight_window, grad_flat, (((0,), (0,)), ((), ())), prefe...  9.77 us
    dot_general x1, matrix products, on_device(): input_term = jnp.dot(columns, flipped, preferred_element_type=jnp.float32)  8.7 us
    dot_general x4, matrix products, taps(): out = jnp.dot(flat, by_row[a], preferred_element_type=jnp.float32)  7.22 us
    psum x1, blocking collectives, on_device(): totals = lax.psum(partial, 'chan')  6.58 us
    reshape x2, local copies, waits for them, and re-layouts, on_device(): input_term.astype(jnp.bfloat16)  5.02 us
  transfers between devices with their start and end apart: 14, of which 6 were waited for; matrix products, arithmetic and copies ran while one was open for 39% of the time, Pallas kernels for 0%

profile of v3, /device:TPU:4, one launch (start us, length us, event | category | flops | bytes accessed | tf_op | source)
XLA Modules:
  0.0 154.1 jit_solution(10401009061906988462)
XLA Ops:
  9.2 1.9 %collective-permute-start.5 = (bf16[1,256,256]{1,2,0:T(8,128)(2,1)S(1)}, bf16[1,256,256]{1,2,0:T(8,128)(2,1)S(1)}, u32[]{:S(2)}, u32[]{:S(2)}) collective-permute-start(bf16[1,256,256]{1,2,0:T(8,128)(2,1)S(1)} %get-tuple-element.9), channel_id=1, source_target_pairs={{4,0},{8,4},{12,8},{16,12},{20,16},{24,20},{28,24},{5,1},{9,5},{13... | collective-permute-start | bytes 393224 | tf_op jit(solution)/shard_map/ppermute | solution.py:16
  11.1 4.8 %collective-permute-start.4 = (bf16[1,256,256]{1,2,0:T(8,128)(2,1)S(1)}, bf16[1,256,256]{1,2,0:T(8,128)(2,1)S(1)}, u32[]{:S(2)}, u32[]{:S(2)}) collective-permute-start(bf16[1,256,256]{1,2,0:T(8,128)(2,1)S(1)} %get-tuple-element.8), channel_id=1, source_target_pairs={{0,4},{4,8},{8,12},{12,16},{16,20},{20,24},{24,28},{1,5},{5,9},{9,... | collective-permute-start | bytes 393224 | tf_op jit(solution)/shard_map/ppermute | solution.py:16
  18.2 3.5 %all-to-all-start = ((bf16[4,2,32768]{2,1,0:T(2,128)(2,1)}), bf16[4,2,32768]{2,1,0:T(2,128)(2,1)S(1)}, u32[]{:S(2)}, u32[]{:S(2)}) async-start(bf16[4,2,32768]{2,1,0:T(2,128)(2,1)} %reshape.196), calls=%async_computation | async-start | bytes 1048576 | tf_op jit(solution)/shard_map/all_to_all | solution.py:40
  22.1 6.7 %copy.17 = bf16[3,3,1024,256]{2,3,1,0:T(8,128)(2,1)} copy(bf16[3,3,1024,256]{3,2,1,0:T(8,128)(2,1)} %param.4) | data formatting | bytes 9437184 | tf_op args[1]
  28.9 1.8 %collective-permute-done.6 = bf16[4,256,128]{1,2,0:T(8,128)(2,1)S(1)} collective-permute-done((bf16[4,256,128]{1,2,0:T(8,128)(2,1)S(1)}, bf16[4,256,128]{1,2,0:T(8,128)(2,1)S(1)}, u32[]{:S(2)}, u32[]{:S(2)}) %collective-permute-start.6) | collective-permute-done | bytes 262176 | tf_op jit(solution)/shard_map/ppermute | solution.py:63
  31.8 4.6 %all-to-all-done = bf16[4,2,32768]{2,1,0:T(2,128)(2,1)S(1)} async-done(((bf16[4,2,32768]{2,1,0:T(2,128)(2,1)}), bf16[4,2,32768]{2,1,0:T(2,128)(2,1)S(1)}, u32[]{:S(2)}, u32[]{:S(2)}) %all-to-all-start) | async-done | bytes 524320 | tf_op jit(solution)/shard_map/all_to_all | solution.py:40
  39.3 2.3 %fusion.23 = f32[1,256,3,256]{3,1,2,0:T(8,128)S(1)} fusion(bf16[3,1024,3,256]{1,3,2,0:T(8,128)(2,1)} %bitcast.227, bf16[4,256,1024]{2,1,0:T(8,128)(2,1)} %all-gather.3.cloned.1.call-done), kind=kOutput, calls=%fused_computation.41 | convolution fusion | flops 402653184 | bytes 2883584 | tf_op jit(solution)/shard_map/dot_general | solution.py:48
  41.7 2.6 %collective-permute-start.1 = (f32[1,256,256]{2,1,0:T(8,128)S(1)}, f32[1,256,256]{2,1,0:T(8,128)S(1)}, u32[]{:S(2)}, u32[]{:S(2)}) collective-permute-start(f32[1,256,256]{2,1,0:T(8,128)S(1)} %fusion.86), channel_id=1, source_target_pairs={{4,0},{8,4},{12,8},{16,12},{20,16},{24,20},{28,24},{5,1},{9,5},{13... | collective-permute-start | bytes 786440 | tf_op jit(solution)/shard_map/ppermute | solution.py:52
  46.0 4.3 %collective-permute-start = (f32[1,256,256]{2,1,0:T(8,128)S(1)}, f32[1,256,256]{2,1,0:T(8,128)S(1)}, u32[]{:S(2)}, u32[]{:S(2)}) collective-permute-start(f32[1,256,256]{2,1,0:T(8,128)S(1)} %fusion.83), channel_id=1, source_target_pairs={{0,4},{4,8},{8,12},{12,16},{16,20},{20,24},{24,28},{1,5},{5,9},{9,... | collective-permute-start | bytes 786440 | tf_op jit(solution)/shard_map/ppermute | solution.py:51
  51.7 1.8 %fusion.6 = f32[4,256,3,256]{3,1,2,0:T(8,128)S(1)} fusion(bf16[4,256,1024]{2,1,0:T(8,128)(2,1)S(1)} %copy-done.2, bf16[3,1024,3,256]{1,3,2,0:T(8,128)(2,1)S(1)} %bitcast.230), kind=kOutput, calls=%fused_computation.17 | convolution fusion | flops 1610612736 | bytes 6815744 | tf_op jit(solution)/shard_map/dot_general | solution.py:48
  53.5 1.8 %pad_add_fusion = f32[4,256,3,256]{3,1,2,0:T(8,128)S(1)} fusion(f32[3,256,3,256]{3,1,2,0:T(8,128)S(1)} %fusion.9, f32[4,256,3,256]{3,1,2,0:T(8,128)S(1)} %fusion.6, bf16[4,256,1024]{2,1,0:T(8,128)(2,1)S(1)} %copy-done.2, bf16[3,1024,3,256]{1,3,2,0:T(8,128)(2,1)S(1)} %bitcast.231), kind=kOutput, calls=%fused_computation.6 | convolution fusion | flops 1209532416 | bytes 11796480 | tf_op jit(solution)/shard_map/jit(_pad)/pad | solution.py:71
  55.4 3.3 %collective-permute-done = f32[1,256,256]{2,1,0:T(8,128)S(1)} collective-permute-done((f32[1,256,256]{2,1,0:T(8,128)S(1)}, f32[1,256,256]{2,1,0:T(8,128)S(1)}, u32[]{:S(2)}, u32[]{:S(2)}) %collective-permute-start) | collective-permute-done | bytes 262176 | tf_op jit(solution)/shard_map/ppermute | solution.py:51
  59.5 6.6 %psum.7 = f32[4,256,2]{1,0,2:T(4,128)S(1)} all-reduce(f32[4,256,2]{1,0,2:T(4,128)S(1)} %pad_maximum_fusion.3), channel_id=1, replica_groups=mesh['hi'=4,'lo'=2,'chan'=4] {'chan'}, use_global_device_ids=true, to_apply=%region_2.3 | all-reduce | flops 2048 | bytes 16384 | tf_op jit(solution)/shard_map/psum | solution.py:84
  66.6 5.0 %rev.3 = bf16[3,3,1024,256]{2,3,1,0:T(8,128)(2,1)} reverse(bf16[3,3,1024,256]{2,3,1,0:T(8,128)(2,1)} %copy.17), dimensions={0,1} | reverse | bytes 9437184 | tf_op jit(solution)/shard_map/rev | solution.py:132
  72.8 3.5 %all-to-all-start.1 = ((bf16[4,256,256]{2,0,1:T(4,128)(2,1)}), bf16[4,256,256]{2,0,1:T(4,128)(2,1)S(1)}, u32[]{:S(2)}, u32[]{:S(2)}) async-start(bf16[4,256,256]{2,0,1:T(4,128)(2,1)} %copy.20), calls=%async_computation.1 | async-start | bytes 1048576 | tf_op jit(solution)/shard_map/all_to_all | solution.py:90
  77.0 3.9 %collective-permute-start.3 = (bf16[1,256,256]{2,1,0:T(8,128)(2,1)}, bf16[1,256,256]{2,1,0:T(8,128)(2,1)S(1)}, u32[]{:S(2)}, u32[]{:S(2)}) collective-permute-start(bf16[1,256,256]{2,1,0:T(8,128)(2,1)} %get-tuple-element.11), channel_id=1, source_target_pairs={{4,0},{8,4},{12,8},{16,12},{20,16},{24,20},{28,24},{5,1},{9,5},{13... | collective-permute-start | bytes 393224 | tf_op jit(solution)/shard_map/ppermute | solution.py:16
  80.9 3.0 %collective-permute-start.2 = (bf16[1,256,256]{2,1,0:T(8,128)(2,1)}, bf16[1,256,256]{2,1,0:T(8,128)(2,1)}, u32[]{:S(2)}, u32[]{:S(2)}) collective-permute-start(bf16[1,256,256]{2,1,0:T(8,128)(2,1)} %get-tuple-element.10), channel_id=1, source_target_pairs={{0,4},{4,8},{8,12},{12,16},{16,20},{20,24},{24,28},{1,5},{5,9},{9,... | collective-permute-start | bytes 393224 | tf_op jit(solution)/shard_map/ppermute | solution.py:16
  85.4 2.9 %fusion.54 = bf16[9,512,256]{2,1,0:T(8,128)(2,1)S(1)} fusion(bf16[8,256,256]{2,1,0:T(8,128)(2,1)} %fusion.66, bf16[10,256,512]{1,2,0:T(8,128)(2,1)} %all-gather.5.cloned.1.call-done), kind=kOutput, calls=%fused_computation.73 | convolution fusion | flops 537001984 | bytes 3932160 | tf_op jit(solution)/shard_map/dot_general | solution.py:108
  99.5 8.7 %convolution_convert_fusion = bf16[1024,1024]{1,0:T(8,128)(2,1)} fusion(bf16[1024,2304]{1,0:T(8,128)(2,1)S(1)} %bitcast.242, bf16[2304,1024]{1,0:T(8,128)(2,1)} %bitcast.232), kind=kOutput, calls=%fused_computation.19 | convolution fusion | flops 4832886784 | bytes 11534336 | tf_op jit(solution)/shard_map/dot_general | solution.py:133
  108.2 3.3 %reshape.171 = bf16[4,256,4,256]{3,2,1,0:T(4,128)(2,1)S(1)} reshape(bf16[1024,1024]{1,0:T(8,128)(2,1)} %convolution_convert_fusion) | data formatting | bytes 4194304 | tf_op jit(solution)/shard_map/reshape | solution.py:134
  111.5 1.7 %copy.23 = bf16[4,256,4,256]{3,1,0,2:T(8,128)(2,1)} copy(bf16[4,256,4,256]{3,2,1,0:T(4,128)(2,1)S(1)} %reshape.171) | data formatting | bytes 4194304 | tf_op jit(solution)/shard_map/reshape | solution.py:134
  113.2 3.6 %all-to-all-start.2 = ((bf16[4,256,4,256]{3,1,0,2:T(8,128)(2,1)}), bf16[4,256,4,256]{3,1,0,2:T(8,128)(2,1)S(1)}, u32[]{:S(2)}, u32[]{:S(2)}) async-start(bf16[4,256,4,256]{3,1,0,2:T(8,128)(2,1)} %copy.23), calls=%async_computation.2 | async-start | bytes 4194304 | tf_op jit(solution)/shard_map/all_to_all | solution.py:135
  118.4 24.1 %all-to-all-done.2 = bf16[4,256,4,256]{3,1,0,2:T(8,128)(2,1)S(1)} async-done(((bf16[4,256,4,256]{3,1,0,2:T(8,128)(2,1)}), bf16[4,256,4,256]{3,1,0,2:T(8,128)(2,1)S(1)}, u32[]{:S(2)}, u32[]{:S(2)}) %all-to-all-start.2) | async-done | bytes 2097184 | tf_op jit(solution)/shard_map/all_to_all | solution.py:135
  145.4 2.2 %convert_element_type.73 = f32[3,3,128,256]{3,2,1,0:T(8,128)} convert(bf16[3,3,128,256]{3,2,1,0:T(8,128)(2,1)} %reduce-scatter.2.cloned.1.call-done) | non-fusion elementwise | flops 294912 | bytes 1769472 | tf_op jit(solution)/shard_map/convert_element_type | solution.py:118
  (77 shorter events, 32.0 us)
Async XLA Ops:
  7.2 8.8 %copy-start.4 = (bf16[4,64,1024]{2,1,0:T(8,128)(2,1)S(1)}, bf16[4,64,1024]{2,1,0:T(8,128)(2,1)}, u32[]{:S(2)}) copy-start(bf16[4,64,1024]{2,1,0:T(8,128)(2,1)} %param.5) | copy-start | bytes 1572868
  7.2 32.1 %all-gather.3.cloned.1.call-start = ((), (), s32[]{:S(2)}) async-start(), calls=%async_computation.4 | async-start | bytes 2621440 | tf_op jit(solution)/shard_map/all_gather | solution.py:41
  9.2 12.6 %collective-permute-start.5 = (bf16[1,256,256]{1,2,0:T(8,128)(2,1)S(1)}, bf16[1,256,256]{1,2,0:T(8,128)(2,1)S(1)}, u32[]{:S(2)}, u32[]{:S(2)}) collective-permute-start(bf16[1,256,256]{1,2,0:T(8,128)(2,1)S(1)} %get-tuple-element.9), channel_id=1, source_target_pairs={{4,0},{8,4},{12,8},{16,12},{20,16},{24,20},{28,24},{5,1},{9,5},{13... | collective-permute-start | bytes 393224 | tf_op jit(solution)/shard_map/ppermute | solution.py:16
  11.1 10.7 %collective-permute-start.4 = (bf16[1,256,256]{1,2,0:T(8,128)(2,1)S(1)}, bf16[1,256,256]{1,2,0:T(8,128)(2,1)S(1)}, u32[]{:S(2)}, u32[]{:S(2)}) collective-permute-start(bf16[1,256,256]{1,2,0:T(8,128)(2,1)S(1)} %get-tuple-element.8), channel_id=1, source_target_pairs={{0,4},{4,8},{8,12},{12,16},{16,20},{20,24},{24,28},{1,5},{5,9},{9,... | collective-permute-start | bytes 393224 | tf_op jit(solution)/shard_map/ppermute | solution.py:16
  18.2 18.2 %all-to-all-start = ((bf16[4,2,32768]{2,1,0:T(2,128)(2,1)}), bf16[4,2,32768]{2,1,0:T(2,128)(2,1)S(1)}, u32[]{:S(2)}, u32[]{:S(2)}) async-start(bf16[4,2,32768]{2,1,0:T(2,128)(2,1)} %reshape.196), calls=%async_computation | async-start | bytes 1048576 | tf_op jit(solution)/shard_map/all_to_all | solution.py:40
  21.7 63.7 %all-gather.5.cloned.1.call-start = ((), (), s32[]{:S(2)}) async-start(), calls=%async_computation.5 | async-start | bytes 3276800 | tf_op jit(solution)/shard_map/all_gather | solution.py:68
  22.0 8.7 %collective-permute-start.6 = (bf16[4,256,128]{1,2,0:T(8,128)(2,1)S(1)}, bf16[4,256,128]{1,2,0:T(8,128)(2,1)S(1)}, u32[]{:S(2)}, u32[]{:S(2)}) collective-permute-start(bf16[4,256,128]{1,2,0:T(8,128)(2,1)S(1)} %dynamic-slice_bitcast_fusion.1), channel_id=1, source_target_pairs={{0,4},{4,0},{1,5},{5,1},{2,6},{6,2},{3,7},{7,3},{8,12},{12,8},{9,1... | collective-permute-start | bytes 786440 | tf_op jit(solution)/shard_map/ppermute | solution.py:63
  39.3 5.0 %copy-start = (bf16[3,3,1024,256]{2,3,1,0:T(8,128)(2,1)S(1)}, bf16[3,3,1024,256]{2,3,1,0:T(8,128)(2,1)}, u32[]{:S(2)}) copy-start(bf16[3,3,1024,256]{2,3,1,0:T(8,128)(2,1)} %copy.17) | copy-start | bytes 14155780
  41.6 8.6 %copy-start.2 = (bf16[4,256,1024]{2,1,0:T(8,128)(2,1)S(1)}, bf16[4,256,1024]{2,1,0:T(8,128)(2,1)}, u32[]{:S(2)}) copy-start(bf16[4,256,1024]{2,1,0:T(8,128)(2,1)} %all-gather.3.cloned.1.call-done) | copy-start | bytes 6291460
  41.7 13.7 %collective-permute-start.1 = (f32[1,256,256]{2,1,0:T(8,128)S(1)}, f32[1,256,256]{2,1,0:T(8,128)S(1)}, u32[]{:S(2)}, u32[]{:S(2)}) collective-permute-start(f32[1,256,256]{2,1,0:T(8,128)S(1)} %fusion.86), channel_id=1, source_target_pairs={{4,0},{8,4},{12,8},{16,12},{20,16},{24,20},{28,24},{5,1},{9,5},{13... | collective-permute-start | bytes 786440 | tf_op jit(solution)/shard_map/ppermute | solution.py:52
  46.0 12.7 %collective-permute-start = (f32[1,256,256]{2,1,0:T(8,128)S(1)}, f32[1,256,256]{2,1,0:T(8,128)S(1)}, u32[]{:S(2)}, u32[]{:S(2)}) collective-permute-start(f32[1,256,256]{2,1,0:T(8,128)S(1)} %fusion.83), channel_id=1, source_target_pairs={{0,4},{4,8},{8,12},{12,16},{16,20},{20,24},{24,28},{1,5},{5,9},{9,... | collective-permute-start | bytes 786440 | tf_op jit(solution)/shard_map/ppermute | solution.py:51
  66.5 17.4 %collective-permute-start.7 = (bf16[4,256,256]{2,1,0:T(8,128)(2,1)S(1)}, bf16[4,256,256]{2,1,0:T(8,128)(2,1)S(1)}, u32[]{:S(2)}, u32[]{:S(2)}) collective-permute-start(bf16[4,256,256]{2,1,0:T(8,128)(2,1)S(1)} %get-tuple-element.6), channel_id=1, source_target_pairs={{0,4},{4,0},{1,5},{5,1},{2,6},{6,2},{3,7},{7,3},{8,12},{12,8},{9,1... | collective-permute-start | bytes 1572872 | tf_op jit(solution)/shard_map/ppermute | solution.py:92
  72.8 40.5 %all-to-all-start.1 = ((bf16[4,256,256]{2,0,1:T(4,128)(2,1)}), bf16[4,256,256]{2,0,1:T(4,128)(2,1)S(1)}, u32[]{:S(2)}, u32[]{:S(2)}) async-start(bf16[4,256,256]{2,0,1:T(4,128)(2,1)} %copy.20), calls=%async_computation.1 | async-start | bytes 1048576 | tf_op jit(solution)/shard_map/all_to_all | solution.py:90
  76.2 69.2 %reduce-scatter.2.cloned.1.call-start = ((), (), s32[]{:S(2)}) async-start(), calls=%async_computation.6 | async-start | bytes 2949120 | tf_op jit(solution)/shard_map/reduce_scatter | solution.py:116
  77.0 19.8 %collective-permute-start.3 = (bf16[1,256,256]{2,1,0:T(8,128)(2,1)}, bf16[1,256,256]{2,1,0:T(8,128)(2,1)S(1)}, u32[]{:S(2)}, u32[]{:S(2)}) collective-permute-start(bf16[1,256,256]{2,1,0:T(8,128)(2,1)} %get-tuple-element.11), channel_id=1, source_target_pairs={{4,0},{8,4},{12,8},{16,12},{20,16},{24,20},{28,24},{5,1},{9,5},{13... | collective-permute-start | bytes 393224 | tf_op jit(solution)/shard_map/ppermute | solution.py:16
  80.9 15.9 %collective-permute-start.2 = (bf16[1,256,256]{2,1,0:T(8,128)(2,1)}, bf16[1,256,256]{2,1,0:T(8,128)(2,1)}, u32[]{:S(2)}, u32[]{:S(2)}) collective-permute-start(bf16[1,256,256]{2,1,0:T(8,128)(2,1)} %get-tuple-element.10), channel_id=1, source_target_pairs={{0,4},{4,8},{8,12},{12,16},{16,20},{20,24},{24,28},{1,5},{5,9},{9,... | collective-permute-start | bytes 393224 | tf_op jit(solution)/shard_map/ppermute | solution.py:16
  85.4 2.9 %copy-start.3 = (bf16[8,256,256]{2,1,0:T(8,128)(2,1)S(1)}, bf16[8,256,256]{2,1,0:T(8,128)(2,1)}, u32[]{:S(2)}) copy-start(bf16[8,256,256]{2,1,0:T(8,128)(2,1)} %fusion.66) | copy-start | bytes 3145732
  85.4 3.0 %copy-start.5 = (bf16[10,256,512]{1,2,0:T(8,128)(2,1)S(1)}, bf16[10,256,512]{1,2,0:T(8,128)(2,1)}, u32[]{:S(2)}) copy-start(bf16[10,256,512]{1,2,0:T(8,128)(2,1)} %all-gather.5.cloned.1.call-done) | copy-start | bytes 7864324
  95.3 1.4 copy-start.1
  113.2 29.3 %all-to-all-start.2 = ((bf16[4,256,4,256]{3,1,0,2:T(8,128)(2,1)}), bf16[4,256,4,256]{3,1,0,2:T(8,128)(2,1)S(1)}, u32[]{:S(2)}, u32[]{:S(2)}) async-start(bf16[4,256,4,256]{3,1,0,2:T(8,128)(2,1)} %copy.23), calls=%async_computation.2 | async-start | bytes 4194304 | tf_op jit(solution)/shard_map/all_to_all | solution.py:135
Sparse Core Ops, SparseCore 0:
  9.6 29.6 all-gather.2
  40.8 25.7 all-gather.4
  96.9 48.4 reduce-scatter.1

commit v4 on v3

--- a/solution.py
+++ b/solution.py
@@ -91,31 +91,26 @@
 
     sent_grad = lax.ppermute(grad_conv, "lo", [(0, 1), (1, 0)])
     img_block = jnp.pad(img_block, ((0, 0), (1, 1), (0, 0)))
-    grad_block = lax.dynamic_slice_in_dim(
-        jnp.concatenate([sent_grad, grad_conv, sent_grad], axis=0), height * (1 - lo), 2 * height, axis=0
-    )
-    pair_rows = 2 * height
-    grad_flat = grad_block.reshape(pair_rows * breadth, local_filters)
     width_w = img_block.shape[2]
-    blocks = []
-    for weight_tap_row in range(3):
-        for weight_tap_col in range(3):
-            weight_window = img_block[
-                weight_tap_row : weight_tap_row + pair_rows,
-                weight_tap_col : weight_tap_col + breadth,
-            ].reshape(pair_rows * breadth, width_w)
-            blocks.append(
-                lax.dot_general(
-                    weight_window,
-                    grad_flat,
-                    (((0,), (0,)), ((), ())),
-                    preferred_element_type=jnp.float32,
+
+    def pair_part(grad_rows, first_row):
+        flat = grad_rows.reshape(height * breadth, local_filters)
+        blocks = []
+        for weight_tap_row in range(3):
+            rows = lax.dynamic_slice_in_dim(img_block, first_row + weight_tap_row, height, axis=0)
+            for weight_tap_col in range(3):
+                weight_window = rows[:, weight_tap_col : weight_tap_col + breadth].reshape(height * breadth, width_w)
+                blocks.append(
+                    lax.dot_general(
+                        weight_window,
+                        flat,
+                        (((0,), (0,)), ((), ())),
+                        preferred_element_type=jnp.float32,
+                    )
                 )
-            )
-    stacked = jnp.stack(blocks).reshape(3, 3, width_w, local_filters)
-    grad_weight = lax.psum_scatter(
-        stacked.astype(jnp.bfloat16), "hi", scatter_dimension=2, tiled=True
-    ).astype(jnp.float32)
+        return jnp.stack(blocks)
+
+    own_part = pair_part(grad_conv, height * lo)
 
     grad_rimmed = jnp.concatenate(
         [shift_rows(grad_conv[-1:], upward=False), grad_conv, shift_rows(grad_conv[:1], upward=True)], axis=0
@@ -123,17 +118,23 @@
     grad_padded = jnp.pad(grad_rimmed, ((0, 0), (1, 1), (0, 0)))
     columns = jnp.concatenate(
         [
-            grad_padded[a : a + height, b : b + breadth]
+            grad_padded[2 - a : 2 - a + height, 2 - b : 2 - b + breadth]
             for a in range(3)
             for b in range(3)
         ],
         axis=-1,
     ).reshape(height * breadth, 9 * local_filters)
-    flipped = jnp.transpose(weight[::-1, ::-1], (0, 1, 3, 2)).reshape(9 * local_filters, all_chans)
-    input_term = jnp.dot(columns, flipped, preferred_element_type=jnp.float32)
+    by_filter = jnp.transpose(weight, (0, 1, 3, 2)).reshape(9 * local_filters, all_chans)
+    input_term = jnp.dot(columns, by_filter, preferred_element_type=jnp.float32)
     split = input_term.astype(jnp.bfloat16).reshape(height, breadth, chans, all_chans // chans)
     received = lax.all_to_all(split, "chan", split_axis=2, concat_axis=2, tiled=True)
     grad_input = jnp.sum(received.astype(jnp.float32), axis=2).astype(jnp.bfloat16)
+    sent_grad, _, own_part = lax.optimization_barrier((sent_grad, split, own_part))
+
+    stacked = (own_part + pair_part(sent_grad, height * (1 - lo))).reshape(3, 3, width_w, local_filters)
+    grad_weight = lax.psum_scatter(
+        stacked.astype(jnp.bfloat16), "hi", scatter_dimension=2, tiled=True
+    ).astype(jnp.float32)
     return (normed, grad_input, grad_weight)
 
 

time: 156 us -> 164 us (1.051)
  waiting for transfers between devices: 37.6 us -> 50.7 us
  local copies, waits for them, and re-layouts: 27.4 us -> 21.2 us
    all_to_all x1, waiting for transfers between devices: 0.01 us -> 7.15 us  [on_device(): lax.all_to_all(normed_filters, 'chan', split_axis=1, concat_axis=2, tiled...]
    rev x1 -> x0, local copies, waits for them, and re-layouts: 4.98 us -> none  [on_device(): weight[::-1, ::-1]]
    ppermute x4, waiting for transfers between devices: 0.01 us -> 3.77 us  [shift_rows(): return lax.ppermute(rows, SLAB, pairs)]
    reduce_scatter x1, waiting for transfers between devices: 1.68 us -> 4.78 us  [on_device(): lax.psum_scatter(stacked.astype(jnp.bfloat16), 'hi', scatter_dimension=2,...]
    convert_element_type x0 -> x1, other arithmetic: none -> 2.07 us  [on_device(): stacked.astype(jnp.bfloat16)]
    dot_general x10 -> x19, matrix products: 18.5 us -> 19.8 us  [the longest x18 10.9 us: pair_part(): lax.dot_general(weight_window, flat, (((0,), (0,)), ((), ())), preferred_...]
    unnamed x23 -> x19, local copies, waits for them, and re-layouts: 12.8 us -> 12.5 us
  transfers between devices with their start and end apart: 14 -> 14, of which waited for: 6 -> 9; matrix products, arithmetic and copies ran while one was open for 39% -> 30% of each run, Pallas kernels for 0% -> 0%
where the time goes in v4:
time: 164 us; the launch traced here: 162 us
  waiting for transfers between devices  50.7 us (31%)
  starting transfers between devices  31.2 us (19%)
  matrix products  28.8 us (18%)
  local copies, waits for them, and re-layouts  21.2 us (13%)
  between operations  14.3 us (9%)
  other arithmetic  9.02 us (6%)
  blocking collectives  6.58 us (4%)
    all_to_all x1, waiting for transfers between devices, on_device(): lax.all_to_all(split, 'chan', split_axis=2, concat_axis=2, tiled=True)  24.1 us
    ppermute x4, starting transfers between devices, shift_rows(): return lax.ppermute(rows, SLAB, pairs)  13.5 us
    unnamed x19, local copies, waits for them, and re-layouts  12.5 us
    dot_general x18, matrix products, pair_part(): lax.dot_general(weight_window, flat, (((0,), (0,)), ((), ())), preferred_...  10.9 us
    dot_general x1, matrix products, on_device(): input_term = jnp.dot(columns, by_filter, preferred_element_type=jnp.float32)  8.89 us
    dot_general x4, matrix products, taps(): out = jnp.dot(flat, by_row[a], preferred_element_type=jnp.float32)  7.22 us
    all_to_all x1, waiting for transfers between devices, on_device(): lax.all_to_all(normed_filters, 'chan', split_axis=1, concat_axis=2, tiled...  7.15 us
    psum x1, blocking collectives, on_device(): totals = lax.psum(partial, 'chan')  6.58 us
  transfers between devices with their start and end apart: 14, of which 9 were waited for; matrix products, arithmetic and copies ran while one was open for 30% of the time, Pallas kernels for 0%

profile of v4, /device:TPU:4, one launch (start us, length us, event | category | flops | bytes accessed | tf_op | source)
XLA Modules:
  0.0 161.8 jit_solution(15221703887619663379)
XLA Ops:
  9.2 1.9 %collective-permute-start.6 = (bf16[1,256,256]{1,2,0:T(8,128)(2,1)S(1)}, bf16[1,256,256]{1,2,0:T(8,128)(2,1)S(1)}, u32[]{:S(2)}, u32[]{:S(2)}) collective-permute-start(bf16[1,256,256]{1,2,0:T(8,128)(2,1)S(1)} %get-tuple-element.13), channel_id=1, source_target_pairs={{4,0},{8,4},{12,8},{16,12},{20,16},{24,20},{28,24},{5,1},{9,5},{13... | collective-permute-start | bytes 393224 | tf_op jit(solution)/shard_map/ppermute | solution.py:16
  11.1 4.8 %collective-permute-start.5 = (bf16[1,256,256]{1,2,0:T(8,128)(2,1)S(1)}, bf16[1,256,256]{1,2,0:T(8,128)(2,1)S(1)}, u32[]{:S(2)}, u32[]{:S(2)}) collective-permute-start(bf16[1,256,256]{1,2,0:T(8,128)(2,1)S(1)} %get-tuple-element.12), channel_id=1, source_target_pairs={{0,4},{4,8},{8,12},{12,16},{16,20},{20,24},{24,28},{1,5},{5,9},{9,... | collective-permute-start | bytes 393224 | tf_op jit(solution)/shard_map/ppermute | solution.py:16
  19.1 3.5 %all-to-all-start = ((bf16[4,2,32768]{2,1,0:T(2,128)(2,1)}), bf16[4,2,32768]{2,1,0:T(2,128)(2,1)S(1)}, u32[]{:S(2)}, u32[]{:S(2)}) async-start(bf16[4,2,32768]{2,1,0:T(2,128)(2,1)} %reshape.215), calls=%async_computation | async-start | bytes 1048576 | tf_op jit(solution)/shard_map/all_to_all | solution.py:40
  22.9 6.7 %copy.17 = bf16[3,3,1024,256]{2,3,1,0:T(8,128)(2,1)} copy(bf16[3,3,1024,256]{3,2,1,0:T(8,128)(2,1)} %param.4) | data formatting | bytes 9437184 | tf_op args[1]
  32.8 4.5 %all-to-all-done = bf16[4,2,32768]{2,1,0:T(2,128)(2,1)S(1)} async-done(((bf16[4,2,32768]{2,1,0:T(2,128)(2,1)}), bf16[4,2,32768]{2,1,0:T(2,128)(2,1)S(1)}, u32[]{:S(2)}, u32[]{:S(2)}) %all-to-all-start) | async-done | bytes 524320 | tf_op jit(solution)/shard_map/all_to_all | solution.py:40
  39.2 2.3 %fusion.17 = f32[1,256,3,256]{3,1,2,0:T(8,128)S(1)} fusion(bf16[3,1024,3,256]{1,3,2,0:T(8,128)(2,1)} %bitcast.216, bf16[4,256,1024]{2,1,0:T(8,128)(2,1)} %all-gather.3.cloned.1.call-done), kind=kOutput, calls=%fused_computation.45 | convolution fusion | flops 402653184 | bytes 2883584 | tf_op jit(solution)/shard_map/dot_general | solution.py:48
  41.6 2.6 %collective-permute-start.1 = (f32[1,256,256]{2,1,0:T(8,128)S(1)}, f32[1,256,256]{2,1,0:T(8,128)S(1)}, u32[]{:S(2)}, u32[]{:S(2)}) collective-permute-start(f32[1,256,256]{2,1,0:T(8,128)S(1)} %fusion.63), channel_id=1, source_target_pairs={{4,0},{8,4},{12,8},{16,12},{20,16},{24,20},{28,24},{5,1},{9,5},{13... | collective-permute-start | bytes 786440 | tf_op jit(solution)/shard_map/ppermute | solution.py:52
  46.0 4.3 %collective-permute-start = (f32[1,256,256]{2,1,0:T(8,128)S(1)}, f32[1,256,256]{2,1,0:T(8,128)S(1)}, u32[]{:S(2)}, u32[]{:S(2)}) collective-permute-start(f32[1,256,256]{2,1,0:T(8,128)S(1)} %fusion.60), channel_id=1, source_target_pairs={{0,4},{4,8},{8,12},{12,16},{16,20},{20,24},{24,28},{1,5},{5,9},{9,... | collective-permute-start | bytes 786440 | tf_op jit(solution)/shard_map/ppermute | solution.py:51
  53.5 1.8 %pad_add_fusion = f32[4,256,3,256]{3,1,2,0:T(8,128)S(1)} fusion(f32[3,256,3,256]{3,1,2,0:T(8,128)S(1)} %fusion.3, f32[4,256,3,256]{3,1,2,0:T(8,128)S(1)} %fusion, bf16[4,256,1024]{2,1,0:T(8,128)(2,1)S(1)} %copy-done.3, bf16[3,1024,3,256]{1,3,2,0:T(8,128)(2,1)S(1)} %bitcast.221), kind=kOutput, calls=%fused_computation.19 | convolution fusion | flops 1209532416 | bytes 11796480 | tf_op jit(solution)/shard_map/jit(_pad)/pad | solution.py:71
  55.4 3.3 %collective-permute-done = f32[1,256,256]{2,1,0:T(8,128)S(1)} collective-permute-done((f32[1,256,256]{2,1,0:T(8,128)S(1)}, f32[1,256,256]{2,1,0:T(8,128)S(1)}, u32[]{:S(2)}, u32[]{:S(2)}) %collective-permute-start) | collective-permute-done | bytes 262176 | tf_op jit(solution)/shard_map/ppermute | solution.py:51
  59.5 6.6 %psum.7 = f32[4,256,2]{1,0,2:T(4,128)S(1)} all-reduce(f32[4,256,2]{1,0,2:T(4,128)S(1)} %pad_maximum_fusion.3), channel_id=1, replica_groups=mesh['hi'=4,'lo'=2,'chan'=4] {'chan'}, use_global_device_ids=true, to_apply=%region_2.3 | all-reduce | flops 2048 | bytes 16384 | tf_op jit(solution)/shard_map/psum | solution.py:84
  67.3 1.9 %collective-permute-start.3 = (bf16[1,256,256]{2,1,0:T(8,128)(2,1)S(1)}, bf16[1,256,256]{2,1,0:T(8,128)(2,1)S(1)}, u32[]{:S(2)}, u32[]{:S(2)}) collective-permute-start(bf16[1,256,256]{2,1,0:T(8,128)(2,1)S(1)} %get-tuple-element.15), channel_id=1, source_target_pairs={{4,0},{8,4},{12,8},{16,12},{20,16},{24,20},{28,24},{5,1},{9,5},{13... | collective-permute-start | bytes 393224 | tf_op jit(solution)/shard_map/ppermute | solution.py:16
  69.2 4.8 %collective-permute-start.2 = (bf16[1,256,256]{2,1,0:T(8,128)(2,1)S(1)}, bf16[1,256,256]{2,1,0:T(8,128)(2,1)S(1)}, u32[]{:S(2)}, u32[]{:S(2)}) collective-permute-start(bf16[1,256,256]{2,1,0:T(8,128)(2,1)S(1)} %get-tuple-element.14), channel_id=1, source_target_pairs={{0,4},{4,8},{8,12},{12,16},{16,20},{20,24},{24,28},{1,5},{5,9},{9,... | collective-permute-start | bytes 393224 | tf_op jit(solution)/shard_map/ppermute | solution.py:16
  75.1 2.8 %collective-permute-done.2 = bf16[1,256,256]{2,1,0:T(8,128)(2,1)S(1)} collective-permute-done((bf16[1,256,256]{2,1,0:T(8,128)(2,1)S(1)}, bf16[1,256,256]{2,1,0:T(8,128)(2,1)S(1)}, u32[]{:S(2)}, u32[]{:S(2)}) %collective-permute-start.2) | collective-permute-done | bytes 131104 | tf_op jit(solution)/shard_map/ppermute | solution.py:16
  78.7 8.9 %convolution_convert_fusion = bf16[1024,1024]{1,0:T(8,128)(2,1)} fusion(bf16[1024,2304]{1,0:T(8,128)(2,1)S(1)} %bitcast.230, bf16[2304,1024]{1,0:T(8,128)(2,1)} %bitcast.217), kind=kOutput, calls=%fused_computation.26 | convolution fusion | flops 4832886784 | bytes 11534336 | tf_op jit(solution)/shard_map/dot_general | solution.py:128
  87.6 3.3 %reshape.181 = bf16[4,256,4,256]{3,2,1,0:T(4,128)(2,1)S(1)} reshape(bf16[1024,1024]{1,0:T(8,128)(2,1)} %convolution_convert_fusion) | data formatting | bytes 4194304 | tf_op jit(solution)/shard_map/reshape | solution.py:129
  91.0 1.9 %fusion.39 = f32[9,512,256]{2,1,0:T(8,128)S(1)} fusion(bf16[4,256,256]{2,1,0:T(8,128)(2,1)S(1)} %get-tuple-element.10, s32[]{:T(128)S(6)} %select_n.36, bf16[10,256,512]{1,2,0:T(8,128)(2,1)} %all-gather.5.cloned.1.call-done), kind=kOutput, calls=%fused_computation.83 | convolution fusion | flops 268435456 | bytes 3670020 | tf_op jit(solution)/shard_map/dot_general | solution.py:104
  102.2 2.1 %add_convert_fusion = bf16[9,512,256]{2,1,0:T(8,128)(2,1)} fusion(f32[9,512,256]{2,1,0:T(8,128)S(1)} %fusion.31, f32[9,512,256]{2,1,0:T(8,128)S(1)} %fusion.22), kind=kLoop, calls=%fused_computation.18 | loop fusion | flops 2359296 | bytes 11796480 | tf_op jit(solution)/shard_map/convert_element_type | solution.py:136
  105.5 3.5 %all-to-all-start.1 = ((bf16[4,256,256]{2,0,1:T(4,128)(2,1)}), bf16[4,256,256]{2,0,1:T(4,128)(2,1)S(1)}, u32[]{:S(2)}, u32[]{:S(2)}) async-start(bf16[4,256,256]{2,0,1:T(4,128)(2,1)} %copy.20), calls=%async_computation.1 | async-start | bytes 1048576 | tf_op jit(solution)/shard_map/all_to_all | solution.py:90
  110.6 7.2 %all-to-all-done.1 = bf16[4,256,256]{2,0,1:T(4,128)(2,1)S(1)} async-done(((bf16[4,256,256]{2,0,1:T(4,128)(2,1)}), bf16[4,256,256]{2,0,1:T(4,128)(2,1)S(1)}, u32[]{:S(2)}, u32[]{:S(2)}) %all-to-all-start.1) | async-done | bytes 524320 | tf_op jit(solution)/shard_map/all_to_all | solution.py:90
  117.8 3.6 %all-to-all-start.2 = ((bf16[4,256,4,256]{3,1,0,2:T(8,128)(2,1)}), bf16[4,256,4,256]{3,1,0,2:T(8,128)(2,1)S(1)}, u32[]{:S(2)}, u32[]{:S(2)}) async-start(bf16[4,256,4,256]{3,1,0,2:T(8,128)(2,1)} %copy.23), calls=%async_computation.2 | async-start | bytes 4194304 | tf_op jit(solution)/shard_map/all_to_all | solution.py:130
  123.0 24.1 %all-to-all-done.2 = bf16[4,256,4,256]{3,1,0,2:T(8,128)(2,1)S(1)} async-done(((bf16[4,256,4,256]{3,1,0,2:T(8,128)(2,1)}), bf16[4,256,4,256]{3,1,0,2:T(8,128)(2,1)S(1)}, u32[]{:S(2)}, u32[]{:S(2)}) %all-to-all-start.2) | async-done | bytes 2097184 | tf_op jit(solution)/shard_map/all_to_all | solution.py:130
  148.3 4.8 %reduce-scatter.2.cloned.1.call-done = bf16[3,3,128,256]{3,2,1,0:T(8,128)(2,1)} async-done(((bf16[3,3,512,256]{3,2,1,0:T(8,128)(2,1)}), bf16[3,3,128,256]{3,2,1,0:T(8,128)(2,1)}) %reduce-scatter.2.cloned.1.call-update) | async-done | bytes 589840 | tf_op jit(solution)/shard_map/reduce_scatter | solution.py:135
  153.1 2.2 %convert_element_type.76 = f32[3,3,128,256]{3,2,1,0:T(8,128)} convert(bf16[3,3,128,256]{3,2,1,0:T(8,128)(2,1)} %reduce-scatter.2.cloned.1.call-done) | non-fusion elementwise | flops 294912 | bytes 1769472 | tf_op jit(solution)/shard_map/convert_element_type | solution.py:137
  (81 shorter events, 34.2 us)
Async XLA Ops:
  7.2 32.1 %all-gather.3.cloned.1.call-start = ((), (), s32[]{:S(2)}) async-start(), calls=%async_computation.4 | async-start | bytes 2621440 | tf_op jit(solution)/shard_map/all_gather | solution.py:41
  9.2 13.5 %collective-permute-start.6 = (bf16[1,256,256]{1,2,0:T(8,128)(2,1)S(1)}, bf16[1,256,256]{1,2,0:T(8,128)(2,1)S(1)}, u32[]{:S(2)}, u32[]{:S(2)}) collective-permute-start(bf16[1,256,256]{1,2,0:T(8,128)(2,1)S(1)} %get-tuple-element.13), channel_id=1, source_target_pairs={{4,0},{8,4},{12,8},{16,12},{20,16},{24,20},{28,24},{5,1},{9,5},{13... | collective-permute-start | bytes 393224 | tf_op jit(solution)/shard_map/ppermute | solution.py:16
  11.1 11.6 %collective-permute-start.5 = (bf16[1,256,256]{1,2,0:T(8,128)(2,1)S(1)}, bf16[1,256,256]{1,2,0:T(8,128)(2,1)S(1)}, u32[]{:S(2)}, u32[]{:S(2)}) collective-permute-start(bf16[1,256,256]{1,2,0:T(8,128)(2,1)S(1)} %get-tuple-element.12), channel_id=1, source_target_pairs={{0,4},{4,8},{8,12},{12,16},{16,20},{20,24},{24,28},{1,5},{5,9},{9,... | collective-permute-start | bytes 393224 | tf_op jit(solution)/shard_map/ppermute | solution.py:16
  19.1 18.2 %all-to-all-start = ((bf16[4,2,32768]{2,1,0:T(2,128)(2,1)}), bf16[4,2,32768]{2,1,0:T(2,128)(2,1)S(1)}, u32[]{:S(2)}, u32[]{:S(2)}) async-start(bf16[4,2,32768]{2,1,0:T(2,128)(2,1)} %reshape.215), calls=%async_computation | async-start | bytes 1048576 | tf_op jit(solution)/shard_map/all_to_all | solution.py:40
  22.6 68.4 %all-gather.5.cloned.1.call-start = ((), (), s32[]{:S(2)}) async-start(), calls=%async_computation.5 | async-start | bytes 3276800 | tf_op jit(solution)/shard_map/all_gather | solution.py:68
  22.9 8.7 %collective-permute-start.7 = (bf16[4,256,128]{1,2,0:T(8,128)(2,1)S(1)}, bf16[4,256,128]{1,2,0:T(8,128)(2,1)S(1)}, u32[]{:S(2)}, u32[]{:S(2)}) collective-permute-start(bf16[4,256,128]{1,2,0:T(8,128)(2,1)S(1)} %dynamic-slice_bitcast_fusion.1), channel_id=1, source_target_pairs={{0,4},{4,0},{1,5},{5,1},{2,6},{6,2},{3,7},{7,3},{8,12},{12,8},{9,1... | collective-permute-start | bytes 786440 | tf_op jit(solution)/shard_map/ppermute | solution.py:63
  32.7 120.4 %reduce-scatter.2.cloned.1.call-start = ((), (), s32[]{:S(2)}) async-start(), calls=%async_computation.6 | async-start | bytes 2949120 | tf_op jit(solution)/shard_map/reduce_scatter | solution.py:135
  39.2 5.0 %copy-start.1 = (bf16[3,3,1024,256]{2,3,1,0:T(8,128)(2,1)S(1)}, bf16[3,3,1024,256]{2,3,1,0:T(8,128)(2,1)}, u32[]{:S(2)}) copy-start(bf16[3,3,1024,256]{2,3,1,0:T(8,128)(2,1)} %copy.17) | copy-start | bytes 14155780
  39.2 11.0 %copy-start.3 = (bf16[4,256,1024]{2,1,0:T(8,128)(2,1)S(1)}, bf16[4,256,1024]{2,1,0:T(8,128)(2,1)}, u32[]{:S(2)}) copy-start(bf16[4,256,1024]{2,1,0:T(8,128)(2,1)} %all-gather.3.cloned.1.call-done) | copy-start | bytes 6291460
  41.6 13.7 %collective-permute-start.1 = (f32[1,256,256]{2,1,0:T(8,128)S(1)}, f32[1,256,256]{2,1,0:T(8,128)S(1)}, u32[]{:S(2)}, u32[]{:S(2)}) collective-permute-start(f32[1,256,256]{2,1,0:T(8,128)S(1)} %fusion.63), channel_id=1, source_target_pairs={{4,0},{8,4},{12,8},{16,12},{20,16},{24,20},{28,24},{5,1},{9,5},{13... | collective-permute-start | bytes 786440 | tf_op jit(solution)/shard_map/ppermute | solution.py:52
  46.0 12.7 %collective-permute-start = (f32[1,256,256]{2,1,0:T(8,128)S(1)}, f32[1,256,256]{2,1,0:T(8,128)S(1)}, u32[]{:S(2)}, u32[]{:S(2)}) collective-permute-start(f32[1,256,256]{2,1,0:T(8,128)S(1)} %fusion.60), channel_id=1, source_target_pairs={{0,4},{4,8},{8,12},{12,16},{16,20},{20,24},{24,28},{1,5},{5,9},{9,... | collective-permute-start | bytes 786440 | tf_op jit(solution)/shard_map/ppermute | solution.py:51
  67.3 7.8 %collective-permute-start.3 = (bf16[1,256,256]{2,1,0:T(8,128)(2,1)S(1)}, bf16[1,256,256]{2,1,0:T(8,128)(2,1)S(1)}, u32[]{:S(2)}, u32[]{:S(2)}) collective-permute-start(bf16[1,256,256]{2,1,0:T(8,128)(2,1)S(1)} %get-tuple-element.15), channel_id=1, source_target_pairs={{4,0},{8,4},{12,8},{16,12},{20,16},{24,20},{28,24},{5,1},{9,5},{13... | collective-permute-start | bytes 393224 | tf_op jit(solution)/shard_map/ppermute | solution.py:16
  69.2 8.7 %collective-permute-start.2 = (bf16[1,256,256]{2,1,0:T(8,128)(2,1)S(1)}, bf16[1,256,256]{2,1,0:T(8,128)(2,1)S(1)}, u32[]{:S(2)}, u32[]{:S(2)}) collective-permute-start(bf16[1,256,256]{2,1,0:T(8,128)(2,1)S(1)} %get-tuple-element.14), channel_id=1, source_target_pairs={{0,4},{4,8},{8,12},{12,16},{16,20},{20,24},{24,28},{1,5},{5,9},{9,... | collective-permute-start | bytes 393224 | tf_op jit(solution)/shard_map/ppermute | solution.py:16
  74.0 23.3 %collective-permute-start.4 = (bf16[4,256,256]{2,1,0:T(8,128)(2,1)S(1)}, bf16[4,256,256]{2,1,0:T(8,128)(2,1)S(1)}, u32[]{:S(2)}, u32[]{:S(2)}) collective-permute-start(bf16[4,256,256]{2,1,0:T(8,128)(2,1)S(1)} %get-tuple-element.10), channel_id=1, source_target_pairs={{0,4},{4,0},{1,5},{5,1},{2,6},{6,2},{3,7},{7,3},{8,12},{12,8},{9,1... | collective-permute-start | bytes 1572872 | tf_op jit(solution)/shard_map/ppermute | solution.py:92
  91.0 2.1 %copy-start = (bf16[10,256,512]{1,2,0:T(8,128)(2,1)S(1)}, bf16[10,256,512]{1,2,0:T(8,128)(2,1)}, u32[]{:S(2)}) copy-start(bf16[10,256,512]{1,2,0:T(8,128)(2,1)} %all-gather.5.cloned.1.call-done) | copy-start | bytes 7864324
  102.2 2.1 %copy-start.2 = (bf16[4,256,256]{2,1,0:T(8,128)(2,1)S(1)}, bf16[4,256,256]{2,1,0:T(8,128)(2,1)}, u32[]{:S(2)}) copy-start(bf16[4,256,256]{2,1,0:T(8,128)(2,1)} %get-tuple-element.11) | copy-start | bytes 1572868
  105.5 12.3 %all-to-all-start.1 = ((bf16[4,256,256]{2,0,1:T(4,128)(2,1)}), bf16[4,256,256]{2,0,1:T(4,128)(2,1)S(1)}, u32[]{:S(2)}, u32[]{:S(2)}) async-start(bf16[4,256,256]{2,0,1:T(4,128)(2,1)} %copy.20), calls=%async_computation.1 | async-start | bytes 1048576 | tf_op jit(solution)/shard_map/all_to_all | solution.py:90
  117.8 29.3 %all-to-all-start.2 = ((bf16[4,256,4,256]{3,1,0,2:T(8,128)(2,1)}), bf16[4,256,4,256]{3,1,0,2:T(8,128)(2,1)S(1)}, u32[]{:S(2)}, u32[]{:S(2)}) async-start(bf16[4,256,4,256]{3,1,0,2:T(8,128)(2,1)} %copy.23), calls=%async_computation.2 | async-start | bytes 4194304 | tf_op jit(solution)/shard_map/all_to_all | solution.py:130
Sparse Core Ops, SparseCore 0:
  9.5 29.6 all-gather.2
  41.4 25.7 all-gather.4
  104.4 48.6 reduce-scatter.1

commit v5 on v4

--- a/solution.py
+++ b/solution.py
@@ -87,7 +87,6 @@
     unit = conv_wide * inverse_rms
     normed_filters = unit.astype(jnp.bfloat16)
     grad_conv = (inverse_rms * (upstream - unit * mean_gu)).astype(jnp.bfloat16)
-    normed = lax.all_to_all(normed_filters, "chan", split_axis=1, concat_axis=2, tiled=True)
 
     sent_grad = lax.ppermute(grad_conv, "lo", [(0, 1), (1, 0)])
     img_block = jnp.pad(img_block, ((0, 0), (1, 1), (0, 0)))
@@ -111,9 +110,17 @@
         return jnp.stack(blocks)
 
     own_part = pair_part(grad_conv, height * lo)
+    sent_grad, own_part = lax.optimization_barrier((sent_grad, own_part))
+    stacked = (own_part + pair_part(sent_grad, height * (1 - lo))).astype(jnp.bfloat16)
+    grad_weight = lax.psum_scatter(
+        stacked.reshape(3, 3, width_w, local_filters), "hi", scatter_dimension=2, tiled=True
+    ).astype(jnp.float32)
+
+    grad_late, normed_late, _ = lax.optimization_barrier((grad_conv, normed_filters, stacked))
+    normed = lax.all_to_all(normed_late, "chan", split_axis=1, concat_axis=2, tiled=True)
 
     grad_rimmed = jnp.concatenate(
-        [shift_rows(grad_conv[-1:], upward=False), grad_conv, shift_rows(grad_conv[:1], upward=True)], axis=0
+        [shift_rows(grad_late[-1:], upward=False), grad_late, shift_rows(grad_late[:1], upward=True)], axis=0
     )
     grad_padded = jnp.pad(grad_rimmed, ((0, 0), (1, 1), (0, 0)))
     columns = jnp.concatenate(
@@ -129,12 +136,6 @@
     split = input_term.astype(jnp.bfloat16).reshape(height, breadth, chans, all_chans // chans)
     received = lax.all_to_all(split, "chan", split_axis=2, concat_axis=2, tiled=True)
     grad_input = jnp.sum(received.astype(jnp.float32), axis=2).astype(jnp.bfloat16)
-    sent_grad, _, own_part = lax.optimization_barrier((sent_grad, split, own_part))
-
-    stacked = (own_part + pair_part(sent_grad, height * (1 - lo))).reshape(3, 3, width_w, local_filters)
-    grad_weight = lax.psum_scatter(
-        stacked.astype(jnp.bfloat16), "hi", scatter_dimension=2, tiled=True
-    ).astype(jnp.float32)
     return (normed, grad_input, grad_weight)
 
 

time: 164 us -> 167 us (1.018)
  waiting for transfers between devices: 50.7 us -> 55.1 us
    all_to_all x1, waiting for transfers between devices: 7.15 us -> 0.01 us  [on_device(): lax.all_to_all(normed_late, 'chan', split_axis=1, concat_axis=2, tiled=True)]
    ppermute x1, waiting for transfers between devices: 0.01 us -> 6.9 us  [on_device(): sent_grad = lax.ppermute(grad_conv, 'lo', [(0, 1), (1, 0)])]
    ppermute x1, waiting for transfers between devices: 1.8 us -> 8.17 us  [on_device(): lax.ppermute(local_subset(send_rows, 1 - lo), 'lo', [(0, 1), (1, 0)])]
    all_to_all x1, waiting for transfers between devices: 4.53 us -> 2.05 us  [on_device(): lax.all_to_all(grad_out, 'chan', split_axis=2, concat_axis=1, tiled=True)]
  transfers between devices with their start and end apart: 14 -> 14, of which waited for: 9 -> 8; matrix products, arithmetic and copies ran while one was open for 30% -> 29% of each run, Pallas kernels for 0% -> 0%
where the time goes in v5:
time: 167 us; the launch traced here: 164 us
  waiting for transfers between devices  55.1 us (33%)
  starting transfers between devices  31.4 us (19%)
  matrix products  28.7 us (17%)
  local copies, waits for them, and re-layouts  20.3 us (12%)
  between operations  14.3 us (9%)
  other arithmetic  8.26 us (5%)
  blocking collectives  6.31 us (4%)
    all_to_all x1, waiting for transfers between devices, on_device(): lax.all_to_all(split, 'chan', split_axis=2, concat_axis=2, tiled=True)  24.1 us
    ppermute x4, starting transfers between devices, shift_rows(): return lax.ppermute(rows, SLAB, pairs)  13.5 us
    unnamed x19, local copies, waits for them, and re-layouts  11.5 us
    dot_general x18, matrix products, pair_part(): lax.dot_general(weight_window, flat, (((0,), (0,)), ((), ())), preferred_...  10.9 us
    dot_general x1, matrix products, on_device(): input_term = jnp.dot(columns, by_filter, preferred_element_type=jnp.float32)  8.7 us
    ppermute x1, waiting for transfers between devices, on_device(): lax.ppermute(local_subset(send_rows, 1 - lo), 'lo', [(0, 1), (1, 0)])  8.17 us
    dot_general x4, matrix products, taps(): out = jnp.dot(flat, by_row[a], preferred_element_type=jnp.float32)  7.23 us
    ppermute x1, waiting for transfers between devices, on_device(): sent_grad = lax.ppermute(grad_conv, 'lo', [(0, 1), (1, 0)])  6.9 us
  transfers between devices with their start and end apart: 14, of which 8 were waited for; matrix products, arithmetic and copies ran while one was open for 29% of the time, Pallas kernels for 0%

profile of v5, /device:TPU:4, one launch (start us, length us, event | category | flops | bytes accessed | tf_op | source)
XLA Modules:
  0.0 164.3 jit_solution(1997553045112770902)
XLA Ops:
  9.2 1.9 %collective-permute-start.4 = (bf16[1,256,256]{1,2,0:T(8,128)(2,1)S(1)}, bf16[1,256,256]{1,2,0:T(8,128)(2,1)S(1)}, u32[]{:S(2)}, u32[]{:S(2)}) collective-permute-start(bf16[1,256,256]{1,2,0:T(8,128)(2,1)S(1)} %get-tuple-element.19), channel_id=1, source_target_pairs={{4,0},{8,4},{12,8},{16,12},{20,16},{24,20},{28,24},{5,1},{9,5},{13... | collective-permute-start | bytes 393224 | tf_op jit(solution)/shard_map/ppermute | solution.py:16
  11.2 4.8 %collective-permute-start.3 = (bf16[1,256,256]{1,2,0:T(8,128)(2,1)S(1)}, bf16[1,256,256]{1,2,0:T(8,128)(2,1)S(1)}, u32[]{:S(2)}, u32[]{:S(2)}) collective-permute-start(bf16[1,256,256]{1,2,0:T(8,128)(2,1)S(1)} %get-tuple-element.18), channel_id=1, source_target_pairs={{0,4},{4,8},{8,12},{12,16},{16,20},{20,24},{24,28},{1,5},{5,9},{9,... | collective-permute-start | bytes 393224 | tf_op jit(solution)/shard_map/ppermute | solution.py:16
  17.4 2.7 %collective-permute-done.3 = bf16[1,256,256]{1,2,0:T(8,128)(2,1)S(1)} collective-permute-done((bf16[1,256,256]{1,2,0:T(8,128)(2,1)S(1)}, bf16[1,256,256]{1,2,0:T(8,128)(2,1)S(1)}, u32[]{:S(2)}, u32[]{:S(2)}) %collective-permute-start.3) | collective-permute-done | bytes 131104 | tf_op jit(solution)/shard_map/ppermute | solution.py:16
  20.4 8.2 %collective-permute-done.5 = bf16[4,256,128]{1,2,0:T(8,128)(2,1)S(1)} collective-permute-done((bf16[4,256,128]{1,2,0:T(8,128)(2,1)S(1)}, bf16[4,256,128]{1,2,0:T(8,128)(2,1)S(1)}, u32[]{:S(2)}, u32[]{:S(2)}) %collective-permute-start.5) | collective-permute-done | bytes 262176 | tf_op jit(solution)/shard_map/ppermute | solution.py:63
  32.0 3.5 %all-to-all-start = ((bf16[4,2,32768]{2,1,0:T(2,128)(2,1)}), bf16[4,2,32768]{2,1,0:T(2,128)(2,1)S(1)}, u32[]{:S(2)}, u32[]{:S(2)}) async-start(bf16[4,2,32768]{2,1,0:T(2,128)(2,1)} %reshape.217), calls=%async_computation | async-start | bytes 1048576 | tf_op jit(solution)/shard_map/all_to_all | solution.py:40
  35.5 6.7 %copy.17 = bf16[3,3,1024,256]{2,3,1,0:T(8,128)(2,1)} copy(bf16[3,3,1024,256]{3,2,1,0:T(8,128)(2,1)} %param.4) | data formatting | bytes 9437184 | tf_op args[1]
  42.2 2.1 %all-to-all-done = bf16[4,2,32768]{2,1,0:T(2,128)(2,1)S(1)} async-done(((bf16[4,2,32768]{2,1,0:T(2,128)(2,1)}), bf16[4,2,32768]{2,1,0:T(2,128)(2,1)S(1)}, u32[]{:S(2)}, u32[]{:S(2)}) %all-to-all-start) | async-done | bytes 524320 | tf_op jit(solution)/shard_map/all_to_all | solution.py:40
  45.7 2.3 %fusion.17 = f32[1,256,3,256]{3,1,2,0:T(8,128)S(1)} fusion(bf16[3,1024,3,256]{1,3,2,0:T(8,128)(2,1)} %bitcast.216, bf16[4,256,1024]{2,1,0:T(8,128)(2,1)} %all-gather.3.cloned.1.call-done), kind=kOutput, calls=%fused_computation.45 | convolution fusion | flops 402653184 | bytes 2883584 | tf_op jit(solution)/shard_map/dot_general | solution.py:48
  48.1 2.3 %collective-permute-start.1 = (f32[1,256,256]{2,1,0:T(8,128)S(1)}, f32[1,256,256]{2,1,0:T(8,128)S(1)}, u32[]{:S(2)}, u32[]{:S(2)}) collective-permute-start(f32[1,256,256]{2,1,0:T(8,128)S(1)} %fusion.63), channel_id=1, source_target_pairs={{4,0},{8,4},{12,8},{16,12},{20,16},{24,20},{28,24},{5,1},{9,5},{13... | collective-permute-start | bytes 786440 | tf_op jit(solution)/shard_map/ppermute | solution.py:52
  52.1 4.6 %collective-permute-start = (f32[1,256,256]{2,1,0:T(8,128)S(1)}, f32[1,256,256]{2,1,0:T(8,128)S(1)}, u32[]{:S(2)}, u32[]{:S(2)}) collective-permute-start(f32[1,256,256]{2,1,0:T(8,128)S(1)} %fusion.60), channel_id=1, source_target_pairs={{0,4},{4,8},{8,12},{12,16},{16,20},{20,24},{24,28},{1,5},{5,9},{9,... | collective-permute-start | bytes 786440 | tf_op jit(solution)/shard_map/ppermute | solution.py:51
  61.8 2.6 %collective-permute-done = f32[1,256,256]{2,1,0:T(8,128)S(1)} collective-permute-done((f32[1,256,256]{2,1,0:T(8,128)S(1)}, f32[1,256,256]{2,1,0:T(8,128)S(1)}, u32[]{:S(2)}, u32[]{:S(2)}) %collective-permute-start) | collective-permute-done | bytes 262176 | tf_op jit(solution)/shard_map/ppermute | solution.py:51
  65.3 6.3 %psum.7 = f32[4,256,2]{1,0,2:T(4,128)S(1)} all-reduce(f32[4,256,2]{1,0,2:T(4,128)S(1)} %pad_maximum_fusion.3), channel_id=1, replica_groups=mesh['hi'=4,'lo'=2,'chan'=4] {'chan'}, use_global_device_ids=true, to_apply=%region_2.3 | all-reduce | flops 2048 | bytes 16384 | tf_op jit(solution)/shard_map/psum | solution.py:84
  72.1 1.9 %fusion.39 = f32[9,512,256]{2,1,0:T(8,128)S(1)} fusion(bf16[4,256,256]{2,1,0:T(8,128)(2,1)S(1)} %get-tuple-element.10, s32[]{:T(128)S(6)} %select_n.36, bf16[10,256,512]{1,2,0:T(8,128)(2,1)} %all-gather.5.cloned.1.call-done), kind=kOutput, calls=%fused_computation.83 | convolution fusion | flops 268435456 | bytes 3670020 | tf_op jit(solution)/shard_map/dot_general | solution.py:103
  78.5 6.9 %collective-permute-done.2 = bf16[4,256,256]{2,1,0:T(8,128)(2,1)S(1)} collective-permute-done((bf16[4,256,256]{2,1,0:T(8,128)(2,1)S(1)}, bf16[4,256,256]{2,1,0:T(8,128)(2,1)S(1)}, u32[]{:S(2)}, u32[]{:S(2)}) %collective-permute-start.2) | collective-permute-done | bytes 524320 | tf_op jit(solution)/shard_map/ppermute | solution.py:91
  90.2 2.1 %add_convert_fusion = bf16[9,512,256]{2,1,0:T(8,128)(2,1)} fusion(f32[9,512,256]{2,1,0:T(8,128)S(1)} %fusion.31, f32[9,512,256]{2,1,0:T(8,128)S(1)} %fusion.22), kind=kLoop, calls=%fused_computation.18 | loop fusion | flops 2359296 | bytes 11796480 | tf_op jit(solution)/shard_map/convert_element_type | solution.py:114
  92.3 2.2 %collective-permute-start.7 = (bf16[1,256,256]{2,1,0:T(8,128)(2,1)S(1)}, bf16[1,256,256]{2,1,0:T(8,128)(2,1)S(1)}, u32[]{:S(2)}, u32[]{:S(2)}) collective-permute-start(bf16[1,256,256]{2,1,0:T(8,128)(2,1)S(1)} %get-tuple-element.17), channel_id=1, source_target_pairs={{4,0},{8,4},{12,8},{16,12},{20,16},{24,20},{28,24},{5,1},{9,5},{13... | collective-permute-start | bytes 393224 | tf_op jit(solution)/shard_map/ppermute | solution.py:16
  94.5 4.6 %collective-permute-start.6 = (bf16[1,256,256]{2,1,0:T(8,128)(2,1)S(1)}, bf16[1,256,256]{2,1,0:T(8,128)(2,1)S(1)}, u32[]{:S(2)}, u32[]{:S(2)}) collective-permute-start(bf16[1,256,256]{2,1,0:T(8,128)(2,1)S(1)} %get-tuple-element.16), channel_id=1, source_target_pairs={{0,4},{4,8},{8,12},{12,16},{16,20},{20,24},{24,28},{1,5},{5,9},{9,... | collective-permute-start | bytes 393224 | tf_op jit(solution)/shard_map/ppermute | solution.py:16
  100.3 3.5 %all-to-all-start.1 = ((bf16[4,256,256]{2,0,1:T(4,128)(2,1)}), bf16[4,256,256]{2,0,1:T(4,128)(2,1)S(1)}, u32[]{:S(2)}, u32[]{:S(2)}) async-start(bf16[4,256,256]{2,0,1:T(4,128)(2,1)} %copy.24), calls=%async_computation.1 | async-start | bytes 1048576 | tf_op jit(solution)/shard_map/all_to_all | solution.py:120
  105.4 8.7 %convolution_convert_fusion = bf16[1024,1024]{1,0:T(8,128)(2,1)} fusion(bf16[1024,2304]{1,0:T(8,128)(2,1)S(1)} %bitcast.230, bf16[2304,1024]{1,0:T(8,128)(2,1)} %bitcast.217), kind=kOutput, calls=%fused_computation.26 | convolution fusion | flops 4832886784 | bytes 11534336 | tf_op jit(solution)/shard_map/dot_general | solution.py:135
  114.1 3.3 %reshape.186 = bf16[4,256,4,256]{3,2,1,0:T(4,128)(2,1)S(1)} reshape(bf16[1024,1024]{1,0:T(8,128)(2,1)} %convolution_convert_fusion) | data formatting | bytes 4194304 | tf_op jit(solution)/shard_map/reshape | solution.py:136
  119.1 3.6 %all-to-all-start.2 = ((bf16[4,256,4,256]{3,1,0,2:T(8,128)(2,1)}), bf16[4,256,4,256]{3,1,0,2:T(8,128)(2,1)S(1)}, u32[]{:S(2)}, u32[]{:S(2)}) async-start(bf16[4,256,4,256]{3,1,0,2:T(8,128)(2,1)} %copy.27), calls=%async_computation.2 | async-start | bytes 4194304 | tf_op jit(solution)/shard_map/all_to_all | solution.py:137
  124.3 24.1 %all-to-all-done.2 = bf16[4,256,4,256]{3,1,0,2:T(8,128)(2,1)S(1)} async-done(((bf16[4,256,4,256]{3,1,0,2:T(8,128)(2,1)}), bf16[4,256,4,256]{3,1,0,2:T(8,128)(2,1)S(1)}, u32[]{:S(2)}, u32[]{:S(2)}) %all-to-all-start.2) | async-done | bytes 2097184 | tf_op jit(solution)/shard_map/all_to_all | solution.py:137
  149.6 6.0 %reduce-scatter.2.cloned.1.call-done = bf16[3,3,128,256]{3,2,1,0:T(8,128)(2,1)} async-done(((bf16[3,3,512,256]{3,2,1,0:T(8,128)(2,1)}), bf16[3,3,128,256]{3,2,1,0:T(8,128)(2,1)}) %reduce-scatter.2.cloned.1.call-update) | async-done | bytes 589840 | tf_op jit(solution)/shard_map/reduce_scatter | solution.py:115
  155.6 2.2 %convert_element_type.72 = f32[3,3,128,256]{3,2,1,0:T(8,128)} convert(bf16[3,3,128,256]{3,2,1,0:T(8,128)(2,1)} %reduce-scatter.2.cloned.1.call-done) | non-fusion elementwise | flops 294912 | bytes 1769472 | tf_op jit(solution)/shard_map/convert_element_type | solution.py:117
  (81 shorter events, 33.1 us)
Async XLA Ops:
  7.2 22.5 %copy-start.3 = (bf16[4,64,1024]{2,1,0:T(8,128)(2,1)S(1)}, bf16[4,64,1024]{2,1,0:T(8,128)(2,1)}, u32[]{:S(2)}) copy-start(bf16[4,64,1024]{2,1,0:T(8,128)(2,1)} %param.5) | copy-start | bytes 1572868
  7.2 38.5 %all-gather.3.cloned.1.call-start = ((), (), s32[]{:S(2)}) async-start(), calls=%async_computation.4 | async-start | bytes 2621440 | tf_op jit(solution)/shard_map/all_gather | solution.py:41
  7.9 64.2 %all-gather.5.cloned.1.call-start = ((), (), s32[]{:S(2)}) async-start(), calls=%async_computation.5 | async-start | bytes 3276800 | tf_op jit(solution)/shard_map/all_gather | solution.py:68
  9.2 8.1 %collective-permute-start.4 = (bf16[1,256,256]{1,2,0:T(8,128)(2,1)S(1)}, bf16[1,256,256]{1,2,0:T(8,128)(2,1)S(1)}, u32[]{:S(2)}, u32[]{:S(2)}) collective-permute-start(bf16[1,256,256]{1,2,0:T(8,128)(2,1)S(1)} %get-tuple-element.19), channel_id=1, source_target_pairs={{4,0},{8,4},{12,8},{16,12},{20,16},{24,20},{28,24},{5,1},{9,5},{13... | collective-permute-start | bytes 393224 | tf_op jit(solution)/shard_map/ppermute | solution.py:16
  11.2 8.9 %collective-permute-start.3 = (bf16[1,256,256]{1,2,0:T(8,128)(2,1)S(1)}, bf16[1,256,256]{1,2,0:T(8,128)(2,1)S(1)}, u32[]{:S(2)}, u32[]{:S(2)}) collective-permute-start(bf16[1,256,256]{1,2,0:T(8,128)(2,1)S(1)} %get-tuple-element.18), channel_id=1, source_target_pairs={{0,4},{4,8},{8,12},{12,16},{16,20},{20,24},{24,28},{1,5},{5,9},{9,... | collective-permute-start | bytes 393224 | tf_op jit(solution)/shard_map/ppermute | solution.py:16
  20.3 8.3 %collective-permute-start.5 = (bf16[4,256,128]{1,2,0:T(8,128)(2,1)S(1)}, bf16[4,256,128]{1,2,0:T(8,128)(2,1)S(1)}, u32[]{:S(2)}, u32[]{:S(2)}) collective-permute-start(bf16[4,256,128]{1,2,0:T(8,128)(2,1)S(1)} %dynamic-slice_bitcast_fusion.1), channel_id=1, source_target_pairs={{0,4},{4,0},{1,5},{5,1},{2,6},{6,2},{3,7},{7,3},{8,12},{12,8},{9,1... | collective-permute-start | bytes 786440 | tf_op jit(solution)/shard_map/ppermute | solution.py:63
  32.0 12.3 %all-to-all-start = ((bf16[4,2,32768]{2,1,0:T(2,128)(2,1)}), bf16[4,2,32768]{2,1,0:T(2,128)(2,1)S(1)}, u32[]{:S(2)}, u32[]{:S(2)}) async-start(bf16[4,2,32768]{2,1,0:T(2,128)(2,1)} %reshape.217), calls=%async_computation | async-start | bytes 1048576 | tf_op jit(solution)/shard_map/all_to_all | solution.py:40
  45.7 4.8 %copy-start.1 = (bf16[3,3,1024,256]{2,3,1,0:T(8,128)(2,1)S(1)}, bf16[3,3,1024,256]{2,3,1,0:T(8,128)(2,1)}, u32[]{:S(2)}) copy-start(bf16[3,3,1024,256]{2,3,1,0:T(8,128)(2,1)} %copy.17) | copy-start | bytes 14155780
  45.7 11.1 %copy-start.2 = (bf16[4,256,1024]{2,1,0:T(8,128)(2,1)S(1)}, bf16[4,256,1024]{2,1,0:T(8,128)(2,1)}, u32[]{:S(2)}) copy-start(bf16[4,256,1024]{2,1,0:T(8,128)(2,1)} %all-gather.3.cloned.1.call-done) | copy-start | bytes 6291460
  48.1 13.7 %collective-permute-start.1 = (f32[1,256,256]{2,1,0:T(8,128)S(1)}, f32[1,256,256]{2,1,0:T(8,128)S(1)}, u32[]{:S(2)}, u32[]{:S(2)}) collective-permute-start(f32[1,256,256]{2,1,0:T(8,128)S(1)} %fusion.63), channel_id=1, source_target_pairs={{4,0},{8,4},{12,8},{16,12},{20,16},{24,20},{28,24},{5,1},{9,5},{13... | collective-permute-start | bytes 786440 | tf_op jit(solution)/shard_map/ppermute | solution.py:52
  52.1 12.3 %collective-permute-start = (f32[1,256,256]{2,1,0:T(8,128)S(1)}, f32[1,256,256]{2,1,0:T(8,128)S(1)}, u32[]{:S(2)}, u32[]{:S(2)}) collective-permute-start(f32[1,256,256]{2,1,0:T(8,128)S(1)} %fusion.60), channel_id=1, source_target_pairs={{0,4},{4,8},{8,12},{12,16},{16,20},{20,24},{24,28},{1,5},{5,9},{9,... | collective-permute-start | bytes 786440 | tf_op jit(solution)/shard_map/ppermute | solution.py:51
  72.0 13.3 %collective-permute-start.2 = (bf16[4,256,256]{2,1,0:T(8,128)(2,1)S(1)}, bf16[4,256,256]{2,1,0:T(8,128)(2,1)S(1)}, u32[]{:S(2)}, u32[]{:S(2)}) collective-permute-start(bf16[4,256,256]{2,1,0:T(8,128)(2,1)S(1)} %get-tuple-element.10), channel_id=1, source_target_pairs={{0,4},{4,0},{1,5},{5,1},{2,6},{6,2},{3,7},{7,3},{8,12},{12,8},{9,1... | collective-permute-start | bytes 1572872 | tf_op jit(solution)/shard_map/ppermute | solution.py:91
  72.1 2.1 %copy-start = (bf16[10,256,512]{1,2,0:T(8,128)(2,1)S(1)}, bf16[10,256,512]{1,2,0:T(8,128)(2,1)}, u32[]{:S(2)}) copy-start(bf16[10,256,512]{1,2,0:T(8,128)(2,1)} %all-gather.5.cloned.1.call-done) | copy-start | bytes 7864324
  92.3 12.2 %collective-permute-start.7 = (bf16[1,256,256]{2,1,0:T(8,128)(2,1)S(1)}, bf16[1,256,256]{2,1,0:T(8,128)(2,1)S(1)}, u32[]{:S(2)}, u32[]{:S(2)}) collective-permute-start(bf16[1,256,256]{2,1,0:T(8,128)(2,1)S(1)} %get-tuple-element.17), channel_id=1, source_target_pairs={{4,0},{8,4},{12,8},{16,12},{20,16},{24,20},{28,24},{5,1},{9,5},{13... | collective-permute-start | bytes 393224 | tf_op jit(solution)/shard_map/ppermute | solution.py:16
  94.5 10.0 %collective-permute-start.6 = (bf16[1,256,256]{2,1,0:T(8,128)(2,1)S(1)}, bf16[1,256,256]{2,1,0:T(8,128)(2,1)S(1)}, u32[]{:S(2)}, u32[]{:S(2)}) collective-permute-start(bf16[1,256,256]{2,1,0:T(8,128)(2,1)S(1)} %get-tuple-element.16), channel_id=1, source_target_pairs={{0,4},{4,8},{8,12},{12,16},{16,20},{20,24},{24,28},{1,5},{5,9},{9,... | collective-permute-start | bytes 393224 | tf_op jit(solution)/shard_map/ppermute | solution.py:16
  100.3 18.8 %all-to-all-start.1 = ((bf16[4,256,256]{2,0,1:T(4,128)(2,1)}), bf16[4,256,256]{2,0,1:T(4,128)(2,1)S(1)}, u32[]{:S(2)}, u32[]{:S(2)}) async-start(bf16[4,256,256]{2,0,1:T(4,128)(2,1)} %copy.24), calls=%async_computation.1 | async-start | bytes 1048576 | tf_op jit(solution)/shard_map/all_to_all | solution.py:120
  103.7 51.9 %reduce-scatter.2.cloned.1.call-start = ((), (), s32[]{:S(2)}) async-start(), calls=%async_computation.6 | async-start | bytes 2949120 | tf_op jit(solution)/shard_map/reduce_scatter | solution.py:115
  119.1 29.3 %all-to-all-start.2 = ((bf16[4,256,4,256]{3,1,0,2:T(8,128)(2,1)}), bf16[4,256,4,256]{3,1,0,2:T(8,128)(2,1)S(1)}, u32[]{:S(2)}, u32[]{:S(2)}) async-start(bf16[4,256,4,256]{3,1,0,2:T(8,128)(2,1)} %copy.27), calls=%async_computation.2 | async-start | bytes 4194304 | tf_op jit(solution)/shard_map/all_to_all | solution.py:137
Sparse Core Ops, SparseCore 0:
  9.6 24.0 all-gather.2
  35.8 25.5 all-gather.4
  106.9 48.6 reduce-scatter.1

commit v6 on v3

--- a/solution.py
+++ b/solution.py
@@ -123,14 +123,14 @@
     grad_padded = jnp.pad(grad_rimmed, ((0, 0), (1, 1), (0, 0)))
     columns = jnp.concatenate(
         [
-            grad_padded[a : a + height, b : b + breadth]
+            grad_padded[2 - a : 2 - a + height, 2 - b : 2 - b + breadth]
             for a in range(3)
             for b in range(3)
         ],
         axis=-1,
     ).reshape(height * breadth, 9 * local_filters)
-    flipped = jnp.transpose(weight[::-1, ::-1], (0, 1, 3, 2)).reshape(9 * local_filters, all_chans)
-    input_term = jnp.dot(columns, flipped, preferred_element_type=jnp.float32)
+    by_filter = jnp.transpose(weight, (0, 1, 3, 2)).reshape(9 * local_filters, all_chans)
+    input_term = jnp.dot(columns, by_filter, preferred_element_type=jnp.float32)
     split = input_term.astype(jnp.bfloat16).reshape(height, breadth, chans, all_chans // chans)
     received = lax.all_to_all(split, "chan", split_axis=2, concat_axis=2, tiled=True)
     grad_input = jnp.sum(received.astype(jnp.float32), axis=2).astype(jnp.bfloat16)

time: 156 us -> 155 us (level)
  local copies, waits for them, and re-layouts: 27.4 us -> 22.3 us
  waiting for transfers between devices: 37.6 us -> 41.3 us
    rev x1 -> x0, local copies, waits for them, and re-layouts: 4.98 us -> none  [on_device(): weight[::-1, ::-1]]
    ppermute x1, waiting for transfers between devices: 0.01 us -> 4.73 us  [on_device(): sent_grad = lax.ppermute(grad_conv, 'lo', [(0, 1), (1, 0)])]
  transfers between devices with their start and end apart: 14 -> 14, of which waited for: 6 -> 7; matrix products, arithmetic and copies ran while one was open for 39% -> 36% of each run, Pallas kernels for 0% -> 0%
where the time goes in v6:
time: 155 us; the launch traced here: 153 us
  waiting for transfers between devices  41.3 us (27%)
  starting transfers between devices  31.4 us (20%)
  matrix products  27.5 us (18%)
  local copies, waits for them, and re-layouts  22.3 us (14%)
  between operations  14.2 us (9%)
  other arithmetic  9.46 us (6%)
  blocking collectives  6.58 us (4%)
    all_to_all x1, waiting for transfers between devices, on_device(): lax.all_to_all(split, 'chan', split_axis=2, concat_axis=2, tiled=True)  24.1 us
    ppermute x4, starting transfers between devices, shift_rows(): return lax.ppermute(rows, SLAB, pairs)  13.7 us
    unnamed x23, local copies, waits for them, and re-layouts  12.9 us
    dot_general x9, matrix products, on_device(): lax.dot_general(weight_window, grad_flat, (((0,), (0,)), ((), ())), prefe...  9.78 us
    dot_general x1, matrix products, on_device(): input_term = jnp.dot(columns, by_filter, preferred_element_type=jnp.float32)  8.71 us
    dot_general x4, matrix products, taps(): out = jnp.dot(flat, by_row[a], preferred_element_type=jnp.float32)  7.22 us
    psum x1, blocking collectives, on_device(): totals = lax.psum(partial, 'chan')  6.58 us
    reshape x2, local copies, waits for them, and re-layouts, on_device(): input_term.astype(jnp.bfloat16)  5.01 us
  transfers between devices with their start and end apart: 14, of which 7 were waited for; matrix products, arithmetic and copies ran while one was open for 36% of the time, Pallas kernels for 0%

profile of v6, /device:TPU:4, one launch (start us, length us, event | category | flops | bytes accessed | tf_op | source)
XLA Modules:
  0.0 152.7 jit_solution(1664163023230641210)
XLA Ops:
  9.2 1.9 %collective-permute-start.5 = (bf16[1,256,256]{1,2,0:T(8,128)(2,1)S(1)}, bf16[1,256,256]{1,2,0:T(8,128)(2,1)S(1)}, u32[]{:S(2)}, u32[]{:S(2)}) collective-permute-start(bf16[1,256,256]{1,2,0:T(8,128)(2,1)S(1)} %get-tuple-element.9), channel_id=1, source_target_pairs={{4,0},{8,4},{12,8},{16,12},{20,16},{24,20},{28,24},{5,1},{9,5},{13... | collective-permute-start | bytes 393224 | tf_op jit(solution)/shard_map/ppermute | solution.py:16
  11.1 4.8 %collective-permute-start.4 = (bf16[1,256,256]{1,2,0:T(8,128)(2,1)S(1)}, bf16[1,256,256]{1,2,0:T(8,128)(2,1)S(1)}, u32[]{:S(2)}, u32[]{:S(2)}) collective-permute-start(bf16[1,256,256]{1,2,0:T(8,128)(2,1)S(1)} %get-tuple-element.8), channel_id=1, source_target_pairs={{0,4},{4,8},{8,12},{12,16},{16,20},{20,24},{24,28},{1,5},{5,9},{9,... | collective-permute-start | bytes 393224 | tf_op jit(solution)/shard_map/ppermute | solution.py:16
  18.2 3.5 %all-to-all-start = ((bf16[4,2,32768]{2,1,0:T(2,128)(2,1)}), bf16[4,2,32768]{2,1,0:T(2,128)(2,1)S(1)}, u32[]{:S(2)}, u32[]{:S(2)}) async-start(bf16[4,2,32768]{2,1,0:T(2,128)(2,1)} %reshape.196), calls=%async_computation | async-start | bytes 1048576 | tf_op jit(solution)/shard_map/all_to_all | solution.py:40
  22.1 6.6 %copy.17 = bf16[3,3,1024,256]{2,3,1,0:T(8,128)(2,1)} copy(bf16[3,3,1024,256]{3,2,1,0:T(8,128)(2,1)} %param.4) | data formatting | bytes 9437184 | tf_op args[1]
  28.8 1.9 %collective-permute-done.6 = bf16[4,256,128]{1,2,0:T(8,128)(2,1)S(1)} collective-permute-done((bf16[4,256,128]{1,2,0:T(8,128)(2,1)S(1)}, bf16[4,256,128]{1,2,0:T(8,128)(2,1)S(1)}, u32[]{:S(2)}, u32[]{:S(2)}) %collective-permute-start.6) | collective-permute-done | bytes 262176 | tf_op jit(solution)/shard_map/ppermute | solution.py:63
  31.8 4.6 %all-to-all-done = bf16[4,2,32768]{2,1,0:T(2,128)(2,1)S(1)} async-done(((bf16[4,2,32768]{2,1,0:T(2,128)(2,1)}), bf16[4,2,32768]{2,1,0:T(2,128)(2,1)S(1)}, u32[]{:S(2)}, u32[]{:S(2)}) %all-to-all-start) | async-done | bytes 524320 | tf_op jit(solution)/shard_map/all_to_all | solution.py:40
  39.3 2.3 %fusion.23 = f32[1,256,3,256]{3,1,2,0:T(8,128)S(1)} fusion(bf16[3,1024,3,256]{1,3,2,0:T(8,128)(2,1)} %bitcast.227, bf16[4,256,1024]{2,1,0:T(8,128)(2,1)} %all-gather.3.cloned.1.call-done), kind=kOutput, calls=%fused_computation.41 | convolution fusion | flops 402653184 | bytes 2883584 | tf_op jit(solution)/shard_map/dot_general | solution.py:48
  41.7 2.6 %collective-permute-start.1 = (f32[1,256,256]{2,1,0:T(8,128)S(1)}, f32[1,256,256]{2,1,0:T(8,128)S(1)}, u32[]{:S(2)}, u32[]{:S(2)}) collective-permute-start(f32[1,256,256]{2,1,0:T(8,128)S(1)} %fusion.86), channel_id=1, source_target_pairs={{4,0},{8,4},{12,8},{16,12},{20,16},{24,20},{28,24},{5,1},{9,5},{13... | collective-permute-start | bytes 786440 | tf_op jit(solution)/shard_map/ppermute | solution.py:52
  46.0 4.3 %collective-permute-start = (f32[1,256,256]{2,1,0:T(8,128)S(1)}, f32[1,256,256]{2,1,0:T(8,128)S(1)}, u32[]{:S(2)}, u32[]{:S(2)}) collective-permute-start(f32[1,256,256]{2,1,0:T(8,128)S(1)} %fusion.83), channel_id=1, source_target_pairs={{0,4},{4,8},{8,12},{12,16},{16,20},{20,24},{24,28},{1,5},{5,9},{9,... | collective-permute-start | bytes 786440 | tf_op jit(solution)/shard_map/ppermute | solution.py:51
  51.7 1.8 %fusion.6 = f32[4,256,3,256]{3,1,2,0:T(8,128)S(1)} fusion(bf16[4,256,1024]{2,1,0:T(8,128)(2,1)S(1)} %copy-done.2, bf16[3,1024,3,256]{1,3,2,0:T(8,128)(2,1)S(1)} %bitcast.231), kind=kOutput, calls=%fused_computation.17 | convolution fusion | flops 1610612736 | bytes 6815744 | tf_op jit(solution)/shard_map/dot_general | solution.py:48
  53.5 1.8 %pad_add_fusion = f32[4,256,3,256]{3,1,2,0:T(8,128)S(1)} fusion(f32[3,256,3,256]{3,1,2,0:T(8,128)S(1)} %fusion.9, f32[4,256,3,256]{3,1,2,0:T(8,128)S(1)} %fusion.6, bf16[4,256,1024]{2,1,0:T(8,128)(2,1)S(1)} %copy-done.2, bf16[3,1024,3,256]{1,3,2,0:T(8,128)(2,1)S(1)} %bitcast.232), kind=kOutput, calls=%fused_computation.6 | convolution fusion | flops 1209532416 | bytes 11796480 | tf_op jit(solution)/shard_map/jit(_pad)/pad | solution.py:71
  55.4 3.3 %collective-permute-done = f32[1,256,256]{2,1,0:T(8,128)S(1)} collective-permute-done((f32[1,256,256]{2,1,0:T(8,128)S(1)}, f32[1,256,256]{2,1,0:T(8,128)S(1)}, u32[]{:S(2)}, u32[]{:S(2)}) %collective-permute-start) | collective-permute-done | bytes 262176 | tf_op jit(solution)/shard_map/ppermute | solution.py:51
  59.5 6.6 %psum.7 = f32[4,256,2]{1,0,2:T(4,128)S(1)} all-reduce(f32[4,256,2]{1,0,2:T(4,128)S(1)} %pad_maximum_fusion.3), channel_id=1, replica_groups=mesh['hi'=4,'lo'=2,'chan'=4] {'chan'}, use_global_device_ids=true, to_apply=%region_2.3 | all-reduce | flops 2048 | bytes 16384 | tf_op jit(solution)/shard_map/psum | solution.py:84
  67.8 3.5 %all-to-all-start.1 = ((bf16[4,256,256]{2,0,1:T(4,128)(2,1)}), bf16[4,256,256]{2,0,1:T(4,128)(2,1)S(1)}, u32[]{:S(2)}, u32[]{:S(2)}) async-start(bf16[4,256,256]{2,0,1:T(4,128)(2,1)} %copy.20), calls=%async_computation.1 | async-start | bytes 1048576 | tf_op jit(solution)/shard_map/all_to_all | solution.py:90
  72.0 3.9 %collective-permute-start.3 = (bf16[1,256,256]{2,1,0:T(8,128)(2,1)}, bf16[1,256,256]{2,1,0:T(8,128)(2,1)}, u32[]{:S(2)}, u32[]{:S(2)}) collective-permute-start(bf16[1,256,256]{2,1,0:T(8,128)(2,1)} %get-tuple-element.11), channel_id=1, source_target_pairs={{4,0},{8,4},{12,8},{16,12},{20,16},{24,20},{28,24},{5,1},{9,5},{13... | collective-permute-start | bytes 393224 | tf_op jit(solution)/shard_map/ppermute | solution.py:16
  75.9 3.0 %collective-permute-start.2 = (bf16[1,256,256]{2,1,0:T(8,128)(2,1)}, bf16[1,256,256]{2,1,0:T(8,128)(2,1)S(1)}, u32[]{:S(2)}, u32[]{:S(2)}) collective-permute-start(bf16[1,256,256]{2,1,0:T(8,128)(2,1)} %get-tuple-element.10), channel_id=1, source_target_pairs={{0,4},{4,8},{8,12},{12,16},{16,20},{20,24},{24,28},{1,5},{5,9},{9,... | collective-permute-start | bytes 393224 | tf_op jit(solution)/shard_map/ppermute | solution.py:16
  79.0 4.7 %collective-permute-done.7 = bf16[4,256,256]{2,1,0:T(8,128)(2,1)S(1)} collective-permute-done((bf16[4,256,256]{2,1,0:T(8,128)(2,1)S(1)}, bf16[4,256,256]{2,1,0:T(8,128)(2,1)S(1)}, u32[]{:S(2)}, u32[]{:S(2)}) %collective-permute-start.7) | collective-permute-done | bytes 524320 | tf_op jit(solution)/shard_map/ppermute | solution.py:92
  85.2 2.9 %fusion.54 = bf16[9,512,256]{2,1,0:T(8,128)(2,1)S(1)} fusion(bf16[8,256,256]{2,1,0:T(8,128)(2,1)} %fusion.66, bf16[10,256,512]{1,2,0:T(8,128)(2,1)} %all-gather.5.cloned.1.call-done), kind=kOutput, calls=%fused_computation.73 | convolution fusion | flops 537001984 | bytes 3932160 | tf_op jit(solution)/shard_map/dot_general | solution.py:108
  99.2 8.7 %convolution_convert_fusion = bf16[1024,1024]{1,0:T(8,128)(2,1)} fusion(bf16[1024,2304]{1,0:T(8,128)(2,1)S(1)} %bitcast.242, bf16[2304,1024]{1,0:T(8,128)(2,1)} %bitcast.228), kind=kOutput, calls=%fused_computation.19 | convolution fusion | flops 4832886784 | bytes 11534336 | tf_op jit(solution)/shard_map/dot_general | solution.py:133
  107.9 3.3 %reshape.171 = bf16[4,256,4,256]{3,2,1,0:T(4,128)(2,1)S(1)} reshape(bf16[1024,1024]{1,0:T(8,128)(2,1)} %convolution_convert_fusion) | data formatting | bytes 4194304 | tf_op jit(solution)/shard_map/reshape | solution.py:134
  111.3 1.7 %copy.23 = bf16[4,256,4,256]{3,1,0,2:T(8,128)(2,1)} copy(bf16[4,256,4,256]{3,2,1,0:T(4,128)(2,1)S(1)} %reshape.171) | data formatting | bytes 4194304 | tf_op jit(solution)/shard_map/reshape | solution.py:134
  112.9 3.6 %all-to-all-start.2 = ((bf16[4,256,4,256]{3,1,0,2:T(8,128)(2,1)}), bf16[4,256,4,256]{3,1,0,2:T(8,128)(2,1)S(1)}, u32[]{:S(2)}, u32[]{:S(2)}) async-start(bf16[4,256,4,256]{3,1,0,2:T(8,128)(2,1)} %copy.23), calls=%async_computation.2 | async-start | bytes 4194304 | tf_op jit(solution)/shard_map/all_to_all | solution.py:135
  118.1 24.1 %all-to-all-done.2 = bf16[4,256,4,256]{3,1,0,2:T(8,128)(2,1)S(1)} async-done(((bf16[4,256,4,256]{3,1,0,2:T(8,128)(2,1)}), bf16[4,256,4,256]{3,1,0,2:T(8,128)(2,1)S(1)}, u32[]{:S(2)}, u32[]{:S(2)}) %all-to-all-start.2) | async-done | bytes 2097184 | tf_op jit(solution)/shard_map/all_to_all | solution.py:135
  144.0 2.2 %convert_element_type.73 = f32[3,3,128,256]{3,2,1,0:T(8,128)} convert(bf16[3,3,128,256]{3,2,1,0:T(8,128)(2,1)} %reduce-scatter.2.cloned.1.call-done) | non-fusion elementwise | flops 294912 | bytes 1769472 | tf_op jit(solution)/shard_map/convert_element_type | solution.py:118
  (76 shorter events, 30.8 us)
Async XLA Ops:
  7.2 8.8 %copy-start.4 = (bf16[4,64,1024]{2,1,0:T(8,128)(2,1)S(1)}, bf16[4,64,1024]{2,1,0:T(8,128)(2,1)}, u32[]{:S(2)}) copy-start(bf16[4,64,1024]{2,1,0:T(8,128)(2,1)} %param.5) | copy-start | bytes 1572868
  7.2 32.1 %all-gather.3.cloned.1.call-start = ((), (), s32[]{:S(2)}) async-start(), calls=%async_computation.4 | async-start | bytes 2621440 | tf_op jit(solution)/shard_map/all_gather | solution.py:41
  9.2 12.6 %collective-permute-start.5 = (bf16[1,256,256]{1,2,0:T(8,128)(2,1)S(1)}, bf16[1,256,256]{1,2,0:T(8,128)(2,1)S(1)}, u32[]{:S(2)}, u32[]{:S(2)}) collective-permute-start(bf16[1,256,256]{1,2,0:T(8,128)(2,1)S(1)} %get-tuple-element.9), channel_id=1, source_target_pairs={{4,0},{8,4},{12,8},{16,12},{20,16},{24,20},{28,24},{5,1},{9,5},{13... | collective-permute-start | bytes 393224 | tf_op jit(solution)/shard_map/ppermute | solution.py:16
  11.1 10.7 %collective-permute-start.4 = (bf16[1,256,256]{1,2,0:T(8,128)(2,1)S(1)}, bf16[1,256,256]{1,2,0:T(8,128)(2,1)S(1)}, u32[]{:S(2)}, u32[]{:S(2)}) collective-permute-start(bf16[1,256,256]{1,2,0:T(8,128)(2,1)S(1)} %get-tuple-element.8), channel_id=1, source_target_pairs={{0,4},{4,8},{8,12},{12,16},{16,20},{20,24},{24,28},{1,5},{5,9},{9,... | collective-permute-start | bytes 393224 | tf_op jit(solution)/shard_map/ppermute | solution.py:16
  18.2 18.2 %all-to-all-start = ((bf16[4,2,32768]{2,1,0:T(2,128)(2,1)}), bf16[4,2,32768]{2,1,0:T(2,128)(2,1)S(1)}, u32[]{:S(2)}, u32[]{:S(2)}) async-start(bf16[4,2,32768]{2,1,0:T(2,128)(2,1)} %reshape.196), calls=%async_computation | async-start | bytes 1048576 | tf_op jit(solution)/shard_map/all_to_all | solution.py:40
  21.7 63.5 %all-gather.5.cloned.1.call-start = ((), (), s32[]{:S(2)}) async-start(), calls=%async_computation.5 | async-start | bytes 3276800 | tf_op jit(solution)/shard_map/all_gather | solution.py:68
  22.0 8.7 %collective-permute-start.6 = (bf16[4,256,128]{1,2,0:T(8,128)(2,1)S(1)}, bf16[4,256,128]{1,2,0:T(8,128)(2,1)S(1)}, u32[]{:S(2)}, u32[]{:S(2)}) collective-permute-start(bf16[4,256,128]{1,2,0:T(8,128)(2,1)S(1)} %dynamic-slice_bitcast_fusion.1), channel_id=1, source_target_pairs={{0,4},{4,0},{1,5},{5,1},{2,6},{6,2},{3,7},{7,3},{8,12},{12,8},{9,1... | collective-permute-start | bytes 786440 | tf_op jit(solution)/shard_map/ppermute | solution.py:63
  39.3 5.0 %copy-start = (bf16[3,3,1024,256]{2,3,1,0:T(8,128)(2,1)S(1)}, bf16[3,3,1024,256]{2,3,1,0:T(8,128)(2,1)}, u32[]{:S(2)}) copy-start(bf16[3,3,1024,256]{2,3,1,0:T(8,128)(2,1)} %copy.17) | copy-start | bytes 14155780
  41.6 8.6 %copy-start.2 = (bf16[4,256,1024]{2,1,0:T(8,128)(2,1)S(1)}, bf16[4,256,1024]{2,1,0:T(8,128)(2,1)}, u32[]{:S(2)}) copy-start(bf16[4,256,1024]{2,1,0:T(8,128)(2,1)} %all-gather.3.cloned.1.call-done) | copy-start | bytes 6291460
  41.7 13.7 %collective-permute-start.1 = (f32[1,256,256]{2,1,0:T(8,128)S(1)}, f32[1,256,256]{2,1,0:T(8,128)S(1)}, u32[]{:S(2)}, u32[]{:S(2)}) collective-permute-start(f32[1,256,256]{2,1,0:T(8,128)S(1)} %fusion.86), channel_id=1, source_target_pairs={{4,0},{8,4},{12,8},{16,12},{20,16},{24,20},{28,24},{5,1},{9,5},{13... | collective-permute-start | bytes 786440 | tf_op jit(solution)/shard_map/ppermute | solution.py:52
  46.0 12.7 %collective-permute-start = (f32[1,256,256]{2,1,0:T(8,128)S(1)}, f32[1,256,256]{2,1,0:T(8,128)S(1)}, u32[]{:S(2)}, u32[]{:S(2)}) collective-permute-start(f32[1,256,256]{2,1,0:T(8,128)S(1)} %fusion.83), channel_id=1, source_target_pairs={{0,4},{4,8},{8,12},{12,16},{16,20},{20,24},{24,28},{1,5},{5,9},{9,... | collective-permute-start | bytes 786440 | tf_op jit(solution)/shard_map/ppermute | solution.py:51
  66.5 17.2 %collective-permute-start.7 = (bf16[4,256,256]{2,1,0:T(8,128)(2,1)S(1)}, bf16[4,256,256]{2,1,0:T(8,128)(2,1)S(1)}, u32[]{:S(2)}, u32[]{:S(2)}) collective-permute-start(bf16[4,256,256]{2,1,0:T(8,128)(2,1)S(1)} %get-tuple-element.6), channel_id=1, source_target_pairs={{0,4},{4,0},{1,5},{5,1},{2,6},{6,2},{3,7},{7,3},{8,12},{12,8},{9,1... | collective-permute-start | bytes 1572872 | tf_op jit(solution)/shard_map/ppermute | solution.py:92
  67.8 45.2 %all-to-all-start.1 = ((bf16[4,256,256]{2,0,1:T(4,128)(2,1)}), bf16[4,256,256]{2,0,1:T(4,128)(2,1)S(1)}, u32[]{:S(2)}, u32[]{:S(2)}) async-start(bf16[4,256,256]{2,0,1:T(4,128)(2,1)} %copy.20), calls=%async_computation.1 | async-start | bytes 1048576 | tf_op jit(solution)/shard_map/all_to_all | solution.py:90
  71.3 72.8 %reduce-scatter.2.cloned.1.call-start = ((), (), s32[]{:S(2)}) async-start(), calls=%async_computation.6 | async-start | bytes 2949120 | tf_op jit(solution)/shard_map/reduce_scatter | solution.py:116
  72.0 24.5 %collective-permute-start.3 = (bf16[1,256,256]{2,1,0:T(8,128)(2,1)}, bf16[1,256,256]{2,1,0:T(8,128)(2,1)}, u32[]{:S(2)}, u32[]{:S(2)}) collective-permute-start(bf16[1,256,256]{2,1,0:T(8,128)(2,1)} %get-tuple-element.11), channel_id=1, source_target_pairs={{4,0},{8,4},{12,8},{16,12},{20,16},{24,20},{28,24},{5,1},{9,5},{13... | collective-permute-start | bytes 393224 | tf_op jit(solution)/shard_map/ppermute | solution.py:16
  75.9 20.6 %collective-permute-start.2 = (bf16[1,256,256]{2,1,0:T(8,128)(2,1)}, bf16[1,256,256]{2,1,0:T(8,128)(2,1)S(1)}, u32[]{:S(2)}, u32[]{:S(2)}) collective-permute-start(bf16[1,256,256]{2,1,0:T(8,128)(2,1)} %get-tuple-element.10), channel_id=1, source_target_pairs={{0,4},{4,8},{8,12},{12,16},{16,20},{20,24},{24,28},{1,5},{5,9},{9,... | collective-permute-start | bytes 393224 | tf_op jit(solution)/shard_map/ppermute | solution.py:16
  85.2 2.9 %copy-start.3 = (bf16[8,256,256]{2,1,0:T(8,128)(2,1)S(1)}, bf16[8,256,256]{2,1,0:T(8,128)(2,1)}, u32[]{:S(2)}) copy-start(bf16[8,256,256]{2,1,0:T(8,128)(2,1)} %fusion.66) | copy-start | bytes 3145732
  85.2 3.0 %copy-start.5 = (bf16[10,256,512]{1,2,0:T(8,128)(2,1)S(1)}, bf16[10,256,512]{1,2,0:T(8,128)(2,1)}, u32[]{:S(2)}) copy-start(bf16[10,256,512]{1,2,0:T(8,128)(2,1)} %all-gather.5.cloned.1.call-done) | copy-start | bytes 7864324
  95.1 1.4 copy-start.1
  112.9 29.3 %all-to-all-start.2 = ((bf16[4,256,4,256]{3,1,0,2:T(8,128)(2,1)}), bf16[4,256,4,256]{3,1,0,2:T(8,128)(2,1)S(1)}, u32[]{:S(2)}, u32[]{:S(2)}) async-start(bf16[4,256,4,256]{3,1,0,2:T(8,128)(2,1)} %copy.23), calls=%async_computation.2 | async-start | bytes 4194304 | tf_op jit(solution)/shard_map/all_to_all | solution.py:135
Sparse Core Ops, SparseCore 0:
  9.6 29.6 all-gather.2
  40.8 25.7 all-gather.4
  96.6 47.3 reduce-scatter.1

commit v7 on v5

--- a/solution.py
+++ b/solution.py
@@ -87,40 +87,36 @@
     unit = conv_wide * inverse_rms
     normed_filters = unit.astype(jnp.bfloat16)
     grad_conv = (inverse_rms * (upstream - unit * mean_gu)).astype(jnp.bfloat16)
+    normed = lax.all_to_all(normed_filters, "chan", split_axis=1, concat_axis=2, tiled=True)
 
     sent_grad = lax.ppermute(grad_conv, "lo", [(0, 1), (1, 0)])
-    img_block = jnp.pad(img_block, ((0, 0), (1, 1), (0, 0)))
     width_w = img_block.shape[2]
 
     def pair_part(grad_rows, first_row):
-        flat = grad_rows.reshape(height * breadth, local_filters)
-        blocks = []
-        for weight_tap_row in range(3):
-            rows = lax.dynamic_slice_in_dim(img_block, first_row + weight_tap_row, height, axis=0)
-            for weight_tap_col in range(3):
-                weight_window = rows[:, weight_tap_col : weight_tap_col + breadth].reshape(height * breadth, width_w)
-                blocks.append(
-                    lax.dot_general(
-                        weight_window,
-                        flat,
-                        (((0,), (0,)), ((), ())),
-                        preferred_element_type=jnp.float32,
-                    )
-                )
-        return jnp.stack(blocks)
+        grad_cols = jnp.pad(grad_rows, ((0, 0), (1, 1), (0, 0)))
+        shifted = jnp.stack([grad_cols[:, 2 - b : 2 - b + breadth] for b in range(3)], axis=2)
+        shifted = shifted.reshape(height * breadth, 3 * local_filters)
+        rows = [
+            lax.dynamic_slice_in_dim(img_block, first_row + a, height, axis=0).reshape(height * breadth, width_w)
+            for a in range(3)
+        ]
+        return jnp.stack(
+            [
+                lax.dot_general(r, shifted, (((0,), (0,)), ((), ())), preferred_element_type=jnp.float32)
+                for r in rows
+            ]
+        )
 
     own_part = pair_part(grad_conv, height * lo)
     sent_grad, own_part = lax.optimization_barrier((sent_grad, own_part))
-    stacked = (own_part + pair_part(sent_grad, height * (1 - lo))).astype(jnp.bfloat16)
+    summed = own_part + pair_part(sent_grad, height * (1 - lo))
+    stacked = jnp.transpose(summed.reshape(3, width_w, 3, local_filters), (0, 2, 1, 3))
     grad_weight = lax.psum_scatter(
-        stacked.reshape(3, 3, width_w, local_filters), "hi", scatter_dimension=2, tiled=True
+        stacked.astype(jnp.bfloat16), "hi", scatter_dimension=2, tiled=True
     ).astype(jnp.float32)
 
-    grad_late, normed_late, _ = lax.optimization_barrier((grad_conv, normed_filters, stacked))
-    normed = lax.all_to_all(normed_late, "chan", split_axis=1, concat_axis=2, tiled=True)
-
     grad_rimmed = jnp.concatenate(
-        [shift_rows(grad_late[-1:], upward=False), grad_late, shift_rows(grad_late[:1], upward=True)], axis=0
+        [shift_rows(grad_conv[-1:], upward=False), grad_conv, shift_rows(grad_conv[:1], upward=True)], axis=0
     )
     grad_padded = jnp.pad(grad_rimmed, ((0, 0), (1, 1), (0, 0)))
     columns = jnp.concatenate(

time: 167 us -> 201 us (1.20)
  local copies, waits for them, and re-layouts: 20.3 us -> 61.9 us
  waiting for transfers between devices: 55.1 us -> 47 us
  other arithmetic: 8.26 us -> 13.5 us
  matrix products: 28.7 us -> 24.6 us
    unnamed x19 -> x37, local copies, waits for them, and re-layouts: 11.5 us -> 36.9 us
    ppermute x4, waiting for transfers between devices: 4.08 us -> 11.4 us  [shift_rows(): return lax.ppermute(rows, SLAB, pairs)]
    ppermute x1, waiting for transfers between devices: 6.9 us -> 0.01 us  [on_device(): sent_grad = lax.ppermute(grad_conv, 'lo', [(0, 1), (1, 0)])]
    ppermute x1, waiting for transfers between devices: 8.17 us -> 1.62 us  [on_device(): lax.ppermute(local_subset(send_rows, 1 - lo), 'lo', [(0, 1), (1, 0)])]
    another operation x0 -> x4, local copies, waits for them, and re-layouts: none -> 6.14 us  [pair_part(): jnp.stack([grad_cols[:, 2 - b:2 - b + breadth] for b in range(3)], axis=2)]
    reduce_scatter x1 -> x0, waiting for transfers between devices: 5.98 us -> none  [on_device(): lax.psum_scatter(stacked.reshape(3, 3, width_w, local_filters), 'hi', sca...]
    convert_element_type x0 -> x2, local copies, waits for them, and re-layouts: none -> 5.48 us  [the longest x1 4.28 us: on_device(): stacked.astype(jnp.bfloat16)]
    dynamic_slice x0 -> x5, local copies, waits for them, and re-layouts: none -> 5.04 us  [the longest x1 4.6 us: pair_part(): lax.dynamic_slice_in_dim(img_block, first_row + a, height, axis=0)]
  transfers between devices with their start and end apart: 14 -> 14, of which waited for: 8 -> 7; matrix products, arithmetic and copies ran while one was open for 29% -> 31% of each run, Pallas kernels for 0% -> 0%
where the time goes in v7:
time: 201 us; the launch traced here: 199 us
  local copies, waits for them, and re-layouts  61.9 us (31%)
  waiting for transfers between devices  47 us (23%)
  starting transfers between devices  31.5 us (16%)
  matrix products  24.6 us (12%)
  between operations  14.2 us (7%)
  other arithmetic  13.5 us (7%)
  blocking collectives  6.58 us (3%)
    unnamed x37, local copies, waits for them, and re-layouts  36.9 us
    all_to_all x1, waiting for transfers between devices, on_device(): lax.all_to_all(split, 'chan', split_axis=2, concat_axis=2, tiled=True)  24.1 us
    ppermute x4, starting transfers between devices, shift_rows(): return lax.ppermute(rows, SLAB, pairs)  13.7 us
    ppermute x4, waiting for transfers between devices, shift_rows(): return lax.ppermute(rows, SLAB, pairs)  11.4 us
    dot_general x1, matrix products, on_device(): input_term = jnp.dot(columns, by_filter, preferred_element_type=jnp.float32)  9.28 us
    dot_general x4, matrix products, taps(): out = jnp.dot(flat, by_row[a], preferred_element_type=jnp.float32)  7.22 us
    psum x1, blocking collectives, on_device(): totals = lax.psum(partial, 'chan')  6.58 us
    dot_general x6, matrix products, pair_part(): lax.dot_general(r, shifted, (((0,), (0,)), ((), ())), preferred_element_t...  6.24 us
  transfers between devices with their start and end apart: 14, of which 7 were waited for; matrix products, arithmetic and copies ran while one was open for 31% of the time, Pallas kernels for 0%

profile of v7, /device:TPU:4, one launch (start us, length us, event | category | flops | bytes accessed | tf_op | source)
XLA Modules:
  0.0 199.3 jit_solution(6354662999415298271)
XLA Ops:
  11.1 4.8 %collective-permute-start.5 = (bf16[1,256,256]{1,2,0:T(8,128)(2,1)S(1)}, bf16[1,256,256]{1,2,0:T(8,128)(2,1)S(1)}, u32[]{:S(2)}, u32[]{:S(2)}) collective-permute-start(bf16[1,256,256]{1,2,0:T(8,128)(2,1)S(1)} %get-tuple-element.32), channel_id=1, source_target_pairs={{0,4},{4,8},{8,12},{12,16},{16,20},{20,24},{24,28},{1,5},{5,9},{9,... | collective-permute-start | bytes 393224 | tf_op jit(solution)/shard_map/ppermute | solution.py:16
  18.2 3.5 %all-to-all-start = ((bf16[4,2,32768]{2,1,0:T(2,128)(2,1)}), bf16[4,2,32768]{2,1,0:T(2,128)(2,1)S(1)}, u32[]{:S(2)}, u32[]{:S(2)}) async-start(bf16[4,2,32768]{2,1,0:T(2,128)(2,1)} %reshape.230), calls=%async_computation | async-start | bytes 1048576 | tf_op jit(solution)/shard_map/all_to_all | solution.py:40
  22.2 6.7 %copy.33 = bf16[3,3,1024,256]{2,3,1,0:T(8,128)(2,1)} copy(bf16[3,3,1024,256]{3,2,1,0:T(8,128)(2,1)} %param.4) | data formatting | bytes 9437184 | tf_op args[1]
  32.1 4.4 %all-to-all-done = bf16[4,2,32768]{2,1,0:T(2,128)(2,1)S(1)} async-done(((bf16[4,2,32768]{2,1,0:T(2,128)(2,1)}), bf16[4,2,32768]{2,1,0:T(2,128)(2,1)S(1)}, u32[]{:S(2)}, u32[]{:S(2)}) %all-to-all-start) | async-done | bytes 524320 | tf_op jit(solution)/shard_map/all_to_all | solution.py:40
  39.3 2.3 %fusion.18 = f32[1,256,3,256]{3,1,2,0:T(8,128)S(1)} fusion(bf16[3,1024,3,256]{1,3,2,0:T(8,128)(2,1)} %bitcast.175, bf16[4,256,1024]{2,1,0:T(8,128)(2,1)} %all-gather.3.cloned.1.call-done), kind=kOutput, calls=%fused_computation.37 | convolution fusion | flops 402653184 | bytes 2883584 | tf_op jit(solution)/shard_map/dot_general | solution.py:48
  41.7 2.6 %collective-permute-start.1 = (f32[1,256,256]{2,1,0:T(8,128)S(1)}, f32[1,256,256]{2,1,0:T(8,128)S(1)}, u32[]{:S(2)}, u32[]{:S(2)}) collective-permute-start(f32[1,256,256]{2,1,0:T(8,128)S(1)} %fusion.49), channel_id=1, source_target_pairs={{4,0},{8,4},{12,8},{16,12},{20,16},{24,20},{28,24},{5,1},{9,5},{13... | collective-permute-start | bytes 786440 | tf_op jit(solution)/shard_map/ppermute | solution.py:52
  46.0 4.3 %collective-permute-start = (f32[1,256,256]{2,1,0:T(8,128)S(1)}, f32[1,256,256]{2,1,0:T(8,128)S(1)}, u32[]{:S(2)}, u32[]{:S(2)}) collective-permute-start(f32[1,256,256]{2,1,0:T(8,128)S(1)} %fusion.46), channel_id=1, source_target_pairs={{0,4},{4,8},{8,12},{12,16},{16,20},{20,24},{24,28},{1,5},{5,9},{9,... | collective-permute-start | bytes 786440 | tf_op jit(solution)/shard_map/ppermute | solution.py:51
  55.4 3.3 %collective-permute-done = f32[1,256,256]{2,1,0:T(8,128)S(1)} collective-permute-done((f32[1,256,256]{2,1,0:T(8,128)S(1)}, f32[1,256,256]{2,1,0:T(8,128)S(1)}, u32[]{:S(2)}, u32[]{:S(2)}) %collective-permute-start) | collective-permute-done | bytes 262176 | tf_op jit(solution)/shard_map/ppermute | solution.py:51
  60.2 6.6 %psum.7 = f32[4,256,2]{1,0,2:T(4,128)S(1)} all-reduce(f32[4,256,2]{1,0,2:T(4,128)S(1)} %pad_maximum_fusion.6), channel_id=1, replica_groups=mesh['hi'=4,'lo'=2,'chan'=4] {'chan'}, use_global_device_ids=true, to_apply=%region_2.3 | all-reduce | flops 2048 | bytes 16384 | tf_op jit(solution)/shard_map/psum | solution.py:84
  69.0 3.9 %collective-permute-start.3 = (bf16[1,256,256]{2,1,0:T(8,128)(2,1)S(1)}, bf16[1,256,256]{2,1,0:T(8,128)(2,1)S(1)}, u32[]{:S(2)}, u32[]{:S(2)}) collective-permute-start(bf16[1,256,256]{2,1,0:T(8,128)(2,1)S(1)} %get-tuple-element.35), channel_id=1, source_target_pairs={{4,0},{8,4},{12,8},{16,12},{20,16},{24,20},{28,24},{5,1},{9,5},{13... | collective-permute-start | bytes 393224 | tf_op jit(solution)/shard_map/ppermute | solution.py:16
  72.9 3.0 %collective-permute-start.2 = (bf16[1,256,256]{2,1,0:T(8,128)(2,1)S(1)}, bf16[1,256,256]{2,1,0:T(8,128)(2,1)S(1)}, u32[]{:S(2)}, u32[]{:S(2)}) collective-permute-start(bf16[1,256,256]{2,1,0:T(8,128)(2,1)S(1)} %get-tuple-element.34), channel_id=1, source_target_pairs={{0,4},{4,8},{8,12},{12,16},{16,20},{20,24},{24,28},{1,5},{5,9},{9,... | collective-permute-start | bytes 393224 | tf_op jit(solution)/shard_map/ppermute | solution.py:16
  76.3 6.4 %collective-permute-done.3 = bf16[1,256,256]{2,1,0:T(8,128)(2,1)S(1)} collective-permute-done((bf16[1,256,256]{2,1,0:T(8,128)(2,1)S(1)}, bf16[1,256,256]{2,1,0:T(8,128)(2,1)S(1)}, u32[]{:S(2)}, u32[]{:S(2)}) %collective-permute-start.3) | collective-permute-done | bytes 131104 | tf_op jit(solution)/shard_map/ppermute | solution.py:16
  82.7 5.0 %collective-permute-done.2 = bf16[1,256,256]{2,1,0:T(8,128)(2,1)S(1)} collective-permute-done((bf16[1,256,256]{2,1,0:T(8,128)(2,1)S(1)}, bf16[1,256,256]{2,1,0:T(8,128)(2,1)S(1)}, u32[]{:S(2)}, u32[]{:S(2)}) %collective-permute-start.2) | collective-permute-done | bytes 131104 | tf_op jit(solution)/shard_map/ppermute | solution.py:16
  90.9 2.2 %copy.46 = bf16[4,256,3,256]{1,0,3,2:T(4,128)(2,1)} copy(bf16[4,256,3,256]{3,1,2,0:T(8,128)(2,1)S(1)} %pad_maximum_fusion.1) | data formatting | bytes 3145728 | tf_op jit(solution)/shard_map/stack | solution.py:97
  94.9 4.6 %constant_dynamic-slice_fusion.2 = (bf16[4,256,512]{2,1,0:T(8,128)(2,1)}, bf16[4,256,512]{2,1,0:T(8,128)(2,1)}, bf16[4,256,512]{2,1,0:T(8,128)(2,1)}, bf16[4,256...) fusion(bf16[10,256,512]{2,1,0:T(8,128)(2,1)} %all-gather.5.cloned.1.call-done, ...), kind=kLoop, calls=%fused_computation.104 | loop fusion | bytes 12582936 | tf_op jit(solution)/shard_map/dynamic_slice | solution.py:100
  102.7 2.5 %pad_maximum_fusion = f32[3,512,768]{2,1,0:T(8,128)} fusion(f32[1,512,768]{2,1,0:T(8,128)S(1)} %convolution_bitcast_fusion.3, f32[1,512,768]{2,1,0:T(8,128)S(1)} %convolution_bitcast_fusion.4, f32[1,512,768]{2,1,0:T(8,128)S(1)} %convolution_bitcast_fusion.5), kind=kLoop, calls=%fused_computation | loop fusion | flops 2359296 | bytes 9437184 | tf_op jit(solution)/shard_map/stack | solution.py:103
  117.9 4.3 %copy.48 = bf16[3,512,768]{1,2,0:T(8,128)(2,1)} copy(bf16[3,512,768]{2,1,0:T(8,128)(2,1)} %fusion) | data formatting | bytes 4718592 | tf_op jit(solution)/shard_map/convert_element_type | solution.py:115
  122.2 5.8 %copy.53 = bf16[3,3,512,256]{3,1,0,2:T(4,128)(2,1)} copy(bf16[3,3,512,256]{2,3,1,0:T(8,128)(2,1)} %bitcast.173) | data formatting | bytes 4718592
  128.0 7.1 %reshape.228 = bf16[512,2304]{1,0:T(8,128)(2,1)} reshape(bf16[512,3,3,256]{3,2,1,0:T(4,128)(2,1)} %bitcast.172) | data formatting | bytes 4718592
  137.3 3.7 %all-to-all-start.1 = ((bf16[4,256,256]{2,0,1:T(4,128)(2,1)}), bf16[4,256,256]{2,0,1:T(4,128)(2,1)S(1)}, u32[]{:S(2)}, u32[]{:S(2)}) async-start(bf16[4,256,256]{2,0,1:T(4,128)(2,1)} %copy.36), calls=%async_computation.1 | async-start | bytes 1048576 | tf_op jit(solution)/shard_map/all_to_all | solution.py:90
  144.7 9.3 %convolution_convert_fusion = bf16[1024,1024]{1,0:T(8,128)(2,1)} fusion(bf16[1024,2304]{1,0:T(8,128)(2,1)} %bitcast.207, bf16[2304,1024]{1,0:T(8,128)(2,1)} %bitcast.176), kind=kOutput, calls=%fused_computation.10 | convolution fusion | flops 4832886784 | bytes 11534336 | tf_op jit(solution)/shard_map/dot_general | solution.py:131
  154.0 3.3 %reshape.202 = bf16[4,256,4,256]{3,2,1,0:T(4,128)(2,1)S(1)} reshape(bf16[1024,1024]{1,0:T(8,128)(2,1)} %convolution_convert_fusion) | data formatting | bytes 4194304 | tf_op jit(solution)/shard_map/reshape | solution.py:132
  159.0 3.6 %all-to-all-start.2 = ((bf16[4,256,4,256]{3,1,0,2:T(8,128)(2,1)}), bf16[4,256,4,256]{3,1,0,2:T(8,128)(2,1)S(1)}, u32[]{:S(2)}, u32[]{:S(2)}) async-start(bf16[4,256,4,256]{3,1,0,2:T(8,128)(2,1)} %copy.39), calls=%async_computation.2 | async-start | bytes 4194304 | tf_op jit(solution)/shard_map/all_to_all | solution.py:133
  164.2 24.1 %all-to-all-done.2 = bf16[4,256,4,256]{3,1,0,2:T(8,128)(2,1)S(1)} async-done(((bf16[4,256,4,256]{3,1,0,2:T(8,128)(2,1)}), bf16[4,256,4,256]{3,1,0,2:T(8,128)(2,1)S(1)}, u32[]{:S(2)}, u32[]{:S(2)}) %all-to-all-start.2) | async-done | bytes 2097184 | tf_op jit(solution)/shard_map/all_to_all | solution.py:133
  (99 shorter events, 57.8 us)
Async XLA Ops:
  7.2 8.8 %copy-start.6 = (bf16[4,64,1024]{2,1,0:T(8,128)(2,1)S(1)}, bf16[4,64,1024]{2,1,0:T(8,128)(2,1)}, u32[]{:S(2)}) copy-start(bf16[4,64,1024]{2,1,0:T(8,128)(2,1)} %param.5) | copy-start | bytes 1572868
  7.2 32.1 %all-gather.3.cloned.1.call-start = ((), (), s32[]{:S(2)}) async-start(), calls=%async_computation.4 | async-start | bytes 2621440 | tf_op jit(solution)/shard_map/all_gather | solution.py:41
  9.2 12.6 %collective-permute-start.6 = (bf16[1,256,256]{1,2,0:T(8,128)(2,1)S(1)}, bf16[1,256,256]{1,2,0:T(8,128)(2,1)S(1)}, u32[]{:S(2)}, u32[]{:S(2)}) collective-permute-start(bf16[1,256,256]{1,2,0:T(8,128)(2,1)S(1)} %get-tuple-element.33), channel_id=1, source_target_pairs={{4,0},{8,4},{12,8},{16,12},{20,16},{24,20},{28,24},{5,1},{9,5},{13... | collective-permute-start | bytes 393224 | tf_op jit(solution)/shard_map/ppermute | solution.py:16
  11.1 10.7 %collective-permute-start.5 = (bf16[1,256,256]{1,2,0:T(8,128)(2,1)S(1)}, bf16[1,256,256]{1,2,0:T(8,128)(2,1)S(1)}, u32[]{:S(2)}, u32[]{:S(2)}) collective-permute-start(bf16[1,256,256]{1,2,0:T(8,128)(2,1)S(1)} %get-tuple-element.32), channel_id=1, source_target_pairs={{0,4},{4,8},{8,12},{12,16},{16,20},{20,24},{24,28},{1,5},{5,9},{9,... | collective-permute-start | bytes 393224 | tf_op jit(solution)/shard_map/ppermute | solution.py:16
  18.2 18.2 %all-to-all-start = ((bf16[4,2,32768]{2,1,0:T(2,128)(2,1)}), bf16[4,2,32768]{2,1,0:T(2,128)(2,1)S(1)}, u32[]{:S(2)}, u32[]{:S(2)}) async-start(bf16[4,2,32768]{2,1,0:T(2,128)(2,1)} %reshape.230), calls=%async_computation | async-start | bytes 1048576 | tf_op jit(solution)/shard_map/all_to_all | solution.py:40
  21.7 73.2 %all-gather.5.cloned.1.call-start = ((), (), s32[]{:S(2)}) async-start(), calls=%async_computation.5 | async-start | bytes 3276800 | tf_op jit(solution)/shard_map/all_gather | solution.py:68
  22.1 8.7 %collective-permute-start.7 = (bf16[4,256,128]{2,1,0:T(8,128)(2,1)S(1)}, bf16[4,256,128]{2,1,0:T(8,128)(2,1)S(1)}, u32[]{:S(2)}, u32[]{:S(2)}) collective-permute-start(bf16[4,256,128]{2,1,0:T(8,128)(2,1)S(1)} %bitcast.206), channel_id=1, source_target_pairs={{0,4},{4,0},{1,5},{5,1},{2,6},{6,2},{3,7},{7,3},{8,12},{12,8},{9,1... | collective-permute-start | bytes 786440 | tf_op jit(solution)/shard_map/ppermute | solution.py:63
  32.0 157.5 %reduce-scatter.4.cloned.1.call-start = ((), (), s32[]{:S(2)}) async-start(), calls=%async_computation.6 | async-start | bytes 2949120
  39.3 5.0 %copy-start = (bf16[3,3,1024,256]{2,3,1,0:T(8,128)(2,1)S(1)}, bf16[3,3,1024,256]{2,3,1,0:T(8,128)(2,1)}, u32[]{:S(2)}) copy-start(bf16[3,3,1024,256]{2,3,1,0:T(8,128)(2,1)} %copy.33) | copy-start | bytes 14155780
  41.6 8.6 %copy-start.2 = (bf16[4,256,1024]{2,1,0:T(8,128)(2,1)S(1)}, bf16[4,256,1024]{2,1,0:T(8,128)(2,1)}, u32[]{:S(2)}) copy-start(bf16[4,256,1024]{2,1,0:T(8,128)(2,1)} %all-gather.3.cloned.1.call-done) | copy-start | bytes 6291460
  41.7 13.7 %collective-permute-start.1 = (f32[1,256,256]{2,1,0:T(8,128)S(1)}, f32[1,256,256]{2,1,0:T(8,128)S(1)}, u32[]{:S(2)}, u32[]{:S(2)}) collective-permute-start(f32[1,256,256]{2,1,0:T(8,128)S(1)} %fusion.49), channel_id=1, source_target_pairs={{4,0},{8,4},{12,8},{16,12},{20,16},{24,20},{28,24},{5,1},{9,5},{13... | collective-permute-start | bytes 786440 | tf_op jit(solution)/shard_map/ppermute | solution.py:52
  46.0 12.7 %collective-permute-start = (f32[1,256,256]{2,1,0:T(8,128)S(1)}, f32[1,256,256]{2,1,0:T(8,128)S(1)}, u32[]{:S(2)}, u32[]{:S(2)}) collective-permute-start(f32[1,256,256]{2,1,0:T(8,128)S(1)} %fusion.46), channel_id=1, source_target_pairs={{0,4},{4,8},{8,12},{12,16},{16,20},{20,24},{24,28},{1,5},{5,9},{9,... | collective-permute-start | bytes 786440 | tf_op jit(solution)/shard_map/ppermute | solution.py:51
  69.0 36.3 %collective-permute-start.4 = (bf16[4,256,256]{2,1,0:T(8,128)(2,1)S(1)}, bf16[4,256,256]{2,1,0:T(8,128)(2,1)}, u32[]{:S(2)}, u32[]{:S(2)}) collective-permute-start(bf16[4,256,256]{2,1,0:T(8,128)(2,1)S(1)} %get-tuple-element.25), channel_id=1, source_target_pairs={{0,4},{4,0},{1,5},{5,1},{2,6},{6,2},{3,7},{7,3},{8,12},{12,8},{9,1... | collective-permute-start | bytes 1572872 | tf_op jit(solution)/shard_map/ppermute | solution.py:92
  69.0 13.7 %collective-permute-start.3 = (bf16[1,256,256]{2,1,0:T(8,128)(2,1)S(1)}, bf16[1,256,256]{2,1,0:T(8,128)(2,1)S(1)}, u32[]{:S(2)}, u32[]{:S(2)}) collective-permute-start(bf16[1,256,256]{2,1,0:T(8,128)(2,1)S(1)} %get-tuple-element.35), channel_id=1, source_target_pairs={{4,0},{8,4},{12,8},{16,12},{20,16},{24,20},{28,24},{5,1},{9,5},{13... | collective-permute-start | bytes 393224 | tf_op jit(solution)/shard_map/ppermute | solution.py:16
  72.9 14.8 %collective-permute-start.2 = (bf16[1,256,256]{2,1,0:T(8,128)(2,1)S(1)}, bf16[1,256,256]{2,1,0:T(8,128)(2,1)S(1)}, u32[]{:S(2)}, u32[]{:S(2)}) collective-permute-start(bf16[1,256,256]{2,1,0:T(8,128)(2,1)S(1)} %get-tuple-element.34), channel_id=1, source_target_pairs={{0,4},{4,8},{8,12},{12,16},{16,20},{20,24},{24,28},{1,5},{5,9},{9,... | collective-permute-start | bytes 393224 | tf_op jit(solution)/shard_map/ppermute | solution.py:16
  88.5 2.2 %copy-start.7 = (bf16[4,256,2304]{2,1,0:T(8,128)(2,1)}, bf16[4,256,2304]{2,1,0:T(8,128)(2,1)S(1)}, u32[]{:S(2)}) copy-start(bf16[4,256,2304]{2,1,0:T(8,128)(2,1)S(1)} %get-tuple-element.31) | copy-start | bytes 14155780
  110.1 1.9 copy-start.5
  112.0 1.2 copy-start.4
  113.2 1.2 copy-start.3
  113.2 2.5 %slice-start = ((s8[4718592]{0:T(1024)(128)(4,1)}), s8[4194304]{0:T(1024)(128)(4,1)S(1)}, s32[]{:S(2)}) async-start(s8[4718592]{0:T(1024)(128)(4,1)} %bitcast.169), calls=%async_computation.7 | async-start | bytes 8388608
  114.2 1.8 slice-start.1
  135.1 1.0 copy-start.1
  137.3 21.7 %all-to-all-start.1 = ((bf16[4,256,256]{2,0,1:T(4,128)(2,1)}), bf16[4,256,256]{2,0,1:T(4,128)(2,1)S(1)}, u32[]{:S(2)}, u32[]{:S(2)}) async-start(bf16[4,256,256]{2,0,1:T(4,128)(2,1)} %copy.36), calls=%async_computation.1 | async-start | bytes 1048576 | tf_op jit(solution)/shard_map/all_to_all | solution.py:90
  159.0 29.3 %all-to-all-start.2 = ((bf16[4,256,4,256]{3,1,0,2:T(8,128)(2,1)}), bf16[4,256,4,256]{3,1,0,2:T(8,128)(2,1)S(1)}, u32[]{:S(2)}, u32[]{:S(2)}) async-start(bf16[4,256,4,256]{3,1,0,2:T(8,128)(2,1)} %copy.39), calls=%async_computation.2 | async-start | bytes 4194304 | tf_op jit(solution)/shard_map/all_to_all | solution.py:133
Sparse Core Ops, SparseCore 0:
  9.6 29.6 all-gather.2
  41.4 26.0 all-gather.4
  135.2 47.1 reduce-scatter.3

commit v8 on v5

--- a/solution.py
+++ b/solution.py
@@ -87,6 +87,7 @@
     unit = conv_wide * inverse_rms
     normed_filters = unit.astype(jnp.bfloat16)
     grad_conv = (inverse_rms * (upstream - unit * mean_gu)).astype(jnp.bfloat16)
+    normed = lax.all_to_all(normed_filters, "chan", split_axis=1, concat_axis=2, tiled=True)
 
     sent_grad = lax.ppermute(grad_conv, "lo", [(0, 1), (1, 0)])
     img_block = jnp.pad(img_block, ((0, 0), (1, 1), (0, 0)))
@@ -111,16 +112,13 @@
 
     own_part = pair_part(grad_conv, height * lo)
     sent_grad, own_part = lax.optimization_barrier((sent_grad, own_part))
-    stacked = (own_part + pair_part(sent_grad, height * (1 - lo))).astype(jnp.bfloat16)
+    stacked = (own_part + pair_part(sent_grad, height * (1 - lo))).reshape(3, 3, width_w, local_filters)
     grad_weight = lax.psum_scatter(
-        stacked.reshape(3, 3, width_w, local_filters), "hi", scatter_dimension=2, tiled=True
+        stacked.astype(jnp.bfloat16), "hi", scatter_dimension=2, tiled=True
     ).astype(jnp.float32)
 
-    grad_late, normed_late, _ = lax.optimization_barrier((grad_conv, normed_filters, stacked))
-    normed = lax.all_to_all(normed_late, "chan", split_axis=1, concat_axis=2, tiled=True)
-
     grad_rimmed = jnp.concatenate(
-        [shift_rows(grad_late[-1:], upward=False), grad_late, shift_rows(grad_late[:1], upward=True)], axis=0
+        [shift_rows(grad_conv[-1:], upward=False), grad_conv, shift_rows(grad_conv[:1], upward=True)], axis=0
     )
     grad_padded = jnp.pad(grad_rimmed, ((0, 0), (1, 1), (0, 0)))
     columns = jnp.concatenate(

time: 167 us -> 154 us (0.922)
  waiting for transfers between devices: 55.1 us -> 42.7 us
    ppermute x1, waiting for transfers between devices: 8.17 us -> 2.36 us  [on_device(): lax.ppermute(local_subset(send_rows, 1 - lo), 'lo', [(0, 1), (1, 0)])]
    reduce_scatter x1, waiting for transfers between devices: 5.98 us -> 3.21 us  [on_device(): lax.psum_scatter(stacked.astype(jnp.bfloat16), 'hi', scatter_dimension=2,...]
    ppermute x1, waiting for transfers between devices: 6.9 us -> 4.19 us  [on_device(): sent_grad = lax.ppermute(grad_conv, 'lo', [(0, 1), (1, 0)])]
  transfers between devices with their start and end apart: 14 -> 14, of which waited for: 8 -> 8; matrix products, arithmetic and copies ran while one was open for 29% -> 35% of each run, Pallas kernels for 0% -> 0%
where the time goes in v8:
time: 154 us; the launch traced here: 152 us
  waiting for transfers between devices  42.7 us (28%)
  starting transfers between devices  31.4 us (20%)
  matrix products  28.9 us (19%)
  local copies, waits for them, and re-layouts  20.3 us (13%)
  between operations  14.3 us (9%)
  other arithmetic  8.26 us (5%)
  blocking collectives  6.14 us (4%)
    all_to_all x1, waiting for transfers between devices, on_device(): lax.all_to_all(split, 'chan', split_axis=2, concat_axis=2, tiled=True)  24.1 us
    ppermute x4, starting transfers between devices, shift_rows(): return lax.ppermute(rows, SLAB, pairs)  13.7 us
    unnamed x19, local copies, waits for them, and re-layouts  11.5 us
    dot_general x18, matrix products, pair_part(): lax.dot_general(weight_window, flat, (((0,), (0,)), ((), ())), preferred_...  10.9 us
    dot_general x1, matrix products, on_device(): input_term = jnp.dot(columns, by_filter, preferred_element_type=jnp.float32)  8.92 us
    dot_general x4, matrix products, taps(): out = jnp.dot(flat, by_row[a], preferred_element_type=jnp.float32)  7.26 us
    psum x1, blocking collectives, on_device(): totals = lax.psum(partial, 'chan')  6.14 us
    reshape x2, local copies, waits for them, and re-layouts, on_device(): input_term.astype(jnp.bfloat16)  5.01 us
  transfers between devices with their start and end apart: 14, of which 8 were waited for; matrix products, arithmetic and copies ran while one was open for 35% of the time, Pallas kernels for 0%

profile of v8, /device:TPU:4, one launch (start us, length us, event | category | flops | bytes accessed | tf_op | source)
XLA Modules:
  0.0 152.0 jit_solution(11664189192779617677)
XLA Ops:
  9.2 1.9 %collective-permute-start.6 = (bf16[1,256,256]{1,2,0:T(8,128)(2,1)S(1)}, bf16[1,256,256]{1,2,0:T(8,128)(2,1)S(1)}, u32[]{:S(2)}, u32[]{:S(2)}) collective-permute-start(bf16[1,256,256]{1,2,0:T(8,128)(2,1)S(1)} %get-tuple-element.13), channel_id=1, source_target_pairs={{4,0},{8,4},{12,8},{16,12},{20,16},{24,20},{28,24},{5,1},{9,5},{13... | collective-permute-start | bytes 393224 | tf_op jit(solution)/shard_map/ppermute | solution.py:16
  11.1 4.8 %collective-permute-start.5 = (bf16[1,256,256]{1,2,0:T(8,128)(2,1)S(1)}, bf16[1,256,256]{1,2,0:T(8,128)(2,1)S(1)}, u32[]{:S(2)}, u32[]{:S(2)}) collective-permute-start(bf16[1,256,256]{1,2,0:T(8,128)(2,1)S(1)} %get-tuple-element.12), channel_id=1, source_target_pairs={{0,4},{4,8},{8,12},{12,16},{16,20},{20,24},{24,28},{1,5},{5,9},{9,... | collective-permute-start | bytes 393224 | tf_op jit(solution)/shard_map/ppermute | solution.py:16
  17.3 2.7 %collective-permute-done.5 = bf16[1,256,256]{1,2,0:T(8,128)(2,1)S(1)} collective-permute-done((bf16[1,256,256]{1,2,0:T(8,128)(2,1)S(1)}, bf16[1,256,256]{1,2,0:T(8,128)(2,1)S(1)}, u32[]{:S(2)}, u32[]{:S(2)}) %collective-permute-start.5) | collective-permute-done | bytes 131104 | tf_op jit(solution)/shard_map/ppermute | solution.py:16
  22.6 3.5 %all-to-all-start = ((bf16[4,2,32768]{2,1,0:T(2,128)(2,1)}), bf16[4,2,32768]{2,1,0:T(2,128)(2,1)S(1)}, u32[]{:S(2)}, u32[]{:S(2)}) async-start(bf16[4,2,32768]{2,1,0:T(2,128)(2,1)} %reshape.215), calls=%async_computation | async-start | bytes 1048576 | tf_op jit(solution)/shard_map/all_to_all | solution.py:40
  26.1 2.4 %collective-permute-done.7 = bf16[4,256,128]{1,2,0:T(8,128)(2,1)S(1)} collective-permute-done((bf16[4,256,128]{1,2,0:T(8,128)(2,1)S(1)}, bf16[4,256,128]{1,2,0:T(8,128)(2,1)S(1)}, u32[]{:S(2)}, u32[]{:S(2)}) %collective-permute-start.7) | collective-permute-done | bytes 262176 | tf_op jit(solution)/shard_map/ppermute | solution.py:63
  29.7 6.7 %copy.17 = bf16[3,3,1024,256]{2,3,1,0:T(8,128)(2,1)} copy(bf16[3,3,1024,256]{3,2,1,0:T(8,128)(2,1)} %param.4) | data formatting | bytes 9437184 | tf_op args[1]
  38.9 2.3 %fusion.17 = f32[1,256,3,256]{3,1,2,0:T(8,128)S(1)} fusion(bf16[3,1024,3,256]{1,3,2,0:T(8,128)(2,1)} %bitcast.216, bf16[4,256,1024]{2,1,0:T(8,128)(2,1)} %all-gather.3.cloned.1.call-done), kind=kOutput, calls=%fused_computation.45 | convolution fusion | flops 402653184 | bytes 2883584 | tf_op jit(solution)/shard_map/dot_general | solution.py:48
  41.3 2.6 %collective-permute-start.1 = (f32[1,256,256]{2,1,0:T(8,128)S(1)}, f32[1,256,256]{2,1,0:T(8,128)S(1)}, u32[]{:S(2)}, u32[]{:S(2)}) collective-permute-start(f32[1,256,256]{2,1,0:T(8,128)S(1)} %fusion.63), channel_id=1, source_target_pairs={{4,0},{8,4},{12,8},{16,12},{20,16},{24,20},{28,24},{5,1},{9,5},{13... | collective-permute-start | bytes 786440 | tf_op jit(solution)/shard_map/ppermute | solution.py:52
  45.6 4.3 %collective-permute-start = (f32[1,256,256]{2,1,0:T(8,128)S(1)}, f32[1,256,256]{2,1,0:T(8,128)S(1)}, u32[]{:S(2)}, u32[]{:S(2)}) collective-permute-start(f32[1,256,256]{2,1,0:T(8,128)S(1)} %fusion.60), channel_id=1, source_target_pairs={{0,4},{4,8},{8,12},{12,16},{16,20},{20,24},{24,28},{1,5},{5,9},{9,... | collective-permute-start | bytes 786440 | tf_op jit(solution)/shard_map/ppermute | solution.py:51
  53.2 1.8 %pad_add_fusion = f32[4,256,3,256]{3,1,2,0:T(8,128)S(1)} fusion(f32[3,256,3,256]{3,1,2,0:T(8,128)S(1)} %fusion.3, f32[4,256,3,256]{3,1,2,0:T(8,128)S(1)} %fusion, bf16[4,256,1024]{2,1,0:T(8,128)(2,1)S(1)} %copy-done.2, bf16[3,1024,3,256]{1,3,2,0:T(8,128)(2,1)S(1)} %bitcast.221), kind=kOutput, calls=%fused_computation.19 | convolution fusion | flops 1209532416 | bytes 11796480 | tf_op jit(solution)/shard_map/jit(_pad)/pad | solution.py:71
  55.1 2.9 %collective-permute-done = f32[1,256,256]{2,1,0:T(8,128)S(1)} collective-permute-done((f32[1,256,256]{2,1,0:T(8,128)S(1)}, f32[1,256,256]{2,1,0:T(8,128)S(1)}, u32[]{:S(2)}, u32[]{:S(2)}) %collective-permute-start) | collective-permute-done | bytes 262176 | tf_op jit(solution)/shard_map/ppermute | solution.py:51
  58.8 6.1 %psum.7 = f32[4,256,2]{1,0,2:T(4,128)S(1)} all-reduce(f32[4,256,2]{1,0,2:T(4,128)S(1)} %pad_maximum_fusion.3), channel_id=1, replica_groups=mesh['hi'=4,'lo'=2,'chan'=4] {'chan'}, use_global_device_ids=true, to_apply=%region_2.3 | all-reduce | flops 2048 | bytes 16384 | tf_op jit(solution)/shard_map/psum | solution.py:84
  66.6 3.5 %all-to-all-start.1 = ((bf16[4,256,256]{2,0,1:T(4,128)(2,1)}), bf16[4,256,256]{2,0,1:T(4,128)(2,1)S(1)}, u32[]{:S(2)}, u32[]{:S(2)}) async-start(bf16[4,256,256]{2,0,1:T(4,128)(2,1)} %copy.20), calls=%async_computation.1 | async-start | bytes 1048576 | tf_op jit(solution)/shard_map/all_to_all | solution.py:90
  70.2 3.9 %collective-permute-start.3 = (bf16[1,256,256]{2,1,0:T(8,128)(2,1)S(1)}, bf16[1,256,256]{2,1,0:T(8,128)(2,1)S(1)}, u32[]{:S(2)}, u32[]{:S(2)}) collective-permute-start(bf16[1,256,256]{2,1,0:T(8,128)(2,1)S(1)} %get-tuple-element.15), channel_id=1, source_target_pairs={{4,0},{8,4},{12,8},{16,12},{20,16},{24,20},{28,24},{5,1},{9,5},{13... | collective-permute-start | bytes 393224 | tf_op jit(solution)/shard_map/ppermute | solution.py:16
  74.1 3.0 %collective-permute-start.2 = (bf16[1,256,256]{2,1,0:T(8,128)(2,1)S(1)}, bf16[1,256,256]{2,1,0:T(8,128)(2,1)S(1)}, u32[]{:S(2)}, u32[]{:S(2)}) collective-permute-start(bf16[1,256,256]{2,1,0:T(8,128)(2,1)S(1)} %get-tuple-element.14), channel_id=1, source_target_pairs={{0,4},{4,8},{8,12},{12,16},{16,20},{20,24},{24,28},{1,5},{5,9},{9,... | collective-permute-start | bytes 393224 | tf_op jit(solution)/shard_map/ppermute | solution.py:16
  77.2 1.9 %fusion.39 = f32[9,512,256]{2,1,0:T(8,128)S(1)} fusion(bf16[4,256,256]{2,1,0:T(8,128)(2,1)S(1)} %get-tuple-element.10, s32[]{:T(128)S(6)} %select_n.36, bf16[10,256,512]{1,2,0:T(8,128)(2,1)} %all-gather.5.cloned.1.call-done), kind=kOutput, calls=%fused_computation.83 | convolution fusion | flops 268435456 | bytes 3670020 | tf_op jit(solution)/shard_map/dot_general | solution.py:104
  83.5 4.2 %collective-permute-done.4 = bf16[4,256,256]{2,1,0:T(8,128)(2,1)S(1)} collective-permute-done((bf16[4,256,256]{2,1,0:T(8,128)(2,1)S(1)}, bf16[4,256,256]{2,1,0:T(8,128)(2,1)S(1)}, u32[]{:S(2)}, u32[]{:S(2)}) %collective-permute-start.4) | collective-permute-done | bytes 524320 | tf_op jit(solution)/shard_map/ppermute | solution.py:92
  92.5 2.1 %add_convert_fusion = bf16[9,512,256]{2,1,0:T(8,128)(2,1)} fusion(f32[9,512,256]{2,1,0:T(8,128)S(1)} %fusion.31, f32[9,512,256]{2,1,0:T(8,128)S(1)} %fusion.22), kind=kLoop, calls=%fused_computation.18 | loop fusion | flops 2359296 | bytes 11796480 | tf_op jit(solution)/shard_map/convert_element_type | solution.py:117
  95.5 8.9 %convolution_convert_fusion = bf16[1024,1024]{1,0:T(8,128)(2,1)} fusion(bf16[1024,2304]{1,0:T(8,128)(2,1)S(1)} %bitcast.230, bf16[2304,1024]{1,0:T(8,128)(2,1)} %bitcast.217), kind=kOutput, calls=%fused_computation.26 | convolution fusion | flops 4832886784 | bytes 11534336 | tf_op jit(solution)/shard_map/dot_general | solution.py:133
  104.5 3.3 %reshape.181 = bf16[4,256,4,256]{3,2,1,0:T(4,128)(2,1)S(1)} reshape(bf16[1024,1024]{1,0:T(8,128)(2,1)} %convolution_convert_fusion) | data formatting | bytes 4194304 | tf_op jit(solution)/shard_map/reshape | solution.py:134
  109.5 3.6 %all-to-all-start.2 = ((bf16[4,256,4,256]{3,1,0,2:T(8,128)(2,1)}), bf16[4,256,4,256]{3,1,0,2:T(8,128)(2,1)S(1)}, u32[]{:S(2)}, u32[]{:S(2)}) async-start(bf16[4,256,4,256]{3,1,0,2:T(8,128)(2,1)} %copy.23), calls=%async_computation.2 | async-start | bytes 4194304 | tf_op jit(solution)/shard_map/all_to_all | solution.py:135
  114.7 24.1 %all-to-all-done.2 = bf16[4,256,4,256]{3,1,0,2:T(8,128)(2,1)S(1)} async-done(((bf16[4,256,4,256]{3,1,0,2:T(8,128)(2,1)}), bf16[4,256,4,256]{3,1,0,2:T(8,128)(2,1)S(1)}, u32[]{:S(2)}, u32[]{:S(2)}) %all-to-all-start.2) | async-done | bytes 2097184 | tf_op jit(solution)/shard_map/all_to_all | solution.py:135
  140.0 3.2 %reduce-scatter.2.cloned.1.call-done = bf16[3,3,128,256]{3,2,1,0:T(8,128)(2,1)} async-done(((bf16[3,3,512,256]{3,2,1,0:T(8,128)(2,1)}), bf16[3,3,128,256]{3,2,1,0:T(8,128)(2,1)}) %reduce-scatter.2.cloned.1.call-update) | async-done | bytes 589840 | tf_op jit(solution)/shard_map/reduce_scatter | solution.py:116
  143.2 2.2 %convert_element_type.76 = f32[3,3,128,256]{3,2,1,0:T(8,128)} convert(bf16[3,3,128,256]{3,2,1,0:T(8,128)(2,1)} %reduce-scatter.2.cloned.1.call-done) | non-fusion elementwise | flops 294912 | bytes 1769472 | tf_op jit(solution)/shard_map/convert_element_type | solution.py:118
  (81 shorter events, 31.7 us)
Async XLA Ops:
  7.2 13.1 %copy-start.3 = (bf16[4,64,1024]{2,1,0:T(8,128)(2,1)S(1)}, bf16[4,64,1024]{2,1,0:T(8,128)(2,1)}, u32[]{:S(2)}) copy-start(bf16[4,64,1024]{2,1,0:T(8,128)(2,1)} %param.5) | copy-start | bytes 1572868
  7.2 31.7 %all-gather.3.cloned.1.call-start = ((), (), s32[]{:S(2)}) async-start(), calls=%async_computation.4 | async-start | bytes 2621440 | tf_op jit(solution)/shard_map/all_gather | solution.py:41
  9.2 8.1 %collective-permute-start.6 = (bf16[1,256,256]{1,2,0:T(8,128)(2,1)S(1)}, bf16[1,256,256]{1,2,0:T(8,128)(2,1)S(1)}, u32[]{:S(2)}, u32[]{:S(2)}) collective-permute-start(bf16[1,256,256]{1,2,0:T(8,128)(2,1)S(1)} %get-tuple-element.13), channel_id=1, source_target_pairs={{4,0},{8,4},{12,8},{16,12},{20,16},{24,20},{28,24},{5,1},{9,5},{13... | collective-permute-start | bytes 393224 | tf_op jit(solution)/shard_map/ppermute | solution.py:16
  11.1 8.9 %collective-permute-start.5 = (bf16[1,256,256]{1,2,0:T(8,128)(2,1)S(1)}, bf16[1,256,256]{1,2,0:T(8,128)(2,1)S(1)}, u32[]{:S(2)}, u32[]{:S(2)}) collective-permute-start(bf16[1,256,256]{1,2,0:T(8,128)(2,1)S(1)} %get-tuple-element.12), channel_id=1, source_target_pairs={{0,4},{4,8},{8,12},{12,16},{16,20},{20,24},{24,28},{1,5},{5,9},{9,... | collective-permute-start | bytes 393224 | tf_op jit(solution)/shard_map/ppermute | solution.py:16
  20.2 8.3 %collective-permute-start.7 = (bf16[4,256,128]{1,2,0:T(8,128)(2,1)S(1)}, bf16[4,256,128]{1,2,0:T(8,128)(2,1)S(1)}, u32[]{:S(2)}, u32[]{:S(2)}) collective-permute-start(bf16[4,256,128]{1,2,0:T(8,128)(2,1)S(1)} %dynamic-slice_bitcast_fusion.1), channel_id=1, source_target_pairs={{0,4},{4,0},{1,5},{5,1},{2,6},{6,2},{3,7},{7,3},{8,12},{12,8},{9,1... | collective-permute-start | bytes 786440 | tf_op jit(solution)/shard_map/ppermute | solution.py:63
  22.6 14.9 %all-to-all-start = ((bf16[4,2,32768]{2,1,0:T(2,128)(2,1)}), bf16[4,2,32768]{2,1,0:T(2,128)(2,1)S(1)}, u32[]{:S(2)}, u32[]{:S(2)}) async-start(bf16[4,2,32768]{2,1,0:T(2,128)(2,1)} %reshape.215), calls=%async_computation | async-start | bytes 1048576 | tf_op jit(solution)/shard_map/all_to_all | solution.py:40
  26.0 51.1 %all-gather.5.cloned.1.call-start = ((), (), s32[]{:S(2)}) async-start(), calls=%async_computation.5 | async-start | bytes 3276800 | tf_op jit(solution)/shard_map/all_gather | solution.py:68
  38.9 5.0 %copy-start.1 = (bf16[3,3,1024,256]{2,3,1,0:T(8,128)(2,1)S(1)}, bf16[3,3,1024,256]{2,3,1,0:T(8,128)(2,1)}, u32[]{:S(2)}) copy-start(bf16[3,3,1024,256]{2,3,1,0:T(8,128)(2,1)} %copy.17) | copy-start | bytes 14155780
  38.9 11.1 %copy-start.2 = (bf16[4,256,1024]{2,1,0:T(8,128)(2,1)S(1)}, bf16[4,256,1024]{2,1,0:T(8,128)(2,1)}, u32[]{:S(2)}) copy-start(bf16[4,256,1024]{2,1,0:T(8,128)(2,1)} %all-gather.3.cloned.1.call-done) | copy-start | bytes 6291460
  41.3 13.8 %collective-permute-start.1 = (f32[1,256,256]{2,1,0:T(8,128)S(1)}, f32[1,256,256]{2,1,0:T(8,128)S(1)}, u32[]{:S(2)}, u32[]{:S(2)}) collective-permute-start(f32[1,256,256]{2,1,0:T(8,128)S(1)} %fusion.63), channel_id=1, source_target_pairs={{4,0},{8,4},{12,8},{16,12},{20,16},{24,20},{28,24},{5,1},{9,5},{13... | collective-permute-start | bytes 786440 | tf_op jit(solution)/shard_map/ppermute | solution.py:52
  45.6 12.3 %collective-permute-start = (f32[1,256,256]{2,1,0:T(8,128)S(1)}, f32[1,256,256]{2,1,0:T(8,128)S(1)}, u32[]{:S(2)}, u32[]{:S(2)}) collective-permute-start(f32[1,256,256]{2,1,0:T(8,128)S(1)} %fusion.60), channel_id=1, source_target_pairs={{0,4},{4,8},{8,12},{12,16},{16,20},{20,24},{24,28},{1,5},{5,9},{9,... | collective-permute-start | bytes 786440 | tf_op jit(solution)/shard_map/ppermute | solution.py:51
  66.6 42.9 %all-to-all-start.1 = ((bf16[4,256,256]{2,0,1:T(4,128)(2,1)}), bf16[4,256,256]{2,0,1:T(4,128)(2,1)S(1)}, u32[]{:S(2)}, u32[]{:S(2)}) async-start(bf16[4,256,256]{2,0,1:T(4,128)(2,1)} %copy.20), calls=%async_computation.1 | async-start | bytes 1048576 | tf_op jit(solution)/shard_map/all_to_all | solution.py:90
  70.0 73.2 %reduce-scatter.2.cloned.1.call-start = ((), (), s32[]{:S(2)}) async-start(), calls=%async_computation.6 | async-start | bytes 2949120 | tf_op jit(solution)/shard_map/reduce_scatter | solution.py:116
  70.1 17.6 %collective-permute-start.4 = (bf16[4,256,256]{2,1,0:T(8,128)(2,1)S(1)}, bf16[4,256,256]{2,1,0:T(8,128)(2,1)S(1)}, u32[]{:S(2)}, u32[]{:S(2)}) collective-permute-start(bf16[4,256,256]{2,1,0:T(8,128)(2,1)S(1)} %get-tuple-element.10), channel_id=1, source_target_pairs={{0,4},{4,0},{1,5},{5,1},{2,6},{6,2},{3,7},{7,3},{8,12},{12,8},{9,1... | collective-permute-start | bytes 1572872 | tf_op jit(solution)/shard_map/ppermute | solution.py:92
  70.2 24.5 %collective-permute-start.3 = (bf16[1,256,256]{2,1,0:T(8,128)(2,1)S(1)}, bf16[1,256,256]{2,1,0:T(8,128)(2,1)S(1)}, u32[]{:S(2)}, u32[]{:S(2)}) collective-permute-start(bf16[1,256,256]{2,1,0:T(8,128)(2,1)S(1)} %get-tuple-element.15), channel_id=1, source_target_pairs={{4,0},{8,4},{12,8},{16,12},{20,16},{24,20},{28,24},{5,1},{9,5},{13... | collective-permute-start | bytes 393224 | tf_op jit(solution)/shard_map/ppermute | solution.py:16
  74.1 20.5 %collective-permute-start.2 = (bf16[1,256,256]{2,1,0:T(8,128)(2,1)S(1)}, bf16[1,256,256]{2,1,0:T(8,128)(2,1)S(1)}, u32[]{:S(2)}, u32[]{:S(2)}) collective-permute-start(bf16[1,256,256]{2,1,0:T(8,128)(2,1)S(1)} %get-tuple-element.14), channel_id=1, source_target_pairs={{0,4},{4,8},{8,12},{12,16},{16,20},{20,24},{24,28},{1,5},{5,9},{9,... | collective-permute-start | bytes 393224 | tf_op jit(solution)/shard_map/ppermute | solution.py:16
  77.2 2.1 %copy-start = (bf16[10,256,512]{1,2,0:T(8,128)(2,1)S(1)}, bf16[10,256,512]{1,2,0:T(8,128)(2,1)}, u32[]{:S(2)}) copy-start(bf16[10,256,512]{1,2,0:T(8,128)(2,1)} %all-gather.5.cloned.1.call-done) | copy-start | bytes 7864324
  109.5 29.3 %all-to-all-start.2 = ((bf16[4,256,4,256]{3,1,0,2:T(8,128)(2,1)}), bf16[4,256,4,256]{3,1,0,2:T(8,128)(2,1)S(1)}, u32[]{:S(2)}, u32[]{:S(2)}) async-start(bf16[4,256,4,256]{3,1,0,2:T(8,128)(2,1)} %copy.23), calls=%async_computation.2 | async-start | bytes 4194304 | tf_op jit(solution)/shard_map/all_to_all | solution.py:135
Sparse Core Ops, SparseCore 0:
  9.6 26.7 all-gather.2
  38.4 24.8 all-gather.4
  94.8 48.4 reduce-scatter.1

commit v9 on v8

--- a/solution.py
+++ b/solution.py
@@ -87,7 +87,6 @@
     unit = conv_wide * inverse_rms
     normed_filters = unit.astype(jnp.bfloat16)
     grad_conv = (inverse_rms * (upstream - unit * mean_gu)).astype(jnp.bfloat16)
-    normed = lax.all_to_all(normed_filters, "chan", split_axis=1, concat_axis=2, tiled=True)
 
     sent_grad = lax.ppermute(grad_conv, "lo", [(0, 1), (1, 0)])
     img_block = jnp.pad(img_block, ((0, 0), (1, 1), (0, 0)))
@@ -113,6 +112,8 @@
     own_part = pair_part(grad_conv, height * lo)
     sent_grad, own_part = lax.optimization_barrier((sent_grad, own_part))
     stacked = (own_part + pair_part(sent_grad, height * (1 - lo))).reshape(3, 3, width_w, local_filters)
+    normed_late, _ = lax.optimization_barrier((normed_filters, stacked))
+    normed = lax.all_to_all(normed_late, "chan", split_axis=1, concat_axis=2, tiled=True)
     grad_weight = lax.psum_scatter(
         stacked.astype(jnp.bfloat16), "hi", scatter_dimension=2, tiled=True
     ).astype(jnp.float32)
@@ -130,10 +131,15 @@
         axis=-1,
     ).reshape(height * breadth, 9 * local_filters)
     by_filter = jnp.transpose(weight, (0, 1, 3, 2)).reshape(9 * local_filters, all_chans)
-    input_term = jnp.dot(columns, by_filter, preferred_element_type=jnp.float32)
-    split = input_term.astype(jnp.bfloat16).reshape(height, breadth, chans, all_chans // chans)
-    received = lax.all_to_all(split, "chan", split_axis=2, concat_axis=2, tiled=True)
-    grad_input = jnp.sum(received.astype(jnp.float32), axis=2).astype(jnp.bfloat16)
+    group = all_chans // chans
+    split = jnp.stack(
+        [
+            jnp.dot(columns, by_filter[:, j * group : (j + 1) * group], preferred_element_type=jnp.float32)
+            for j in range(chans)
+        ]
+    ).astype(jnp.bfloat16)
+    received = lax.all_to_all(split, "chan", split_axis=0, concat_axis=0, tiled=True)
+    grad_input = jnp.sum(received.astype(jnp.float32), axis=0).astype(jnp.bfloat16).reshape(height, breadth, group)
     return (normed, grad_input, grad_weight)
 
 

time: 154 us -> 167 us (1.084)
  matrix products: 28.9 us -> 36.2 us
  other arithmetic: 8.26 us -> 11.5 us
  waiting for transfers between devices: 42.7 us -> 45.5 us
  starting transfers between devices: 31.4 us -> 29 us
  local copies, waits for them, and re-layouts: 20.3 us -> 22.2 us
    dot_general x1 -> x4, matrix products: 8.92 us -> 16.2 us  [on_device(): jnp.dot(columns, by_filter[:, j * group:(j + 1) * group], preferred_eleme...]
    unnamed x19 -> x21, local copies, waits for them, and re-layouts: 11.5 us -> 17.6 us
    reshape x2 -> x0, local copies, waits for them, and re-layouts: 5.01 us -> none  [on_device(): input_term.astype(jnp.bfloat16)]
    ppermute x1, waiting for transfers between devices: 4.19 us -> 0.66 us  [on_device(): sent_grad = lax.ppermute(grad_conv, 'lo', [(0, 1), (1, 0)])]
    all_to_all x1, waiting for transfers between devices: 1.06 us -> 4.58 us  [on_device(): lax.all_to_all(grad_out, 'chan', split_axis=2, concat_axis=1, tiled=True)]
    ppermute x1, waiting for transfers between devices: 0.01 us -> 3.4 us  [on_device(): lax.ppermute(shift_sum(taps(gathered[:1], 2)), SLAB, [(i + 1, i) for i in...]
    reduce_scatter x1, waiting for transfers between devices: 3.21 us -> 0.01 us  [on_device(): lax.psum_scatter(stacked.astype(jnp.bfloat16), 'hi', scatter_dimension=2,...]
    all_to_all x2, waiting for transfers between devices: 24.1 us -> 27.2 us  [the longest x1 24.1 us: on_device(): lax.all_to_all(split, 'chan', split_axis=0, concat_axis=0, tiled=True)]
  transfers between devices with their start and end apart: 14 -> 14, of which waited for: 8 -> 9; matrix products, arithmetic and copies ran while one was open for 35% -> 36% of each run, Pallas kernels for 0% -> 0%
where the time goes in v9:
time: 167 us; the launch traced here: 165 us
  waiting for transfers between devices  45.5 us (27%)
  matrix products  36.2 us (22%)
  starting transfers between devices  29 us (17%)
  local copies, waits for them, and re-layouts  22.2 us (13%)
  between operations  14.2 us (9%)
  other arithmetic  11.5 us (7%)
  blocking collectives  6.52 us (4%)
    all_to_all x1, waiting for transfers between devices, on_device(): lax.all_to_all(split, 'chan', split_axis=0, concat_axis=0, tiled=True)  24.1 us
    unnamed x21, local copies, waits for them, and re-layouts  17.6 us
    dot_general x4, matrix products, on_device(): jnp.dot(columns, by_filter[:, j * group:(j + 1) * group], preferred_eleme...  16.2 us
    ppermute x4, starting transfers between devices, shift_rows(): return lax.ppermute(rows, SLAB, pairs)  12.2 us
    dot_general x18, matrix products, pair_part(): lax.dot_general(weight_window, flat, (((0,), (0,)), ((), ())), preferred_...  10.9 us
    dot_general x4, matrix products, taps(): out = jnp.dot(flat, by_row[a], preferred_element_type=jnp.float32)  7.22 us
    psum x1, blocking collectives, on_device(): totals = lax.psum(partial, 'chan')  6.52 us
    ppermute x4, waiting for transfers between devices, shift_rows(): return lax.ppermute(rows, SLAB, pairs)  5.67 us
  transfers between devices with their start and end apart: 14, of which 9 were waited for; matrix products, arithmetic and copies ran while one was open for 36% of the time, Pallas kernels for 0%

profile of v9, /device:TPU:4, one launch (start us, length us, event | category | flops | bytes accessed | tf_op | source)
XLA Modules:
  0.0 165.1 jit_solution(18192523036326032523)
XLA Ops:
  9.2 3.4 %collective-permute-start.3 = (bf16[1,256,256]{1,2,0:T(8,128)(2,1)S(1)}, bf16[1,256,256]{1,2,0:T(8,128)(2,1)S(1)}, u32[]{:S(2)}, u32[]{:S(2)}) collective-permute-start(bf16[1,256,256]{1,2,0:T(8,128)(2,1)S(1)} %get-tuple-element.16), channel_id=1, source_target_pairs={{0,4},{4,8},{8,12},{12,16},{16,20},{20,24},{24,28},{1,5},{5,9},{9,... | collective-permute-start | bytes 393224 | tf_op jit(solution)/shard_map/ppermute | solution.py:16
  12.6 2.4 %collective-permute-start.4 = (bf16[1,256,256]{1,2,0:T(8,128)(2,1)S(1)}, bf16[1,256,256]{1,2,0:T(8,128)(2,1)S(1)}, u32[]{:S(2)}, u32[]{:S(2)}) collective-permute-start(bf16[1,256,256]{1,2,0:T(8,128)(2,1)S(1)} %get-tuple-element.17), channel_id=1, source_target_pairs={{4,0},{8,4},{12,8},{16,12},{20,16},{24,20},{28,24},{5,1},{9,5},{13... | collective-permute-start | bytes 393224 | tf_op jit(solution)/shard_map/ppermute | solution.py:16
  18.2 3.5 %all-to-all-start = ((bf16[4,2,32768]{2,1,0:T(2,128)(2,1)}), bf16[4,2,32768]{2,1,0:T(2,128)(2,1)S(1)}, u32[]{:S(2)}, u32[]{:S(2)}) async-start(bf16[4,2,32768]{2,1,0:T(2,128)(2,1)} %reshape.217), calls=%async_computation | async-start | bytes 1048576 | tf_op jit(solution)/shard_map/all_to_all | solution.py:40
  22.0 6.7 %copy.17 = bf16[3,3,1024,256]{2,3,1,0:T(8,128)(2,1)} copy(bf16[3,3,1024,256]{3,2,1,0:T(8,128)(2,1)} %param.4) | data formatting | bytes 9437184 | tf_op args[1]
  31.9 4.6 %all-to-all-done = bf16[4,2,32768]{2,1,0:T(2,128)(2,1)S(1)} async-done(((bf16[4,2,32768]{2,1,0:T(2,128)(2,1)}), bf16[4,2,32768]{2,1,0:T(2,128)(2,1)S(1)}, u32[]{:S(2)}, u32[]{:S(2)}) %all-to-all-start) | async-done | bytes 524320 | tf_op jit(solution)/shard_map/all_to_all | solution.py:40
  39.2 2.3 %fusion.14 = f32[1,256,3,256]{3,1,2,0:T(8,128)S(1)} fusion(bf16[3,1024,3,256]{1,3,2,0:T(8,128)(2,1)} %bitcast.227, bf16[4,256,1024]{2,1,0:T(8,128)(2,1)} %all-gather.3.cloned.1.call-done), kind=kOutput, calls=%fused_computation.47 | convolution fusion | flops 402653184 | bytes 2883584 | tf_op jit(solution)/shard_map/dot_general | solution.py:48
  41.6 3.5 %collective-permute-start = (f32[1,256,256]{2,1,0:T(8,128)S(1)}, f32[1,256,256]{2,1,0:T(8,128)S(1)}, u32[]{:S(2)}, u32[]{:S(2)}) collective-permute-start(f32[1,256,256]{2,1,0:T(8,128)S(1)} %fusion.68), channel_id=1, source_target_pairs={{0,4},{4,8},{8,12},{12,16},{16,20},{20,24},{24,28},{1,5},{5,9},{9,... | collective-permute-start | bytes 786440 | tf_op jit(solution)/shard_map/ppermute | solution.py:51
  46.9 2.5 %collective-permute-start.1 = (f32[1,256,256]{2,1,0:T(8,128)S(1)}, f32[1,256,256]{2,1,0:T(8,128)S(1)}, u32[]{:S(2)}, u32[]{:S(2)}) collective-permute-start(f32[1,256,256]{2,1,0:T(8,128)S(1)} %fusion.71), channel_id=1, source_target_pairs={{4,0},{8,4},{12,8},{16,12},{20,16},{24,20},{28,24},{5,1},{9,5},{13... | collective-permute-start | bytes 786440 | tf_op jit(solution)/shard_map/ppermute | solution.py:52
  54.5 3.4 %collective-permute-done.1 = f32[1,256,256]{2,1,0:T(8,128)S(1)} collective-permute-done((f32[1,256,256]{2,1,0:T(8,128)S(1)}, f32[1,256,256]{2,1,0:T(8,128)S(1)}, u32[]{:S(2)}, u32[]{:S(2)}) %collective-permute-start.1) | collective-permute-done | bytes 262176 | tf_op jit(solution)/shard_map/ppermute | solution.py:52
  58.8 6.5 %psum.7 = f32[4,256,2]{1,0,2:T(4,128)S(1)} all-reduce(f32[4,256,2]{1,0,2:T(4,128)S(1)} %pad_maximum_fusion.4), channel_id=1, replica_groups=mesh['hi'=4,'lo'=2,'chan'=4] {'chan'}, use_global_device_ids=true, to_apply=%region_2.3 | all-reduce | flops 2048 | bytes 16384 | tf_op jit(solution)/shard_map/psum | solution.py:84
  65.7 4.2 %collective-permute-start.6 = (bf16[1,256,256]{2,1,0:T(8,128)(2,1)S(1)}, bf16[1,256,256]{2,1,0:T(8,128)(2,1)S(1)}, u32[]{:S(2)}, u32[]{:S(2)}) collective-permute-start(bf16[1,256,256]{2,1,0:T(8,128)(2,1)S(1)} %get-tuple-element.14), channel_id=1, source_target_pairs={{0,4},{4,8},{8,12},{12,16},{16,20},{20,24},{24,28},{1,5},{5,9},{9,... | collective-permute-start | bytes 393224 | tf_op jit(solution)/shard_map/ppermute | solution.py:16
  69.9 2.1 %collective-permute-start.7 = (bf16[1,256,256]{2,1,0:T(8,128)(2,1)S(1)}, bf16[1,256,256]{2,1,0:T(8,128)(2,1)S(1)}, u32[]{:S(2)}, u32[]{:S(2)}) collective-permute-start(bf16[1,256,256]{2,1,0:T(8,128)(2,1)S(1)} %get-tuple-element.15), channel_id=1, source_target_pairs={{4,0},{8,4},{12,8},{16,12},{20,16},{24,20},{28,24},{5,1},{9,5},{13... | collective-permute-start | bytes 393224 | tf_op jit(solution)/shard_map/ppermute | solution.py:16
  72.5 5.2 %collective-permute-done.7 = bf16[1,256,256]{2,1,0:T(8,128)(2,1)S(1)} collective-permute-done((bf16[1,256,256]{2,1,0:T(8,128)(2,1)S(1)}, bf16[1,256,256]{2,1,0:T(8,128)(2,1)S(1)}, u32[]{:S(2)}, u32[]{:S(2)}) %collective-permute-start.7) | collective-permute-done | bytes 131104 | tf_op jit(solution)/shard_map/ppermute | solution.py:16
  80.7 1.9 %fusion.43 = f32[9,512,256]{2,1,0:T(8,128)S(1)} fusion(bf16[4,256,256]{2,1,0:T(8,128)(2,1)S(1)} %get-tuple-element.12, s32[]{:T(128)S(6)} %select_n.36, bf16[10,256,512]{1,2,0:T(8,128)(2,1)} %all-gather.5.cloned.1.call-done), kind=kOutput, calls=%fused_computation.90 | convolution fusion | flops 268435456 | bytes 3670020 | tf_op jit(solution)/shard_map/dot_general | solution.py:103
  92.6 2.0 %add.190 = bf16[9,512,256]{2,1,0:T(8,128)(2,1)} add(f32[9,512,256]{2,1,0:T(8,128)S(1)} %fusion.35, f32[9,512,256]{2,1,0:T(8,128)S(1)} %fusion.26) | non-fusion elementwise | flops 1179648 | bytes 11796480 | tf_op jit(solution)/shard_map/add | solution.py:114
  100.3 4.4 %fusion.22 = bf16[1,1024,256]{2,1,0:T(8,128)(2,1)S(1)} fusion(bf16[1024,2304]{1,0:T(8,128)(2,1)} %bitcast.84, bf16[2304,1024]{1,0:T(8,128)(2,1)} %bitcast.228), kind=kOutput, calls=%fused_computation.51 | convolution fusion | flops 1208221696 | bytes 6422528 | tf_op jit(solution)/shard_map/dot_general | solution.py:137
  104.6 4.0 %fusion.23 = bf16[1,1024,256]{2,1,0:T(8,128)(2,1)S(1)} fusion(bf16[1024,2304]{1,0:T(8,128)(2,1)} %bitcast.84, bf16[2304,1024]{1,0:T(8,128)(2,1)S(1)} %bitcast.236), kind=kOutput, calls=%fused_computation.52 | convolution fusion | flops 1208221696 | bytes 6422528 | tf_op jit(solution)/shard_map/dot_general | solution.py:137
  108.6 3.8 %fusion.24 = bf16[1,1024,256]{2,1,0:T(8,128)(2,1)S(1)} fusion(bf16[1024,2304]{1,0:T(8,128)(2,1)} %bitcast.84, bf16[2304,1024]{1,0:T(8,128)(2,1)S(1)} %bitcast.237), kind=kOutput, calls=%fused_computation.53 | convolution fusion | flops 1208221696 | bytes 6422528 | tf_op jit(solution)/shard_map/dot_general | solution.py:137
  113.6 3.5 %all-to-all-start.1 = ((bf16[4,256,256]{2,0,1:T(4,128)(2,1)}), bf16[4,256,256]{2,0,1:T(4,128)(2,1)S(1)}, u32[]{:S(2)}, u32[]{:S(2)}) async-start(bf16[4,256,256]{2,0,1:T(4,128)(2,1)} %copy.24), calls=%async_computation.1 | async-start | bytes 1048576 | tf_op jit(solution)/shard_map/all_to_all | solution.py:116
  117.1 4.1 %fusion.25 = bf16[1,1024,256]{2,1,0:T(8,128)(2,1)S(1)} fusion(bf16[1024,2304]{1,0:T(8,128)(2,1)} %bitcast.84, bf16[2304,1024]{1,0:T(8,128)(2,1)} %bitcast.229), kind=kOutput, calls=%fused_computation.54 | convolution fusion | flops 1208221696 | bytes 6422528 | tf_op jit(solution)/shard_map/dot_general | solution.py:137
  122.8 3.1 %all-to-all-done.1 = bf16[4,256,256]{2,0,1:T(4,128)(2,1)S(1)} async-done(((bf16[4,256,256]{2,0,1:T(4,128)(2,1)}), bf16[4,256,256]{2,0,1:T(4,128)(2,1)S(1)}, u32[]{:S(2)}, u32[]{:S(2)}) %all-to-all-start.1) | async-done | bytes 524320 | tf_op jit(solution)/shard_map/all_to_all | solution.py:116
  125.9 3.6 %all-to-all-start.2 = ((bf16[4,1024,256]{2,1,0:T(8,128)(2,1)}), bf16[4,1024,256]{2,1,0:T(8,128)(2,1)S(1)}, u32[]{:S(2)}, u32[]{:S(2)}) async-start(bf16[4,1024,256]{2,1,0:T(8,128)(2,1)} %pad_maximum_fusion), calls=%async_computation.2 | async-start | bytes 4194304 | tf_op jit(solution)/shard_map/all_to_all | solution.py:141
  131.1 24.1 %all-to-all-done.2 = bf16[4,1024,256]{2,1,0:T(8,128)(2,1)S(1)} async-done(((bf16[4,1024,256]{2,1,0:T(8,128)(2,1)}), bf16[4,1024,256]{2,1,0:T(8,128)(2,1)S(1)}, u32[]{:S(2)}, u32[]{:S(2)}) %all-to-all-start.2) | async-done | bytes 2097184 | tf_op jit(solution)/shard_map/all_to_all | solution.py:141
  156.4 2.2 %convert_element_type.69 = f32[3,3,128,256]{3,2,1,0:T(8,128)} convert(bf16[3,3,128,256]{3,2,1,0:T(8,128)(2,1)} %reduce-scatter.2.cloned.1.call-done) | non-fusion elementwise | flops 294912 | bytes 1769472 | tf_op jit(solution)/shard_map/convert_element_type | solution.py:119
  (86 shorter events, 43.9 us)
Async XLA Ops:
  7.2 32.1 %all-gather.3.cloned.1.call-start = ((), (), s32[]{:S(2)}) async-start(), calls=%async_computation.4 | async-start | bytes 2621440 | tf_op jit(solution)/shard_map/all_gather | solution.py:41
  9.2 12.6 %collective-permute-start.3 = (bf16[1,256,256]{1,2,0:T(8,128)(2,1)S(1)}, bf16[1,256,256]{1,2,0:T(8,128)(2,1)S(1)}, u32[]{:S(2)}, u32[]{:S(2)}) collective-permute-start(bf16[1,256,256]{1,2,0:T(8,128)(2,1)S(1)} %get-tuple-element.16), channel_id=1, source_target_pairs={{0,4},{4,8},{8,12},{12,16},{16,20},{20,24},{24,28},{1,5},{5,9},{9,... | collective-permute-start | bytes 393224 | tf_op jit(solution)/shard_map/ppermute | solution.py:16
  12.6 9.1 %collective-permute-start.4 = (bf16[1,256,256]{1,2,0:T(8,128)(2,1)S(1)}, bf16[1,256,256]{1,2,0:T(8,128)(2,1)S(1)}, u32[]{:S(2)}, u32[]{:S(2)}) collective-permute-start(bf16[1,256,256]{1,2,0:T(8,128)(2,1)S(1)} %get-tuple-element.17), channel_id=1, source_target_pairs={{4,0},{8,4},{12,8},{16,12},{20,16},{24,20},{28,24},{5,1},{9,5},{13... | collective-permute-start | bytes 393224 | tf_op jit(solution)/shard_map/ppermute | solution.py:16
  18.2 18.2 %all-to-all-start = ((bf16[4,2,32768]{2,1,0:T(2,128)(2,1)}), bf16[4,2,32768]{2,1,0:T(2,128)(2,1)S(1)}, u32[]{:S(2)}, u32[]{:S(2)}) async-start(bf16[4,2,32768]{2,1,0:T(2,128)(2,1)} %reshape.217), calls=%async_computation | async-start | bytes 1048576 | tf_op jit(solution)/shard_map/all_to_all | solution.py:40
  21.7 59.0 %all-gather.5.cloned.1.call-start = ((), (), s32[]{:S(2)}) async-start(), calls=%async_computation.5 | async-start | bytes 3276800 | tf_op jit(solution)/shard_map/all_gather | solution.py:68
  22.0 8.7 %collective-permute-start.5 = (bf16[4,256,128]{1,2,0:T(8,128)(2,1)S(1)}, bf16[4,256,128]{1,2,0:T(8,128)(2,1)S(1)}, u32[]{:S(2)}, u32[]{:S(2)}) collective-permute-start(bf16[4,256,128]{1,2,0:T(8,128)(2,1)S(1)} %dynamic-slice_bitcast_fusion.1), channel_id=1, source_target_pairs={{0,4},{4,0},{1,5},{5,1},{2,6},{6,2},{3,7},{7,3},{8,12},{12,8},{9,1... | collective-permute-start | bytes 786440 | tf_op jit(solution)/shard_map/ppermute | solution.py:63
  31.8 124.6 %reduce-scatter.2.cloned.1.call-start = ((), (), s32[]{:S(2)}) async-start(), calls=%async_computation.6 | async-start | bytes 2949120 | tf_op jit(solution)/shard_map/reduce_scatter | solution.py:117
  39.2 5.9 %copy-start.1 = (bf16[3,3,1024,256]{2,3,1,0:T(8,128)(2,1)S(1)}, bf16[3,3,1024,256]{2,3,1,0:T(8,128)(2,1)}, u32[]{:S(2)}) copy-start(bf16[3,3,1024,256]{2,3,1,0:T(8,128)(2,1)} %copy.17) | copy-start | bytes 14155780
  39.2 10.1 %copy-start.2 = (bf16[4,256,1024]{2,1,0:T(8,128)(2,1)S(1)}, bf16[4,256,1024]{2,1,0:T(8,128)(2,1)}, u32[]{:S(2)}) copy-start(bf16[4,256,1024]{2,1,0:T(8,128)(2,1)} %all-gather.3.cloned.1.call-done) | copy-start | bytes 6291460
  41.6 12.8 %collective-permute-start = (f32[1,256,256]{2,1,0:T(8,128)S(1)}, f32[1,256,256]{2,1,0:T(8,128)S(1)}, u32[]{:S(2)}, u32[]{:S(2)}) collective-permute-start(f32[1,256,256]{2,1,0:T(8,128)S(1)} %fusion.68), channel_id=1, source_target_pairs={{0,4},{4,8},{8,12},{12,16},{16,20},{20,24},{24,28},{1,5},{5,9},{9,... | collective-permute-start | bytes 786440 | tf_op jit(solution)/shard_map/ppermute | solution.py:51
  46.9 11.0 %collective-permute-start.1 = (f32[1,256,256]{2,1,0:T(8,128)S(1)}, f32[1,256,256]{2,1,0:T(8,128)S(1)}, u32[]{:S(2)}, u32[]{:S(2)}) collective-permute-start(f32[1,256,256]{2,1,0:T(8,128)S(1)} %fusion.71), channel_id=1, source_target_pairs={{4,0},{8,4},{12,8},{16,12},{20,16},{24,20},{28,24},{5,1},{9,5},{13... | collective-permute-start | bytes 786440 | tf_op jit(solution)/shard_map/ppermute | solution.py:52
  65.7 6.9 %collective-permute-start.6 = (bf16[1,256,256]{2,1,0:T(8,128)(2,1)S(1)}, bf16[1,256,256]{2,1,0:T(8,128)(2,1)S(1)}, u32[]{:S(2)}, u32[]{:S(2)}) collective-permute-start(bf16[1,256,256]{2,1,0:T(8,128)(2,1)S(1)} %get-tuple-element.14), channel_id=1, source_target_pairs={{0,4},{4,8},{8,12},{12,16},{16,20},{20,24},{24,28},{1,5},{5,9},{9,... | collective-permute-start | bytes 393224 | tf_op jit(solution)/shard_map/ppermute | solution.py:16
  69.9 7.9 %collective-permute-start.7 = (bf16[1,256,256]{2,1,0:T(8,128)(2,1)S(1)}, bf16[1,256,256]{2,1,0:T(8,128)(2,1)S(1)}, u32[]{:S(2)}, u32[]{:S(2)}) collective-permute-start(bf16[1,256,256]{2,1,0:T(8,128)(2,1)S(1)} %get-tuple-element.15), channel_id=1, source_target_pairs={{4,0},{8,4},{12,8},{16,12},{20,16},{24,20},{28,24},{5,1},{9,5},{13... | collective-permute-start | bytes 393224 | tf_op jit(solution)/shard_map/ppermute | solution.py:16
  72.0 15.7 %collective-permute-start.2 = (bf16[4,256,256]{2,1,0:T(8,128)(2,1)S(1)}, bf16[4,256,256]{2,1,0:T(8,128)(2,1)S(1)}, u32[]{:S(2)}, u32[]{:S(2)}) collective-permute-start(bf16[4,256,256]{2,1,0:T(8,128)(2,1)S(1)} %get-tuple-element.12), channel_id=1, source_target_pairs={{0,4},{4,0},{1,5},{5,1},{2,6},{6,2},{3,7},{7,3},{8,12},{12,8},{9,1... | collective-permute-start | bytes 1572872 | tf_op jit(solution)/shard_map/ppermute | solution.py:91
  80.7 2.1 %copy-start = (bf16[10,256,512]{1,2,0:T(8,128)(2,1)S(1)}, bf16[10,256,512]{1,2,0:T(8,128)(2,1)}, u32[]{:S(2)}) copy-start(bf16[10,256,512]{1,2,0:T(8,128)(2,1)} %all-gather.5.cloned.1.call-done) | copy-start | bytes 7864324
  98.5 6.1 %slice-start = ((s8[4718592]{0:T(1024)(128)(4,1)}), s8[4194304]{0:T(1024)(128)(4,1)S(1)}, s32[]{:S(2)}) async-start(s8[4718592]{0:T(1024)(128)(4,1)} %bitcast.234), calls=%async_computation.7 | async-start | bytes 8388608
  100.3 4.4 %slice-start.1 = ((s8[4718592]{0:T(1024)(128)(4,1)}), s8[524288]{0:T(1024)(128)(4,1)S(1)}, s32[]{:S(2)}) async-start(s8[4718592]{0:T(1024)(128)(4,1)} %bitcast.234), calls=%async_computation.8 | async-start | bytes 1048576
  113.6 12.3 %all-to-all-start.1 = ((bf16[4,256,256]{2,0,1:T(4,128)(2,1)}), bf16[4,256,256]{2,0,1:T(4,128)(2,1)S(1)}, u32[]{:S(2)}, u32[]{:S(2)}) async-start(bf16[4,256,256]{2,0,1:T(4,128)(2,1)} %copy.24), calls=%async_computation.1 | async-start | bytes 1048576 | tf_op jit(solution)/shard_map/all_to_all | solution.py:116
  125.9 29.3 %all-to-all-start.2 = ((bf16[4,1024,256]{2,1,0:T(8,128)(2,1)}), bf16[4,1024,256]{2,1,0:T(8,128)(2,1)S(1)}, u32[]{:S(2)}, u32[]{:S(2)}) async-start(bf16[4,1024,256]{2,1,0:T(8,128)(2,1)} %pad_maximum_fusion), calls=%async_computation.2 | async-start | bytes 4194304 | tf_op jit(solution)/shard_map/all_to_all | solution.py:141
Sparse Core Ops, SparseCore 0:
  9.5 29.6 all-gather.2
  41.4 25.8 all-gather.4
  94.8 47.4 reduce-scatter.1

commit v10 on v8

--- a/solution.py
+++ b/solution.py
@@ -117,9 +117,12 @@
         stacked.astype(jnp.bfloat16), "hi", scatter_dimension=2, tiled=True
     ).astype(jnp.float32)
 
-    grad_rimmed = jnp.concatenate(
-        [shift_rows(grad_conv[-1:], upward=False), grad_conv, shift_rows(grad_conv[:1], upward=True)], axis=0
-    )
+    count = lax.axis_size(SLAB)
+    crossing = [(s, s + 1) for s in range(1, count - 1, 2)] + [(s, s - 1) for s in range(2, count, 2)]
+    cross = lax.ppermute(jnp.where(lo == 1, grad_conv[-1:], grad_conv[:1]), SLAB, crossing)
+    top = jnp.where(lo == 0, cross, sent_grad[-1:])
+    bottom = jnp.where(lo == 0, sent_grad[:1], cross)
+    grad_rimmed = jnp.concatenate([top, grad_conv, bottom], axis=0)
     grad_padded = jnp.pad(grad_rimmed, ((0, 0), (1, 1), (0, 0)))
     columns = jnp.concatenate(
         [
@@ -130,10 +133,14 @@
         axis=-1,
     ).reshape(height * breadth, 9 * local_filters)
     by_filter = jnp.transpose(weight, (0, 1, 3, 2)).reshape(9 * local_filters, all_chans)
-    input_term = jnp.dot(columns, by_filter, preferred_element_type=jnp.float32)
-    split = input_term.astype(jnp.bfloat16).reshape(height, breadth, chans, all_chans // chans)
-    received = lax.all_to_all(split, "chan", split_axis=2, concat_axis=2, tiled=True)
-    grad_input = jnp.sum(received.astype(jnp.float32), axis=2).astype(jnp.bfloat16)
+    input_term = lax.dot_general(
+        by_filter, columns, (((0,), (1,)), ((), ())), preferred_element_type=jnp.float32
+    )
+    group = all_chans // chans
+    split = input_term.astype(jnp.bfloat16).reshape(chans, group, height * breadth)
+    received = lax.all_to_all(split, "chan", split_axis=0, concat_axis=0, tiled=True)
+    summed = jnp.sum(received.astype(jnp.float32), axis=0)
+    grad_input = jnp.transpose(summed).astype(jnp.bfloat16).reshape(height, breadth, group)
     return (normed, grad_input, grad_weight)
 
 

time: 154 us -> 147 us (0.955)
  local copies, waits for them, and re-layouts: 20.3 us -> 16.2 us
  starting transfers between devices: 31.4 us -> 27.7 us
  waiting for transfers between devices: 42.7 us -> 44.5 us
    ppermute x4 -> x2, starting transfers between devices: 13.7 us -> 5.85 us  [shift_rows(): return lax.ppermute(rows, SLAB, pairs)]
    reshape x2 -> x0, local copies, waits for them, and re-layouts: 5.01 us -> none  [on_device(): input_term.astype(jnp.bfloat16)]
    reduce_scatter x1, waiting for transfers between devices: 3.21 us -> 7.82 us  [on_device(): lax.psum_scatter(stacked.astype(jnp.bfloat16), 'hi', scatter_dimension=2,...]
    ppermute x0 -> x1, starting transfers between devices: none -> 4.58 us  [on_device(): lax.ppermute(jnp.where(lo == 1, grad_conv[-1:], grad_conv[:1]), SLAB, cro...]
    ppermute x1, waiting for transfers between devices: 4.19 us -> 0.31 us  [on_device(): sent_grad = lax.ppermute(grad_conv, 'lo', [(0, 1), (1, 0)])]
    ppermute x1, waiting for transfers between devices: 0.01 us -> 3.07 us  [on_device(): lax.ppermute(shift_sum(taps(gathered[:1], 2)), SLAB, [(i + 1, i) for i in...]
    ppermute x1, waiting for transfers between devices: 2.91 us -> 0.01 us  [on_device(): lax.ppermute(shift_sum(taps(gathered[-1:], 0)), SLAB, [(i, i + 1) for i i...]
    ppermute x1, waiting for transfers between devices: 2.36 us -> 0.75 us  [on_device(): lax.ppermute(local_subset(send_rows, 1 - lo), 'lo', [(0, 1), (1, 0)])]
  transfers between devices with their start and end apart: 14 -> 13, of which waited for: 8 -> 8; matrix products, arithmetic and copies ran while one was open for 35% -> 34% of each run, Pallas kernels for 0% -> 0%
where the time goes in v10:
time: 147 us; the launch traced here: 145 us
  waiting for transfers between devices  44.5 us (30%)
  matrix products  29 us (20%)
  starting transfers between devices  27.7 us (19%)
  local copies, waits for them, and re-layouts  16.2 us (11%)
  between operations  14.3 us (10%)
  other arithmetic  7.46 us (5%)
  blocking collectives  5.75 us (4%)
    all_to_all x1, waiting for transfers between devices, on_device(): lax.all_to_all(split, 'chan', split_axis=0, concat_axis=0, tiled=True)  24.1 us
    unnamed x20, local copies, waits for them, and re-layouts  12.5 us
    dot_general x18, matrix products, pair_part(): lax.dot_general(weight_window, flat, (((0,), (0,)), ((), ())), preferred_...  10.9 us
    dot_general x1, matrix products, on_device(): lax.dot_general(by_filter, columns, (((0,), (1,)), ((), ())), preferred_e...  8.97 us
    reduce_scatter x1, waiting for transfers between devices, on_device(): lax.psum_scatter(stacked.astype(jnp.bfloat16), 'hi', scatter_dimension=2,...  7.82 us
    dot_general x4, matrix products, taps(): out = jnp.dot(flat, by_row[a], preferred_element_type=jnp.float32)  7.27 us
    ppermute x2, starting transfers between devices, shift_rows(): return lax.ppermute(rows, SLAB, pairs)  5.85 us
    psum x1, blocking collectives, on_device(): totals = lax.psum(partial, 'chan')  5.75 us
  transfers between devices with their start and end apart: 13, of which 8 were waited for; matrix products, arithmetic and copies ran while one was open for 34% of the time, Pallas kernels for 0%

profile of v10, /device:TPU:4, one launch (start us, length us, event | category | flops | bytes accessed | tf_op | source)
XLA Modules:
  0.0 144.8 jit_solution(15592876787346318979)
XLA Ops:
  9.2 3.4 %collective-permute-start.4 = (bf16[1,256,256]{1,2,0:T(8,128)(2,1)S(1)}, bf16[1,256,256]{1,2,0:T(8,128)(2,1)S(1)}, u32[]{:S(2)}, u32[]{:S(2)}) collective-permute-start(bf16[1,256,256]{1,2,0:T(8,128)(2,1)S(1)} %get-tuple-element.17), channel_id=1, source_target_pairs={{0,4},{4,8},{8,12},{12,16},{16,20},{20,24},{24,28},{1,5},{5,9},{9,... | collective-permute-start | bytes 393224 | tf_op jit(solution)/shard_map/ppermute | solution.py:16
  12.6 2.4 %collective-permute-start.5 = (bf16[1,256,256]{1,2,0:T(8,128)(2,1)S(1)}, bf16[1,256,256]{1,2,0:T(8,128)(2,1)S(1)}, u32[]{:S(2)}, u32[]{:S(2)}) collective-permute-start(bf16[1,256,256]{1,2,0:T(8,128)(2,1)S(1)} %get-tuple-element.18), channel_id=1, source_target_pairs={{4,0},{8,4},{12,8},{16,12},{20,16},{24,20},{28,24},{5,1},{9,5},{13... | collective-permute-start | bytes 393224 | tf_op jit(solution)/shard_map/ppermute | solution.py:16
  16.3 4.1 %collective-permute-done.5 = bf16[1,256,256]{1,2,0:T(8,128)(2,1)S(1)} collective-permute-done((bf16[1,256,256]{1,2,0:T(8,128)(2,1)S(1)}, bf16[1,256,256]{1,2,0:T(8,128)(2,1)S(1)}, u32[]{:S(2)}, u32[]{:S(2)}) %collective-permute-start.5) | collective-permute-done | bytes 131104 | tf_op jit(solution)/shard_map/ppermute | solution.py:16
  21.4 1.6 %reshape.219 = bf16[4,2,32768]{2,1,0:T(2,128)(2,1)} reshape(bf16[1024,4,64]{2,1,0:T(4,128)(2,1)S(1)} %bitcast.227) | data formatting | bytes 1048576
  22.9 3.5 %all-to-all-start = ((bf16[4,2,32768]{2,1,0:T(2,128)(2,1)}), bf16[4,2,32768]{2,1,0:T(2,128)(2,1)S(1)}, u32[]{:S(2)}, u32[]{:S(2)}) async-start(bf16[4,2,32768]{2,1,0:T(2,128)(2,1)} %reshape.219), calls=%async_computation | async-start | bytes 1048576 | tf_op jit(solution)/shard_map/all_to_all | solution.py:40
  28.4 6.6 %copy.17 = bf16[3,3,1024,256]{2,3,1,0:T(8,128)(2,1)} copy(bf16[3,3,1024,256]{3,2,1,0:T(8,128)(2,1)} %param.4) | data formatting | bytes 9437184 | tf_op args[1]
  35.1 2.3 %all-to-all-done = bf16[4,2,32768]{2,1,0:T(2,128)(2,1)S(1)} async-done(((bf16[4,2,32768]{2,1,0:T(2,128)(2,1)}), bf16[4,2,32768]{2,1,0:T(2,128)(2,1)S(1)}, u32[]{:S(2)}, u32[]{:S(2)}) %all-to-all-start) | async-done | bytes 524320 | tf_op jit(solution)/shard_map/all_to_all | solution.py:40
  38.9 2.3 %fusion.14 = f32[1,256,3,256]{3,1,2,0:T(8,128)S(1)} fusion(bf16[3,1024,3,256]{1,3,2,0:T(8,128)(2,1)} %bitcast.221, bf16[4,256,1024]{2,1,0:T(8,128)(2,1)} %all-gather.3.cloned.1.call-done), kind=kOutput, calls=%fused_computation.44 | convolution fusion | flops 402653184 | bytes 2883584 | tf_op jit(solution)/shard_map/dot_general | solution.py:48
  41.3 3.5 %collective-permute-start = (f32[1,256,256]{2,1,0:T(8,128)S(1)}, f32[1,256,256]{2,1,0:T(8,128)S(1)}, u32[]{:S(2)}, u32[]{:S(2)}) collective-permute-start(f32[1,256,256]{2,1,0:T(8,128)S(1)} %fusion.60), channel_id=1, source_target_pairs={{0,4},{4,8},{8,12},{12,16},{16,20},{20,24},{24,28},{1,5},{5,9},{9,... | collective-permute-start | bytes 786440 | tf_op jit(solution)/shard_map/ppermute | solution.py:51
  44.8 1.7 %fusion.17 = f32[1,256,3,256]{3,1,2,0:T(8,128)S(1)} fusion(bf16[3,1024,3,256]{1,3,2,0:T(8,128)(2,1)S(1)} %bitcast.223, bf16[4,256,1024]{2,1,0:T(8,128)(2,1)} %all-gather.3.cloned.1.call-done), kind=kOutput, calls=%fused_computation.45 | convolution fusion | flops 402653184 | bytes 2883584 | tf_op jit(solution)/shard_map/dot_general | solution.py:48
  46.6 2.4 %collective-permute-start.1 = (f32[1,256,256]{2,1,0:T(8,128)S(1)}, f32[1,256,256]{2,1,0:T(8,128)S(1)}, u32[]{:S(2)}, u32[]{:S(2)}) collective-permute-start(f32[1,256,256]{2,1,0:T(8,128)S(1)} %fusion.63), channel_id=1, source_target_pairs={{4,0},{8,4},{12,8},{16,12},{20,16},{24,20},{28,24},{5,1},{9,5},{13... | collective-permute-start | bytes 786440 | tf_op jit(solution)/shard_map/ppermute | solution.py:52
  50.5 1.8 %fusion = f32[4,256,3,256]{3,1,2,0:T(8,128)S(1)} fusion(bf16[4,256,1024]{2,1,0:T(8,128)(2,1)S(1)} %copy-done.2, bf16[3,1024,3,256]{1,3,2,0:T(8,128)(2,1)S(1)} %bitcast.225), kind=kOutput, calls=%fused_computation.24 | convolution fusion | flops 1610612736 | bytes 6815744 | tf_op jit(solution)/shard_map/dot_general | solution.py:48
  52.3 1.8 %pad_add_fusion = f32[4,256,3,256]{3,1,2,0:T(8,128)S(1)} fusion(f32[3,256,3,256]{3,1,2,0:T(8,128)S(1)} %fusion.3, f32[4,256,3,256]{3,1,2,0:T(8,128)S(1)} %fusion, bf16[4,256,1024]{2,1,0:T(8,128)(2,1)S(1)} %copy-done.2, bf16[3,1024,3,256]{1,3,2,0:T(8,128)(2,1)S(1)} %bitcast.226), kind=kOutput, calls=%fused_computation.19 | convolution fusion | flops 1209532416 | bytes 11796480 | tf_op jit(solution)/shard_map/jit(_pad)/pad | solution.py:71
  54.2 3.1 %collective-permute-done.1 = f32[1,256,256]{2,1,0:T(8,128)S(1)} collective-permute-done((f32[1,256,256]{2,1,0:T(8,128)S(1)}, f32[1,256,256]{2,1,0:T(8,128)S(1)}, u32[]{:S(2)}, u32[]{:S(2)}) %collective-permute-start.1) | collective-permute-done | bytes 262176 | tf_op jit(solution)/shard_map/ppermute | solution.py:52
  58.1 5.8 %psum.7 = f32[4,256,2]{1,0,2:T(4,128)S(1)} all-reduce(f32[4,256,2]{1,0,2:T(4,128)S(1)} %pad_maximum_fusion.3), channel_id=1, replica_groups=mesh['hi'=4,'lo'=2,'chan'=4] {'chan'}, use_global_device_ids=true, to_apply=%region_2.3 | all-reduce | flops 2048 | bytes 16384 | tf_op jit(solution)/shard_map/psum | solution.py:84
  64.6 4.6 %collective-permute-start.2 = (bf16[1,256,256]{2,1,0:T(8,128)(2,1)S(1)}, bf16[1,256,256]{2,1,0:T(8,128)(2,1)S(1)}, u32[]{:S(2)}, u32[]{:S(2)}) collective-permute-start(bf16[1,256,256]{2,1,0:T(8,128)(2,1)S(1)} %slice_select_fusion), channel_id=1, source_target_pairs={{4,8},{12,16},{20,24},{8,4},{16,12},{24,20},{5,9},{13,17},{21,25},... | collective-permute-start | bytes 393224 | tf_op jit(solution)/shard_map/ppermute | solution.py:122
  70.4 3.5 %all-to-all-start.1 = ((bf16[4,256,256]{2,0,1:T(4,128)(2,1)}), bf16[4,256,256]{2,0,1:T(4,128)(2,1)S(1)}, u32[]{:S(2)}, u32[]{:S(2)}) async-start(bf16[4,256,256]{2,0,1:T(4,128)(2,1)} %copy.20), calls=%async_computation.1 | async-start | bytes 1048576 | tf_op jit(solution)/shard_map/all_to_all | solution.py:90
  74.1 1.9 %fusion.39 = f32[9,512,256]{2,1,0:T(8,128)S(1)} fusion(bf16[4,256,256]{2,1,0:T(8,128)(2,1)S(1)} %get-tuple-element.15, s32[]{:T(128)S(6)} %select_n.57, bf16[10,256,512]{1,2,0:T(8,128)(2,1)} %all-gather.5.cloned.1.call-done), kind=kOutput, calls=%fused_computation.83 | convolution fusion | flops 268435456 | bytes 3670020 | tf_op jit(solution)/shard_map/dot_general | solution.py:104
  85.6 2.1 %add_convert_fusion = bf16[9,512,256]{2,1,0:T(8,128)(2,1)} fusion(f32[9,512,256]{2,1,0:T(8,128)S(1)} %fusion.31, f32[9,512,256]{2,1,0:T(8,128)S(1)} %fusion.22), kind=kLoop, calls=%fused_computation.18 | loop fusion | flops 2359296 | bytes 11796480 | tf_op jit(solution)/shard_map/convert_element_type | solution.py:117
  88.6 9.0 %convolution_convert_fusion = bf16[1024,1024]{0,1:T(8,128)(2,1)} fusion(bf16[1024,2304]{1,0:T(8,128)(2,1)S(1)} %bitcast.238, bf16[2304,1024]{1,0:T(8,128)(2,1)} %bitcast.222), kind=kOutput, calls=%fused_computation.26 | convolution fusion | flops 4832886784 | bytes 11534336 | tf_op jit(solution)/shard_map/dot_general | solution.py:136
  97.6 3.6 %all-to-all-start.2 = ((bf16[4,256,1024]{2,1,0:T(8,128)(2,1)}), bf16[4,256,1024]{2,1,0:T(8,128)(2,1)S(1)}, u32[]{:S(2)}, u32[]{:S(2)}) async-start(bf16[4,256,1024]{2,1,0:T(8,128)(2,1)} %bitcast.231), calls=%async_computation.2 | async-start | bytes 4194304 | tf_op jit(solution)/shard_map/all_to_all | solution.py:141
  102.8 24.1 %all-to-all-done.2 = bf16[4,256,1024]{2,1,0:T(8,128)(2,1)S(1)} async-done(((bf16[4,256,1024]{2,1,0:T(8,128)(2,1)}), bf16[4,256,1024]{2,1,0:T(8,128)(2,1)S(1)}, u32[]{:S(2)}, u32[]{:S(2)}) %all-to-all-start.2) | async-done | bytes 2097184 | tf_op jit(solution)/shard_map/all_to_all | solution.py:141
  128.3 7.8 %reduce-scatter.2.cloned.1.call-done = bf16[3,3,128,256]{3,2,1,0:T(8,128)(2,1)} async-done(((bf16[3,3,512,256]{3,2,1,0:T(8,128)(2,1)}), bf16[3,3,128,256]{3,2,1,0:T(8,128)(2,1)}) %reduce-scatter.2.cloned.1.call-update) | async-done | bytes 589840 | tf_op jit(solution)/shard_map/reduce_scatter | solution.py:116
  136.1 2.2 %convert_element_type.84 = f32[3,3,128,256]{3,2,1,0:T(8,128)} convert(bf16[3,3,128,256]{3,2,1,0:T(8,128)(2,1)} %reduce-scatter.2.cloned.1.call-done) | non-fusion elementwise | flops 294912 | bytes 1769472 | tf_op jit(solution)/shard_map/convert_element_type | solution.py:118
  (79 shorter events, 25.4 us)
Async XLA Ops:
  7.2 13.5 %copy-start.3 = (bf16[4,64,1024]{2,1,0:T(8,128)(2,1)S(1)}, bf16[4,64,1024]{2,1,0:T(8,128)(2,1)}, u32[]{:S(2)}) copy-start(bf16[4,64,1024]{2,1,0:T(8,128)(2,1)} %param.5) | copy-start | bytes 1572868
  7.2 31.7 %all-gather.3.cloned.1.call-start = ((), (), s32[]{:S(2)}) async-start(), calls=%async_computation.4 | async-start | bytes 2621440 | tf_op jit(solution)/shard_map/all_gather | solution.py:41
  9.2 7.1 %collective-permute-start.4 = (bf16[1,256,256]{1,2,0:T(8,128)(2,1)S(1)}, bf16[1,256,256]{1,2,0:T(8,128)(2,1)S(1)}, u32[]{:S(2)}, u32[]{:S(2)}) collective-permute-start(bf16[1,256,256]{1,2,0:T(8,128)(2,1)S(1)} %get-tuple-element.17), channel_id=1, source_target_pairs={{0,4},{4,8},{8,12},{12,16},{16,20},{20,24},{24,28},{1,5},{5,9},{9,... | collective-permute-start | bytes 393224 | tf_op jit(solution)/shard_map/ppermute | solution.py:16
  12.6 7.8 %collective-permute-start.5 = (bf16[1,256,256]{1,2,0:T(8,128)(2,1)S(1)}, bf16[1,256,256]{1,2,0:T(8,128)(2,1)S(1)}, u32[]{:S(2)}, u32[]{:S(2)}) collective-permute-start(bf16[1,256,256]{1,2,0:T(8,128)(2,1)S(1)} %get-tuple-element.18), channel_id=1, source_target_pairs={{4,0},{8,4},{12,8},{16,12},{20,16},{24,20},{28,24},{5,1},{9,5},{13... | collective-permute-start | bytes 393224 | tf_op jit(solution)/shard_map/ppermute | solution.py:16
  20.6 6.7 %collective-permute-start.6 = (bf16[4,256,128]{1,2,0:T(8,128)(2,1)S(1)}, bf16[4,256,128]{1,2,0:T(8,128)(2,1)S(1)}, u32[]{:S(2)}, u32[]{:S(2)}) collective-permute-start(bf16[4,256,128]{1,2,0:T(8,128)(2,1)S(1)} %dynamic-slice_bitcast_fusion.1), channel_id=1, source_target_pairs={{0,4},{4,0},{1,5},{5,1},{2,6},{6,2},{3,7},{7,3},{8,12},{12,8},{9,1... | collective-permute-start | bytes 786440 | tf_op jit(solution)/shard_map/ppermute | solution.py:63
  22.9 14.5 %all-to-all-start = ((bf16[4,2,32768]{2,1,0:T(2,128)(2,1)}), bf16[4,2,32768]{2,1,0:T(2,128)(2,1)S(1)}, u32[]{:S(2)}, u32[]{:S(2)}) async-start(bf16[4,2,32768]{2,1,0:T(2,128)(2,1)} %reshape.219), calls=%async_computation | async-start | bytes 1048576 | tf_op jit(solution)/shard_map/all_to_all | solution.py:40
  26.4 47.7 %all-gather.5.cloned.1.call-start = ((), (), s32[]{:S(2)}) async-start(), calls=%async_computation.5 | async-start | bytes 3276800 | tf_op jit(solution)/shard_map/all_gather | solution.py:68
  38.9 5.9 %copy-start.1 = (bf16[3,3,1024,256]{2,3,1,0:T(8,128)(2,1)S(1)}, bf16[3,3,1024,256]{2,3,1,0:T(8,128)(2,1)}, u32[]{:S(2)}) copy-start(bf16[3,3,1024,256]{2,3,1,0:T(8,128)(2,1)} %copy.17) | copy-start | bytes 14155780
  38.9 10.2 %copy-start.2 = (bf16[4,256,1024]{2,1,0:T(8,128)(2,1)S(1)}, bf16[4,256,1024]{2,1,0:T(8,128)(2,1)}, u32[]{:S(2)}) copy-start(bf16[4,256,1024]{2,1,0:T(8,128)(2,1)} %all-gather.3.cloned.1.call-done) | copy-start | bytes 6291460
  41.3 12.9 %collective-permute-start = (f32[1,256,256]{2,1,0:T(8,128)S(1)}, f32[1,256,256]{2,1,0:T(8,128)S(1)}, u32[]{:S(2)}, u32[]{:S(2)}) collective-permute-start(f32[1,256,256]{2,1,0:T(8,128)S(1)} %fusion.60), channel_id=1, source_target_pairs={{0,4},{4,8},{8,12},{12,16},{16,20},{20,24},{24,28},{1,5},{5,9},{9,... | collective-permute-start | bytes 786440 | tf_op jit(solution)/shard_map/ppermute | solution.py:51
  46.6 10.6 %collective-permute-start.1 = (f32[1,256,256]{2,1,0:T(8,128)S(1)}, f32[1,256,256]{2,1,0:T(8,128)S(1)}, u32[]{:S(2)}, u32[]{:S(2)}) collective-permute-start(f32[1,256,256]{2,1,0:T(8,128)S(1)} %fusion.63), channel_id=1, source_target_pairs={{4,0},{8,4},{12,8},{16,12},{20,16},{24,20},{28,24},{5,1},{9,5},{13... | collective-permute-start | bytes 786440 | tf_op jit(solution)/shard_map/ppermute | solution.py:52
  64.2 16.5 %collective-permute-start.3 = (bf16[4,256,256]{2,1,0:T(8,128)(2,1)S(1)}, bf16[4,256,256]{2,1,0:T(8,128)(2,1)S(1)}, u32[]{:S(2)}, u32[]{:S(2)}) collective-permute-start(bf16[4,256,256]{2,1,0:T(8,128)(2,1)S(1)} %get-tuple-element.15), channel_id=1, source_target_pairs={{0,4},{4,0},{1,5},{5,1},{2,6},{6,2},{3,7},{7,3},{8,12},{12,8},{9,1... | collective-permute-start | bytes 1572872 | tf_op jit(solution)/shard_map/ppermute | solution.py:92
  64.6 23.1 %collective-permute-start.2 = (bf16[1,256,256]{2,1,0:T(8,128)(2,1)S(1)}, bf16[1,256,256]{2,1,0:T(8,128)(2,1)S(1)}, u32[]{:S(2)}, u32[]{:S(2)}) collective-permute-start(bf16[1,256,256]{2,1,0:T(8,128)(2,1)S(1)} %slice_select_fusion), channel_id=1, source_target_pairs={{4,8},{12,16},{20,24},{8,4},{16,12},{24,20},{5,9},{13,17},{21,25},... | collective-permute-start | bytes 393224 | tf_op jit(solution)/shard_map/ppermute | solution.py:122
  70.4 27.2 %all-to-all-start.1 = ((bf16[4,256,256]{2,0,1:T(4,128)(2,1)}), bf16[4,256,256]{2,0,1:T(4,128)(2,1)S(1)}, u32[]{:S(2)}, u32[]{:S(2)}) async-start(bf16[4,256,256]{2,0,1:T(4,128)(2,1)} %copy.20), calls=%async_computation.1 | async-start | bytes 1048576 | tf_op jit(solution)/shard_map/all_to_all | solution.py:90
  73.9 62.2 %reduce-scatter.2.cloned.1.call-start = ((), (), s32[]{:S(2)}) async-start(), calls=%async_computation.6 | async-start | bytes 2949120 | tf_op jit(solution)/shard_map/reduce_scatter | solution.py:116
  74.1 2.1 %copy-start = (bf16[10,256,512]{1,2,0:T(8,128)(2,1)S(1)}, bf16[10,256,512]{1,2,0:T(8,128)(2,1)}, u32[]{:S(2)}) copy-start(bf16[10,256,512]{1,2,0:T(8,128)(2,1)} %all-gather.5.cloned.1.call-done) | copy-start | bytes 7864324
  97.6 29.3 %all-to-all-start.2 = ((bf16[4,256,1024]{2,1,0:T(8,128)(2,1)}), bf16[4,256,1024]{2,1,0:T(8,128)(2,1)S(1)}, u32[]{:S(2)}, u32[]{:S(2)}) async-start(bf16[4,256,1024]{2,1,0:T(8,128)(2,1)} %bitcast.231), calls=%async_computation.2 | async-start | bytes 4194304 | tf_op jit(solution)/shard_map/all_to_all | solution.py:141
Sparse Core Ops, SparseCore 0:
  9.6 26.3 all-gather.2
  38.1 25.5 all-gather.4
  87.8 48.2 reduce-scatter.1

commit v11 on v10

--- a/solution.py
+++ b/solution.py
@@ -40,12 +40,12 @@
     grad_filters = lax.all_to_all(grad_out, "chan", split_axis=2, concat_axis=1, tiled=True)
     gathered = lax.all_gather(image, "chan", axis=2, tiled=True)
 
-    by_row = jnp.transpose(weight, (0, 2, 1, 3)).reshape(3, all_chans, 3 * local_filters)
-
     def taps(rows, a):
         count = rows.shape[0]
         flat = rows.reshape(count * breadth, all_chans)
-        out = jnp.dot(flat, by_row[a], preferred_element_type=jnp.float32)
+        out = jnp.stack(
+            [jnp.dot(flat, weight[a, b], preferred_element_type=jnp.float32) for b in range(3)], axis=1
+        )
         return out.reshape(count, breadth, 3, local_filters)
 
     to_next = lax.ppermute(shift_sum(taps(gathered[-1:], 0)), SLAB, [(i, i + 1) for i in range(lax.axis_size(SLAB) - 1)])
@@ -132,7 +132,8 @@
         ],
         axis=-1,
     ).reshape(height * breadth, 9 * local_filters)
-    by_filter = jnp.transpose(weight, (0, 1, 3, 2)).reshape(9 * local_filters, all_chans)
+    weight_late, _ = lax.optimization_barrier((weight, stacked))
+    by_filter = jnp.transpose(weight_late, (0, 1, 3, 2)).reshape(9 * local_filters, all_chans)
     input_term = lax.dot_general(
         by_filter, columns, (((0,), (1,)), ((), ())), preferred_element_type=jnp.float32
     )

time: 147 us -> 157 us (1.068)
  local copies, waits for them, and re-layouts: 16.2 us -> 19.3 us
  waiting for transfers between devices: 44.5 us -> 47 us
  matrix products: 29 us -> 30.7 us
  starting transfers between devices: 27.7 us -> 29.3 us
    ppermute x1, waiting for transfers between devices: 0.75 us -> 8.49 us  [on_device(): lax.ppermute(local_subset(send_rows, 1 - lo), 'lo', [(0, 1), (1, 0)])]
    optimization_barrier x0 -> x1, local copies, waits for them, and re-layouts: none -> 6.87 us  [on_device(): weight_late, _ = lax.optimization_barrier((weight, stacked))]
    dot_general x4 -> x15, matrix products: 7.27 us -> 13.5 us  [taps(): jnp.dot(flat, weight[a, b], preferred_element_type=jnp.float32)]
    reduce_scatter x1, waiting for transfers between devices: 7.82 us -> 2.34 us  [on_device(): lax.psum_scatter(stacked.astype(jnp.bfloat16), 'hi', scatter_dimension=2,...]
    ppermute x2, waiting for transfers between devices: 5.33 us -> 0.01 us  [shift_rows(): return lax.ppermute(rows, SLAB, pairs)]
    ppermute x1, waiting for transfers between devices: 0.31 us -> 5.57 us  [on_device(): sent_grad = lax.ppermute(grad_conv, 'lo', [(0, 1), (1, 0)])]
    unnamed x20 -> x21, local copies, waits for them, and re-layouts: 12.5 us -> 8.7 us
    ppermute x1, waiting for transfers between devices: 3.07 us -> 0.01 us  [on_device(): lax.ppermute(shift_sum(taps(gathered[:1], 2)), SLAB, [(i + 1, i) for i in...]
  transfers between devices with their start and end apart: 13 -> 13, of which waited for: 8 -> 7; matrix products, arithmetic and copies ran while one was open for 34% -> 34% of each run, Pallas kernels for 0% -> 0%
where the time goes in v11:
time: 157 us; the launch traced here: 155 us
  waiting for transfers between devices  47 us (30%)
  matrix products  30.7 us (20%)
  starting transfers between devices  29.3 us (19%)
  local copies, waits for them, and re-layouts  19.3 us (12%)
  between operations  14.4 us (9%)
  other arithmetic  8.13 us (5%)
  blocking collectives  6.03 us (4%)
    all_to_all x1, waiting for transfers between devices, on_device(): lax.all_to_all(split, 'chan', split_axis=0, concat_axis=0, tiled=True)  24.1 us
    dot_general x15, matrix products, taps(): jnp.dot(flat, weight[a, b], preferred_element_type=jnp.float32)  13.5 us
    dot_general x18, matrix products, pair_part(): lax.dot_general(weight_window, flat, (((0,), (0,)), ((), ())), preferred_...  10.9 us
    unnamed x21, local copies, waits for them, and re-layouts  8.7 us
    ppermute x1, waiting for transfers between devices, on_device(): lax.ppermute(local_subset(send_rows, 1 - lo), 'lo', [(0, 1), (1, 0)])  8.49 us
    optimization_barrier x1, local copies, waits for them, and re-layouts, on_device(): weight_late, _ = lax.optimization_barrier((weight, stacked))  6.87 us
    ppermute x2, starting transfers between devices, shift_rows(): return lax.ppermute(rows, SLAB, pairs)  6.74 us
    dot_general x1, matrix products, on_device(): lax.dot_general(by_filter, columns, (((0,), (1,)), ((), ())), preferred_e...  6.37 us
  transfers between devices with their start and end apart: 13, of which 7 were waited for; matrix products, arithmetic and copies ran while one was open for 34% of the time, Pallas kernels for 0%

profile of v11, /device:TPU:4, one launch (start us, length us, event | category | flops | bytes accessed | tf_op | source)
XLA Modules:
  0.0 154.9 jit_solution(9941082520833990587)
XLA Ops:
  9.2 1.9 %collective-permute-start.4 = (bf16[1,256,256]{1,2,0:T(8,128)(2,1)S(1)}, bf16[1,256,256]{1,2,0:T(8,128)(2,1)S(1)}, u32[]{:S(2)}, u32[]{:S(2)}) collective-permute-start(bf16[1,256,256]{1,2,0:T(8,128)(2,1)S(1)} %get-tuple-element.20), channel_id=1, source_target_pairs={{4,0},{8,4},{12,8},{16,12},{20,16},{24,20},{28,24},{5,1},{9,5},{13... | collective-permute-start | bytes 393224 | tf_op jit(solution)/shard_map/ppermute | solution.py:16
  11.1 4.8 %collective-permute-start.3 = (bf16[1,256,256]{1,2,0:T(8,128)(2,1)S(1)}, bf16[1,256,256]{1,2,0:T(8,128)(2,1)S(1)}, u32[]{:S(2)}, u32[]{:S(2)}) collective-permute-start(bf16[1,256,256]{1,2,0:T(8,128)(2,1)S(1)} %get-tuple-element.19), channel_id=1, source_target_pairs={{0,4},{4,8},{8,12},{12,16},{16,20},{20,24},{24,28},{1,5},{5,9},{9,... | collective-permute-start | bytes 393224 | tf_op jit(solution)/shard_map/ppermute | solution.py:16
  15.9 1.6 %copy.16 = bf16[4,64,1024]{1,0,2:T(4,128)(2,1)S(1)} copy(bf16[4,64,1024]{2,1,0:T(8,128)(2,1)} %param.5) | data formatting | bytes 1048576 | tf_op args[2]
  17.6 1.6 %reshape.274 = bf16[4,2,32768]{2,1,0:T(2,128)(2,1)} reshape(bf16[1024,4,64]{2,1,0:T(4,128)(2,1)S(1)} %bitcast.269) | data formatting | bytes 1048576
  19.1 3.5 %all-to-all-start = ((bf16[4,2,32768]{2,1,0:T(2,128)(2,1)}), bf16[4,2,32768]{2,1,0:T(2,128)(2,1)S(1)}, u32[]{:S(2)}, u32[]{:S(2)}) async-start(bf16[4,2,32768]{2,1,0:T(2,128)(2,1)} %reshape.274), calls=%async_computation | async-start | bytes 1048576 | tf_op jit(solution)/shard_map/all_to_all | solution.py:40
  23.1 8.5 %collective-permute-done.5 = bf16[4,256,128]{1,2,0:T(8,128)(2,1)S(1)} collective-permute-done((bf16[4,256,128]{1,2,0:T(8,128)(2,1)S(1)}, bf16[4,256,128]{1,2,0:T(8,128)(2,1)S(1)}, u32[]{:S(2)}, u32[]{:S(2)}) %collective-permute-start.5) | collective-permute-done | bytes 262176 | tf_op jit(solution)/shard_map/ppermute | solution.py:63
  32.7 4.6 %all-to-all-done = bf16[4,2,32768]{2,1,0:T(2,128)(2,1)S(1)} async-done(((bf16[4,2,32768]{2,1,0:T(2,128)(2,1)}), bf16[4,2,32768]{2,1,0:T(2,128)(2,1)S(1)}, u32[]{:S(2)}, u32[]{:S(2)}) %all-to-all-start) | async-done | bytes 524320 | tf_op jit(solution)/shard_map/all_to_all | solution.py:40
  39.2 1.6 %convolution_bitcast_fusion.27 = f32[256,1,256]{2,0,1:T(8,128)S(1)} fusion(bf16[3,3,1024,256]{3,2,1,0:T(8,128)(2,1)} %param.4, bf16[4,256,1024]{2,1,0:T(8,128)(2,1)} %all-gather.3.cloned.1.call-done), kind=kOutput, calls=%fused_computation.81 | convolution fusion | flops 134217728 | bytes 1310720 | tf_op jit(solution)/shard_map/dot_general | solution.py:47
  40.9 1.6 %convolution_bitcast_fusion.28 = f32[256,1,256]{2,0,1:T(8,128)S(1)} fusion(bf16[3,3,1024,256]{3,2,1,0:T(8,128)(2,1)} %param.4, bf16[4,256,1024]{2,1,0:T(8,128)(2,1)} %all-gather.3.cloned.1.call-done), kind=kOutput, calls=%fused_computation.82 | convolution fusion | flops 134217728 | bytes 1310720 | tf_op jit(solution)/shard_map/dot_general | solution.py:47
  44.2 2.5 %collective-permute-start.1 = (f32[1,256,256]{2,1,0:T(8,128)S(1)}, f32[1,256,256]{2,1,0:T(8,128)S(1)}, u32[]{:S(2)}, u32[]{:S(2)}) collective-permute-start(f32[1,256,256]{2,1,0:T(8,128)S(1)} %fusion.76), channel_id=1, source_target_pairs={{4,0},{8,4},{12,8},{16,12},{20,16},{24,20},{28,24},{5,1},{9,5},{13... | collective-permute-start | bytes 786440 | tf_op jit(solution)/shard_map/ppermute | solution.py:52
  49.9 4.3 %collective-permute-start = (f32[1,256,256]{2,1,0:T(8,128)S(1)}, f32[1,256,256]{2,1,0:T(8,128)S(1)}, u32[]{:S(2)}, u32[]{:S(2)}) collective-permute-start(f32[1,256,256]{2,1,0:T(8,128)S(1)} %fusion.73), channel_id=1, source_target_pairs={{0,4},{4,8},{8,12},{12,16},{16,20},{20,24},{24,28},{1,5},{5,9},{9,... | collective-permute-start | bytes 786440 | tf_op jit(solution)/shard_map/ppermute | solution.py:51
  62.0 6.0 %psum.7 = f32[4,256,2]{1,0,2:T(4,128)S(1)} all-reduce(f32[4,256,2]{1,0,2:T(4,128)S(1)} %pad_maximum_fusion.3), channel_id=1, replica_groups=mesh['hi'=4,'lo'=2,'chan'=4] {'chan'}, use_global_device_ids=true, to_apply=%region_2.3 | all-reduce | flops 2048 | bytes 16384 | tf_op jit(solution)/shard_map/psum | solution.py:84
  69.6 3.5 %all-to-all-start.1 = ((bf16[4,256,256]{2,0,1:T(4,128)(2,1)}), bf16[4,256,256]{2,0,1:T(4,128)(2,1)S(1)}, u32[]{:S(2)}, u32[]{:S(2)}) async-start(bf16[4,256,256]{2,0,1:T(4,128)(2,1)} %copy.18), calls=%async_computation.1 | async-start | bytes 1048576 | tf_op jit(solution)/shard_map/all_to_all | solution.py:90
  73.2 5.0 %collective-permute-start.6 = (bf16[1,256,256]{2,1,0:T(8,128)(2,1)S(1)}, bf16[1,256,256]{2,1,0:T(8,128)(2,1)S(1)}, u32[]{:S(2)}, u32[]{:S(2)}) collective-permute-start(bf16[1,256,256]{2,1,0:T(8,128)(2,1)S(1)} %slice_select_fusion), channel_id=1, source_target_pairs={{4,8},{12,16},{20,24},{8,4},{16,12},{24,20},{5,9},{13,17},{21,25},... | collective-permute-start | bytes 393224 | tf_op jit(solution)/shard_map/ppermute | solution.py:122
  78.3 1.9 %fusion.22 = f32[9,512,256]{2,1,0:T(8,128)S(1)} fusion(bf16[4,256,256]{2,1,0:T(8,128)(2,1)S(1)} %get-tuple-element.17, s32[]{:T(128)S(6)} %select_n.54, bf16[10,256,512]{1,2,0:T(8,128)(2,1)} %all-gather.5.cloned.1.call-done), kind=kOutput, calls=%fused_computation.80 | convolution fusion | flops 268435456 | bytes 3670020 | tf_op jit(solution)/shard_map/dot_general | solution.py:104
  84.6 5.6 %collective-permute-done.2 = bf16[4,256,256]{2,1,0:T(8,128)(2,1)S(1)} collective-permute-done((bf16[4,256,256]{2,1,0:T(8,128)(2,1)S(1)}, bf16[4,256,256]{2,1,0:T(8,128)(2,1)S(1)}, u32[]{:S(2)}, u32[]{:S(2)}) %collective-permute-start.2) | collective-permute-done | bytes 524320 | tf_op jit(solution)/shard_map/ppermute | solution.py:92
  95.0 2.1 %add.190 = bf16[9,512,256]{2,1,0:T(8,128)(2,1)} add(f32[9,512,256]{2,1,0:T(8,128)S(1)} %fusion.14, f32[9,512,256]{2,1,0:T(8,128)S(1)} %fusion.5) | non-fusion elementwise | flops 1179648 | bytes 11796480 | tf_op jit(solution)/shard_map/add | solution.py:115
  97.3 6.9 %copy.24 = bf16[3,3,1024,256]{2,3,1,0:T(8,128)(2,1)} copy(bf16[3,3,1024,256]{3,2,1,0:T(8,128)(2,1)} %param.4) | data formatting | bytes 9437184 | tf_op jit(solution)/shard_map/optimization_barrier | solution.py:135
  104.8 1.9 %copy-done.2 = bf16[3,3,1024,256]{2,3,1,0:T(8,128)(2,1)S(1)} copy-done((bf16[3,3,1024,256]{2,3,1,0:T(8,128)(2,1)S(1)}, bf16[3,3,1024,256]{2,3,1,0:T(8,128)(2,1)}, u32[]{:S(2)}) %copy-start.2) | copy-done | bytes 4718616
  106.8 6.4 %convolution_convert_fusion = bf16[1024,1024]{1,0:T(8,128)(2,1)} fusion(bf16[2304,1024]{1,0:T(8,128)(2,1)S(1)} %bitcast.268, bf16[1024,2304]{1,0:T(8,128)(2,1)S(1)} %bitcast.280), kind=kOutput, calls=%fused_computation.30 | convolution fusion | flops 4832886784 | bytes 11534336 | tf_op jit(solution)/shard_map/dot_general | solution.py:137
  113.2 3.6 %all-to-all-start.2 = ((bf16[4,256,1024]{2,1,0:T(8,128)(2,1)}), bf16[4,256,1024]{2,1,0:T(8,128)(2,1)S(1)}, u32[]{:S(2)}, u32[]{:S(2)}) async-start(bf16[4,256,1024]{2,1,0:T(8,128)(2,1)} %bitcast.273), calls=%async_computation.2 | async-start | bytes 4194304 | tf_op jit(solution)/shard_map/all_to_all | solution.py:142
  118.3 24.1 %all-to-all-done.2 = bf16[4,256,1024]{2,1,0:T(8,128)(2,1)S(1)} async-done(((bf16[4,256,1024]{2,1,0:T(8,128)(2,1)}), bf16[4,256,1024]{2,1,0:T(8,128)(2,1)S(1)}, u32[]{:S(2)}, u32[]{:S(2)}) %all-to-all-start.2) | async-done | bytes 2097184 | tf_op jit(solution)/shard_map/all_to_all | solution.py:142
  143.9 2.3 %reduce-scatter.2.cloned.1.call-done = bf16[3,3,128,256]{3,2,1,0:T(8,128)(2,1)} async-done(((bf16[3,3,512,256]{3,2,1,0:T(8,128)(2,1)}), bf16[3,3,128,256]{3,2,1,0:T(8,128)(2,1)}) %reduce-scatter.2.cloned.1.call-update) | async-done | bytes 589840 | tf_op jit(solution)/shard_map/reduce_scatter | solution.py:116
  146.2 2.2 %convert_element_type.76 = f32[3,3,128,256]{3,2,1,0:T(8,128)} convert(bf16[3,3,128,256]{3,2,1,0:T(8,128)(2,1)} %reduce-scatter.2.cloned.1.call-done) | non-fusion elementwise | flops 294912 | bytes 1769472 | tf_op jit(solution)/shard_map/convert_element_type | solution.py:118
  (95 shorter events, 32.5 us)
Async XLA Ops:
  7.2 32.1 %all-gather.3.cloned.1.call-start = ((), (), s32[]{:S(2)}) async-start(), calls=%async_computation.4 | async-start | bytes 2621440 | tf_op jit(solution)/shard_map/all_gather | solution.py:41
  9.2 13.5 %collective-permute-start.4 = (bf16[1,256,256]{1,2,0:T(8,128)(2,1)S(1)}, bf16[1,256,256]{1,2,0:T(8,128)(2,1)S(1)}, u32[]{:S(2)}, u32[]{:S(2)}) collective-permute-start(bf16[1,256,256]{1,2,0:T(8,128)(2,1)S(1)} %get-tuple-element.20), channel_id=1, source_target_pairs={{4,0},{8,4},{12,8},{16,12},{20,16},{24,20},{28,24},{5,1},{9,5},{13... | collective-permute-start | bytes 393224 | tf_op jit(solution)/shard_map/ppermute | solution.py:16
  11.1 11.6 %collective-permute-start.3 = (bf16[1,256,256]{1,2,0:T(8,128)(2,1)S(1)}, bf16[1,256,256]{1,2,0:T(8,128)(2,1)S(1)}, u32[]{:S(2)}, u32[]{:S(2)}) collective-permute-start(bf16[1,256,256]{1,2,0:T(8,128)(2,1)S(1)} %get-tuple-element.19), channel_id=1, source_target_pairs={{0,4},{4,8},{8,12},{12,16},{16,20},{20,24},{24,28},{1,5},{5,9},{9,... | collective-permute-start | bytes 393224 | tf_op jit(solution)/shard_map/ppermute | solution.py:16
  19.1 18.2 %all-to-all-start = ((bf16[4,2,32768]{2,1,0:T(2,128)(2,1)}), bf16[4,2,32768]{2,1,0:T(2,128)(2,1)S(1)}, u32[]{:S(2)}, u32[]{:S(2)}) async-start(bf16[4,2,32768]{2,1,0:T(2,128)(2,1)} %reshape.274), calls=%async_computation | async-start | bytes 1048576 | tf_op jit(solution)/shard_map/all_to_all | solution.py:40
  22.6 55.7 %all-gather.5.cloned.1.call-start = ((), (), s32[]{:S(2)}) async-start(), calls=%async_computation.5 | async-start | bytes 3276800 | tf_op jit(solution)/shard_map/all_gather | solution.py:68
  22.9 8.7 %collective-permute-start.5 = (bf16[4,256,128]{1,2,0:T(8,128)(2,1)S(1)}, bf16[4,256,128]{1,2,0:T(8,128)(2,1)S(1)}, u32[]{:S(2)}, u32[]{:S(2)}) collective-permute-start(bf16[4,256,128]{1,2,0:T(8,128)(2,1)S(1)} %dynamic-slice_bitcast_fusion.1), channel_id=1, source_target_pairs={{0,4},{4,0},{1,5},{5,1},{2,6},{6,2},{3,7},{7,3},{8,12},{12,8},{9,1... | collective-permute-start | bytes 786440 | tf_op jit(solution)/shard_map/ppermute | solution.py:63
  31.6 17.9 %slice-start = ((s8[4718592]{0:T(1024)(128)(4,1)}), s8[524288]{0:T(1024)(128)(4,1)S(1)}, s32[]{:S(2)}) async-start(s8[4718592]{0:T(1024)(128)(4,1)} %bitcast.265), calls=%async_computation.7 | async-start | bytes 1048576
  39.2 7.4 %copy-start.1 = (bf16[4,256,1024]{2,1,0:T(8,128)(2,1)S(1)}, bf16[4,256,1024]{2,1,0:T(8,128)(2,1)}, u32[]{:S(2)}) copy-start(bf16[4,256,1024]{2,1,0:T(8,128)(2,1)} %all-gather.3.cloned.1.call-done) | copy-start | bytes 6291460
  40.9 8.6 %slice-start.1 = ((s8[4718592]{0:T(1024)(128)(4,1)}), s8[4194304]{0:T(1024)(128)(4,1)S(1)}, s32[]{:S(2)}) async-start(s8[4718592]{0:T(1024)(128)(4,1)} %bitcast.265), calls=%async_computation.8 | async-start | bytes 8388608
  44.2 16.2 %collective-permute-start.1 = (f32[1,256,256]{2,1,0:T(8,128)S(1)}, f32[1,256,256]{2,1,0:T(8,128)S(1)}, u32[]{:S(2)}, u32[]{:S(2)}) collective-permute-start(f32[1,256,256]{2,1,0:T(8,128)S(1)} %fusion.76), channel_id=1, source_target_pairs={{4,0},{8,4},{12,8},{16,12},{20,16},{24,20},{28,24},{5,1},{9,5},{13... | collective-permute-start | bytes 786440 | tf_op jit(solution)/shard_map/ppermute | solution.py:52
  49.9 11.2 %collective-permute-start = (f32[1,256,256]{2,1,0:T(8,128)S(1)}, f32[1,256,256]{2,1,0:T(8,128)S(1)}, u32[]{:S(2)}, u32[]{:S(2)}) collective-permute-start(f32[1,256,256]{2,1,0:T(8,128)S(1)} %fusion.73), channel_id=1, source_target_pairs={{0,4},{4,8},{8,12},{12,16},{16,20},{20,24},{24,28},{1,5},{5,9},{9,... | collective-permute-start | bytes 786440 | tf_op jit(solution)/shard_map/ppermute | solution.py:51
  69.6 43.6 %all-to-all-start.1 = ((bf16[4,256,256]{2,0,1:T(4,128)(2,1)}), bf16[4,256,256]{2,0,1:T(4,128)(2,1)S(1)}, u32[]{:S(2)}, u32[]{:S(2)}) async-start(bf16[4,256,256]{2,0,1:T(4,128)(2,1)} %copy.18), calls=%async_computation.1 | async-start | bytes 1048576 | tf_op jit(solution)/shard_map/all_to_all | solution.py:90
  73.0 73.2 %reduce-scatter.2.cloned.1.call-start = ((), (), s32[]{:S(2)}) async-start(), calls=%async_computation.6 | async-start | bytes 2949120 | tf_op jit(solution)/shard_map/reduce_scatter | solution.py:116
  73.1 17.1 %collective-permute-start.2 = (bf16[4,256,256]{2,1,0:T(8,128)(2,1)S(1)}, bf16[4,256,256]{2,1,0:T(8,128)(2,1)S(1)}, u32[]{:S(2)}, u32[]{:S(2)}) collective-permute-start(bf16[4,256,256]{2,1,0:T(8,128)(2,1)S(1)} %get-tuple-element.17), channel_id=1, source_target_pairs={{0,4},{4,0},{1,5},{5,1},{2,6},{6,2},{3,7},{7,3},{8,12},{12,8},{9,1... | collective-permute-start | bytes 1572872 | tf_op jit(solution)/shard_map/ppermute | solution.py:92
  73.2 23.9 %collective-permute-start.6 = (bf16[1,256,256]{2,1,0:T(8,128)(2,1)S(1)}, bf16[1,256,256]{2,1,0:T(8,128)(2,1)S(1)}, u32[]{:S(2)}, u32[]{:S(2)}) collective-permute-start(bf16[1,256,256]{2,1,0:T(8,128)(2,1)S(1)} %slice_select_fusion), channel_id=1, source_target_pairs={{4,8},{12,16},{20,24},{8,4},{16,12},{24,20},{5,9},{13,17},{21,25},... | collective-permute-start | bytes 393224 | tf_op jit(solution)/shard_map/ppermute | solution.py:122
  78.3 2.1 %copy-start = (bf16[10,256,512]{1,2,0:T(8,128)(2,1)S(1)}, bf16[10,256,512]{1,2,0:T(8,128)(2,1)}, u32[]{:S(2)}) copy-start(bf16[10,256,512]{1,2,0:T(8,128)(2,1)} %all-gather.5.cloned.1.call-done) | copy-start | bytes 7864324
  104.3 2.4 %copy-start.2 = (bf16[3,3,1024,256]{2,3,1,0:T(8,128)(2,1)S(1)}, bf16[3,3,1024,256]{2,3,1,0:T(8,128)(2,1)}, u32[]{:S(2)}) copy-start(bf16[3,3,1024,256]{2,3,1,0:T(8,128)(2,1)} %copy.24) | copy-start | bytes 14155780
  113.2 29.3 %all-to-all-start.2 = ((bf16[4,256,1024]{2,1,0:T(8,128)(2,1)}), bf16[4,256,1024]{2,1,0:T(8,128)(2,1)S(1)}, u32[]{:S(2)}, u32[]{:S(2)}) async-start(bf16[4,256,1024]{2,1,0:T(8,128)(2,1)} %bitcast.273), calls=%async_computation.2 | async-start | bytes 4194304 | tf_op jit(solution)/shard_map/all_to_all | solution.py:142
Sparse Core Ops, SparseCore 0:
  9.5 29.6 all-gather.2
  41.4 25.5 all-gather.4
  97.2 48.9 reduce-scatter.1

commit v12 on v10

--- a/solution.py
+++ b/solution.py
@@ -56,14 +56,16 @@
         taken = lax.dynamic_index_in_dim(shaped, which, axis=3, keepdims=False)
         return taken.reshape(x.shape[0], x.shape[1], per_chan * piece)
 
-    raw6 = jnp.concatenate(
-        [shift_rows(image[-1:], upward=False), image, shift_rows(image[:1], upward=True)], axis=0
+    count = lax.axis_size(SLAB)
+    crossing = [(s, s + 1) for s in range(1, count - 1, 2)] + [(s, s - 1) for s in range(2, count, 2)]
+    edge = lax.ppermute(jnp.where(lo == 1, image[-1:], image[:1]), SLAB, crossing)
+    mine = jnp.where(
+        lo == 0, jnp.concatenate([edge, image], axis=0), jnp.concatenate([image, edge], axis=0)
     )
-    send_rows = lax.dynamic_slice_in_dim(raw6, 2 * lo, height, axis=0)
-    sent_img = lax.ppermute(local_subset(send_rows, 1 - lo), "lo", [(0, 1), (1, 0)])
-    own_img = local_subset(raw6, lo)
+    sent_img = lax.ppermute(local_subset(mine, 1 - lo), "lo", [(0, 1), (1, 0)])
+    own_img = local_subset(mine, lo)
     block_piece = lax.dynamic_slice_in_dim(
-        jnp.concatenate([sent_img, own_img, sent_img], axis=0), height * (1 - lo), 2 * height + 2, axis=0
+        jnp.concatenate([sent_img, own_img, sent_img], axis=0), (height + 1) * (1 - lo), 2 * height + 2, axis=0
     )
     img_block = lax.all_gather(block_piece, "chan", axis=2, tiled=True)
 

time: 147 us -> 148 us (level)
  starting transfers between devices: 27.7 us -> 24.7 us
    ppermute x1, waiting for transfers between devices: 0.01 us -> 3.28 us  [on_device(): lax.ppermute(shift_sum(taps(gathered[-1:], 0)), SLAB, [(i, i + 1) for i i...]
    ppermute x1, waiting for transfers between devices: 3.07 us -> 0.01 us  [on_device(): lax.ppermute(shift_sum(taps(gathered[:1], 2)), SLAB, [(i + 1, i) for i in...]
    ppermute x3 -> x2, starting transfers between devices: 5.92 us -> 3.5 us  [the longest x1 3.43 us: on_device(): lax.ppermute(jnp.where(lo == 1, image[-1:], image[:1]), SLAB, crossing)]
    concatenate x0 -> x3, local copies, waits for them, and re-layouts: none -> 1.68 us  [on_device(): jnp.concatenate([edge, image], axis=0)]
    unnamed x20 -> x19, local copies, waits for them, and re-layouts: 12.5 us -> 11.3 us
    ppermute x3 -> x2, waiting for transfers between devices: 6.08 us -> 5.74 us  [the longest x1 2.99 us: on_device(): lax.ppermute(jnp.where(lo == 1, image[-1:], image[:1]), SLAB, crossing)]
  transfers between devices with their start and end apart: 13 -> 12, of which waited for: 8 -> 8; matrix products, arithmetic and copies ran while one was open for 34% -> 35% of each run, Pallas kernels for 0% -> 0%
where the time goes in v12:
time: 148 us; the launch traced here: 145 us
  waiting for transfers between devices  45.9 us (31%)
  matrix products  28.9 us (20%)
  starting transfers between devices  24.7 us (17%)
  local copies, waits for them, and re-layouts  16.7 us (11%)
  between operations  14.3 us (10%)
  other arithmetic  8.46 us (6%)
  blocking collectives  6.53 us (4%)
    all_to_all x1, waiting for transfers between devices, on_device(): lax.all_to_all(split, 'chan', split_axis=0, concat_axis=0, tiled=True)  24.1 us
    unnamed x19, local copies, waits for them, and re-layouts  11.3 us
    dot_general x18, matrix products, pair_part(): lax.dot_general(weight_window, flat, (((0,), (0,)), ((), ())), preferred_...  10.9 us
    dot_general x1, matrix products, on_device(): lax.dot_general(by_filter, columns, (((0,), (1,)), ((), ())), preferred_e...  8.98 us
    reduce_scatter x1, waiting for transfers between devices, on_device(): lax.psum_scatter(stacked.astype(jnp.bfloat16), 'hi', scatter_dimension=2,...  7.81 us
    dot_general x4, matrix products, taps(): out = jnp.dot(flat, by_row[a], preferred_element_type=jnp.float32)  7.22 us
    psum x1, blocking collectives, on_device(): totals = lax.psum(partial, 'chan')  6.53 us
    ppermute x1, starting transfers between devices, on_device(): lax.ppermute(jnp.where(lo == 1, grad_conv[-1:], grad_conv[:1]), SLAB, cro...  4.31 us
  transfers between devices with their start and end apart: 12, of which 8 were waited for; matrix products, arithmetic and copies ran while one was open for 35% of the time, Pallas kernels for 0%

profile of v12, /device:TPU:4, one launch (start us, length us, event | category | flops | bytes accessed | tf_op | source)
XLA Modules:
  0.0 145.5 jit_solution(4187124229517153342)
XLA Ops:
  8.9 3.4 %collective-permute-start.4 = (bf16[1,256,256]{2,1,0:T(8,128)(2,1)S(1)}, bf16[1,256,256]{2,1,0:T(8,128)(2,1)S(1)}, u32[]{:S(2)}, u32[]{:S(2)}) collective-permute-start(bf16[1,256,256]{2,1,0:T(8,128)(2,1)S(1)} %slice_select_fusion.3), channel_id=1, source_target_pairs={{4,8},{12,16},{20,24},{8,4},{16,12},{24,20},{5,9},{13,17},{21,25},... | collective-permute-start | bytes 393224 | tf_op jit(solution)/shard_map/ppermute | solution.py:61
  13.9 3.0 %collective-permute-done.4 = bf16[1,256,256]{2,1,0:T(8,128)(2,1)S(1)} collective-permute-done((bf16[1,256,256]{2,1,0:T(8,128)(2,1)S(1)}, bf16[1,256,256]{2,1,0:T(8,128)(2,1)S(1)}, u32[]{:S(2)}, u32[]{:S(2)}) %collective-permute-start.4) | collective-permute-done | bytes 131104 | tf_op jit(solution)/shard_map/ppermute | solution.py:61
  18.0 1.6 %reshape.268 = bf16[4,2,32768]{2,1,0:T(2,128)(2,1)} reshape(bf16[1024,4,64]{2,1,0:T(4,128)(2,1)S(1)} %bitcast.224) | data formatting | bytes 1048576
  19.5 3.5 %all-to-all-start = ((bf16[4,2,32768]{2,1,0:T(2,128)(2,1)}), bf16[4,2,32768]{2,1,0:T(2,128)(2,1)S(1)}, u32[]{:S(2)}, u32[]{:S(2)}) async-start(bf16[4,2,32768]{2,1,0:T(2,128)(2,1)} %reshape.268), calls=%async_computation | async-start | bytes 1048576 | tf_op jit(solution)/shard_map/all_to_all | solution.py:40
  23.1 2.8 %collective-permute-done.5 = bf16[5,256,128]{1,2,0:T(8,128)(2,1)S(1)} collective-permute-done((bf16[5,256,128]{1,2,0:T(8,128)(2,1)S(1)}, bf16[5,256,128]{1,2,0:T(8,128)(2,1)S(1)}, u32[]{:S(2)}, u32[]{:S(2)}) %collective-permute-start.5) | collective-permute-done | bytes 327712 | tf_op jit(solution)/shard_map/ppermute | solution.py:65
  27.0 6.7 %copy.20 = bf16[3,3,1024,256]{2,3,1,0:T(8,128)(2,1)} copy(bf16[3,3,1024,256]{3,2,1,0:T(8,128)(2,1)} %param.4) | data formatting | bytes 9437184 | tf_op args[1]
  33.8 3.7 %all-to-all-done = bf16[4,2,32768]{2,1,0:T(2,128)(2,1)S(1)} async-done(((bf16[4,2,32768]{2,1,0:T(2,128)(2,1)}), bf16[4,2,32768]{2,1,0:T(2,128)(2,1)S(1)}, u32[]{:S(2)}, u32[]{:S(2)}) %all-to-all-start) | async-done | bytes 524320 | tf_op jit(solution)/shard_map/all_to_all | solution.py:40
  39.2 2.3 %fusion.14 = f32[1,256,3,256]{3,1,2,0:T(8,128)S(1)} fusion(bf16[3,1024,3,256]{1,3,2,0:T(8,128)(2,1)} %bitcast.218, bf16[4,256,1024]{2,1,0:T(8,128)(2,1)} %all-gather.3.cloned.1.call-done), kind=kOutput, calls=%fused_computation.44 | convolution fusion | flops 402653184 | bytes 2883584 | tf_op jit(solution)/shard_map/dot_general | solution.py:48
  41.6 3.2 %collective-permute-start = (f32[1,256,256]{2,1,0:T(8,128)S(1)}, f32[1,256,256]{2,1,0:T(8,128)S(1)}, u32[]{:S(2)}, u32[]{:S(2)}) collective-permute-start(f32[1,256,256]{2,1,0:T(8,128)S(1)} %fusion.60), channel_id=1, source_target_pairs={{0,4},{4,8},{8,12},{12,16},{16,20},{20,24},{24,28},{1,5},{5,9},{9,... | collective-permute-start | bytes 786440 | tf_op jit(solution)/shard_map/ppermute | solution.py:51
  44.8 1.6 %fusion.17 = f32[1,256,3,256]{3,1,2,0:T(8,128)S(1)} fusion(bf16[3,1024,3,256]{1,3,2,0:T(8,128)(2,1)S(1)} %bitcast.220, bf16[4,256,1024]{2,1,0:T(8,128)(2,1)} %all-gather.3.cloned.1.call-done), kind=kOutput, calls=%fused_computation.45 | convolution fusion | flops 402653184 | bytes 2883584 | tf_op jit(solution)/shard_map/dot_general | solution.py:48
  46.5 2.8 %collective-permute-start.1 = (f32[1,256,256]{2,1,0:T(8,128)S(1)}, f32[1,256,256]{2,1,0:T(8,128)S(1)}, u32[]{:S(2)}, u32[]{:S(2)}) collective-permute-start(f32[1,256,256]{2,1,0:T(8,128)S(1)} %fusion.63), channel_id=1, source_target_pairs={{4,0},{8,4},{12,8},{16,12},{20,16},{24,20},{28,24},{5,1},{9,5},{13... | collective-permute-start | bytes 786440 | tf_op jit(solution)/shard_map/ppermute | solution.py:52
  50.8 1.8 %fusion = f32[4,256,3,256]{3,1,2,0:T(8,128)S(1)} fusion(bf16[4,256,1024]{2,1,0:T(8,128)(2,1)S(1)} %copy-done.2, bf16[3,1024,3,256]{1,3,2,0:T(8,128)(2,1)S(1)} %bitcast.222), kind=kOutput, calls=%fused_computation.24 | convolution fusion | flops 1610612736 | bytes 6815744 | tf_op jit(solution)/shard_map/dot_general | solution.py:48
  52.6 1.8 %pad_add_fusion = f32[4,256,3,256]{3,1,2,0:T(8,128)S(1)} fusion(f32[3,256,3,256]{3,1,2,0:T(8,128)S(1)} %fusion.3, f32[4,256,3,256]{3,1,2,0:T(8,128)S(1)} %fusion, bf16[4,256,1024]{2,1,0:T(8,128)(2,1)S(1)} %copy-done.2, bf16[3,1024,3,256]{1,3,2,0:T(8,128)(2,1)S(1)} %bitcast.223), kind=kOutput, calls=%fused_computation.19 | convolution fusion | flops 1209532416 | bytes 11796480 | tf_op jit(solution)/shard_map/jit(_pad)/pad | solution.py:73
  54.4 3.3 %collective-permute-done = f32[1,256,256]{2,1,0:T(8,128)S(1)} collective-permute-done((f32[1,256,256]{2,1,0:T(8,128)S(1)}, f32[1,256,256]{2,1,0:T(8,128)S(1)}, u32[]{:S(2)}, u32[]{:S(2)}) %collective-permute-start) | collective-permute-done | bytes 262176 | tf_op jit(solution)/shard_map/ppermute | solution.py:51
  58.6 6.5 %psum.7 = f32[4,256,2]{1,0,2:T(4,128)S(1)} all-reduce(f32[4,256,2]{1,0,2:T(4,128)S(1)} %pad_maximum_fusion.2), channel_id=1, replica_groups=mesh['hi'=4,'lo'=2,'chan'=4] {'chan'}, use_global_device_ids=true, to_apply=%region_2.3 | all-reduce | flops 2048 | bytes 16384 | tf_op jit(solution)/shard_map/psum | solution.py:86
  65.6 4.3 %collective-permute-start.2 = (bf16[1,256,256]{2,1,0:T(8,128)(2,1)S(1)}, bf16[1,256,256]{2,1,0:T(8,128)(2,1)S(1)}, u32[]{:S(2)}, u32[]{:S(2)}) collective-permute-start(bf16[1,256,256]{2,1,0:T(8,128)(2,1)S(1)} %slice_select_fusion), channel_id=1, source_target_pairs={{4,8},{12,16},{20,24},{8,4},{16,12},{24,20},{5,9},{13,17},{21,25},... | collective-permute-start | bytes 393224 | tf_op jit(solution)/shard_map/ppermute | solution.py:124
  71.1 3.5 %all-to-all-start.1 = ((bf16[4,256,256]{2,0,1:T(4,128)(2,1)}), bf16[4,256,256]{2,0,1:T(4,128)(2,1)S(1)}, u32[]{:S(2)}, u32[]{:S(2)}) async-start(bf16[4,256,256]{2,0,1:T(4,128)(2,1)} %copy.23), calls=%async_computation.1 | async-start | bytes 1048576 | tf_op jit(solution)/shard_map/all_to_all | solution.py:92
  74.9 1.9 %fusion.39 = f32[9,512,256]{2,1,0:T(8,128)S(1)} fusion(bf16[4,256,256]{2,1,0:T(8,128)(2,1)S(1)} %get-tuple-element.17, s32[]{:T(128)S(6)} %select_n.74, bf16[10,256,512]{1,2,0:T(8,128)(2,1)} %all-gather.5.cloned.1.call-done), kind=kOutput, calls=%fused_computation.83 | convolution fusion | flops 268435456 | bytes 3670020 | tf_op jit(solution)/shard_map/dot_general | solution.py:106
  86.2 2.1 %add_convert_fusion = bf16[9,512,256]{2,1,0:T(8,128)(2,1)} fusion(f32[9,512,256]{2,1,0:T(8,128)S(1)} %fusion.31, f32[9,512,256]{2,1,0:T(8,128)S(1)} %fusion.22), kind=kLoop, calls=%fused_computation.18 | loop fusion | flops 2359296 | bytes 11796480 | tf_op jit(solution)/shard_map/convert_element_type | solution.py:119
  89.2 9.0 %convolution_convert_fusion = bf16[1024,1024]{0,1:T(8,128)(2,1)} fusion(bf16[1024,2304]{1,0:T(8,128)(2,1)S(1)} %bitcast.234, bf16[2304,1024]{1,0:T(8,128)(2,1)} %bitcast.219), kind=kOutput, calls=%fused_computation.26 | convolution fusion | flops 4832886784 | bytes 11534336 | tf_op jit(solution)/shard_map/dot_general | solution.py:138
  98.2 3.6 %all-to-all-start.2 = ((bf16[4,256,1024]{2,1,0:T(8,128)(2,1)}), bf16[4,256,1024]{2,1,0:T(8,128)(2,1)S(1)}, u32[]{:S(2)}, u32[]{:S(2)}) async-start(bf16[4,256,1024]{2,1,0:T(8,128)(2,1)} %bitcast.227), calls=%async_computation.2 | async-start | bytes 4194304 | tf_op jit(solution)/shard_map/all_to_all | solution.py:143
  103.4 24.1 %all-to-all-done.2 = bf16[4,256,1024]{2,1,0:T(8,128)(2,1)S(1)} async-done(((bf16[4,256,1024]{2,1,0:T(8,128)(2,1)}), bf16[4,256,1024]{2,1,0:T(8,128)(2,1)S(1)}, u32[]{:S(2)}, u32[]{:S(2)}) %all-to-all-start.2) | async-done | bytes 2097184 | tf_op jit(solution)/shard_map/all_to_all | solution.py:143
  128.9 7.8 %reduce-scatter.2.cloned.1.call-done = bf16[3,3,128,256]{3,2,1,0:T(8,128)(2,1)} async-done(((bf16[3,3,512,256]{3,2,1,0:T(8,128)(2,1)}), bf16[3,3,128,256]{3,2,1,0:T(8,128)(2,1)}) %reduce-scatter.2.cloned.1.call-update) | async-done | bytes 589840 | tf_op jit(solution)/shard_map/reduce_scatter | solution.py:118
  136.7 2.2 %convert_element_type.84 = f32[3,3,128,256]{3,2,1,0:T(8,128)} convert(bf16[3,3,128,256]{3,2,1,0:T(8,128)(2,1)} %reduce-scatter.2.cloned.1.call-done) | non-fusion elementwise | flops 294912 | bytes 1769472 | tf_op jit(solution)/shard_map/convert_element_type | solution.py:120
  (77 shorter events, 24.8 us)
Async XLA Ops:
  7.2 10.1 %copy-start.3 = (bf16[4,64,1024]{2,1,0:T(8,128)(2,1)S(1)}, bf16[4,64,1024]{2,1,0:T(8,128)(2,1)}, u32[]{:S(2)}) copy-start(bf16[4,64,1024]{2,1,0:T(8,128)(2,1)} %param.5) | copy-start | bytes 1572868
  7.2 32.0 %all-gather.3.cloned.1.call-start = ((), (), s32[]{:S(2)}) async-start(), calls=%async_computation.4 | async-start | bytes 2621440 | tf_op jit(solution)/shard_map/all_gather | solution.py:41
  8.9 8.0 %collective-permute-start.4 = (bf16[1,256,256]{2,1,0:T(8,128)(2,1)S(1)}, bf16[1,256,256]{2,1,0:T(8,128)(2,1)S(1)}, u32[]{:S(2)}, u32[]{:S(2)}) collective-permute-start(bf16[1,256,256]{2,1,0:T(8,128)(2,1)S(1)} %slice_select_fusion.3), channel_id=1, source_target_pairs={{4,8},{12,16},{20,24},{8,4},{16,12},{24,20},{5,9},{13,17},{21,25},... | collective-permute-start | bytes 393224 | tf_op jit(solution)/shard_map/ppermute | solution.py:61
  17.2 8.6 %collective-permute-start.5 = (bf16[5,256,128]{1,2,0:T(8,128)(2,1)S(1)}, bf16[5,256,128]{1,2,0:T(8,128)(2,1)S(1)}, u32[]{:S(2)}, u32[]{:S(2)}) collective-permute-start(bf16[5,256,128]{1,2,0:T(8,128)(2,1)S(1)} %get-tuple-element.16), channel_id=1, source_target_pairs={{0,4},{4,0},{1,5},{5,1},{2,6},{6,2},{3,7},{7,3},{8,12},{12,8},{9,1... | collective-permute-start | bytes 983048 | tf_op jit(solution)/shard_map/ppermute | solution.py:65
  19.5 17.9 %all-to-all-start = ((bf16[4,2,32768]{2,1,0:T(2,128)(2,1)}), bf16[4,2,32768]{2,1,0:T(2,128)(2,1)S(1)}, u32[]{:S(2)}, u32[]{:S(2)}) async-start(bf16[4,2,32768]{2,1,0:T(2,128)(2,1)} %reshape.268), calls=%async_computation | async-start | bytes 1048576 | tf_op jit(solution)/shard_map/all_to_all | solution.py:40
  23.0 51.8 %all-gather.5.cloned.1.call-start = ((), (), s32[]{:S(2)}) async-start(), calls=%async_computation.5 | async-start | bytes 3276800 | tf_op jit(solution)/shard_map/all_gather | solution.py:70
  39.2 5.6 %copy-start.1 = (bf16[3,3,1024,256]{2,3,1,0:T(8,128)(2,1)S(1)}, bf16[3,3,1024,256]{2,3,1,0:T(8,128)(2,1)}, u32[]{:S(2)}) copy-start(bf16[3,3,1024,256]{2,3,1,0:T(8,128)(2,1)} %copy.20) | copy-start | bytes 14155780
  39.2 10.1 %copy-start.2 = (bf16[4,256,1024]{2,1,0:T(8,128)(2,1)S(1)}, bf16[4,256,1024]{2,1,0:T(8,128)(2,1)}, u32[]{:S(2)}) copy-start(bf16[4,256,1024]{2,1,0:T(8,128)(2,1)} %all-gather.3.cloned.1.call-done) | copy-start | bytes 6291460
  41.6 16.1 %collective-permute-start = (f32[1,256,256]{2,1,0:T(8,128)S(1)}, f32[1,256,256]{2,1,0:T(8,128)S(1)}, u32[]{:S(2)}, u32[]{:S(2)}) collective-permute-start(f32[1,256,256]{2,1,0:T(8,128)S(1)} %fusion.60), channel_id=1, source_target_pairs={{0,4},{4,8},{8,12},{12,16},{16,20},{20,24},{24,28},{1,5},{5,9},{9,... | collective-permute-start | bytes 786440 | tf_op jit(solution)/shard_map/ppermute | solution.py:51
  46.5 11.2 %collective-permute-start.1 = (f32[1,256,256]{2,1,0:T(8,128)S(1)}, f32[1,256,256]{2,1,0:T(8,128)S(1)}, u32[]{:S(2)}, u32[]{:S(2)}) collective-permute-start(f32[1,256,256]{2,1,0:T(8,128)S(1)} %fusion.63), channel_id=1, source_target_pairs={{4,0},{8,4},{12,8},{16,12},{20,16},{24,20},{28,24},{5,1},{9,5},{13... | collective-permute-start | bytes 786440 | tf_op jit(solution)/shard_map/ppermute | solution.py:52
  65.5 15.9 %collective-permute-start.3 = (bf16[4,256,256]{2,1,0:T(8,128)(2,1)S(1)}, bf16[4,256,256]{2,1,0:T(8,128)(2,1)S(1)}, u32[]{:S(2)}, u32[]{:S(2)}) collective-permute-start(bf16[4,256,256]{2,1,0:T(8,128)(2,1)S(1)} %get-tuple-element.17), channel_id=1, source_target_pairs={{0,4},{4,0},{1,5},{5,1},{2,6},{6,2},{3,7},{7,3},{8,12},{12,8},{9,1... | collective-permute-start | bytes 1572872 | tf_op jit(solution)/shard_map/ppermute | solution.py:94
  65.6 22.7 %collective-permute-start.2 = (bf16[1,256,256]{2,1,0:T(8,128)(2,1)S(1)}, bf16[1,256,256]{2,1,0:T(8,128)(2,1)S(1)}, u32[]{:S(2)}, u32[]{:S(2)}) collective-permute-start(bf16[1,256,256]{2,1,0:T(8,128)(2,1)S(1)} %slice_select_fusion), channel_id=1, source_target_pairs={{4,8},{12,16},{20,24},{8,4},{16,12},{24,20},{5,9},{13,17},{21,25},... | collective-permute-start | bytes 393224 | tf_op jit(solution)/shard_map/ppermute | solution.py:124
  71.1 27.1 %all-to-all-start.1 = ((bf16[4,256,256]{2,0,1:T(4,128)(2,1)}), bf16[4,256,256]{2,0,1:T(4,128)(2,1)S(1)}, u32[]{:S(2)}, u32[]{:S(2)}) async-start(bf16[4,256,256]{2,0,1:T(4,128)(2,1)} %copy.23), calls=%async_computation.1 | async-start | bytes 1048576 | tf_op jit(solution)/shard_map/all_to_all | solution.py:92
  74.6 62.1 %reduce-scatter.2.cloned.1.call-start = ((), (), s32[]{:S(2)}) async-start(), calls=%async_computation.6 | async-start | bytes 2949120 | tf_op jit(solution)/shard_map/reduce_scatter | solution.py:118
  74.9 2.1 %copy-start = (bf16[10,256,512]{1,2,0:T(8,128)(2,1)S(1)}, bf16[10,256,512]{1,2,0:T(8,128)(2,1)}, u32[]{:S(2)}) copy-start(bf16[10,256,512]{1,2,0:T(8,128)(2,1)} %all-gather.5.cloned.1.call-done) | copy-start | bytes 7864324
  98.2 29.3 %all-to-all-start.2 = ((bf16[4,256,1024]{2,1,0:T(8,128)(2,1)}), bf16[4,256,1024]{2,1,0:T(8,128)(2,1)S(1)}, u32[]{:S(2)}, u32[]{:S(2)}) async-start(bf16[4,256,1024]{2,1,0:T(8,128)(2,1)} %bitcast.227), calls=%async_computation.2 | async-start | bytes 4194304 | tf_op jit(solution)/shard_map/all_to_all | solution.py:143
Sparse Core Ops, SparseCore 0:
  9.6 29.6 all-gather.2
  41.3 25.5 all-gather.4
  88.4 48.2 reduce-scatter.1

commit v13 on v10

--- a/solution.py
+++ b/solution.py
@@ -87,7 +87,6 @@
     unit = conv_wide * inverse_rms
     normed_filters = unit.astype(jnp.bfloat16)
     grad_conv = (inverse_rms * (upstream - unit * mean_gu)).astype(jnp.bfloat16)
-    normed = lax.all_to_all(normed_filters, "chan", split_axis=1, concat_axis=2, tiled=True)
 
     sent_grad = lax.ppermute(grad_conv, "lo", [(0, 1), (1, 0)])
     img_block = jnp.pad(img_block, ((0, 0), (1, 1), (0, 0)))
@@ -139,6 +138,8 @@
     group = all_chans // chans
     split = input_term.astype(jnp.bfloat16).reshape(chans, group, height * breadth)
     received = lax.all_to_all(split, "chan", split_axis=0, concat_axis=0, tiled=True)
+    normed_late, _ = lax.optimization_barrier((normed_filters, split))
+    normed = lax.all_to_all(normed_late, "chan", split_axis=1, concat_axis=2, tiled=True)
     summed = jnp.sum(received.astype(jnp.float32), axis=0)
     grad_input = jnp.transpose(summed).astype(jnp.bfloat16).reshape(height, breadth, group)
     return (normed, grad_input, grad_weight)

time: 147 us -> 150 us (1.020)
  blocking collectives: 5.75 us -> 17 us
  starting transfers between devices: 27.7 us -> 24.2 us
  waiting for transfers between devices: 44.5 us -> 41.3 us
    all_to_all x0 -> x1, blocking collectives: none -> 11.2 us  [on_device(): lax.all_to_all(normed_late, 'chan', split_axis=1, concat_axis=2, tiled=True)]
    reduce_scatter x1, waiting for transfers between devices: 7.82 us -> 0.01 us  [on_device(): lax.psum_scatter(stacked.astype(jnp.bfloat16), 'hi', scatter_dimension=2,...]
    ppermute x1, waiting for transfers between devices: 0.31 us -> 5.03 us  [on_device(): sent_grad = lax.ppermute(grad_conv, 'lo', [(0, 1), (1, 0)])]
    all_to_all x1 -> x0, starting transfers between devices: 3.47 us -> none  [on_device(): lax.all_to_all(normed_filters, 'chan', split_axis=1, concat_axis=2, tiled...]
  transfers between devices with their start and end apart: 13 -> 12, of which waited for: 8 -> 7; matrix products, arithmetic and copies ran while one was open for 34% -> 33% of each run, Pallas kernels for 0% -> 0%
where the time goes in v13:
time: 150 us; the launch traced here: 149 us
  waiting for transfers between devices  41.3 us (28%)
  matrix products  29 us (19%)
  starting transfers between devices  24.2 us (16%)
  blocking collectives  17 us (11%)
  local copies, waits for them, and re-layouts  15.4 us (10%)
  between operations  14.3 us (10%)
  other arithmetic  7.47 us (5%)
    all_to_all x1, waiting for transfers between devices, on_device(): lax.all_to_all(split, 'chan', split_axis=0, concat_axis=0, tiled=True)  24.1 us
    unnamed x20, local copies, waits for them, and re-layouts  12.5 us
    all_to_all x1, blocking collectives, on_device(): lax.all_to_all(normed_late, 'chan', split_axis=1, concat_axis=2, tiled=True)  11.2 us
    dot_general x18, matrix products, pair_part(): lax.dot_general(weight_window, flat, (((0,), (0,)), ((), ())), preferred_...  10.9 us
    dot_general x1, matrix products, on_device(): lax.dot_general(by_filter, columns, (((0,), (1,)), ((), ())), preferred_e...  8.96 us
    dot_general x4, matrix products, taps(): out = jnp.dot(flat, by_row[a], preferred_element_type=jnp.float32)  7.27 us
    ppermute x2, starting transfers between devices, shift_rows(): return lax.ppermute(rows, SLAB, pairs)  5.85 us
    psum x1, blocking collectives, on_device(): totals = lax.psum(partial, 'chan')  5.75 us
  transfers between devices with their start and end apart: 12, of which 7 were waited for; matrix products, arithmetic and copies ran while one was open for 33% of the time, Pallas kernels for 0%

profile of v13, /device:TPU:4, one launch (start us, length us, event | category | flops | bytes accessed | tf_op | source)
XLA Modules:
  0.0 148.7 jit_solution(593339235598548484)
XLA Ops:
  9.2 3.4 %collective-permute-start.4 = (bf16[1,256,256]{1,2,0:T(8,128)(2,1)S(1)}, bf16[1,256,256]{1,2,0:T(8,128)(2,1)S(1)}, u32[]{:S(2)}, u32[]{:S(2)}) collective-permute-start(bf16[1,256,256]{1,2,0:T(8,128)(2,1)S(1)} %get-tuple-element.19), channel_id=1, source_target_pairs={{0,4},{4,8},{8,12},{12,16},{16,20},{20,24},{24,28},{1,5},{5,9},{9,... | collective-permute-start | bytes 393224 | tf_op jit(solution)/shard_map/ppermute | solution.py:16
  12.6 2.4 %collective-permute-start.5 = (bf16[1,256,256]{1,2,0:T(8,128)(2,1)S(1)}, bf16[1,256,256]{1,2,0:T(8,128)(2,1)S(1)}, u32[]{:S(2)}, u32[]{:S(2)}) collective-permute-start(bf16[1,256,256]{1,2,0:T(8,128)(2,1)S(1)} %get-tuple-element.20), channel_id=1, source_target_pairs={{4,0},{8,4},{12,8},{16,12},{20,16},{24,20},{28,24},{5,1},{9,5},{13... | collective-permute-start | bytes 393224 | tf_op jit(solution)/shard_map/ppermute | solution.py:16
  16.3 4.1 %collective-permute-done.5 = bf16[1,256,256]{1,2,0:T(8,128)(2,1)S(1)} collective-permute-done((bf16[1,256,256]{1,2,0:T(8,128)(2,1)S(1)}, bf16[1,256,256]{1,2,0:T(8,128)(2,1)S(1)}, u32[]{:S(2)}, u32[]{:S(2)}) %collective-permute-start.5) | collective-permute-done | bytes 131104 | tf_op jit(solution)/shard_map/ppermute | solution.py:16
  21.4 1.6 %reshape.219 = bf16[4,2,32768]{2,1,0:T(2,128)(2,1)} reshape(bf16[1024,4,64]{2,1,0:T(4,128)(2,1)S(1)} %bitcast.227) | data formatting | bytes 1048576
  22.9 3.5 %all-to-all-start = ((bf16[4,2,32768]{2,1,0:T(2,128)(2,1)}), bf16[4,2,32768]{2,1,0:T(2,128)(2,1)S(1)}, u32[]{:S(2)}, u32[]{:S(2)}) async-start(bf16[4,2,32768]{2,1,0:T(2,128)(2,1)} %reshape.219), calls=%async_computation | async-start | bytes 1048576 | tf_op jit(solution)/shard_map/all_to_all | solution.py:40
  28.5 6.7 %copy.17 = bf16[3,3,1024,256]{2,3,1,0:T(8,128)(2,1)} copy(bf16[3,3,1024,256]{3,2,1,0:T(8,128)(2,1)} %param.4) | data formatting | bytes 9437184 | tf_op args[1]
  35.2 2.3 %all-to-all-done = bf16[4,2,32768]{2,1,0:T(2,128)(2,1)S(1)} async-done(((bf16[4,2,32768]{2,1,0:T(2,128)(2,1)}), bf16[4,2,32768]{2,1,0:T(2,128)(2,1)S(1)}, u32[]{:S(2)}, u32[]{:S(2)}) %all-to-all-start) | async-done | bytes 524320 | tf_op jit(solution)/shard_map/all_to_all | solution.py:40
  38.9 2.3 %fusion.14 = f32[1,256,3,256]{3,1,2,0:T(8,128)S(1)} fusion(bf16[3,1024,3,256]{1,3,2,0:T(8,128)(2,1)} %bitcast.221, bf16[4,256,1024]{2,1,0:T(8,128)(2,1)} %all-gather.3.cloned.1.call-done), kind=kOutput, calls=%fused_computation.44 | convolution fusion | flops 402653184 | bytes 2883584 | tf_op jit(solution)/shard_map/dot_general | solution.py:48
  41.3 3.5 %collective-permute-start = (f32[1,256,256]{2,1,0:T(8,128)S(1)}, f32[1,256,256]{2,1,0:T(8,128)S(1)}, u32[]{:S(2)}, u32[]{:S(2)}) collective-permute-start(f32[1,256,256]{2,1,0:T(8,128)S(1)} %fusion.60), channel_id=1, source_target_pairs={{0,4},{4,8},{8,12},{12,16},{16,20},{20,24},{24,28},{1,5},{5,9},{9,... | collective-permute-start | bytes 786440 | tf_op jit(solution)/shard_map/ppermute | solution.py:51
  44.8 1.7 %fusion.17 = f32[1,256,3,256]{3,1,2,0:T(8,128)S(1)} fusion(bf16[3,1024,3,256]{1,3,2,0:T(8,128)(2,1)S(1)} %bitcast.223, bf16[4,256,1024]{2,1,0:T(8,128)(2,1)} %all-gather.3.cloned.1.call-done), kind=kOutput, calls=%fused_computation.45 | convolution fusion | flops 402653184 | bytes 2883584 | tf_op jit(solution)/shard_map/dot_general | solution.py:48
  46.6 2.4 %collective-permute-start.1 = (f32[1,256,256]{2,1,0:T(8,128)S(1)}, f32[1,256,256]{2,1,0:T(8,128)S(1)}, u32[]{:S(2)}, u32[]{:S(2)}) collective-permute-start(f32[1,256,256]{2,1,0:T(8,128)S(1)} %fusion.63), channel_id=1, source_target_pairs={{4,0},{8,4},{12,8},{16,12},{20,16},{24,20},{28,24},{5,1},{9,5},{13... | collective-permute-start | bytes 786440 | tf_op jit(solution)/shard_map/ppermute | solution.py:52
  50.5 1.8 %fusion = f32[4,256,3,256]{3,1,2,0:T(8,128)S(1)} fusion(bf16[4,256,1024]{2,1,0:T(8,128)(2,1)S(1)} %copy-done.2, bf16[3,1024,3,256]{1,3,2,0:T(8,128)(2,1)S(1)} %bitcast.225), kind=kOutput, calls=%fused_computation.24 | convolution fusion | flops 1610612736 | bytes 6815744 | tf_op jit(solution)/shard_map/dot_general | solution.py:48
  52.3 1.8 %pad_add_fusion = f32[4,256,3,256]{3,1,2,0:T(8,128)S(1)} fusion(f32[3,256,3,256]{3,1,2,0:T(8,128)S(1)} %fusion.3, f32[4,256,3,256]{3,1,2,0:T(8,128)S(1)} %fusion, bf16[4,256,1024]{2,1,0:T(8,128)(2,1)S(1)} %copy-done.2, bf16[3,1024,3,256]{1,3,2,0:T(8,128)(2,1)S(1)} %bitcast.226), kind=kOutput, calls=%fused_computation.19 | convolution fusion | flops 1209532416 | bytes 11796480 | tf_op jit(solution)/shard_map/jit(_pad)/pad | solution.py:71
  54.2 3.1 %collective-permute-done.1 = f32[1,256,256]{2,1,0:T(8,128)S(1)} collective-permute-done((f32[1,256,256]{2,1,0:T(8,128)S(1)}, f32[1,256,256]{2,1,0:T(8,128)S(1)}, u32[]{:S(2)}, u32[]{:S(2)}) %collective-permute-start.1) | collective-permute-done | bytes 262176 | tf_op jit(solution)/shard_map/ppermute | solution.py:52
  58.1 5.8 %psum.7 = f32[4,256,2]{1,0,2:T(4,128)S(1)} all-reduce(f32[4,256,2]{1,0,2:T(4,128)S(1)} %pad_maximum_fusion.3), channel_id=1, replica_groups=mesh['hi'=4,'lo'=2,'chan'=4] {'chan'}, use_global_device_ids=true, to_apply=%region_2.3 | all-reduce | flops 2048 | bytes 16384 | tf_op jit(solution)/shard_map/psum | solution.py:84
  64.6 4.8 %collective-permute-start.2 = (bf16[1,256,256]{2,1,0:T(8,128)(2,1)S(1)}, bf16[1,256,256]{2,1,0:T(8,128)(2,1)S(1)}, u32[]{:S(2)}, u32[]{:S(2)}) collective-permute-start(bf16[1,256,256]{2,1,0:T(8,128)(2,1)S(1)} %slice_select_fusion), channel_id=1, source_target_pairs={{4,8},{12,16},{20,24},{8,4},{16,12},{24,20},{5,9},{13,17},{21,25},... | collective-permute-start | bytes 393224 | tf_op jit(solution)/shard_map/ppermute | solution.py:121
  69.4 1.9 %fusion.39 = f32[9,512,256]{2,1,0:T(8,128)S(1)} fusion(bf16[4,256,256]{2,1,0:T(8,128)(2,1)S(1)} %get-tuple-element.17, s32[]{:T(128)S(6)} %select_n.57, bf16[10,256,512]{1,2,0:T(8,128)(2,1)} %all-gather.5.cloned.1.call-done), kind=kOutput, calls=%fused_computation.83 | convolution fusion | flops 268435456 | bytes 3670020 | tf_op jit(solution)/shard_map/dot_general | solution.py:103
  75.7 5.0 %collective-permute-done.3 = bf16[4,256,256]{2,1,0:T(8,128)(2,1)S(1)} collective-permute-done((bf16[4,256,256]{2,1,0:T(8,128)(2,1)S(1)}, bf16[4,256,256]{2,1,0:T(8,128)(2,1)S(1)}, u32[]{:S(2)}, u32[]{:S(2)}) %collective-permute-start.3) | collective-permute-done | bytes 524320 | tf_op jit(solution)/shard_map/ppermute | solution.py:91
  85.6 2.1 %add_convert_fusion = bf16[9,512,256]{2,1,0:T(8,128)(2,1)} fusion(f32[9,512,256]{2,1,0:T(8,128)S(1)} %fusion.31, f32[9,512,256]{2,1,0:T(8,128)S(1)} %fusion.22), kind=kLoop, calls=%fused_computation.18 | loop fusion | flops 2359296 | bytes 11796480 | tf_op jit(solution)/shard_map/convert_element_type | solution.py:116
  88.6 9.0 %convolution_convert_fusion = bf16[1024,1024]{0,1:T(8,128)(2,1)} fusion(bf16[1024,2304]{1,0:T(8,128)(2,1)S(1)} %bitcast.238, bf16[2304,1024]{1,0:T(8,128)(2,1)} %bitcast.222), kind=kOutput, calls=%fused_computation.26 | convolution fusion | flops 4832886784 | bytes 11534336 | tf_op jit(solution)/shard_map/dot_general | solution.py:135
  98.0 11.2 %all_to_all.32 = bf16[4,256,256]{2,0,1:T(4,128)(2,1)S(1)} all-to-all(bf16[4,256,256]{2,0,1:T(4,128)(2,1)S(1)} %copy.25), channel_id=1, replica_groups=mesh['hi'=4,'lo'=2,'chan'=4] {'chan'}, dimensions={1} | all-to-all | bytes 1048576 | tf_op jit(solution)/shard_map/all_to_all | solution.py:142
  109.2 3.6 %all-to-all-start.2 = ((bf16[4,256,1024]{2,1,0:T(8,128)(2,1)}), bf16[4,256,1024]{2,1,0:T(8,128)(2,1)S(1)}, u32[]{:S(2)}, u32[]{:S(2)}) async-start(bf16[4,256,1024]{2,1,0:T(8,128)(2,1)} %bitcast.231), calls=%async_computation.2 | async-start | bytes 4194304 | tf_op jit(solution)/shard_map/all_to_all | solution.py:140
  114.4 24.1 %all-to-all-done.2 = bf16[4,256,1024]{2,1,0:T(8,128)(2,1)S(1)} async-done(((bf16[4,256,1024]{2,1,0:T(8,128)(2,1)}), bf16[4,256,1024]{2,1,0:T(8,128)(2,1)S(1)}, u32[]{:S(2)}, u32[]{:S(2)}) %all-to-all-start.2) | async-done | bytes 2097184 | tf_op jit(solution)/shard_map/all_to_all | solution.py:140
  139.9 2.2 %convert_element_type.84 = f32[3,3,128,256]{3,2,1,0:T(8,128)} convert(bf16[3,3,128,256]{3,2,1,0:T(8,128)(2,1)} %reduce-scatter.2.cloned.1.call-done) | non-fusion elementwise | flops 294912 | bytes 1769472 | tf_op jit(solution)/shard_map/convert_element_type | solution.py:117
  (78 shorter events, 24.2 us)
Async XLA Ops:
  7.2 13.5 %copy-start.3 = (bf16[4,64,1024]{2,1,0:T(8,128)(2,1)S(1)}, bf16[4,64,1024]{2,1,0:T(8,128)(2,1)}, u32[]{:S(2)}) copy-start(bf16[4,64,1024]{2,1,0:T(8,128)(2,1)} %param.5) | copy-start | bytes 1572868
  7.2 31.7 %all-gather.3.cloned.1.call-start = ((), (), s32[]{:S(2)}) async-start(), calls=%async_computation.4 | async-start | bytes 2621440 | tf_op jit(solution)/shard_map/all_gather | solution.py:41
  9.2 7.1 %collective-permute-start.4 = (bf16[1,256,256]{1,2,0:T(8,128)(2,1)S(1)}, bf16[1,256,256]{1,2,0:T(8,128)(2,1)S(1)}, u32[]{:S(2)}, u32[]{:S(2)}) collective-permute-start(bf16[1,256,256]{1,2,0:T(8,128)(2,1)S(1)} %get-tuple-element.19), channel_id=1, source_target_pairs={{0,4},{4,8},{8,12},{12,16},{16,20},{20,24},{24,28},{1,5},{5,9},{9,... | collective-permute-start | bytes 393224 | tf_op jit(solution)/shard_map/ppermute | solution.py:16
  12.6 7.8 %collective-permute-start.5 = (bf16[1,256,256]{1,2,0:T(8,128)(2,1)S(1)}, bf16[1,256,256]{1,2,0:T(8,128)(2,1)S(1)}, u32[]{:S(2)}, u32[]{:S(2)}) collective-permute-start(bf16[1,256,256]{1,2,0:T(8,128)(2,1)S(1)} %get-tuple-element.20), channel_id=1, source_target_pairs={{4,0},{8,4},{12,8},{16,12},{20,16},{24,20},{28,24},{5,1},{9,5},{13... | collective-permute-start | bytes 393224 | tf_op jit(solution)/shard_map/ppermute | solution.py:16
  20.6 6.7 %collective-permute-start.6 = (bf16[4,256,128]{1,2,0:T(8,128)(2,1)S(1)}, bf16[4,256,128]{1,2,0:T(8,128)(2,1)S(1)}, u32[]{:S(2)}, u32[]{:S(2)}) collective-permute-start(bf16[4,256,128]{1,2,0:T(8,128)(2,1)S(1)} %dynamic-slice_bitcast_fusion.1), channel_id=1, source_target_pairs={{0,4},{4,0},{1,5},{5,1},{2,6},{6,2},{3,7},{7,3},{8,12},{12,8},{9,1... | collective-permute-start | bytes 786440 | tf_op jit(solution)/shard_map/ppermute | solution.py:63
  22.9 14.5 %all-to-all-start = ((bf16[4,2,32768]{2,1,0:T(2,128)(2,1)}), bf16[4,2,32768]{2,1,0:T(2,128)(2,1)S(1)}, u32[]{:S(2)}, u32[]{:S(2)}) async-start(bf16[4,2,32768]{2,1,0:T(2,128)(2,1)} %reshape.219), calls=%async_computation | async-start | bytes 1048576 | tf_op jit(solution)/shard_map/all_to_all | solution.py:40
  26.4 43.0 %all-gather.5.cloned.1.call-start = ((), (), s32[]{:S(2)}) async-start(), calls=%async_computation.5 | async-start | bytes 3276800 | tf_op jit(solution)/shard_map/all_gather | solution.py:68
  28.4 111.5 %reduce-scatter.2.cloned.1.call-start = ((), (), s32[]{:S(2)}) async-start(), calls=%async_computation.6 | async-start | bytes 2949120 | tf_op jit(solution)/shard_map/reduce_scatter | solution.py:115
  38.9 5.9 %copy-start.1 = (bf16[3,3,1024,256]{2,3,1,0:T(8,128)(2,1)S(1)}, bf16[3,3,1024,256]{2,3,1,0:T(8,128)(2,1)}, u32[]{:S(2)}) copy-start(bf16[3,3,1024,256]{2,3,1,0:T(8,128)(2,1)} %copy.17) | copy-start | bytes 14155780
  38.9 10.2 %copy-start.2 = (bf16[4,256,1024]{2,1,0:T(8,128)(2,1)S(1)}, bf16[4,256,1024]{2,1,0:T(8,128)(2,1)}, u32[]{:S(2)}) copy-start(bf16[4,256,1024]{2,1,0:T(8,128)(2,1)} %all-gather.3.cloned.1.call-done) | copy-start | bytes 6291460
  41.3 12.9 %collective-permute-start = (f32[1,256,256]{2,1,0:T(8,128)S(1)}, f32[1,256,256]{2,1,0:T(8,128)S(1)}, u32[]{:S(2)}, u32[]{:S(2)}) collective-permute-start(f32[1,256,256]{2,1,0:T(8,128)S(1)} %fusion.60), channel_id=1, source_target_pairs={{0,4},{4,8},{8,12},{12,16},{16,20},{20,24},{24,28},{1,5},{5,9},{9,... | collective-permute-start | bytes 786440 | tf_op jit(solution)/shard_map/ppermute | solution.py:51
  46.6 10.6 %collective-permute-start.1 = (f32[1,256,256]{2,1,0:T(8,128)S(1)}, f32[1,256,256]{2,1,0:T(8,128)S(1)}, u32[]{:S(2)}, u32[]{:S(2)}) collective-permute-start(f32[1,256,256]{2,1,0:T(8,128)S(1)} %fusion.63), channel_id=1, source_target_pairs={{4,0},{8,4},{12,8},{16,12},{20,16},{24,20},{28,24},{5,1},{9,5},{13... | collective-permute-start | bytes 786440 | tf_op jit(solution)/shard_map/ppermute | solution.py:52
  64.2 16.5 %collective-permute-start.3 = (bf16[4,256,256]{2,1,0:T(8,128)(2,1)S(1)}, bf16[4,256,256]{2,1,0:T(8,128)(2,1)S(1)}, u32[]{:S(2)}, u32[]{:S(2)}) collective-permute-start(bf16[4,256,256]{2,1,0:T(8,128)(2,1)S(1)} %get-tuple-element.17), channel_id=1, source_target_pairs={{0,4},{4,0},{1,5},{5,1},{2,6},{6,2},{3,7},{7,3},{8,12},{12,8},{9,1... | collective-permute-start | bytes 1572872 | tf_op jit(solution)/shard_map/ppermute | solution.py:91
  64.6 23.1 %collective-permute-start.2 = (bf16[1,256,256]{2,1,0:T(8,128)(2,1)S(1)}, bf16[1,256,256]{2,1,0:T(8,128)(2,1)S(1)}, u32[]{:S(2)}, u32[]{:S(2)}) collective-permute-start(bf16[1,256,256]{2,1,0:T(8,128)(2,1)S(1)} %slice_select_fusion), channel_id=1, source_target_pairs={{4,8},{12,16},{20,24},{8,4},{16,12},{24,20},{5,9},{13,17},{21,25},... | collective-permute-start | bytes 393224 | tf_op jit(solution)/shard_map/ppermute | solution.py:121
  69.4 2.1 %copy-start = (bf16[10,256,512]{1,2,0:T(8,128)(2,1)S(1)}, bf16[10,256,512]{1,2,0:T(8,128)(2,1)}, u32[]{:S(2)}) copy-start(bf16[10,256,512]{1,2,0:T(8,128)(2,1)} %all-gather.5.cloned.1.call-done) | copy-start | bytes 7864324
  109.2 29.3 %all-to-all-start.2 = ((bf16[4,256,1024]{2,1,0:T(8,128)(2,1)}), bf16[4,256,1024]{2,1,0:T(8,128)(2,1)S(1)}, u32[]{:S(2)}, u32[]{:S(2)}) async-start(bf16[4,256,1024]{2,1,0:T(8,128)(2,1)} %bitcast.231), calls=%async_computation.2 | async-start | bytes 4194304 | tf_op jit(solution)/shard_map/all_to_all | solution.py:140
Sparse Core Ops, SparseCore 0:
  9.6 26.3 all-gather.2
  38.1 25.5 all-gather.4
  87.8 47.9 reduce-scatter.1

commit v14 on v11

--- a/solution.py
+++ b/solution.py
@@ -43,9 +43,7 @@
     def taps(rows, a):
         count = rows.shape[0]
         flat = rows.reshape(count * breadth, all_chans)
-        out = jnp.stack(
-            [jnp.dot(flat, weight[a, b], preferred_element_type=jnp.float32) for b in range(3)], axis=1
-        )
+        out = lax.dot_general(flat, weight[a], (((1,), (1,)), ((), ())), preferred_element_type=jnp.float32)
         return out.reshape(count, breadth, 3, local_filters)
 
     to_next = lax.ppermute(shift_sum(taps(gathered[-1:], 0)), SLAB, [(i, i + 1) for i in range(lax.axis_size(SLAB) - 1)])

time: 157 us -> 153 us (0.975)
  matrix products: 30.7 us -> 28 us
    ppermute x1, waiting for transfers between devices: 8.49 us -> 2.36 us  [on_device(): lax.ppermute(local_subset(send_rows, 1 - lo), 'lo', [(0, 1), (1, 0)])]
    dot_general x15 -> x4, matrix products: 13.5 us -> 8.95 us  [taps(): lax.dot_general(flat, weight[a], (((1,), (1,)), ((), ())), preferred_elem...]
    ppermute x2, waiting for transfers between devices: 0.01 us -> 4.08 us  [shift_rows(): return lax.ppermute(rows, SLAB, pairs)]
    all_to_all x1, waiting for transfers between devices: 4.57 us -> 7.72 us  [on_device(): lax.all_to_all(grad_out, 'chan', split_axis=2, concat_axis=1, tiled=True)]
    pad x0 -> x1, matrix products: none -> 1.79 us  [on_device(): jnp.pad(taps(gathered[:-1], 0), ((1, 0), (0, 0), (0, 0), (0, 0)))]
    unnamed x21 -> x23, local copies, waits for them, and re-layouts: 8.7 us -> 7.71 us
  transfers between devices with their start and end apart: 13 -> 13, of which waited for: 7 -> 8; matrix products, arithmetic and copies ran while one was open for 34% -> 32% of each run, Pallas kernels for 0% -> 0%
where the time goes in v14:
time: 153 us; the launch traced here: 151 us
  waiting for transfers between devices  47.1 us (31%)
  starting transfers between devices  29.6 us (19%)
  matrix products  28 us (18%)
  local copies, waits for them, and re-layouts  18.3 us (12%)
  between operations  14.3 us (9%)
  other arithmetic  7.48 us (5%)
  blocking collectives  6.15 us (4%)
    all_to_all x1, waiting for transfers between devices, on_device(): lax.all_to_all(split, 'chan', split_axis=0, concat_axis=0, tiled=True)  24.1 us
    dot_general x18, matrix products, pair_part(): lax.dot_general(weight_window, flat, (((0,), (0,)), ((), ())), preferred_...  10.9 us
    dot_general x4, matrix products, taps(): lax.dot_general(flat, weight[a], (((1,), (1,)), ((), ())), preferred_elem...  8.95 us
    all_to_all x1, waiting for transfers between devices, on_device(): lax.all_to_all(grad_out, 'chan', split_axis=2, concat_axis=1, tiled=True)  7.72 us
    unnamed x23, local copies, waits for them, and re-layouts  7.71 us
    optimization_barrier x1, local copies, waits for them, and re-layouts, on_device(): weight_late, _ = lax.optimization_barrier((weight, stacked))  6.9 us
    ppermute x2, starting transfers between devices, shift_rows(): return lax.ppermute(rows, SLAB, pairs)  6.74 us
    dot_general x1, matrix products, on_device(): lax.dot_general(by_filter, columns, (((0,), (1,)), ((), ())), preferred_e...  6.37 us
  transfers between devices with their start and end apart: 13, of which 8 were waited for; matrix products, arithmetic and copies ran while one was open for 32% of the time, Pallas kernels for 0%

profile of v14, /device:TPU:4, one launch (start us, length us, event | category | flops | bytes accessed | tf_op | source)
XLA Modules:
  0.0 151.0 jit_solution(15376678448180559600)
XLA Ops:
  9.2 1.9 %collective-permute-start.4 = (bf16[1,256,256]{1,2,0:T(8,128)(2,1)S(1)}, bf16[1,256,256]{1,2,0:T(8,128)(2,1)S(1)}, u32[]{:S(2)}, u32[]{:S(2)}) collective-permute-start(bf16[1,256,256]{1,2,0:T(8,128)(2,1)S(1)} %get-tuple-element.20), channel_id=1, source_target_pairs={{4,0},{8,4},{12,8},{16,12},{20,16},{24,20},{28,24},{5,1},{9,5},{13... | collective-permute-start | bytes 393224 | tf_op jit(solution)/shard_map/ppermute | solution.py:16
  11.1 4.8 %collective-permute-start.3 = (bf16[1,256,256]{1,2,0:T(8,128)(2,1)S(1)}, bf16[1,256,256]{1,2,0:T(8,128)(2,1)S(1)}, u32[]{:S(2)}, u32[]{:S(2)}) collective-permute-start(bf16[1,256,256]{1,2,0:T(8,128)(2,1)S(1)} %get-tuple-element.19), channel_id=1, source_target_pairs={{0,4},{4,8},{8,12},{12,16},{16,20},{20,24},{24,28},{1,5},{5,9},{9,... | collective-permute-start | bytes 393224 | tf_op jit(solution)/shard_map/ppermute | solution.py:16
  17.3 2.7 %collective-permute-done.3 = bf16[1,256,256]{1,2,0:T(8,128)(2,1)S(1)} collective-permute-done((bf16[1,256,256]{1,2,0:T(8,128)(2,1)S(1)}, bf16[1,256,256]{1,2,0:T(8,128)(2,1)S(1)}, u32[]{:S(2)}, u32[]{:S(2)}) %collective-permute-start.3) | collective-permute-done | bytes 131104 | tf_op jit(solution)/shard_map/ppermute | solution.py:16
  22.6 3.5 %all-to-all-start = ((bf16[4,2,32768]{2,1,0:T(2,128)(2,1)}), bf16[4,2,32768]{2,1,0:T(2,128)(2,1)S(1)}, u32[]{:S(2)}, u32[]{:S(2)}) async-start(bf16[4,2,32768]{2,1,0:T(2,128)(2,1)} %reshape.207), calls=%async_computation | async-start | bytes 1048576 | tf_op jit(solution)/shard_map/all_to_all | solution.py:40
  26.1 2.4 %collective-permute-done.5 = bf16[4,256,128]{1,2,0:T(8,128)(2,1)S(1)} collective-permute-done((bf16[4,256,128]{1,2,0:T(8,128)(2,1)S(1)}, bf16[4,256,128]{1,2,0:T(8,128)(2,1)S(1)}, u32[]{:S(2)}, u32[]{:S(2)}) %collective-permute-start.5) | collective-permute-done | bytes 262176 | tf_op jit(solution)/shard_map/ppermute | solution.py:61
  29.7 7.7 %all-to-all-done = bf16[4,2,32768]{2,1,0:T(2,128)(2,1)S(1)} async-done(((bf16[4,2,32768]{2,1,0:T(2,128)(2,1)}), bf16[4,2,32768]{2,1,0:T(2,128)(2,1)S(1)}, u32[]{:S(2)}, u32[]{:S(2)}) %all-to-all-start) | async-done | bytes 524320 | tf_op jit(solution)/shard_map/all_to_all | solution.py:40
  38.9 2.3 %fusion.19 = f32[1,256,3,256]{3,1,2,0:T(8,128)S(1)} fusion(bf16[3,3,1024,256]{3,2,1,0:T(8,128)(2,1)} %param.4, bf16[4,256,1024]{2,1,0:T(8,128)(2,1)} %all-gather.3.cloned.1.call-done), kind=kOutput, calls=%fused_computation.45 | convolution fusion | flops 402653184 | bytes 2883584 | tf_op jit(solution)/shard_map/dot_general | solution.py:46
  41.2 2.5 %collective-permute-start.1 = (f32[1,256,256]{2,1,0:T(8,128)S(1)}, f32[1,256,256]{2,1,0:T(8,128)S(1)}, u32[]{:S(2)}, u32[]{:S(2)}) collective-permute-start(f32[1,256,256]{2,1,0:T(8,128)S(1)} %fusion.65), channel_id=1, source_target_pairs={{4,0},{8,4},{12,8},{16,12},{20,16},{24,20},{28,24},{5,1},{9,5},{13... | collective-permute-start | bytes 786440 | tf_op jit(solution)/shard_map/ppermute | solution.py:50
  43.7 2.1 %fusion.16 = f32[1,256,3,256]{3,1,2,0:T(8,128)S(1)} fusion(bf16[3,3,1024,256]{3,2,1,0:T(8,128)(2,1)} %param.4, bf16[4,256,1024]{2,1,0:T(8,128)(2,1)S(1)} %copy-done.2), kind=kOutput, calls=%fused_computation.44 | convolution fusion | flops 402653184 | bytes 2883584 | tf_op jit(solution)/shard_map/dot_general | solution.py:46
  45.9 4.5 %collective-permute-start = (f32[1,256,256]{2,1,0:T(8,128)S(1)}, f32[1,256,256]{2,1,0:T(8,128)S(1)}, u32[]{:S(2)}, u32[]{:S(2)}) collective-permute-start(f32[1,256,256]{2,1,0:T(8,128)S(1)} %fusion.62), channel_id=1, source_target_pairs={{0,4},{4,8},{8,12},{12,16},{16,20},{20,24},{24,28},{1,5},{5,9},{9,... | collective-permute-start | bytes 786440 | tf_op jit(solution)/shard_map/ppermute | solution.py:49
  50.4 2.8 %fusion.3 = f32[3,256,3,256]{3,1,2,0:T(8,128)S(1)} fusion(bf16[4,256,1024]{2,1,0:T(8,128)(2,1)S(1)} %copy-done.2, bf16[3,3,1024,256]{3,2,1,0:T(8,128)(2,1)} %param.4), kind=kOutput, calls=%fused_computation.28 | convolution fusion | flops 1207959552 | bytes 5505024 | tf_op jit(solution)/shard_map/dot_general | solution.py:46
  55.1 1.8 %pad_add_fusion = f32[4,256,3,256]{3,1,2,0:T(8,128)S(1)} fusion(f32[3,256,3,256]{3,1,2,0:T(8,128)S(1)} %fusion.3, f32[4,256,3,256]{3,1,2,0:T(8,128)S(1)} %fusion, bf16[4,256,1024]{2,1,0:T(8,128)(2,1)S(1)} %copy-done.2, bf16[3,3,1024,256]{3,2,1,0:T(8,128)(2,1)S(1)} %bitcast.204), kind=kOutput, calls=%fused_computation.18 | convolution fusion | flops 1209532416 | bytes 11796480 | tf_op jit(solution)/shard_map/jit(_pad)/pad | solution.py:69
  58.7 6.2 %psum.7 = f32[4,256,2]{1,0,2:T(4,128)S(1)} all-reduce(f32[4,256,2]{1,0,2:T(4,128)S(1)} %pad_maximum_fusion.3), channel_id=1, replica_groups=mesh['hi'=4,'lo'=2,'chan'=4] {'chan'}, use_global_device_ids=true, to_apply=%region_2.3 | all-reduce | flops 2048 | bytes 16384 | tf_op jit(solution)/shard_map/psum | solution.py:82
  66.4 3.5 %all-to-all-start.1 = ((bf16[4,256,256]{2,0,1:T(4,128)(2,1)}), bf16[4,256,256]{2,0,1:T(4,128)(2,1)S(1)}, u32[]{:S(2)}, u32[]{:S(2)}) async-start(bf16[4,256,256]{2,0,1:T(4,128)(2,1)} %copy.18), calls=%async_computation.1 | async-start | bytes 1048576 | tf_op jit(solution)/shard_map/all_to_all | solution.py:88
  70.0 5.0 %collective-permute-start.6 = (bf16[1,256,256]{2,1,0:T(8,128)(2,1)S(1)}, bf16[1,256,256]{2,1,0:T(8,128)(2,1)S(1)}, u32[]{:S(2)}, u32[]{:S(2)}) collective-permute-start(bf16[1,256,256]{2,1,0:T(8,128)(2,1)S(1)} %slice_select_fusion), channel_id=1, source_target_pairs={{4,8},{12,16},{20,24},{8,4},{16,12},{24,20},{5,9},{13,17},{21,25},... | collective-permute-start | bytes 393224 | tf_op jit(solution)/shard_map/ppermute | solution.py:120
  75.1 1.9 %fusion.41 = f32[9,512,256]{2,1,0:T(8,128)S(1)} fusion(bf16[4,256,256]{2,1,0:T(8,128)(2,1)S(1)} %get-tuple-element.17, s32[]{:T(128)S(6)} %select_n.54, bf16[10,256,512]{1,2,0:T(8,128)(2,1)} %all-gather.5.cloned.1.call-done), kind=kOutput, calls=%fused_computation.83 | convolution fusion | flops 268435456 | bytes 3670020 | tf_op jit(solution)/shard_map/dot_general | solution.py:102
  81.4 5.6 %collective-permute-done.2 = bf16[4,256,256]{2,1,0:T(8,128)(2,1)S(1)} collective-permute-done((bf16[4,256,256]{2,1,0:T(8,128)(2,1)S(1)}, bf16[4,256,256]{2,1,0:T(8,128)(2,1)S(1)}, u32[]{:S(2)}, u32[]{:S(2)}) %collective-permute-start.2) | collective-permute-done | bytes 524320 | tf_op jit(solution)/shard_map/ppermute | solution.py:90
  91.8 2.1 %add.190 = bf16[9,512,256]{2,1,0:T(8,128)(2,1)} add(f32[9,512,256]{2,1,0:T(8,128)S(1)} %fusion.33, f32[9,512,256]{2,1,0:T(8,128)S(1)} %fusion.24) | non-fusion elementwise | flops 1179648 | bytes 11796480 | tf_op jit(solution)/shard_map/add | solution.py:113
  94.2 6.9 %copy.24 = bf16[3,3,1024,256]{2,3,1,0:T(8,128)(2,1)} copy(bf16[3,3,1024,256]{3,2,1,0:T(8,128)(2,1)} %param.4) | data formatting | bytes 9437184 | tf_op jit(solution)/shard_map/optimization_barrier | solution.py:133
  101.7 1.8 %copy-done.1 = bf16[3,3,1024,256]{2,3,1,0:T(8,128)(2,1)S(1)} copy-done((bf16[3,3,1024,256]{2,3,1,0:T(8,128)(2,1)S(1)}, bf16[3,3,1024,256]{2,3,1,0:T(8,128)(2,1)}, u32[]{:S(2)}) %copy-start.1) | copy-done | bytes 4718616
  103.6 6.4 %convolution_convert_fusion = bf16[1024,1024]{1,0:T(8,128)(2,1)} fusion(bf16[2304,1024]{1,0:T(8,128)(2,1)S(1)} %bitcast.205, bf16[1024,2304]{1,0:T(8,128)(2,1)S(1)} %bitcast.217), kind=kOutput, calls=%fused_computation.25 | convolution fusion | flops 4832886784 | bytes 11534336 | tf_op jit(solution)/shard_map/dot_general | solution.py:135
  109.9 3.6 %all-to-all-start.2 = ((bf16[4,256,1024]{2,1,0:T(8,128)(2,1)}), bf16[4,256,1024]{2,1,0:T(8,128)(2,1)S(1)}, u32[]{:S(2)}, u32[]{:S(2)}) async-start(bf16[4,256,1024]{2,1,0:T(8,128)(2,1)} %bitcast.210), calls=%async_computation.2 | async-start | bytes 4194304 | tf_op jit(solution)/shard_map/all_to_all | solution.py:140
  115.1 24.1 %all-to-all-done.2 = bf16[4,256,1024]{2,1,0:T(8,128)(2,1)S(1)} async-done(((bf16[4,256,1024]{2,1,0:T(8,128)(2,1)}), bf16[4,256,1024]{2,1,0:T(8,128)(2,1)S(1)}, u32[]{:S(2)}, u32[]{:S(2)}) %all-to-all-start.2) | async-done | bytes 2097184 | tf_op jit(solution)/shard_map/all_to_all | solution.py:140
  142.3 2.2 %convert_element_type.76 = f32[3,3,128,256]{3,2,1,0:T(8,128)} convert(bf16[3,3,128,256]{3,2,1,0:T(8,128)(2,1)} %reduce-scatter.2.cloned.1.call-done) | non-fusion elementwise | flops 294912 | bytes 1769472 | tf_op jit(solution)/shard_map/convert_element_type | solution.py:116
  (84 shorter events, 28.5 us)
Async XLA Ops:
  7.2 13.1 %copy-start.3 = (bf16[4,64,1024]{2,1,0:T(8,128)(2,1)S(1)}, bf16[4,64,1024]{2,1,0:T(8,128)(2,1)}, u32[]{:S(2)}) copy-start(bf16[4,64,1024]{2,1,0:T(8,128)(2,1)} %param.5) | copy-start | bytes 1572868
  7.2 31.7 %all-gather.3.cloned.1.call-start = ((), (), s32[]{:S(2)}) async-start(), calls=%async_computation.4 | async-start | bytes 2621440 | tf_op jit(solution)/shard_map/all_gather | solution.py:41
  9.2 8.1 %collective-permute-start.4 = (bf16[1,256,256]{1,2,0:T(8,128)(2,1)S(1)}, bf16[1,256,256]{1,2,0:T(8,128)(2,1)S(1)}, u32[]{:S(2)}, u32[]{:S(2)}) collective-permute-start(bf16[1,256,256]{1,2,0:T(8,128)(2,1)S(1)} %get-tuple-element.20), channel_id=1, source_target_pairs={{4,0},{8,4},{12,8},{16,12},{20,16},{24,20},{28,24},{5,1},{9,5},{13... | collective-permute-start | bytes 393224 | tf_op jit(solution)/shard_map/ppermute | solution.py:16
  11.1 8.9 %collective-permute-start.3 = (bf16[1,256,256]{1,2,0:T(8,128)(2,1)S(1)}, bf16[1,256,256]{1,2,0:T(8,128)(2,1)S(1)}, u32[]{:S(2)}, u32[]{:S(2)}) collective-permute-start(bf16[1,256,256]{1,2,0:T(8,128)(2,1)S(1)} %get-tuple-element.19), channel_id=1, source_target_pairs={{0,4},{4,8},{8,12},{12,16},{16,20},{20,24},{24,28},{1,5},{5,9},{9,... | collective-permute-start | bytes 393224 | tf_op jit(solution)/shard_map/ppermute | solution.py:16
  20.2 8.3 %collective-permute-start.5 = (bf16[4,256,128]{1,2,0:T(8,128)(2,1)S(1)}, bf16[4,256,128]{1,2,0:T(8,128)(2,1)S(1)}, u32[]{:S(2)}, u32[]{:S(2)}) collective-permute-start(bf16[4,256,128]{1,2,0:T(8,128)(2,1)S(1)} %dynamic-slice_bitcast_fusion.1), channel_id=1, source_target_pairs={{0,4},{4,0},{1,5},{5,1},{2,6},{6,2},{3,7},{7,3},{8,12},{12,8},{9,1... | collective-permute-start | bytes 786440 | tf_op jit(solution)/shard_map/ppermute | solution.py:61
  22.6 14.9 %all-to-all-start = ((bf16[4,2,32768]{2,1,0:T(2,128)(2,1)}), bf16[4,2,32768]{2,1,0:T(2,128)(2,1)S(1)}, u32[]{:S(2)}, u32[]{:S(2)}) async-start(bf16[4,2,32768]{2,1,0:T(2,128)(2,1)} %reshape.207), calls=%async_computation | async-start | bytes 1048576 | tf_op jit(solution)/shard_map/all_to_all | solution.py:40
  26.0 49.0 %all-gather.5.cloned.1.call-start = ((), (), s32[]{:S(2)}) async-start(), calls=%async_computation.5 | async-start | bytes 3276800 | tf_op jit(solution)/shard_map/all_gather | solution.py:66
  38.9 4.9 %copy-start.2 = (bf16[4,256,1024]{2,1,0:T(8,128)(2,1)S(1)}, bf16[4,256,1024]{2,1,0:T(8,128)(2,1)}, u32[]{:S(2)}) copy-start(bf16[4,256,1024]{2,1,0:T(8,128)(2,1)} %all-gather.3.cloned.1.call-done) | copy-start | bytes 6291460
  41.2 15.6 %collective-permute-start.1 = (f32[1,256,256]{2,1,0:T(8,128)S(1)}, f32[1,256,256]{2,1,0:T(8,128)S(1)}, u32[]{:S(2)}, u32[]{:S(2)}) collective-permute-start(f32[1,256,256]{2,1,0:T(8,128)S(1)} %fusion.65), channel_id=1, source_target_pairs={{4,0},{8,4},{12,8},{16,12},{20,16},{24,20},{28,24},{5,1},{9,5},{13... | collective-permute-start | bytes 786440 | tf_op jit(solution)/shard_map/ppermute | solution.py:50
  45.8 7.4 %slice-start = ((s8[4718592]{0:T(1024)(128)(4,1)}), s8[4194304]{0:T(1024)(128)(4,1)S(1)}, s32[]{:S(2)}) async-start(s8[4718592]{0:T(1024)(128)(4,1)} %bitcast.203), calls=%async_computation.7 | async-start | bytes 8388608
  45.9 7.3 %slice-start.1 = ((s8[4718592]{0:T(1024)(128)(4,1)}), s8[524288]{0:T(1024)(128)(4,1)S(1)}, s32[]{:S(2)}) async-start(s8[4718592]{0:T(1024)(128)(4,1)} %bitcast.203), calls=%async_computation.8 | async-start | bytes 1048576
  45.9 11.9 %collective-permute-start = (f32[1,256,256]{2,1,0:T(8,128)S(1)}, f32[1,256,256]{2,1,0:T(8,128)S(1)}, u32[]{:S(2)}, u32[]{:S(2)}) collective-permute-start(f32[1,256,256]{2,1,0:T(8,128)S(1)} %fusion.62), channel_id=1, source_target_pairs={{0,4},{4,8},{8,12},{12,16},{16,20},{20,24},{24,28},{1,5},{5,9},{9,... | collective-permute-start | bytes 786440 | tf_op jit(solution)/shard_map/ppermute | solution.py:49
  66.4 43.6 %all-to-all-start.1 = ((bf16[4,256,256]{2,0,1:T(4,128)(2,1)}), bf16[4,256,256]{2,0,1:T(4,128)(2,1)S(1)}, u32[]{:S(2)}, u32[]{:S(2)}) async-start(bf16[4,256,256]{2,0,1:T(4,128)(2,1)} %copy.18), calls=%async_computation.1 | async-start | bytes 1048576 | tf_op jit(solution)/shard_map/all_to_all | solution.py:88
  69.9 72.4 %reduce-scatter.2.cloned.1.call-start = ((), (), s32[]{:S(2)}) async-start(), calls=%async_computation.6 | async-start | bytes 2949120 | tf_op jit(solution)/shard_map/reduce_scatter | solution.py:114
  69.9 17.1 %collective-permute-start.2 = (bf16[4,256,256]{2,1,0:T(8,128)(2,1)S(1)}, bf16[4,256,256]{2,1,0:T(8,128)(2,1)S(1)}, u32[]{:S(2)}, u32[]{:S(2)}) collective-permute-start(bf16[4,256,256]{2,1,0:T(8,128)(2,1)S(1)} %get-tuple-element.17), channel_id=1, source_target_pairs={{0,4},{4,0},{1,5},{5,1},{2,6},{6,2},{3,7},{7,3},{8,12},{12,8},{9,1... | collective-permute-start | bytes 1572872 | tf_op jit(solution)/shard_map/ppermute | solution.py:90
  70.0 23.9 %collective-permute-start.6 = (bf16[1,256,256]{2,1,0:T(8,128)(2,1)S(1)}, bf16[1,256,256]{2,1,0:T(8,128)(2,1)S(1)}, u32[]{:S(2)}, u32[]{:S(2)}) collective-permute-start(bf16[1,256,256]{2,1,0:T(8,128)(2,1)S(1)} %slice_select_fusion), channel_id=1, source_target_pairs={{4,8},{12,16},{20,24},{8,4},{16,12},{24,20},{5,9},{13,17},{21,25},... | collective-permute-start | bytes 393224 | tf_op jit(solution)/shard_map/ppermute | solution.py:120
  75.1 2.1 %copy-start = (bf16[10,256,512]{1,2,0:T(8,128)(2,1)S(1)}, bf16[10,256,512]{1,2,0:T(8,128)(2,1)}, u32[]{:S(2)}) copy-start(bf16[10,256,512]{1,2,0:T(8,128)(2,1)} %all-gather.5.cloned.1.call-done) | copy-start | bytes 7864324
  101.2 2.3 %copy-start.1 = (bf16[3,3,1024,256]{2,3,1,0:T(8,128)(2,1)S(1)}, bf16[3,3,1024,256]{2,3,1,0:T(8,128)(2,1)}, u32[]{:S(2)}) copy-start(bf16[3,3,1024,256]{2,3,1,0:T(8,128)(2,1)} %copy.24) | copy-start | bytes 14155780
  109.9 29.3 %all-to-all-start.2 = ((bf16[4,256,1024]{2,1,0:T(8,128)(2,1)}), bf16[4,256,1024]{2,1,0:T(8,128)(2,1)S(1)}, u32[]{:S(2)}, u32[]{:S(2)}) async-start(bf16[4,256,1024]{2,1,0:T(8,128)(2,1)} %bitcast.210), calls=%async_computation.2 | async-start | bytes 4194304 | tf_op jit(solution)/shard_map/all_to_all | solution.py:140
Sparse Core Ops, SparseCore 0:
  9.6 26.7 all-gather.2
  38.4 24.8 all-gather.4
  94.0 48.2 reduce-scatter.1

commit v15 on v10

--- a/solution.py
+++ b/solution.py
@@ -112,10 +112,11 @@
 
     own_part = pair_part(grad_conv, height * lo)
     sent_grad, own_part = lax.optimization_barrier((sent_grad, own_part))
-    stacked = (own_part + pair_part(sent_grad, height * (1 - lo))).reshape(3, 3, width_w, local_filters)
-    grad_weight = lax.psum_scatter(
-        stacked.astype(jnp.bfloat16), "hi", scatter_dimension=2, tiled=True
-    ).astype(jnp.float32)
+    partner_part = pair_part(sent_grad, height * (1 - lo))
+    stacked = jnp.stack(
+        [(partner_part[t] + own_part[t]).astype(jnp.bfloat16) for t in range(9)]
+    ).reshape(3, 3, width_w, local_filters)
+    grad_weight = lax.psum_scatter(stacked, "hi", scatter_dimension=2, tiled=True).astype(jnp.float32)
 
     count = lax.axis_size(SLAB)
     crossing = [(s, s + 1) for s in range(1, count - 1, 2)] + [(s, s - 1) for s in range(2, count, 2)]

time: 147 us -> 147 us (level)
  local copies, waits for them, and re-layouts: 16.2 us -> 18.7 us
  waiting for transfers between devices: 44.5 us -> 42.5 us
    convert_element_type x2 -> x1, other arithmetic: 4.26 us -> 2.19 us  [on_device(): lax.psum_scatter(stacked, 'hi', scatter_dimension=2, tiled=True)]
    unnamed x20 -> x22, local copies, waits for them, and re-layouts: 12.5 us -> 14 us
  transfers between devices with their start and end apart: 13 -> 13, of which waited for: 8 -> 7; matrix products, arithmetic and copies ran while one was open for 34% -> 34% of each run, Pallas kernels for 0% -> 0%
where the time goes in v15:
time: 147 us; the launch traced here: 145 us
  waiting for transfers between devices  42.5 us (29%)
  matrix products  28.9 us (20%)
  starting transfers between devices  28 us (19%)
  local copies, waits for them, and re-layouts  18.7 us (13%)
  between operations  14.3 us (10%)
  other arithmetic  6.29 us (4%)
  blocking collectives  6.05 us (4%)
    all_to_all x1, waiting for transfers between devices, on_device(): lax.all_to_all(split, 'chan', split_axis=0, concat_axis=0, tiled=True)  23.1 us
    unnamed x22, local copies, waits for them, and re-layouts  14 us
    dot_general x18, matrix products, pair_part(): lax.dot_general(weight_window, flat, (((0,), (0,)), ((), ())), preferred_...  10.9 us
    dot_general x1, matrix products, on_device(): lax.dot_general(by_filter, columns, (((0,), (1,)), ((), ())), preferred_e...  8.97 us
    dot_general x4, matrix products, taps(): out = jnp.dot(flat, by_row[a], preferred_element_type=jnp.float32)  7.27 us
    reduce_scatter x1, waiting for transfers between devices, on_device(): lax.psum_scatter(stacked, 'hi', scatter_dimension=2, tiled=True)  7.22 us
    psum x1, blocking collectives, on_device(): totals = lax.psum(partial, 'chan')  6.05 us
    ppermute x2, starting transfers between devices, shift_rows(): return lax.ppermute(rows, SLAB, pairs)  5.85 us
  transfers between devices with their start and end apart: 13, of which 7 were waited for; matrix products, arithmetic and copies ran while one was open for 34% of the time, Pallas kernels for 0%

profile of v15, /device:TPU:4, one launch (start us, length us, event | category | flops | bytes accessed | tf_op | source)
XLA Modules:
  0.0 144.8 jit_solution(4526791331758244344)
XLA Ops:
  9.2 3.4 %collective-permute-start.4 = (bf16[1,256,256]{1,2,0:T(8,128)(2,1)S(1)}, bf16[1,256,256]{1,2,0:T(8,128)(2,1)S(1)}, u32[]{:S(2)}, u32[]{:S(2)}) collective-permute-start(bf16[1,256,256]{1,2,0:T(8,128)(2,1)S(1)} %get-tuple-element.17), channel_id=1, source_target_pairs={{0,4},{4,8},{8,12},{12,16},{16,20},{20,24},{24,28},{1,5},{5,9},{9,... | collective-permute-start | bytes 393224 | tf_op jit(solution)/shard_map/ppermute | solution.py:16
  12.6 2.4 %collective-permute-start.5 = (bf16[1,256,256]{1,2,0:T(8,128)(2,1)S(1)}, bf16[1,256,256]{1,2,0:T(8,128)(2,1)S(1)}, u32[]{:S(2)}, u32[]{:S(2)}) collective-permute-start(bf16[1,256,256]{1,2,0:T(8,128)(2,1)S(1)} %get-tuple-element.18), channel_id=1, source_target_pairs={{4,0},{8,4},{12,8},{16,12},{20,16},{24,20},{28,24},{5,1},{9,5},{13... | collective-permute-start | bytes 393224 | tf_op jit(solution)/shard_map/ppermute | solution.py:16
  16.3 4.1 %collective-permute-done.5 = bf16[1,256,256]{1,2,0:T(8,128)(2,1)S(1)} collective-permute-done((bf16[1,256,256]{1,2,0:T(8,128)(2,1)S(1)}, bf16[1,256,256]{1,2,0:T(8,128)(2,1)S(1)}, u32[]{:S(2)}, u32[]{:S(2)}) %collective-permute-start.5) | collective-permute-done | bytes 131104 | tf_op jit(solution)/shard_map/ppermute | solution.py:16
  21.4 1.6 %reshape.221 = bf16[4,2,32768]{2,1,0:T(2,128)(2,1)} reshape(bf16[1024,4,64]{2,1,0:T(4,128)(2,1)S(1)} %bitcast.325) | data formatting | bytes 1048576
  22.9 3.5 %all-to-all-start = ((bf16[4,2,32768]{2,1,0:T(2,128)(2,1)}), bf16[4,2,32768]{2,1,0:T(2,128)(2,1)S(1)}, u32[]{:S(2)}, u32[]{:S(2)}) async-start(bf16[4,2,32768]{2,1,0:T(2,128)(2,1)} %reshape.221), calls=%async_computation | async-start | bytes 1048576 | tf_op jit(solution)/shard_map/all_to_all | solution.py:40
  28.4 6.7 %copy.17 = bf16[3,3,1024,256]{2,3,1,0:T(8,128)(2,1)} copy(bf16[3,3,1024,256]{3,2,1,0:T(8,128)(2,1)} %param.4) | data formatting | bytes 9437184 | tf_op args[1]
  35.2 2.3 %all-to-all-done = bf16[4,2,32768]{2,1,0:T(2,128)(2,1)S(1)} async-done(((bf16[4,2,32768]{2,1,0:T(2,128)(2,1)}), bf16[4,2,32768]{2,1,0:T(2,128)(2,1)S(1)}, u32[]{:S(2)}, u32[]{:S(2)}) %all-to-all-start) | async-done | bytes 524320 | tf_op jit(solution)/shard_map/all_to_all | solution.py:40
  38.9 2.3 %fusion.14 = f32[1,256,3,256]{3,1,2,0:T(8,128)S(1)} fusion(bf16[3,1024,3,256]{1,3,2,0:T(8,128)(2,1)} %bitcast.319, bf16[4,256,1024]{2,1,0:T(8,128)(2,1)} %all-gather.3.cloned.1.call-done), kind=kOutput, calls=%fused_computation.43 | convolution fusion | flops 402653184 | bytes 2883584 | tf_op jit(solution)/shard_map/dot_general | solution.py:48
  41.3 3.5 %collective-permute-start = (f32[1,256,256]{2,1,0:T(8,128)S(1)}, f32[1,256,256]{2,1,0:T(8,128)S(1)}, u32[]{:S(2)}, u32[]{:S(2)}) collective-permute-start(f32[1,256,256]{2,1,0:T(8,128)S(1)} %fusion.87), channel_id=1, source_target_pairs={{0,4},{4,8},{8,12},{12,16},{16,20},{20,24},{24,28},{1,5},{5,9},{9,... | collective-permute-start | bytes 786440 | tf_op jit(solution)/shard_map/ppermute | solution.py:51
  44.8 1.7 %fusion.17 = f32[1,256,3,256]{3,1,2,0:T(8,128)S(1)} fusion(bf16[3,1024,3,256]{1,3,2,0:T(8,128)(2,1)S(1)} %bitcast.321, bf16[4,256,1024]{2,1,0:T(8,128)(2,1)} %all-gather.3.cloned.1.call-done), kind=kOutput, calls=%fused_computation.44 | convolution fusion | flops 402653184 | bytes 2883584 | tf_op jit(solution)/shard_map/dot_general | solution.py:48
  46.6 2.5 %collective-permute-start.1 = (f32[1,256,256]{2,1,0:T(8,128)S(1)}, f32[1,256,256]{2,1,0:T(8,128)S(1)}, u32[]{:S(2)}, u32[]{:S(2)}) collective-permute-start(f32[1,256,256]{2,1,0:T(8,128)S(1)} %fusion.90), channel_id=1, source_target_pairs={{4,0},{8,4},{12,8},{16,12},{20,16},{24,20},{28,24},{5,1},{9,5},{13... | collective-permute-start | bytes 786440 | tf_op jit(solution)/shard_map/ppermute | solution.py:52
  50.5 1.8 %fusion = f32[4,256,3,256]{3,1,2,0:T(8,128)S(1)} fusion(bf16[4,256,1024]{2,1,0:T(8,128)(2,1)S(1)} %copy-done.3, bf16[3,1024,3,256]{1,3,2,0:T(8,128)(2,1)S(1)} %bitcast.323), kind=kOutput, calls=%fused_computation.23 | convolution fusion | flops 1610612736 | bytes 6815744 | tf_op jit(solution)/shard_map/dot_general | solution.py:48
  52.3 1.8 %pad_add_fusion = f32[4,256,3,256]{3,1,2,0:T(8,128)S(1)} fusion(f32[3,256,3,256]{3,1,2,0:T(8,128)S(1)} %fusion.3, f32[4,256,3,256]{3,1,2,0:T(8,128)S(1)} %fusion, bf16[4,256,1024]{2,1,0:T(8,128)(2,1)S(1)} %copy-done.3, bf16[3,1024,3,256]{1,3,2,0:T(8,128)(2,1)S(1)} %bitcast.324), kind=kOutput, calls=%fused_computation.18 | convolution fusion | flops 1209532416 | bytes 11796480 | tf_op jit(solution)/shard_map/jit(_pad)/pad | solution.py:71
  54.2 3.1 %collective-permute-done.1 = f32[1,256,256]{2,1,0:T(8,128)S(1)} collective-permute-done((f32[1,256,256]{2,1,0:T(8,128)S(1)}, f32[1,256,256]{2,1,0:T(8,128)S(1)}, u32[]{:S(2)}, u32[]{:S(2)}) %collective-permute-start.1) | collective-permute-done | bytes 262176 | tf_op jit(solution)/shard_map/ppermute | solution.py:52
  58.1 6.1 %psum.7 = f32[4,256,2]{1,0,2:T(4,128)S(1)} all-reduce(f32[4,256,2]{1,0,2:T(4,128)S(1)} %pad_maximum_fusion.3), channel_id=1, replica_groups=mesh['hi'=4,'lo'=2,'chan'=4] {'chan'}, use_global_device_ids=true, to_apply=%region_2.3 | all-reduce | flops 2048 | bytes 16384 | tf_op jit(solution)/shard_map/psum | solution.py:84
  64.6 4.5 %collective-permute-start.2 = (bf16[1,256,256]{2,1,0:T(8,128)(2,1)S(1)}, bf16[1,256,256]{2,1,0:T(8,128)(2,1)}, u32[]{:S(2)}, u32[]{:S(2)}) collective-permute-start(bf16[1,256,256]{2,1,0:T(8,128)(2,1)S(1)} %slice_select_fusion), channel_id=1, source_target_pairs={{4,8},{12,16},{20,24},{8,4},{16,12},{24,20},{5,9},{13,17},{21,25},... | collective-permute-start | bytes 393224 | tf_op jit(solution)/shard_map/ppermute | solution.py:123
  70.4 4.1 %all-to-all-start.1 = ((bf16[4,256,256]{2,0,1:T(4,128)(2,1)}), bf16[4,256,256]{2,0,1:T(4,128)(2,1)}, u32[]{:S(2)}, u32[]{:S(2)}) async-start(bf16[4,256,256]{2,0,1:T(4,128)(2,1)} %copy.20), calls=%async_computation.1 | async-start | bytes 1048576 | tf_op jit(solution)/shard_map/all_to_all | solution.py:90
  74.8 1.9 %fusion.30 = f32[9,512,256]{2,1,0:T(8,128)S(1)} fusion(bf16[4,256,256]{2,1,0:T(8,128)(2,1)S(1)} %get-tuple-element.15, s32[]{:T(128)S(6)} %select_n.57, bf16[10,256,512]{1,2,0:T(8,128)(2,1)} %all-gather.5.cloned.1.call-done), kind=kOutput, calls=%fused_computation.73 | convolution fusion | flops 268435456 | bytes 3670020 | tf_op jit(solution)/shard_map/dot_general | solution.py:104
  89.2 9.0 %convolution_convert_fusion = bf16[1024,1024]{0,1:T(8,128)(2,1)} fusion(bf16[1024,2304]{1,0:T(8,128)(2,1)S(1)} %bitcast.336, bf16[2304,1024]{1,0:T(8,128)(2,1)} %bitcast.320), kind=kOutput, calls=%fused_computation.25 | convolution fusion | flops 4832886784 | bytes 11534336 | tf_op jit(solution)/shard_map/dot_general | solution.py:137
  98.2 3.6 %all-to-all-start.2 = ((bf16[4,256,1024]{2,1,0:T(8,128)(2,1)}), bf16[4,256,1024]{2,1,0:T(8,128)(2,1)S(1)}, u32[]{:S(2)}, u32[]{:S(2)}) async-start(bf16[4,256,1024]{2,1,0:T(8,128)(2,1)} %bitcast.330), calls=%async_computation.2 | async-start | bytes 4194304 | tf_op jit(solution)/shard_map/all_to_all | solution.py:142
  101.8 1.4 %copy.21 = bf16[4,64,4,256]{3,2,1,0:T(4,128)(2,1)S(1)} copy(bf16[4,64,4,256]{3,0,1,2:T(4,128)(2,1)} %bitcast.40) | data formatting | bytes 1048576 | tf_op jit(solution)/shard_map/all_to_all | solution.py:90
  104.4 23.1 %all-to-all-done.2 = bf16[4,256,1024]{2,1,0:T(8,128)(2,1)S(1)} async-done(((bf16[4,256,1024]{2,1,0:T(8,128)(2,1)}), bf16[4,256,1024]{2,1,0:T(8,128)(2,1)S(1)}, u32[]{:S(2)}, u32[]{:S(2)}) %all-to-all-start.2) | async-done | bytes 2097184 | tf_op jit(solution)/shard_map/all_to_all | solution.py:142
  128.9 7.2 %reduce-scatter.2.cloned.1.call-done = bf16[3,3,128,256]{3,2,1,0:T(8,128)(2,1)} async-done(((bf16[3,3,512,256]{3,2,1,0:T(8,128)(2,1)}), bf16[3,3,128,256]{3,2,1,0:T(8,128)(2,1)}) %reduce-scatter.2.cloned.1.call-update) | async-done | bytes 589840 | tf_op jit(solution)/shard_map/reduce_scatter | solution.py:119
  136.1 2.2 %convert_element_type.112 = f32[3,3,128,256]{3,2,1,0:T(8,128)} convert(bf16[3,3,128,256]{3,2,1,0:T(8,128)(2,1)} %reduce-scatter.2.cloned.1.call-done) | non-fusion elementwise | flops 294912 | bytes 1769472 | tf_op jit(solution)/shard_map/convert_element_type | solution.py:119
  (80 shorter events, 26.8 us)
Async XLA Ops:
  7.2 13.5 %copy-start.4 = (bf16[4,64,1024]{2,1,0:T(8,128)(2,1)S(1)}, bf16[4,64,1024]{2,1,0:T(8,128)(2,1)}, u32[]{:S(2)}) copy-start(bf16[4,64,1024]{2,1,0:T(8,128)(2,1)} %param.5) | copy-start | bytes 1572868
  7.2 31.7 %all-gather.3.cloned.1.call-start = ((), (), s32[]{:S(2)}) async-start(), calls=%async_computation.4 | async-start | bytes 2621440 | tf_op jit(solution)/shard_map/all_gather | solution.py:41
  9.2 7.1 %collective-permute-start.4 = (bf16[1,256,256]{1,2,0:T(8,128)(2,1)S(1)}, bf16[1,256,256]{1,2,0:T(8,128)(2,1)S(1)}, u32[]{:S(2)}, u32[]{:S(2)}) collective-permute-start(bf16[1,256,256]{1,2,0:T(8,128)(2,1)S(1)} %get-tuple-element.17), channel_id=1, source_target_pairs={{0,4},{4,8},{8,12},{12,16},{16,20},{20,24},{24,28},{1,5},{5,9},{9,... | collective-permute-start | bytes 393224 | tf_op jit(solution)/shard_map/ppermute | solution.py:16
  12.6 7.8 %collective-permute-start.5 = (bf16[1,256,256]{1,2,0:T(8,128)(2,1)S(1)}, bf16[1,256,256]{1,2,0:T(8,128)(2,1)S(1)}, u32[]{:S(2)}, u32[]{:S(2)}) collective-permute-start(bf16[1,256,256]{1,2,0:T(8,128)(2,1)S(1)} %get-tuple-element.18), channel_id=1, source_target_pairs={{4,0},{8,4},{12,8},{16,12},{20,16},{24,20},{28,24},{5,1},{9,5},{13... | collective-permute-start | bytes 393224 | tf_op jit(solution)/shard_map/ppermute | solution.py:16
  20.6 6.7 %collective-permute-start.6 = (bf16[4,256,128]{1,2,0:T(8,128)(2,1)S(1)}, bf16[4,256,128]{1,2,0:T(8,128)(2,1)S(1)}, u32[]{:S(2)}, u32[]{:S(2)}) collective-permute-start(bf16[4,256,128]{1,2,0:T(8,128)(2,1)S(1)} %dynamic-slice_bitcast_fusion.1), channel_id=1, source_target_pairs={{0,4},{4,0},{1,5},{5,1},{2,6},{6,2},{3,7},{7,3},{8,12},{12,8},{9,1... | collective-permute-start | bytes 786440 | tf_op jit(solution)/shard_map/ppermute | solution.py:63
  22.9 14.5 %all-to-all-start = ((bf16[4,2,32768]{2,1,0:T(2,128)(2,1)}), bf16[4,2,32768]{2,1,0:T(2,128)(2,1)S(1)}, u32[]{:S(2)}, u32[]{:S(2)}) async-start(bf16[4,2,32768]{2,1,0:T(2,128)(2,1)} %reshape.221), calls=%async_computation | async-start | bytes 1048576 | tf_op jit(solution)/shard_map/all_to_all | solution.py:40
  26.4 48.4 %all-gather.5.cloned.1.call-start = ((), (), s32[]{:S(2)}) async-start(), calls=%async_computation.5 | async-start | bytes 3276800 | tf_op jit(solution)/shard_map/all_gather | solution.py:68
  38.9 5.9 %copy-start.1 = (bf16[3,3,1024,256]{2,3,1,0:T(8,128)(2,1)S(1)}, bf16[3,3,1024,256]{2,3,1,0:T(8,128)(2,1)}, u32[]{:S(2)}) copy-start(bf16[3,3,1024,256]{2,3,1,0:T(8,128)(2,1)} %copy.17) | copy-start | bytes 14155780
  41.2 7.8 %copy-start.3 = (bf16[4,256,1024]{2,1,0:T(8,128)(2,1)S(1)}, bf16[4,256,1024]{2,1,0:T(8,128)(2,1)}, u32[]{:S(2)}) copy-start(bf16[4,256,1024]{2,1,0:T(8,128)(2,1)} %all-gather.3.cloned.1.call-done) | copy-start | bytes 6291460
  41.3 12.9 %collective-permute-start = (f32[1,256,256]{2,1,0:T(8,128)S(1)}, f32[1,256,256]{2,1,0:T(8,128)S(1)}, u32[]{:S(2)}, u32[]{:S(2)}) collective-permute-start(f32[1,256,256]{2,1,0:T(8,128)S(1)} %fusion.87), channel_id=1, source_target_pairs={{0,4},{4,8},{8,12},{12,16},{16,20},{20,24},{24,28},{1,5},{5,9},{9,... | collective-permute-start | bytes 786440 | tf_op jit(solution)/shard_map/ppermute | solution.py:51
  46.6 10.7 %collective-permute-start.1 = (f32[1,256,256]{2,1,0:T(8,128)S(1)}, f32[1,256,256]{2,1,0:T(8,128)S(1)}, u32[]{:S(2)}, u32[]{:S(2)}) collective-permute-start(f32[1,256,256]{2,1,0:T(8,128)S(1)} %fusion.90), channel_id=1, source_target_pairs={{4,0},{8,4},{12,8},{16,12},{20,16},{24,20},{28,24},{5,1},{9,5},{13... | collective-permute-start | bytes 786440 | tf_op jit(solution)/shard_map/ppermute | solution.py:52
  64.5 16.6 %collective-permute-start.3 = (bf16[4,256,256]{2,1,0:T(8,128)(2,1)S(1)}, bf16[4,256,256]{2,1,0:T(8,128)(2,1)S(1)}, u32[]{:S(2)}, u32[]{:S(2)}) collective-permute-start(bf16[4,256,256]{2,1,0:T(8,128)(2,1)S(1)} %get-tuple-element.15), channel_id=1, source_target_pairs={{0,4},{4,0},{1,5},{5,1},{2,6},{6,2},{3,7},{7,3},{8,12},{12,8},{9,1... | collective-permute-start | bytes 1572872 | tf_op jit(solution)/shard_map/ppermute | solution.py:92
  64.6 22.8 %collective-permute-start.2 = (bf16[1,256,256]{2,1,0:T(8,128)(2,1)S(1)}, bf16[1,256,256]{2,1,0:T(8,128)(2,1)}, u32[]{:S(2)}, u32[]{:S(2)}) collective-permute-start(bf16[1,256,256]{2,1,0:T(8,128)(2,1)S(1)} %slice_select_fusion), channel_id=1, source_target_pairs={{4,8},{12,16},{20,24},{8,4},{16,12},{24,20},{5,9},{13,17},{21,25},... | collective-permute-start | bytes 393224 | tf_op jit(solution)/shard_map/ppermute | solution.py:123
  70.4 27.8 %all-to-all-start.1 = ((bf16[4,256,256]{2,0,1:T(4,128)(2,1)}), bf16[4,256,256]{2,0,1:T(4,128)(2,1)}, u32[]{:S(2)}, u32[]{:S(2)}) async-start(bf16[4,256,256]{2,0,1:T(4,128)(2,1)} %copy.20), calls=%async_computation.1 | async-start | bytes 1048576 | tf_op jit(solution)/shard_map/all_to_all | solution.py:90
  74.5 61.6 %reduce-scatter.2.cloned.1.call-start = ((), (), s32[]{:S(2)}) async-start(), calls=%async_computation.6 | async-start | bytes 2949120 | tf_op jit(solution)/shard_map/reduce_scatter | solution.py:119
  74.8 2.1 %copy-start = (bf16[10,256,512]{1,2,0:T(8,128)(2,1)S(1)}, bf16[10,256,512]{1,2,0:T(8,128)(2,1)}, u32[]{:S(2)}) copy-start(bf16[10,256,512]{1,2,0:T(8,128)(2,1)} %all-gather.5.cloned.1.call-done) | copy-start | bytes 7864324
  85.9 1.5 %copy-start.2 = (bf16[9,512,256]{2,1,0:T(8,128)(2,1)}, bf16[9,512,256]{2,1,0:T(8,128)(2,1)S(1)}, u32[]{:S(2)}) copy-start(bf16[9,512,256]{2,1,0:T(8,128)(2,1)S(1)} %fusion.66) | copy-start | bytes 7077892
  98.2 29.3 %all-to-all-start.2 = ((bf16[4,256,1024]{2,1,0:T(8,128)(2,1)}), bf16[4,256,1024]{2,1,0:T(8,128)(2,1)S(1)}, u32[]{:S(2)}, u32[]{:S(2)}) async-start(bf16[4,256,1024]{2,1,0:T(8,128)(2,1)} %bitcast.330), calls=%async_computation.2 | async-start | bytes 4194304 | tf_op jit(solution)/shard_map/all_to_all | solution.py:142
Sparse Core Ops, SparseCore 0:
  9.6 26.3 all-gather.2
  38.1 25.5 all-gather.4
  87.5 48.5 reduce-scatter.1

commit v16 on v15

--- a/solution.py
+++ b/solution.py
@@ -89,7 +89,11 @@
     grad_conv = (inverse_rms * (upstream - unit * mean_gu)).astype(jnp.bfloat16)
     normed = lax.all_to_all(normed_filters, "chan", split_axis=1, concat_axis=2, tiled=True)
 
-    sent_grad = lax.ppermute(grad_conv, "lo", [(0, 1), (1, 0)])
+    half = height // 2
+    sent_grad = jnp.concatenate(
+        [lax.ppermute(grad_conv[:half], "lo", [(0, 1), (1, 0)]), lax.ppermute(grad_conv[half:], "lo", [(0, 1), (1, 0)])],
+        axis=0,
+    )
     img_block = jnp.pad(img_block, ((0, 0), (1, 1), (0, 0)))
     width_w = img_block.shape[2]
 

time: 147 us -> 154 us (1.048)
  waiting for transfers between devices: 42.5 us -> 45.8 us
  starting transfers between devices: 28 us -> 29.7 us
    ppermute x2, waiting for transfers between devices: 5.33 us -> 0.01 us  [shift_rows(): return lax.ppermute(rows, SLAB, pairs)]
    ppermute x1 -> x2, waiting for transfers between devices: 0.01 us -> 3.98 us  [the longest x1 3.79 us: on_device(): lax.ppermute(grad_conv[half:], 'lo', [(0, 1), (1, 0)])]
    all_to_all x1, waiting for transfers between devices: 2.31 us -> 4.63 us  [on_device(): lax.all_to_all(grad_out, 'chan', split_axis=2, concat_axis=1, tiled=True)]
    ppermute x1 -> x2, starting transfers between devices: 0.07 us -> 2.08 us  [the longest x1 2.01 us: on_device(): lax.ppermute(grad_conv[half:], 'lo', [(0, 1), (1, 0)])]
    unnamed x22 -> x20, local copies, waits for them, and re-layouts: 14 us -> 14.9 us
  transfers between devices with their start and end apart: 13 -> 14, of which waited for: 7 -> 8; matrix products, arithmetic and copies ran while one was open for 34% -> 33% of each run, Pallas kernels for 0% -> 0%
where the time goes in v16:
time: 154 us; the launch traced here: 151 us
  waiting for transfers between devices  45.8 us (30%)
  starting transfers between devices  29.7 us (19%)
  matrix products  28.9 us (19%)
  local copies, waits for them, and re-layouts  19.7 us (13%)
  between operations  14.3 us (9%)
  blocking collectives  6.52 us (4%)
  other arithmetic  6.34 us (4%)
    all_to_all x1, waiting for transfers between devices, on_device(): lax.all_to_all(split, 'chan', split_axis=0, concat_axis=0, tiled=True)  23.1 us
    unnamed x20, local copies, waits for them, and re-layouts  14.9 us
    dot_general x18, matrix products, pair_part(): lax.dot_general(weight_window, flat, (((0,), (0,)), ((), ())), preferred_...  10.9 us
    dot_general x1, matrix products, on_device(): lax.dot_general(by_filter, columns, (((0,), (1,)), ((), ())), preferred_e...  8.97 us
    dot_general x4, matrix products, taps(): out = jnp.dot(flat, by_row[a], preferred_element_type=jnp.float32)  7.22 us
    reduce_scatter x1, waiting for transfers between devices, on_device(): lax.psum_scatter(stacked, 'hi', scatter_dimension=2, tiled=True)  6.71 us
    psum x1, blocking collectives, on_device(): totals = lax.psum(partial, 'chan')  6.52 us
    ppermute x2, starting transfers between devices, shift_rows(): return lax.ppermute(rows, SLAB, pairs)  5.85 us
  transfers between devices with their start and end apart: 14, of which 8 were waited for; matrix products, arithmetic and copies ran while one was open for 33% of the time, Pallas kernels for 0%

profile of v16, /device:TPU:4, one launch (start us, length us, event | category | flops | bytes accessed | tf_op | source)
XLA Modules:
  0.0 151.2 jit_solution(13382823332084275041)
XLA Ops:
  9.2 3.4 %collective-permute-start.5 = (bf16[1,256,256]{1,2,0:T(8,128)(2,1)S(1)}, bf16[1,256,256]{1,2,0:T(8,128)(2,1)S(1)}, u32[]{:S(2)}, u32[]{:S(2)}) collective-permute-start(bf16[1,256,256]{1,2,0:T(8,128)(2,1)S(1)} %get-tuple-element.17), channel_id=1, source_target_pairs={{0,4},{4,8},{8,12},{12,16},{16,20},{20,24},{24,28},{1,5},{5,9},{9,... | collective-permute-start | bytes 393224 | tf_op jit(solution)/shard_map/ppermute | solution.py:16
  12.6 2.4 %collective-permute-start.6 = (bf16[1,256,256]{1,2,0:T(8,128)(2,1)S(1)}, bf16[1,256,256]{1,2,0:T(8,128)(2,1)S(1)}, u32[]{:S(2)}, u32[]{:S(2)}) collective-permute-start(bf16[1,256,256]{1,2,0:T(8,128)(2,1)S(1)} %get-tuple-element.18), channel_id=1, source_target_pairs={{4,0},{8,4},{12,8},{16,12},{20,16},{24,20},{28,24},{5,1},{9,5},{13... | collective-permute-start | bytes 393224 | tf_op jit(solution)/shard_map/ppermute | solution.py:16
  18.2 3.5 %all-to-all-start = ((bf16[4,2,32768]{2,1,0:T(2,128)(2,1)}), bf16[4,2,32768]{2,1,0:T(2,128)(2,1)S(1)}, u32[]{:S(2)}, u32[]{:S(2)}) async-start(bf16[4,2,32768]{2,1,0:T(2,128)(2,1)} %reshape.221), calls=%async_computation | async-start | bytes 1048576 | tf_op jit(solution)/shard_map/all_to_all | solution.py:40
  22.0 6.7 %copy.17 = bf16[3,3,1024,256]{2,3,1,0:T(8,128)(2,1)} copy(bf16[3,3,1024,256]{3,2,1,0:T(8,128)(2,1)} %param.4) | data formatting | bytes 9437184 | tf_op args[1]
  28.8 1.8 %collective-permute-done.7 = bf16[4,256,128]{1,2,0:T(8,128)(2,1)S(1)} collective-permute-done((bf16[4,256,128]{1,2,0:T(8,128)(2,1)S(1)}, bf16[4,256,128]{1,2,0:T(8,128)(2,1)S(1)}, u32[]{:S(2)}, u32[]{:S(2)}) %collective-permute-start.7) | collective-permute-done | bytes 262176 | tf_op jit(solution)/shard_map/ppermute | solution.py:63
  31.8 4.6 %all-to-all-done = bf16[4,2,32768]{2,1,0:T(2,128)(2,1)S(1)} async-done(((bf16[4,2,32768]{2,1,0:T(2,128)(2,1)}), bf16[4,2,32768]{2,1,0:T(2,128)(2,1)S(1)}, u32[]{:S(2)}, u32[]{:S(2)}) %all-to-all-start) | async-done | bytes 524320 | tf_op jit(solution)/shard_map/all_to_all | solution.py:40
  39.2 2.3 %fusion.14 = f32[1,256,3,256]{3,1,2,0:T(8,128)S(1)} fusion(bf16[3,1024,3,256]{1,3,2,0:T(8,128)(2,1)} %bitcast.319, bf16[4,256,1024]{2,1,0:T(8,128)(2,1)} %all-gather.3.cloned.1.call-done), kind=kOutput, calls=%fused_computation.43 | convolution fusion | flops 402653184 | bytes 2883584 | tf_op jit(solution)/shard_map/dot_general | solution.py:48
  41.7 3.5 %collective-permute-start = (f32[1,256,256]{2,1,0:T(8,128)S(1)}, f32[1,256,256]{2,1,0:T(8,128)S(1)}, u32[]{:S(2)}, u32[]{:S(2)}) collective-permute-start(f32[1,256,256]{2,1,0:T(8,128)S(1)} %fusion.87), channel_id=1, source_target_pairs={{0,4},{4,8},{8,12},{12,16},{16,20},{20,24},{24,28},{1,5},{5,9},{9,... | collective-permute-start | bytes 786440 | tf_op jit(solution)/shard_map/ppermute | solution.py:51
  45.2 1.7 %fusion.17 = f32[1,256,3,256]{3,1,2,0:T(8,128)S(1)} fusion(bf16[3,1024,3,256]{1,3,2,0:T(8,128)(2,1)S(1)} %bitcast.321, bf16[4,256,1024]{2,1,0:T(8,128)(2,1)} %all-gather.3.cloned.1.call-done), kind=kOutput, calls=%fused_computation.44 | convolution fusion | flops 402653184 | bytes 2883584 | tf_op jit(solution)/shard_map/dot_general | solution.py:48
  46.9 2.5 %collective-permute-start.1 = (f32[1,256,256]{2,1,0:T(8,128)S(1)}, f32[1,256,256]{2,1,0:T(8,128)S(1)}, u32[]{:S(2)}, u32[]{:S(2)}) collective-permute-start(f32[1,256,256]{2,1,0:T(8,128)S(1)} %fusion.90), channel_id=1, source_target_pairs={{4,0},{8,4},{12,8},{16,12},{20,16},{24,20},{28,24},{5,1},{9,5},{13... | collective-permute-start | bytes 786440 | tf_op jit(solution)/shard_map/ppermute | solution.py:52
  50.8 1.8 %fusion = f32[4,256,3,256]{3,1,2,0:T(8,128)S(1)} fusion(bf16[4,256,1024]{2,1,0:T(8,128)(2,1)S(1)} %copy-done.3, bf16[3,1024,3,256]{1,3,2,0:T(8,128)(2,1)S(1)} %bitcast.323), kind=kOutput, calls=%fused_computation.23 | convolution fusion | flops 1610612736 | bytes 6815744 | tf_op jit(solution)/shard_map/dot_general | solution.py:48
  52.7 1.8 %pad_add_fusion = f32[4,256,3,256]{3,1,2,0:T(8,128)S(1)} fusion(f32[3,256,3,256]{3,1,2,0:T(8,128)S(1)} %fusion.3, f32[4,256,3,256]{3,1,2,0:T(8,128)S(1)} %fusion, bf16[4,256,1024]{2,1,0:T(8,128)(2,1)S(1)} %copy-done.3, bf16[3,1024,3,256]{1,3,2,0:T(8,128)(2,1)S(1)} %bitcast.324), kind=kOutput, calls=%fused_computation.18 | convolution fusion | flops 1209532416 | bytes 11796480 | tf_op jit(solution)/shard_map/jit(_pad)/pad | solution.py:71
  54.5 3.4 %collective-permute-done.1 = f32[1,256,256]{2,1,0:T(8,128)S(1)} collective-permute-done((f32[1,256,256]{2,1,0:T(8,128)S(1)}, f32[1,256,256]{2,1,0:T(8,128)S(1)}, u32[]{:S(2)}, u32[]{:S(2)}) %collective-permute-start.1) | collective-permute-done | bytes 262176 | tf_op jit(solution)/shard_map/ppermute | solution.py:52
  58.8 6.5 %psum.7 = f32[4,256,2]{1,0,2:T(4,128)S(1)} all-reduce(f32[4,256,2]{1,0,2:T(4,128)S(1)} %pad_maximum_fusion.4), channel_id=1, replica_groups=mesh['hi'=4,'lo'=2,'chan'=4] {'chan'}, use_global_device_ids=true, to_apply=%region_2.3 | all-reduce | flops 2048 | bytes 16384 | tf_op jit(solution)/shard_map/psum | solution.py:84
  65.8 2.0 %collective-permute-start.4 = (bf16[2,256,256]{2,1,0:T(8,128)(2,1)S(1)}, bf16[2,256,256]{2,1,0:T(8,128)(2,1)S(1)}, u32[]{:S(2)}, u32[]{:S(2)}) collective-permute-start(bf16[2,256,256]{2,1,0:T(8,128)(2,1)S(1)} %get-tuple-element.20), channel_id=1, source_target_pairs={{0,4},{4,0},{1,5},{5,1},{2,6},{6,2},{3,7},{7,3},{8,12},{12,8},{9,1... | collective-permute-start | bytes 786440 | tf_op jit(solution)/shard_map/ppermute | solution.py:94
  67.8 4.2 %collective-permute-start.2 = (bf16[1,256,256]{2,1,0:T(8,128)(2,1)S(1)}, bf16[1,256,256]{2,1,0:T(8,128)(2,1)}, u32[]{:S(2)}, u32[]{:S(2)}) collective-permute-start(bf16[1,256,256]{2,1,0:T(8,128)(2,1)S(1)} %slice_select_fusion), channel_id=1, source_target_pairs={{4,8},{12,16},{20,24},{8,4},{16,12},{24,20},{5,9},{13,17},{21,25},... | collective-permute-start | bytes 393224 | tf_op jit(solution)/shard_map/ppermute | solution.py:127
  73.2 4.1 %all-to-all-start.1 = ((bf16[4,256,256]{2,0,1:T(4,128)(2,1)}), bf16[4,256,256]{2,0,1:T(4,128)(2,1)}, u32[]{:S(2)}, u32[]{:S(2)}) async-start(bf16[4,256,256]{2,0,1:T(4,128)(2,1)} %copy.20), calls=%async_computation.1 | async-start | bytes 1048576 | tf_op jit(solution)/shard_map/all_to_all | solution.py:90
  77.8 3.8 %collective-permute-done.4 = bf16[2,256,256]{2,1,0:T(8,128)(2,1)S(1)} collective-permute-done((bf16[2,256,256]{2,1,0:T(8,128)(2,1)S(1)}, bf16[2,256,256]{2,1,0:T(8,128)(2,1)S(1)}, u32[]{:S(2)}, u32[]{:S(2)}) %collective-permute-start.4) | collective-permute-done | bytes 262176 | tf_op jit(solution)/shard_map/ppermute | solution.py:94
  81.7 1.9 %fusion.30 = f32[9,512,256]{2,1,0:T(8,128)S(1)} fusion(bf16[4,256,256]{2,1,0:T(8,128)(2,1)S(1)} %get-tuple-element.15, s32[]{:T(128)S(6)} %select_n.57, bf16[10,256,512]{1,2,0:T(8,128)(2,1)} %all-gather.5.cloned.1.call-done), kind=kOutput, calls=%fused_computation.73 | convolution fusion | flops 268435456 | bytes 3670020 | tf_op jit(solution)/shard_map/dot_general | solution.py:108
  96.1 9.0 %convolution_convert_fusion = bf16[1024,1024]{0,1:T(8,128)(2,1)} fusion(bf16[1024,2304]{1,0:T(8,128)(2,1)S(1)} %bitcast.336, bf16[2304,1024]{1,0:T(8,128)(2,1)} %bitcast.320), kind=kOutput, calls=%fused_computation.25 | convolution fusion | flops 4832886784 | bytes 11534336 | tf_op jit(solution)/shard_map/dot_general | solution.py:141
  105.1 3.6 %all-to-all-start.2 = ((bf16[4,256,1024]{2,1,0:T(8,128)(2,1)}), bf16[4,256,1024]{2,1,0:T(8,128)(2,1)S(1)}, u32[]{:S(2)}, u32[]{:S(2)}) async-start(bf16[4,256,1024]{2,1,0:T(8,128)(2,1)} %bitcast.330), calls=%async_computation.2 | async-start | bytes 4194304 | tf_op jit(solution)/shard_map/all_to_all | solution.py:146
  111.3 23.1 %all-to-all-done.2 = bf16[4,256,1024]{2,1,0:T(8,128)(2,1)S(1)} async-done(((bf16[4,256,1024]{2,1,0:T(8,128)(2,1)}), bf16[4,256,1024]{2,1,0:T(8,128)(2,1)S(1)}, u32[]{:S(2)}, u32[]{:S(2)}) %all-to-all-start.2) | async-done | bytes 2097184 | tf_op jit(solution)/shard_map/all_to_all | solution.py:146
  135.8 6.7 %reduce-scatter.2.cloned.1.call-done = bf16[3,3,128,256]{3,2,1,0:T(8,128)(2,1)} async-done(((bf16[3,3,512,256]{3,2,1,0:T(8,128)(2,1)}), bf16[3,3,128,256]{3,2,1,0:T(8,128)(2,1)}) %reduce-scatter.2.cloned.1.call-update) | async-done | bytes 589840 | tf_op jit(solution)/shard_map/reduce_scatter | solution.py:123
  142.5 2.2 %convert_element_type.112 = f32[3,3,128,256]{3,2,1,0:T(8,128)} convert(bf16[3,3,128,256]{3,2,1,0:T(8,128)(2,1)} %reduce-scatter.2.cloned.1.call-done) | non-fusion elementwise | flops 294912 | bytes 1769472 | tf_op jit(solution)/shard_map/convert_element_type | solution.py:123
  (82 shorter events, 30.3 us)
Async XLA Ops:
  7.2 32.1 %all-gather.3.cloned.1.call-start = ((), (), s32[]{:S(2)}) async-start(), calls=%async_computation.4 | async-start | bytes 2621440 | tf_op jit(solution)/shard_map/all_gather | solution.py:41
  9.2 12.6 %collective-permute-start.5 = (bf16[1,256,256]{1,2,0:T(8,128)(2,1)S(1)}, bf16[1,256,256]{1,2,0:T(8,128)(2,1)S(1)}, u32[]{:S(2)}, u32[]{:S(2)}) collective-permute-start(bf16[1,256,256]{1,2,0:T(8,128)(2,1)S(1)} %get-tuple-element.17), channel_id=1, source_target_pairs={{0,4},{4,8},{8,12},{12,16},{16,20},{20,24},{24,28},{1,5},{5,9},{9,... | collective-permute-start | bytes 393224 | tf_op jit(solution)/shard_map/ppermute | solution.py:16
  12.6 9.1 %collective-permute-start.6 = (bf16[1,256,256]{1,2,0:T(8,128)(2,1)S(1)}, bf16[1,256,256]{1,2,0:T(8,128)(2,1)S(1)}, u32[]{:S(2)}, u32[]{:S(2)}) collective-permute-start(bf16[1,256,256]{1,2,0:T(8,128)(2,1)S(1)} %get-tuple-element.18), channel_id=1, source_target_pairs={{4,0},{8,4},{12,8},{16,12},{20,16},{24,20},{28,24},{5,1},{9,5},{13... | collective-permute-start | bytes 393224 | tf_op jit(solution)/shard_map/ppermute | solution.py:16
  18.2 18.2 %all-to-all-start = ((bf16[4,2,32768]{2,1,0:T(2,128)(2,1)}), bf16[4,2,32768]{2,1,0:T(2,128)(2,1)S(1)}, u32[]{:S(2)}, u32[]{:S(2)}) async-start(bf16[4,2,32768]{2,1,0:T(2,128)(2,1)} %reshape.221), calls=%async_computation | async-start | bytes 1048576 | tf_op jit(solution)/shard_map/all_to_all | solution.py:40
  21.7 60.0 %all-gather.5.cloned.1.call-start = ((), (), s32[]{:S(2)}) async-start(), calls=%async_computation.5 | async-start | bytes 3276800 | tf_op jit(solution)/shard_map/all_gather | solution.py:68
  22.0 8.7 %collective-permute-start.7 = (bf16[4,256,128]{1,2,0:T(8,128)(2,1)S(1)}, bf16[4,256,128]{1,2,0:T(8,128)(2,1)S(1)}, u32[]{:S(2)}, u32[]{:S(2)}) collective-permute-start(bf16[4,256,128]{1,2,0:T(8,128)(2,1)S(1)} %dynamic-slice_bitcast_fusion.1), channel_id=1, source_target_pairs={{0,4},{4,0},{1,5},{5,1},{2,6},{6,2},{3,7},{7,3},{8,12},{12,8},{9,1... | collective-permute-start | bytes 786440 | tf_op jit(solution)/shard_map/ppermute | solution.py:63
  39.2 5.9 %copy-start.1 = (bf16[3,3,1024,256]{2,3,1,0:T(8,128)(2,1)S(1)}, bf16[3,3,1024,256]{2,3,1,0:T(8,128)(2,1)}, u32[]{:S(2)}) copy-start(bf16[3,3,1024,256]{2,3,1,0:T(8,128)(2,1)} %copy.17) | copy-start | bytes 14155780
  41.6 7.8 %copy-start.3 = (bf16[4,256,1024]{2,1,0:T(8,128)(2,1)S(1)}, bf16[4,256,1024]{2,1,0:T(8,128)(2,1)}, u32[]{:S(2)}) copy-start(bf16[4,256,1024]{2,1,0:T(8,128)(2,1)} %all-gather.3.cloned.1.call-done) | copy-start | bytes 6291460
  41.7 12.8 %collective-permute-start = (f32[1,256,256]{2,1,0:T(8,128)S(1)}, f32[1,256,256]{2,1,0:T(8,128)S(1)}, u32[]{:S(2)}, u32[]{:S(2)}) collective-permute-start(f32[1,256,256]{2,1,0:T(8,128)S(1)} %fusion.87), channel_id=1, source_target_pairs={{0,4},{4,8},{8,12},{12,16},{16,20},{20,24},{24,28},{1,5},{5,9},{9,... | collective-permute-start | bytes 786440 | tf_op jit(solution)/shard_map/ppermute | solution.py:51
  46.9 11.0 %collective-permute-start.1 = (f32[1,256,256]{2,1,0:T(8,128)S(1)}, f32[1,256,256]{2,1,0:T(8,128)S(1)}, u32[]{:S(2)}, u32[]{:S(2)}) collective-permute-start(f32[1,256,256]{2,1,0:T(8,128)S(1)} %fusion.90), channel_id=1, source_target_pairs={{4,0},{8,4},{12,8},{16,12},{20,16},{24,20},{28,24},{5,1},{9,5},{13... | collective-permute-start | bytes 786440 | tf_op jit(solution)/shard_map/ppermute | solution.py:52
  65.7 12.1 %collective-permute-start.3 = (bf16[2,256,256]{2,1,0:T(8,128)(2,1)S(1)}, bf16[2,256,256]{2,1,0:T(8,128)(2,1)S(1)}, u32[]{:S(2)}, u32[]{:S(2)}) collective-permute-start(bf16[2,256,256]{2,1,0:T(8,128)(2,1)S(1)} %get-tuple-element.19), channel_id=1, source_target_pairs={{0,4},{4,0},{1,5},{5,1},{2,6},{6,2},{3,7},{7,3},{8,12},{12,8},{9,1... | collective-permute-start | bytes 786440 | tf_op jit(solution)/shard_map/ppermute | solution.py:94
  65.8 15.8 %collective-permute-start.4 = (bf16[2,256,256]{2,1,0:T(8,128)(2,1)S(1)}, bf16[2,256,256]{2,1,0:T(8,128)(2,1)S(1)}, u32[]{:S(2)}, u32[]{:S(2)}) collective-permute-start(bf16[2,256,256]{2,1,0:T(8,128)(2,1)S(1)} %get-tuple-element.20), channel_id=1, source_target_pairs={{0,4},{4,0},{1,5},{5,1},{2,6},{6,2},{3,7},{7,3},{8,12},{12,8},{9,1... | collective-permute-start | bytes 786440 | tf_op jit(solution)/shard_map/ppermute | solution.py:94
  67.8 26.5 %collective-permute-start.2 = (bf16[1,256,256]{2,1,0:T(8,128)(2,1)S(1)}, bf16[1,256,256]{2,1,0:T(8,128)(2,1)}, u32[]{:S(2)}, u32[]{:S(2)}) collective-permute-start(bf16[1,256,256]{2,1,0:T(8,128)(2,1)S(1)} %slice_select_fusion), channel_id=1, source_target_pairs={{4,8},{12,16},{20,24},{8,4},{16,12},{24,20},{5,9},{13,17},{21,25},... | collective-permute-start | bytes 393224 | tf_op jit(solution)/shard_map/ppermute | solution.py:127
  73.2 31.8 %all-to-all-start.1 = ((bf16[4,256,256]{2,0,1:T(4,128)(2,1)}), bf16[4,256,256]{2,0,1:T(4,128)(2,1)}, u32[]{:S(2)}, u32[]{:S(2)}) async-start(bf16[4,256,256]{2,0,1:T(4,128)(2,1)} %copy.20), calls=%async_computation.1 | async-start | bytes 1048576 | tf_op jit(solution)/shard_map/all_to_all | solution.py:90
  77.4 65.1 %reduce-scatter.2.cloned.1.call-start = ((), (), s32[]{:S(2)}) async-start(), calls=%async_computation.6 | async-start | bytes 2949120 | tf_op jit(solution)/shard_map/reduce_scatter | solution.py:123
  81.7 2.1 %copy-start = (bf16[10,256,512]{1,2,0:T(8,128)(2,1)S(1)}, bf16[10,256,512]{1,2,0:T(8,128)(2,1)}, u32[]{:S(2)}) copy-start(bf16[10,256,512]{1,2,0:T(8,128)(2,1)} %all-gather.5.cloned.1.call-done) | copy-start | bytes 7864324
  92.8 1.4 copy-start.2
  105.1 29.3 %all-to-all-start.2 = ((bf16[4,256,1024]{2,1,0:T(8,128)(2,1)}), bf16[4,256,1024]{2,1,0:T(8,128)(2,1)S(1)}, u32[]{:S(2)}, u32[]{:S(2)}) async-start(bf16[4,256,1024]{2,1,0:T(8,128)(2,1)} %bitcast.330), calls=%async_computation.2 | async-start | bytes 4194304 | tf_op jit(solution)/shard_map/all_to_all | solution.py:146
Sparse Core Ops, SparseCore 0:
  9.5 29.6 all-gather.2
  41.4 25.8 all-gather.4
  94.4 48.0 reduce-scatter.1

commit v17 on v10

--- a/solution.py
+++ b/solution.py
@@ -112,10 +112,11 @@
 
     own_part = pair_part(grad_conv, height * lo)
     sent_grad, own_part = lax.optimization_barrier((sent_grad, own_part))
-    stacked = (own_part + pair_part(sent_grad, height * (1 - lo))).reshape(3, 3, width_w, local_filters)
-    grad_weight = lax.psum_scatter(
-        stacked.astype(jnp.bfloat16), "hi", scatter_dimension=2, tiled=True
-    ).astype(jnp.float32)
+    stacked = jnp.transpose(own_part + pair_part(sent_grad, height * (1 - lo)), (1, 0, 2))
+    scattered = lax.psum_scatter(stacked.astype(jnp.bfloat16), "hi", scatter_dimension=0, tiled=True)
+    grad_weight = jnp.transpose(scattered, (1, 0, 2)).astype(jnp.float32).reshape(
+        3, 3, scattered.shape[0], local_filters
+    )
 
     count = lax.axis_size(SLAB)
     crossing = [(s, s + 1) for s in range(1, count - 1, 2)] + [(s, s - 1) for s in range(2, count, 2)]

time: 147 us -> 147 us (level)
    convert_element_type x1 -> x0, other arithmetic: 2.19 us -> none  [on_device(): grad_weight = lax.psum_scatter(stacked.astype(jnp.bfloat16), 'hi', scatte...]
    reshape x0 -> x1, other arithmetic: none -> 2.19 us  [on_device(): jnp.transpose(scattered, (1, 0, 2)).astype(jnp.float32)]
where the time goes in v17:
time: 147 us; the launch traced here: 145 us
  waiting for transfers between devices  44.5 us (30%)
  matrix products  29 us (20%)
  starting transfers between devices  27.7 us (19%)
  local copies, waits for them, and re-layouts  16.2 us (11%)
  between operations  14.3 us (10%)
  other arithmetic  7.46 us (5%)
  blocking collectives  5.75 us (4%)
    all_to_all x1, waiting for transfers between devices, on_device(): lax.all_to_all(split, 'chan', split_axis=0, concat_axis=0, tiled=True)  24.1 us
    unnamed x20, local copies, waits for them, and re-layouts  12.5 us
    dot_general x18, matrix products, pair_part(): lax.dot_general(weight_window, flat, (((0,), (0,)), ((), ())), preferred_...  10.9 us
    dot_general x1, matrix products, on_device(): lax.dot_general(by_filter, columns, (((0,), (1,)), ((), ())), preferred_e...  8.97 us
    reduce_scatter x1, waiting for transfers between devices, on_device(): lax.psum_scatter(stacked.astype(jnp.bfloat16), 'hi', scatter_dimension=0,...  7.82 us
    dot_general x4, matrix products, taps(): out = jnp.dot(flat, by_row[a], preferred_element_type=jnp.float32)  7.27 us
    ppermute x2, starting transfers between devices, shift_rows(): return lax.ppermute(rows, SLAB, pairs)  5.85 us
    psum x1, blocking collectives, on_device(): totals = lax.psum(partial, 'chan')  5.75 us
  transfers between devices with their start and end apart: 13, of which 8 were waited for; matrix products, arithmetic and copies ran while one was open for 34% of the time, Pallas kernels for 0%

profile of v17, /device:TPU:4, one launch (start us, length us, event | category | flops | bytes accessed | tf_op | source)
XLA Modules:
  0.0 144.8 jit_solution(12785616999031120445)
XLA Ops:
  9.2 3.4 %collective-permute-start.4 = (bf16[1,256,256]{1,2,0:T(8,128)(2,1)S(1)}, bf16[1,256,256]{1,2,0:T(8,128)(2,1)S(1)}, u32[]{:S(2)}, u32[]{:S(2)}) collective-permute-start(bf16[1,256,256]{1,2,0:T(8,128)(2,1)S(1)} %get-tuple-element.17), channel_id=1, source_target_pairs={{0,4},{4,8},{8,12},{12,16},{16,20},{20,24},{24,28},{1,5},{5,9},{9,... | collective-permute-start | bytes 393224 | tf_op jit(solution)/shard_map/ppermute | solution.py:16
  12.6 2.4 %collective-permute-start.5 = (bf16[1,256,256]{1,2,0:T(8,128)(2,1)S(1)}, bf16[1,256,256]{1,2,0:T(8,128)(2,1)S(1)}, u32[]{:S(2)}, u32[]{:S(2)}) collective-permute-start(bf16[1,256,256]{1,2,0:T(8,128)(2,1)S(1)} %get-tuple-element.18), channel_id=1, source_target_pairs={{4,0},{8,4},{12,8},{16,12},{20,16},{24,20},{28,24},{5,1},{9,5},{13... | collective-permute-start | bytes 393224 | tf_op jit(solution)/shard_map/ppermute | solution.py:16
  16.3 4.1 %collective-permute-done.5 = bf16[1,256,256]{1,2,0:T(8,128)(2,1)S(1)} collective-permute-done((bf16[1,256,256]{1,2,0:T(8,128)(2,1)S(1)}, bf16[1,256,256]{1,2,0:T(8,128)(2,1)S(1)}, u32[]{:S(2)}, u32[]{:S(2)}) %collective-permute-start.5) | collective-permute-done | bytes 131104 | tf_op jit(solution)/shard_map/ppermute | solution.py:16
  21.4 1.6 %reshape.228 = bf16[4,2,32768]{2,1,0:T(2,128)(2,1)} reshape(bf16[1024,4,64]{2,1,0:T(4,128)(2,1)S(1)} %bitcast.230) | data formatting | bytes 1048576
  22.9 3.5 %all-to-all-start = ((bf16[4,2,32768]{2,1,0:T(2,128)(2,1)}), bf16[4,2,32768]{2,1,0:T(2,128)(2,1)S(1)}, u32[]{:S(2)}, u32[]{:S(2)}) async-start(bf16[4,2,32768]{2,1,0:T(2,128)(2,1)} %reshape.228), calls=%async_computation | async-start | bytes 1048576 | tf_op jit(solution)/shard_map/all_to_all | solution.py:40
  28.4 6.6 %copy.17 = bf16[3,3,1024,256]{2,3,1,0:T(8,128)(2,1)} copy(bf16[3,3,1024,256]{3,2,1,0:T(8,128)(2,1)} %param.4) | data formatting | bytes 9437184 | tf_op args[1]
  35.1 2.3 %all-to-all-done = bf16[4,2,32768]{2,1,0:T(2,128)(2,1)S(1)} async-done(((bf16[4,2,32768]{2,1,0:T(2,128)(2,1)}), bf16[4,2,32768]{2,1,0:T(2,128)(2,1)S(1)}, u32[]{:S(2)}, u32[]{:S(2)}) %all-to-all-start) | async-done | bytes 524320 | tf_op jit(solution)/shard_map/all_to_all | solution.py:40
  38.9 2.3 %fusion.15 = f32[1,256,3,256]{3,1,2,0:T(8,128)S(1)} fusion(bf16[3,1024,3,256]{1,3,2,0:T(8,128)(2,1)} %bitcast.224, bf16[4,256,1024]{2,1,0:T(8,128)(2,1)} %all-gather.3.cloned.1.call-done), kind=kOutput, calls=%fused_computation.45 | convolution fusion | flops 402653184 | bytes 2883584 | tf_op jit(solution)/shard_map/dot_general | solution.py:48
  41.3 3.5 %collective-permute-start = (f32[1,256,256]{2,1,0:T(8,128)S(1)}, f32[1,256,256]{2,1,0:T(8,128)S(1)}, u32[]{:S(2)}, u32[]{:S(2)}) collective-permute-start(f32[1,256,256]{2,1,0:T(8,128)S(1)} %fusion.61), channel_id=1, source_target_pairs={{0,4},{4,8},{8,12},{12,16},{16,20},{20,24},{24,28},{1,5},{5,9},{9,... | collective-permute-start | bytes 786440 | tf_op jit(solution)/shard_map/ppermute | solution.py:51
  44.8 1.7 %fusion.18 = f32[1,256,3,256]{3,1,2,0:T(8,128)S(1)} fusion(bf16[3,1024,3,256]{1,3,2,0:T(8,128)(2,1)S(1)} %bitcast.226, bf16[4,256,1024]{2,1,0:T(8,128)(2,1)} %all-gather.3.cloned.1.call-done), kind=kOutput, calls=%fused_computation.46 | convolution fusion | flops 402653184 | bytes 2883584 | tf_op jit(solution)/shard_map/dot_general | solution.py:48
  46.6 2.4 %collective-permute-start.1 = (f32[1,256,256]{2,1,0:T(8,128)S(1)}, f32[1,256,256]{2,1,0:T(8,128)S(1)}, u32[]{:S(2)}, u32[]{:S(2)}) collective-permute-start(f32[1,256,256]{2,1,0:T(8,128)S(1)} %fusion.64), channel_id=1, source_target_pairs={{4,0},{8,4},{12,8},{16,12},{20,16},{24,20},{28,24},{5,1},{9,5},{13... | collective-permute-start | bytes 786440 | tf_op jit(solution)/shard_map/ppermute | solution.py:52
  50.5 1.8 %fusion.1 = f32[4,256,3,256]{3,1,2,0:T(8,128)S(1)} fusion(bf16[4,256,1024]{2,1,0:T(8,128)(2,1)S(1)} %copy-done.2, bf16[3,1024,3,256]{1,3,2,0:T(8,128)(2,1)S(1)} %bitcast.228), kind=kOutput, calls=%fused_computation.25 | convolution fusion | flops 1610612736 | bytes 6815744 | tf_op jit(solution)/shard_map/dot_general | solution.py:48
  52.3 1.8 %pad_add_fusion = f32[4,256,3,256]{3,1,2,0:T(8,128)S(1)} fusion(f32[3,256,3,256]{3,1,2,0:T(8,128)S(1)} %fusion.4, f32[4,256,3,256]{3,1,2,0:T(8,128)S(1)} %fusion.1, bf16[4,256,1024]{2,1,0:T(8,128)(2,1)S(1)} %copy-done.2, bf16[3,1024,3,256]{1,3,2,0:T(8,128)(2,1)S(1)} %bitcast.229), kind=kOutput, calls=%fused_computation.19 | convolution fusion | flops 1209532416 | bytes 11796480 | tf_op jit(solution)/shard_map/jit(_pad)/pad | solution.py:71
  54.2 3.1 %collective-permute-done.1 = f32[1,256,256]{2,1,0:T(8,128)S(1)} collective-permute-done((f32[1,256,256]{2,1,0:T(8,128)S(1)}, f32[1,256,256]{2,1,0:T(8,128)S(1)}, u32[]{:S(2)}, u32[]{:S(2)}) %collective-permute-start.1) | collective-permute-done | bytes 262176 | tf_op jit(solution)/shard_map/ppermute | solution.py:52
  58.1 5.8 %psum.7 = f32[4,256,2]{1,0,2:T(4,128)S(1)} all-reduce(f32[4,256,2]{1,0,2:T(4,128)S(1)} %pad_maximum_fusion.3), channel_id=1, replica_groups=mesh['hi'=4,'lo'=2,'chan'=4] {'chan'}, use_global_device_ids=true, to_apply=%region_2.3 | all-reduce | flops 2048 | bytes 16384 | tf_op jit(solution)/shard_map/psum | solution.py:84
  64.6 4.6 %collective-permute-start.2 = (bf16[1,256,256]{2,1,0:T(8,128)(2,1)S(1)}, bf16[1,256,256]{2,1,0:T(8,128)(2,1)S(1)}, u32[]{:S(2)}, u32[]{:S(2)}) collective-permute-start(bf16[1,256,256]{2,1,0:T(8,128)(2,1)S(1)} %slice_select_fusion), channel_id=1, source_target_pairs={{4,8},{12,16},{20,24},{8,4},{16,12},{24,20},{5,9},{13,17},{21,25},... | collective-permute-start | bytes 393224 | tf_op jit(solution)/shard_map/ppermute | solution.py:123
  70.4 3.5 %all-to-all-start.1 = ((bf16[4,256,256]{2,0,1:T(4,128)(2,1)}), bf16[4,256,256]{2,0,1:T(4,128)(2,1)S(1)}, u32[]{:S(2)}, u32[]{:S(2)}) async-start(bf16[4,256,256]{2,0,1:T(4,128)(2,1)} %copy.20), calls=%async_computation.1 | async-start | bytes 1048576 | tf_op jit(solution)/shard_map/all_to_all | solution.py:90
  74.1 1.9 %fusion.40 = f32[9,512,256]{2,1,0:T(8,128)S(1)} fusion(bf16[4,256,256]{2,1,0:T(8,128)(2,1)S(1)} %get-tuple-element.15, s32[]{:T(128)S(6)} %select_n.57, bf16[10,256,512]{1,2,0:T(8,128)(2,1)} %all-gather.5.cloned.1.call-done), kind=kOutput, calls=%fused_computation.84 | convolution fusion | flops 268435456 | bytes 3670020 | tf_op jit(solution)/shard_map/dot_general | solution.py:104
  85.6 2.1 %fusion = bf16[512,9,256]{2,0,1:T(8,128)(2,1)} fusion(f32[9,512,256]{2,1,0:T(8,128)S(1)} %fusion.32, f32[9,512,256]{2,1,0:T(8,128)S(1)} %fusion.23), kind=kLoop, calls=%fused_computation.24 | loop fusion | flops 2359296 | bytes 11796480 | tf_op jit(solution)/shard_map/convert_element_type | solution.py:116
  88.6 9.0 %convolution_convert_fusion = bf16[1024,1024]{0,1:T(8,128)(2,1)} fusion(bf16[1024,2304]{1,0:T(8,128)(2,1)S(1)} %bitcast.242, bf16[2304,1024]{1,0:T(8,128)(2,1)} %bitcast.225), kind=kOutput, calls=%fused_computation.27 | convolution fusion | flops 4832886784 | bytes 11534336 | tf_op jit(solution)/shard_map/dot_general | solution.py:137
  97.6 3.6 %all-to-all-start.2 = ((bf16[4,256,1024]{2,1,0:T(8,128)(2,1)}), bf16[4,256,1024]{2,1,0:T(8,128)(2,1)S(1)}, u32[]{:S(2)}, u32[]{:S(2)}) async-start(bf16[4,256,1024]{2,1,0:T(8,128)(2,1)} %bitcast.234), calls=%async_computation.2 | async-start | bytes 4194304 | tf_op jit(solution)/shard_map/all_to_all | solution.py:142
  102.8 24.1 %all-to-all-done.2 = bf16[4,256,1024]{2,1,0:T(8,128)(2,1)S(1)} async-done(((bf16[4,256,1024]{2,1,0:T(8,128)(2,1)}), bf16[4,256,1024]{2,1,0:T(8,128)(2,1)S(1)}, u32[]{:S(2)}, u32[]{:S(2)}) %all-to-all-start.2) | async-done | bytes 2097184 | tf_op jit(solution)/shard_map/all_to_all | solution.py:142
  128.3 7.8 %reduce-scatter.2.cloned.1.call-done = bf16[128,9,256]{2,0,1:T(8,128)(2,1)} async-done(((bf16[512,9,256]{2,0,1:T(8,128)(2,1)}), bf16[128,9,256]{2,0,1:T(8,128)(2,1)}) %reduce-scatter.2.cloned.1.call-update) | async-done | bytes 589840 | tf_op jit(solution)/shard_map/reduce_scatter | solution.py:116
  136.1 2.2 %reshape.199 = f32[128,9,256]{2,0,1:T(8,128)} convert(bf16[128,9,256]{2,0,1:T(8,128)(2,1)} %reduce-scatter.2.cloned.1.call-done) | non-fusion elementwise | flops 294912 | bytes 1769472 | tf_op jit(solution)/shard_map/reshape | solution.py:117
  (79 shorter events, 25.4 us)
Async XLA Ops:
  7.2 13.5 %copy-start.3 = (bf16[4,64,1024]{2,1,0:T(8,128)(2,1)S(1)}, bf16[4,64,1024]{2,1,0:T(8,128)(2,1)}, u32[]{:S(2)}) copy-start(bf16[4,64,1024]{2,1,0:T(8,128)(2,1)} %param.5) | copy-start | bytes 1572868
  7.2 31.7 %all-gather.3.cloned.1.call-start = ((), (), s32[]{:S(2)}) async-start(), calls=%async_computation.4 | async-start | bytes 2621440 | tf_op jit(solution)/shard_map/all_gather | solution.py:41
  9.2 7.1 %collective-permute-start.4 = (bf16[1,256,256]{1,2,0:T(8,128)(2,1)S(1)}, bf16[1,256,256]{1,2,0:T(8,128)(2,1)S(1)}, u32[]{:S(2)}, u32[]{:S(2)}) collective-permute-start(bf16[1,256,256]{1,2,0:T(8,128)(2,1)S(1)} %get-tuple-element.17), channel_id=1, source_target_pairs={{0,4},{4,8},{8,12},{12,16},{16,20},{20,24},{24,28},{1,5},{5,9},{9,... | collective-permute-start | bytes 393224 | tf_op jit(solution)/shard_map/ppermute | solution.py:16
  12.6 7.8 %collective-permute-start.5 = (bf16[1,256,256]{1,2,0:T(8,128)(2,1)S(1)}, bf16[1,256,256]{1,2,0:T(8,128)(2,1)S(1)}, u32[]{:S(2)}, u32[]{:S(2)}) collective-permute-start(bf16[1,256,256]{1,2,0:T(8,128)(2,1)S(1)} %get-tuple-element.18), channel_id=1, source_target_pairs={{4,0},{8,4},{12,8},{16,12},{20,16},{24,20},{28,24},{5,1},{9,5},{13... | collective-permute-start | bytes 393224 | tf_op jit(solution)/shard_map/ppermute | solution.py:16
  20.6 6.7 %collective-permute-start.6 = (bf16[4,256,128]{1,2,0:T(8,128)(2,1)S(1)}, bf16[4,256,128]{1,2,0:T(8,128)(2,1)S(1)}, u32[]{:S(2)}, u32[]{:S(2)}) collective-permute-start(bf16[4,256,128]{1,2,0:T(8,128)(2,1)S(1)} %dynamic-slice_bitcast_fusion.1), channel_id=1, source_target_pairs={{0,4},{4,0},{1,5},{5,1},{2,6},{6,2},{3,7},{7,3},{8,12},{12,8},{9,1... | collective-permute-start | bytes 786440 | tf_op jit(solution)/shard_map/ppermute | solution.py:63
  22.9 14.5 %all-to-all-start = ((bf16[4,2,32768]{2,1,0:T(2,128)(2,1)}), bf16[4,2,32768]{2,1,0:T(2,128)(2,1)S(1)}, u32[]{:S(2)}, u32[]{:S(2)}) async-start(bf16[4,2,32768]{2,1,0:T(2,128)(2,1)} %reshape.228), calls=%async_computation | async-start | bytes 1048576 | tf_op jit(solution)/shard_map/all_to_all | solution.py:40
  26.4 47.7 %all-gather.5.cloned.1.call-start = ((), (), s32[]{:S(2)}) async-start(), calls=%async_computation.5 | async-start | bytes 3276800 | tf_op jit(solution)/shard_map/all_gather | solution.py:68
  38.9 5.9 %copy-start.1 = (bf16[3,3,1024,256]{2,3,1,0:T(8,128)(2,1)S(1)}, bf16[3,3,1024,256]{2,3,1,0:T(8,128)(2,1)}, u32[]{:S(2)}) copy-start(bf16[3,3,1024,256]{2,3,1,0:T(8,128)(2,1)} %copy.17) | copy-start | bytes 14155780
  38.9 10.2 %copy-start.2 = (bf16[4,256,1024]{2,1,0:T(8,128)(2,1)S(1)}, bf16[4,256,1024]{2,1,0:T(8,128)(2,1)}, u32[]{:S(2)}) copy-start(bf16[4,256,1024]{2,1,0:T(8,128)(2,1)} %all-gather.3.cloned.1.call-done) | copy-start | bytes 6291460
  41.3 12.9 %collective-permute-start = (f32[1,256,256]{2,1,0:T(8,128)S(1)}, f32[1,256,256]{2,1,0:T(8,128)S(1)}, u32[]{:S(2)}, u32[]{:S(2)}) collective-permute-start(f32[1,256,256]{2,1,0:T(8,128)S(1)} %fusion.61), channel_id=1, source_target_pairs={{0,4},{4,8},{8,12},{12,16},{16,20},{20,24},{24,28},{1,5},{5,9},{9,... | collective-permute-start | bytes 786440 | tf_op jit(solution)/shard_map/ppermute | solution.py:51
  46.6 10.6 %collective-permute-start.1 = (f32[1,256,256]{2,1,0:T(8,128)S(1)}, f32[1,256,256]{2,1,0:T(8,128)S(1)}, u32[]{:S(2)}, u32[]{:S(2)}) collective-permute-start(f32[1,256,256]{2,1,0:T(8,128)S(1)} %fusion.64), channel_id=1, source_target_pairs={{4,0},{8,4},{12,8},{16,12},{20,16},{24,20},{28,24},{5,1},{9,5},{13... | collective-permute-start | bytes 786440 | tf_op jit(solution)/shard_map/ppermute | solution.py:52
  64.2 16.5 %collective-permute-start.3 = (bf16[4,256,256]{2,1,0:T(8,128)(2,1)S(1)}, bf16[4,256,256]{2,1,0:T(8,128)(2,1)S(1)}, u32[]{:S(2)}, u32[]{:S(2)}) collective-permute-start(bf16[4,256,256]{2,1,0:T(8,128)(2,1)S(1)} %get-tuple-element.15), channel_id=1, source_target_pairs={{0,4},{4,0},{1,5},{5,1},{2,6},{6,2},{3,7},{7,3},{8,12},{12,8},{9,1... | collective-permute-start | bytes 1572872 | tf_op jit(solution)/shard_map/ppermute | solution.py:92
  64.6 23.1 %collective-permute-start.2 = (bf16[1,256,256]{2,1,0:T(8,128)(2,1)S(1)}, bf16[1,256,256]{2,1,0:T(8,128)(2,1)S(1)}, u32[]{:S(2)}, u32[]{:S(2)}) collective-permute-start(bf16[1,256,256]{2,1,0:T(8,128)(2,1)S(1)} %slice_select_fusion), channel_id=1, source_target_pairs={{4,8},{12,16},{20,24},{8,4},{16,12},{24,20},{5,9},{13,17},{21,25},... | collective-permute-start | bytes 393224 | tf_op jit(solution)/shard_map/ppermute | solution.py:123
  70.4 27.2 %all-to-all-start.1 = ((bf16[4,256,256]{2,0,1:T(4,128)(2,1)}), bf16[4,256,256]{2,0,1:T(4,128)(2,1)S(1)}, u32[]{:S(2)}, u32[]{:S(2)}) async-start(bf16[4,256,256]{2,0,1:T(4,128)(2,1)} %copy.20), calls=%async_computation.1 | async-start | bytes 1048576 | tf_op jit(solution)/shard_map/all_to_all | solution.py:90
  73.9 62.2 %reduce-scatter.2.cloned.1.call-start = ((), (), s32[]{:S(2)}) async-start(), calls=%async_computation.6 | async-start | bytes 2949120 | tf_op jit(solution)/shard_map/reduce_scatter | solution.py:116
  74.1 2.1 %copy-start = (bf16[10,256,512]{1,2,0:T(8,128)(2,1)S(1)}, bf16[10,256,512]{1,2,0:T(8,128)(2,1)}, u32[]{:S(2)}) copy-start(bf16[10,256,512]{1,2,0:T(8,128)(2,1)} %all-gather.5.cloned.1.call-done) | copy-start | bytes 7864324
  97.6 29.3 %all-to-all-start.2 = ((bf16[4,256,1024]{2,1,0:T(8,128)(2,1)}), bf16[4,256,1024]{2,1,0:T(8,128)(2,1)S(1)}, u32[]{:S(2)}, u32[]{:S(2)}) async-start(bf16[4,256,1024]{2,1,0:T(8,128)(2,1)} %bitcast.234), calls=%async_computation.2 | async-start | bytes 4194304 | tf_op jit(solution)/shard_map/all_to_all | solution.py:142
Sparse Core Ops, SparseCore 0:
  9.6 26.3 all-gather.2
  38.1 25.5 all-gather.4
  87.8 48.2 reduce-scatter.1

commit v18 on v10

--- a/solution.py
+++ b/solution.py
@@ -37,8 +37,9 @@
     piece = all_chans // (n_hi * n_lo)
     per_chan = local_chans // (n_lo * piece)
 
-    grad_filters = lax.all_to_all(grad_out, "chan", split_axis=2, concat_axis=1, tiled=True)
     gathered = lax.all_gather(image, "chan", axis=2, tiled=True)
+    grad_late, _ = lax.optimization_barrier((grad_out, gathered))
+    grad_filters = lax.all_to_all(grad_late, "chan", split_axis=2, concat_axis=1, tiled=True)
 
     by_row = jnp.transpose(weight, (0, 2, 1, 3)).reshape(3, all_chans, 3 * local_filters)
 

time: 147 us -> 157 us (1.068)
  other arithmetic: 7.46 us -> 11.9 us
  waiting for transfers between devices: 44.5 us -> 46.6 us
  matrix products: 29 us -> 30.9 us
    ppermute x1, waiting for transfers between devices: 0.75 us -> 6.56 us  [on_device(): lax.ppermute(local_subset(send_rows, 1 - lo), 'lo', [(0, 1), (1, 0)])]
    ppermute x1, waiting for transfers between devices: 3.07 us -> 0.01 us  [on_device(): lax.ppermute(shift_sum(taps(gathered[:1], 2)), SLAB, [(i + 1, i) for i in...]
    dot_general x4, matrix products: 7.27 us -> 9.24 us  [taps(): out = jnp.dot(flat, by_row[a], preferred_element_type=jnp.float32)]
    reduce_sum x1, other arithmetic: 0.42 us -> 2.26 us  [on_device(): jnp.sum(conv_wide * conv_wide, axis=-1)]
    optimization_barrier x0 -> x1, local copies, waits for them, and re-layouts: none -> 1.61 us  [on_device(): grad_late, _ = lax.optimization_barrier((grad_out, gathered))]
    unnamed x20 -> x19, local copies, waits for them, and re-layouts: 12.5 us -> 11.8 us
  transfers between devices with their start and end apart: 13 -> 13, of which waited for: 8 -> 6; matrix products, arithmetic and copies ran while one was open for 34% -> 37% of each run, Pallas kernels for 0% -> 0%
where the time goes in v18:
time: 157 us; the launch traced here: 155 us
  waiting for transfers between devices  46.6 us (30%)
  matrix products  30.9 us (20%)
  starting transfers between devices  27.7 us (18%)
  local copies, waits for them, and re-layouts  17.1 us (11%)
  between operations  14.3 us (9%)
  other arithmetic  11.9 us (8%)
  blocking collectives  6.03 us (4%)
    all_to_all x1, waiting for transfers between devices, on_device(): lax.all_to_all(split, 'chan', split_axis=0, concat_axis=0, tiled=True)  24.1 us
    unnamed x19, local copies, waits for them, and re-layouts  11.8 us
    dot_general x18, matrix products, pair_part(): lax.dot_general(weight_window, flat, (((0,), (0,)), ((), ())), preferred_...  10.9 us
    dot_general x4, matrix products, taps(): out = jnp.dot(flat, by_row[a], preferred_element_type=jnp.float32)  9.24 us
    dot_general x1, matrix products, on_device(): lax.dot_general(by_filter, columns, (((0,), (1,)), ((), ())), preferred_e...  8.97 us
    reduce_scatter x1, waiting for transfers between devices, on_device(): lax.psum_scatter(stacked.astype(jnp.bfloat16), 'hi', scatter_dimension=2,...  7.85 us
    ppermute x1, waiting for transfers between devices, on_device(): lax.ppermute(local_subset(send_rows, 1 - lo), 'lo', [(0, 1), (1, 0)])  6.56 us
    psum x1, blocking collectives, on_device(): totals = lax.psum(partial, 'chan')  6.03 us
  transfers between devices with their start and end apart: 13, of which 6 were waited for; matrix products, arithmetic and copies ran while one was open for 37% of the time, Pallas kernels for 0%

profile of v18, /device:TPU:4, one launch (start us, length us, event | category | flops | bytes accessed | tf_op | source)
XLA Modules:
  0.0 154.6 jit_solution(18255715370087004218)
XLA Ops:
  9.2 3.4 %collective-permute-start.4 = (bf16[1,256,256]{1,2,0:T(8,128)(2,1)S(1)}, bf16[1,256,256]{1,2,0:T(8,128)(2,1)S(1)}, u32[]{:S(2)}, u32[]{:S(2)}) collective-permute-start(bf16[1,256,256]{1,2,0:T(8,128)(2,1)S(1)} %get-tuple-element.19), channel_id=1, source_target_pairs={{0,4},{4,8},{8,12},{12,16},{16,20},{20,24},{24,28},{1,5},{5,9},{9,... | collective-permute-start | bytes 393224 | tf_op jit(solution)/shard_map/ppermute | solution.py:16
  12.7 2.4 %collective-permute-start.5 = (bf16[1,256,256]{1,2,0:T(8,128)(2,1)S(1)}, bf16[1,256,256]{1,2,0:T(8,128)(2,1)S(1)}, u32[]{:S(2)}, u32[]{:S(2)}) collective-permute-start(bf16[1,256,256]{1,2,0:T(8,128)(2,1)S(1)} %get-tuple-element.20), channel_id=1, source_target_pairs={{4,0},{8,4},{12,8},{16,12},{20,16},{24,20},{28,24},{5,1},{9,5},{13... | collective-permute-start | bytes 393224 | tf_op jit(solution)/shard_map/ppermute | solution.py:16
  16.4 4.1 %collective-permute-done.5 = bf16[1,256,256]{1,2,0:T(8,128)(2,1)S(1)} collective-permute-done((bf16[1,256,256]{1,2,0:T(8,128)(2,1)S(1)}, bf16[1,256,256]{1,2,0:T(8,128)(2,1)S(1)}, u32[]{:S(2)}, u32[]{:S(2)}) %collective-permute-start.5) | collective-permute-done | bytes 131104 | tf_op jit(solution)/shard_map/ppermute | solution.py:16
  20.7 6.6 %collective-permute-done.6 = bf16[4,256,128]{1,2,0:T(8,128)(2,1)S(1)} collective-permute-done((bf16[4,256,128]{1,2,0:T(8,128)(2,1)S(1)}, bf16[4,256,128]{1,2,0:T(8,128)(2,1)S(1)}, u32[]{:S(2)}, u32[]{:S(2)}) %collective-permute-start.6) | collective-permute-done | bytes 262176 | tf_op jit(solution)/shard_map/ppermute | solution.py:64
  28.5 6.7 %copy.17 = bf16[3,3,1024,256]{2,3,1,0:T(8,128)(2,1)} copy(bf16[3,3,1024,256]{3,2,1,0:T(8,128)(2,1)} %param.4) | data formatting | bytes 9437184 | tf_op args[1]
  35.2 2.3 %fusion.14 = f32[1,256,3,256]{3,1,2,0:T(8,128)S(1)} fusion(bf16[3,1024,3,256]{1,3,2,0:T(8,128)(2,1)} %bitcast.221, bf16[4,256,1024]{2,1,0:T(8,128)(2,1)} %all-gather.3.cloned.1.call-done), kind=kOutput, calls=%fused_computation.44 | convolution fusion | flops 402653184 | bytes 2883584 | tf_op jit(solution)/shard_map/dot_general | solution.py:49
  38.3 3.8 %collective-permute-start = (f32[1,256,256]{2,1,0:T(8,128)}, f32[1,256,256]{2,1,0:T(8,128)S(1)}, u32[]{:S(2)}, u32[]{:S(2)}) collective-permute-start(f32[1,256,256]{2,1,0:T(8,128)} %fusion.60), channel_id=1, source_target_pairs={{0,4},{4,8},{8,12},{12,16},{16,20},{20,24},{24,28},{1,5},{5,9},{9,... | collective-permute-start | bytes 786440 | tf_op jit(solution)/shard_map/ppermute | solution.py:52
  42.2 2.1 %fusion.17 = f32[1,256,3,256]{3,1,2,0:T(8,128)S(1)} fusion(bf16[3,1024,3,256]{1,3,2,0:T(8,128)(2,1)} %bitcast.222, bf16[4,256,1024]{2,1,0:T(8,128)(2,1)S(1)} %copy-done.1), kind=kOutput, calls=%fused_computation.45 | convolution fusion | flops 402653184 | bytes 2883584 | tf_op jit(solution)/shard_map/dot_general | solution.py:49
  45.1 2.0 %collective-permute-start.1 = (f32[1,256,256]{2,1,0:T(8,128)}, f32[1,256,256]{2,1,0:T(8,128)}, u32[]{:S(2)}, u32[]{:S(2)}) collective-permute-start(f32[1,256,256]{2,1,0:T(8,128)} %fusion.63), channel_id=1, source_target_pairs={{4,0},{8,4},{12,8},{16,12},{20,16},{24,20},{28,24},{5,1},{9,5},{13... | collective-permute-start | bytes 786440 | tf_op jit(solution)/shard_map/ppermute | solution.py:53
  50.2 3.6 %all-to-all-start = ((bf16[4,2,32768]{2,1,0:T(2,128)(2,1)}), bf16[4,2,32768]{2,1,0:T(2,128)(2,1)S(1)}, u32[]{:S(2)}, u32[]{:S(2)}) async-start(bf16[4,2,32768]{2,1,0:T(2,128)(2,1)} %reshape.219), calls=%async_computation | async-start | bytes 1048576 | tf_op jit(solution)/shard_map/all_to_all | solution.py:42
  53.9 3.0 %fusion.3 = f32[3,256,3,256]{3,1,2,0:T(8,128)S(1)} fusion(bf16[4,256,1024]{2,1,0:T(8,128)(2,1)S(1)} %copy-done.1, bf16[3,1024,3,256]{1,3,2,0:T(8,128)(2,1)} %bitcast.223), kind=kOutput, calls=%fused_computation.29 | convolution fusion | flops 1207959552 | bytes 5505024 | tf_op jit(solution)/shard_map/dot_general | solution.py:49
  58.7 1.8 %pad_add_fusion = f32[4,256,3,256]{3,1,2,0:T(8,128)S(1)} fusion(f32[3,256,3,256]{3,1,2,0:T(8,128)S(1)} %fusion.3, f32[4,256,3,256]{3,1,2,0:T(8,128)S(1)} %fusion, bf16[4,256,1024]{2,1,0:T(8,128)(2,1)S(1)} %copy-done.1, bf16[3,1024,3,256]{1,3,2,0:T(8,128)(2,1)S(1)} %bitcast.228), kind=kOutput, calls=%fused_computation.19 | convolution fusion | flops 1209532416 | bytes 11796480 | tf_op jit(solution)/shard_map/jit(_pad)/pad | solution.py:72
  60.5 2.3 %fusion.43 = (f32[4,256]{1,0:T(4,128)S(1)}, bf16[4,256,256]{2,1,0:T(8,128)(2,1)S(1)}, f32[4,256,1,256]{3,1,2,0:T(8,128)}) fusion(f32[1,256,256]{2,1,0:T(8,128)} %collective-permute-done.1, f32[4]{0:T(128)S(1)} %pad.53.clone, f32[1,256,256]{2,1,0:T(8,128)S(1)} %collective-permute-done, f32[4,256,3,256]{3,1,2,0:T(8,128)S(1)} %pad_add_fusion), kind=kLoop, calls=%fused_computation.87 | loop fusion | flops 2358272 | bytes 6296064 | tf_op jit(solution)/shard_map/reduce_sum | solution.py:83
  62.8 2.0 %all-to-all-done = bf16[4,2,32768]{2,1,0:T(2,128)(2,1)S(1)} async-done(((bf16[4,2,32768]{2,1,0:T(2,128)(2,1)}), bf16[4,2,32768]{2,1,0:T(2,128)(2,1)S(1)}, u32[]{:S(2)}, u32[]{:S(2)}) %all-to-all-start) | async-done | bytes 524320 | tf_op jit(solution)/shard_map/all_to_all | solution.py:42
  67.9 6.0 %psum.7 = f32[4,256,2]{1,0,2:T(4,128)S(1)} all-reduce(f32[4,256,2]{1,0,2:T(4,128)S(1)} %pad_maximum_fusion.3), channel_id=1, replica_groups=mesh['hi'=4,'lo'=2,'chan'=4] {'chan'}, use_global_device_ids=true, to_apply=%region_2.3 | all-reduce | flops 2048 | bytes 16384 | tf_op jit(solution)/shard_map/psum | solution.py:85
  74.7 4.5 %collective-permute-start.2 = (bf16[1,256,256]{2,1,0:T(8,128)(2,1)S(1)}, bf16[1,256,256]{2,1,0:T(8,128)(2,1)S(1)}, u32[]{:S(2)}, u32[]{:S(2)}) collective-permute-start(bf16[1,256,256]{2,1,0:T(8,128)(2,1)S(1)} %slice_select_fusion), channel_id=1, source_target_pairs={{4,8},{12,16},{20,24},{8,4},{16,12},{24,20},{5,9},{13,17},{21,25},... | collective-permute-start | bytes 393224 | tf_op jit(solution)/shard_map/ppermute | solution.py:123
  80.4 3.5 %all-to-all-start.1 = ((bf16[4,256,256]{2,0,1:T(4,128)(2,1)}), bf16[4,256,256]{2,0,1:T(4,128)(2,1)S(1)}, u32[]{:S(2)}, u32[]{:S(2)}) async-start(bf16[4,256,256]{2,0,1:T(4,128)(2,1)} %copy.20), calls=%async_computation.1 | async-start | bytes 1048576 | tf_op jit(solution)/shard_map/all_to_all | solution.py:91
  84.2 1.9 %fusion.39 = f32[9,512,256]{2,1,0:T(8,128)S(1)} fusion(bf16[4,256,256]{2,1,0:T(8,128)(2,1)S(1)} %get-tuple-element.17, s32[]{:T(128)S(6)} %select_n.57, bf16[10,256,512]{1,2,0:T(8,128)(2,1)} %all-gather.5.cloned.1.call-done), kind=kOutput, calls=%fused_computation.83 | convolution fusion | flops 268435456 | bytes 3670020 | tf_op jit(solution)/shard_map/dot_general | solution.py:105
  95.4 2.1 %add_convert_fusion = bf16[9,512,256]{2,1,0:T(8,128)(2,1)} fusion(f32[9,512,256]{2,1,0:T(8,128)S(1)} %fusion.31, f32[9,512,256]{2,1,0:T(8,128)S(1)} %fusion.22), kind=kLoop, calls=%fused_computation.18 | loop fusion | flops 2359296 | bytes 11796480 | tf_op jit(solution)/shard_map/convert_element_type | solution.py:118
  98.4 9.0 %convolution_convert_fusion = bf16[1024,1024]{0,1:T(8,128)(2,1)} fusion(bf16[1024,2304]{1,0:T(8,128)(2,1)S(1)} %bitcast.239, bf16[2304,1024]{1,0:T(8,128)(2,1)} %bitcast.224), kind=kOutput, calls=%fused_computation.26 | convolution fusion | flops 4832886784 | bytes 11534336 | tf_op jit(solution)/shard_map/dot_general | solution.py:137
  107.4 3.6 %all-to-all-start.2 = ((bf16[4,256,1024]{2,1,0:T(8,128)(2,1)}), bf16[4,256,1024]{2,1,0:T(8,128)(2,1)S(1)}, u32[]{:S(2)}, u32[]{:S(2)}) async-start(bf16[4,256,1024]{2,1,0:T(8,128)(2,1)} %bitcast.233), calls=%async_computation.2 | async-start | bytes 4194304 | tf_op jit(solution)/shard_map/all_to_all | solution.py:142
  112.5 24.1 %all-to-all-done.2 = bf16[4,256,1024]{2,1,0:T(8,128)(2,1)S(1)} async-done(((bf16[4,256,1024]{2,1,0:T(8,128)(2,1)}), bf16[4,256,1024]{2,1,0:T(8,128)(2,1)S(1)}, u32[]{:S(2)}, u32[]{:S(2)}) %all-to-all-start.2) | async-done | bytes 2097184 | tf_op jit(solution)/shard_map/all_to_all | solution.py:142
  138.1 7.8 %reduce-scatter.2.cloned.1.call-done = bf16[3,3,128,256]{3,2,1,0:T(8,128)(2,1)} async-done(((bf16[3,3,512,256]{3,2,1,0:T(8,128)(2,1)}), bf16[3,3,128,256]{3,2,1,0:T(8,128)(2,1)}) %reduce-scatter.2.cloned.1.call-update) | async-done | bytes 589840 | tf_op jit(solution)/shard_map/reduce_scatter | solution.py:117
  145.9 2.2 %convert_element_type.84 = f32[3,3,128,256]{3,2,1,0:T(8,128)} convert(bf16[3,3,128,256]{3,2,1,0:T(8,128)(2,1)} %reduce-scatter.2.cloned.1.call-done) | non-fusion elementwise | flops 294912 | bytes 1769472 | tf_op jit(solution)/shard_map/convert_element_type | solution.py:119
  (80 shorter events, 29.5 us)
Async XLA Ops:
  7.2 28.1 %all-gather.3.cloned.1.call-start = ((), (), s32[]{:S(2)}) async-start(), calls=%async_computation.4 | async-start | bytes 2621440 | tf_op jit(solution)/shard_map/all_gather | solution.py:40
  7.9 76.2 %all-gather.5.cloned.1.call-start = ((), (), s32[]{:S(2)}) async-start(), calls=%async_computation.5 | async-start | bytes 3276800 | tf_op jit(solution)/shard_map/all_gather | solution.py:69
  9.2 7.1 %collective-permute-start.4 = (bf16[1,256,256]{1,2,0:T(8,128)(2,1)S(1)}, bf16[1,256,256]{1,2,0:T(8,128)(2,1)S(1)}, u32[]{:S(2)}, u32[]{:S(2)}) collective-permute-start(bf16[1,256,256]{1,2,0:T(8,128)(2,1)S(1)} %get-tuple-element.19), channel_id=1, source_target_pairs={{0,4},{4,8},{8,12},{12,16},{16,20},{20,24},{24,28},{1,5},{5,9},{9,... | collective-permute-start | bytes 393224 | tf_op jit(solution)/shard_map/ppermute | solution.py:16
  12.7 7.8 %collective-permute-start.5 = (bf16[1,256,256]{1,2,0:T(8,128)(2,1)S(1)}, bf16[1,256,256]{1,2,0:T(8,128)(2,1)S(1)}, u32[]{:S(2)}, u32[]{:S(2)}) collective-permute-start(bf16[1,256,256]{1,2,0:T(8,128)(2,1)S(1)} %get-tuple-element.20), channel_id=1, source_target_pairs={{4,0},{8,4},{12,8},{16,12},{20,16},{24,20},{28,24},{5,1},{9,5},{13... | collective-permute-start | bytes 393224 | tf_op jit(solution)/shard_map/ppermute | solution.py:16
  20.6 6.7 %collective-permute-start.6 = (bf16[4,256,128]{1,2,0:T(8,128)(2,1)S(1)}, bf16[4,256,128]{1,2,0:T(8,128)(2,1)S(1)}, u32[]{:S(2)}, u32[]{:S(2)}) collective-permute-start(bf16[4,256,128]{1,2,0:T(8,128)(2,1)S(1)} %dynamic-slice_bitcast_fusion.1), channel_id=1, source_target_pairs={{0,4},{4,0},{1,5},{5,1},{2,6},{6,2},{3,7},{7,3},{8,12},{12,8},{9,1... | collective-permute-start | bytes 786440 | tf_op jit(solution)/shard_map/ppermute | solution.py:64
  35.2 6.9 %copy-start.1 = (bf16[4,256,1024]{2,1,0:T(8,128)(2,1)S(1)}, bf16[4,256,1024]{2,1,0:T(8,128)(2,1)}, u32[]{:S(2)}) copy-start(bf16[4,256,1024]{2,1,0:T(8,128)(2,1)} %all-gather.3.cloned.1.call-done) | copy-start | bytes 6291460
  38.3 22.2 %collective-permute-start = (f32[1,256,256]{2,1,0:T(8,128)}, f32[1,256,256]{2,1,0:T(8,128)S(1)}, u32[]{:S(2)}, u32[]{:S(2)}) collective-permute-start(f32[1,256,256]{2,1,0:T(8,128)} %fusion.60), channel_id=1, source_target_pairs={{0,4},{4,8},{8,12},{12,16},{16,20},{20,24},{24,28},{1,5},{5,9},{9,... | collective-permute-start | bytes 786440 | tf_op jit(solution)/shard_map/ppermute | solution.py:52
  45.1 15.5 %collective-permute-start.1 = (f32[1,256,256]{2,1,0:T(8,128)}, f32[1,256,256]{2,1,0:T(8,128)}, u32[]{:S(2)}, u32[]{:S(2)}) collective-permute-start(f32[1,256,256]{2,1,0:T(8,128)} %fusion.63), channel_id=1, source_target_pairs={{4,0},{8,4},{12,8},{16,12},{20,16},{24,20},{28,24},{5,1},{9,5},{13... | collective-permute-start | bytes 786440 | tf_op jit(solution)/shard_map/ppermute | solution.py:53
  50.2 6.6 %slice-start = ((s8[4718592]{0:T(1024)(128)(4,1)}), s8[524288]{0:T(1024)(128)(4,1)S(1)}, s32[]{:S(2)}) async-start(s8[4718592]{0:T(1024)(128)(4,1)} %bitcast.225), calls=%async_computation.7 | async-start | bytes 1048576
  50.2 14.6 %all-to-all-start = ((bf16[4,2,32768]{2,1,0:T(2,128)(2,1)}), bf16[4,2,32768]{2,1,0:T(2,128)(2,1)S(1)}, u32[]{:S(2)}, u32[]{:S(2)}) async-start(bf16[4,2,32768]{2,1,0:T(2,128)(2,1)} %reshape.219), calls=%async_computation | async-start | bytes 1048576 | tf_op jit(solution)/shard_map/all_to_all | solution.py:42
  53.8 3.0 %slice-start.1 = ((s8[4718592]{0:T(1024)(128)(4,1)}), s8[4194304]{0:T(1024)(128)(4,1)S(1)}, s32[]{:S(2)}) async-start(s8[4718592]{0:T(1024)(128)(4,1)} %bitcast.225), calls=%async_computation.8 | async-start | bytes 8388608
  74.3 16.3 %collective-permute-start.3 = (bf16[4,256,256]{2,1,0:T(8,128)(2,1)S(1)}, bf16[4,256,256]{2,1,0:T(8,128)(2,1)S(1)}, u32[]{:S(2)}, u32[]{:S(2)}) collective-permute-start(bf16[4,256,256]{2,1,0:T(8,128)(2,1)S(1)} %get-tuple-element.17), channel_id=1, source_target_pairs={{0,4},{4,0},{1,5},{5,1},{2,6},{6,2},{3,7},{7,3},{8,12},{12,8},{9,1... | collective-permute-start | bytes 1572872 | tf_op jit(solution)/shard_map/ppermute | solution.py:93
  74.7 22.7 %collective-permute-start.2 = (bf16[1,256,256]{2,1,0:T(8,128)(2,1)S(1)}, bf16[1,256,256]{2,1,0:T(8,128)(2,1)S(1)}, u32[]{:S(2)}, u32[]{:S(2)}) collective-permute-start(bf16[1,256,256]{2,1,0:T(8,128)(2,1)S(1)} %slice_select_fusion), channel_id=1, source_target_pairs={{4,8},{12,16},{20,24},{8,4},{16,12},{24,20},{5,9},{13,17},{21,25},... | collective-permute-start | bytes 393224 | tf_op jit(solution)/shard_map/ppermute | solution.py:123
  80.4 26.9 %all-to-all-start.1 = ((bf16[4,256,256]{2,0,1:T(4,128)(2,1)}), bf16[4,256,256]{2,0,1:T(4,128)(2,1)S(1)}, u32[]{:S(2)}, u32[]{:S(2)}) async-start(bf16[4,256,256]{2,0,1:T(4,128)(2,1)} %copy.20), calls=%async_computation.1 | async-start | bytes 1048576 | tf_op jit(solution)/shard_map/all_to_all | solution.py:91
  83.9 62.0 %reduce-scatter.2.cloned.1.call-start = ((), (), s32[]{:S(2)}) async-start(), calls=%async_computation.6 | async-start | bytes 2949120 | tf_op jit(solution)/shard_map/reduce_scatter | solution.py:117
  84.2 2.1 %copy-start = (bf16[10,256,512]{1,2,0:T(8,128)(2,1)S(1)}, bf16[10,256,512]{1,2,0:T(8,128)(2,1)}, u32[]{:S(2)}) copy-start(bf16[10,256,512]{1,2,0:T(8,128)(2,1)} %all-gather.5.cloned.1.call-done) | copy-start | bytes 7864324
  107.4 29.3 %all-to-all-start.2 = ((bf16[4,256,1024]{2,1,0:T(8,128)(2,1)}), bf16[4,256,1024]{2,1,0:T(8,128)(2,1)S(1)}, u32[]{:S(2)}, u32[]{:S(2)}) async-start(bf16[4,256,1024]{2,1,0:T(8,128)(2,1)} %bitcast.233), calls=%async_computation.2 | async-start | bytes 4194304 | tf_op jit(solution)/shard_map/all_to_all | solution.py:142
Sparse Core Ops, SparseCore 0:
  9.5 24.0 all-gather.2
  35.2 27.8 all-gather.4
  97.6 48.2 reduce-scatter.1
